TPU v7x, 32 devices: a whole 2x2x4 slice. The times are simulated.
32 devices in a mesh: visit: 4 (over z), row: 2 (over core), col: 4 (over y, x).
Axes of the slice: x: 2, y: 2, z: 4, core: 2. Of those that a mesh axis runs over, the one named last changes fastest.
Arguments:
- images: bfloat16 [16, 1024, 2048], P('visit', 'row', 'col'), may hold values from -10 to 10, as said below
- coeffs: float32 [16, 3], P('visit'), may hold values from 0.3 to 1.2
- pair_list: int32 [8, 3], replicated, may hold values from 0 to 480, as said below
- weights: bfloat16 [16, 2, 4], P('visit', 'row', 'col'), may hold values from 0.5 to 4
- resample_bank: bfloat16 [12, 512, 512], replicated, may hold values from -0.25 to 0.25
- warp_index: int32 [16, 2, 4, 2], P('visit', 'row', 'col'), may hold values from 0 to 11
- destinations: int32 [16, 2, 4, 4], P('visit', 'row', 'col'), may hold values from 0 to 3, as said below
- counts: int32 [16, 2, 4], P('visit', 'row', 'col'), may hold values from 3 to 4
Outputs:
- coadd_patch: float32 [4, 1024, 2048], P('visit', 'row', 'col')
- plane_fit: float32 [16, 3], P('visit')
Inputs may be any that keep to these rules, and one draw needn't show every extreme that they name: `images`: noise plus a per-exposure sky plane. `pair_list`: every exposure appears in exactly one pair; offsets lie in 0 to 480, both ends used. `destinations`: the used entries of one tile's list are distinct; each tile lists the patch of its own visit index; a patch drawn with skew, which may be the device's own visit patch, is listed by all 4 tiles at each device position.
All inputs are finite; a program needn't handle non-finite values.
Results may differ from a plain program's by a relative error of at most 0.015.
Values may be sent and summed in bfloat16 or wider, within the bound.
No kernel may reach another device: no remote copies, remote signals or barrier semaphores. Data moves between devices by JAX's collectives and lax.ppermute only.
A program may use at most 192 MiB of HBM per device.

v0:
```python
import jax
import jax.numpy as jnp
from jax import lax
from jax.sharding import PartitionSpec as P

HALO = 16
STRIP = 32
MAXD = 4


SIGMA_PARTS = (0.0625, 0.125, 0.25)


def extended(value, sides, width):
    for axis, dim in sides:
        devices, length = (lax.axis_size(axis), value.shape[dim])
        up = [(i, (i + 1) % devices) for i in range(devices - 1)]
        down = [(j, i) for i, j in up]
        last = lax.slice_in_dim(value, length - width, length, axis=dim)
        initial = lax.slice_in_dim(value, 0, width, axis=dim)
        before = lax.ppermute(last, axis, up)
        after = lax.ppermute(initial, axis, down)
        value = jnp.concatenate([before, value, after], axis=dim)
    return value


def band_table(length, width, sigma):
    spread = (jnp.arange(2 * width + 1) - width).astype(jnp.float32)
    curve = jnp.exp(-spread * spread / (2.0 * sigma * sigma))
    total = jnp.sum(curve)
    rows_grid = lax.broadcasted_iota(jnp.int32, (length, length + 2 * width), 0)
    cols_grid = lax.broadcasted_iota(jnp.int32, (length, length + 2 * width), 1)
    offset = (cols_grid - rows_grid - width).astype(jnp.float32)
    values = jnp.exp(-offset * offset / (2.0 * sigma * sigma)) / total
    return jnp.where(jnp.abs(offset) <= width, values, 0.0).astype(jnp.bfloat16)


def centred(index, length):
    return (index.astype(jnp.float32) + 0.5) / length * 2.0 - 1.0


def solve_three(normal, moments):
    lower = jnp.linalg.cholesky(normal)
    first = moments[..., 0] / lower[..., 0, 0]
    second = (moments[..., 1] - lower[..., 1, 0] * first) / lower[..., 1, 1]
    third = (moments[..., 2] - lower[..., 2, 0] * first - lower[..., 2, 1] * second) / lower[
        ..., 2, 2
    ]
    upper_top = third / lower[..., 2, 2]
    upper_mid = (second - lower[..., 2, 1] * upper_top) / lower[..., 1, 1]
    upper_low = (first - lower[..., 1, 0] * upper_mid - lower[..., 2, 0] * upper_top) / lower[
        ..., 0, 0
    ]
    return jnp.stack([upper_low, upper_mid, upper_top], -1)


def rows_from(source, anchor):
    return lax.dynamic_slice_in_dim(source, anchor, STRIP, 0)


def shards(images, coeffs, pair_list, weights, resample_bank, warp_index, destinations, counts):
    exp_dev = images.shape[0]
    tile_len = images.shape[1]
    row_count = lax.axis_size("row")
    col_count = lax.axis_size("col")
    visit_count = lax.axis_size("visit")
    row_pos = lax.axis_index("row")
    col_pos = lax.axis_index("col")
    visit_pos = lax.axis_index("visit")
    height = row_count * tile_len
    breadth = col_count * tile_len
    padded = extended(images, (("row", 1), ("col", 2)), HALO)
    matched = jnp.zeros((exp_dev, tile_len, tile_len), jnp.float32)
    for kernel in range(len(SIGMA_PARTS)):
        table = band_table(tile_len, HALO, HALO * SIGMA_PARTS[kernel])
        across = jnp.einsum(
            "ij,ejl->eil", table, padded, preferred_element_type=jnp.float32
        ).astype(jnp.bfloat16)
        smoothed = jnp.einsum("eil,ml->eim", across, table, preferred_element_type=jnp.float32)
        matched = matched + coeffs[:, kernel, None, None] * smoothed
    own_ids = visit_pos * exp_dev + jnp.arange(exp_dev, dtype=jnp.int32)
    first_col = pair_list[:, 0]
    second_col = pair_list[:, 1]
    offsets = pair_list[:, 2]
    hit_first = first_col[None, :] == own_ids[:, None]
    hit_second = second_col[None, :] == own_ids[:, None]
    partner = jnp.sum(
        jnp.where(hit_first, second_col[None, :], 0) + jnp.where(hit_second, first_col[None, :], 0),
        axis=1,
    )
    offset = jnp.sum(jnp.where(hit_first | hit_second, offsets[None, :], 0), axis=1)
    own_strip = jax.vmap(rows_from)(images, offset)
    everyone = lax.all_gather(own_strip, "visit", axis=0, tiled=True)
    theirs = jnp.take(everyone, partner, axis=0).astype(jnp.float32)
    nearby = jax.vmap(rows_from)(matched, offset)
    difference = nearby - theirs
    pixel_weight = 1.0 / (1.0 + theirs * theirs)
    strip_rows = row_pos * tile_len + offset[:, None] + jnp.arange(STRIP, dtype=jnp.int32)[None, :]
    ycoord = centred(strip_rows, height)[:, :, None]
    xcoord = centred(col_pos * tile_len + jnp.arange(tile_len, dtype=jnp.int32), breadth)
    xgrid = xcoord[None, None, :]
    weight_x = pixel_weight * xgrid
    weight_y = pixel_weight * ycoord
    sum_w = jnp.sum(pixel_weight, axis=(1, 2))
    sum_x = jnp.sum(weight_x, axis=(1, 2))
    sum_y = jnp.sum(weight_y, axis=(1, 2))
    sum_xx = jnp.sum(weight_x * xgrid, axis=(1, 2))
    sum_xy = jnp.sum(weight_x * ycoord, axis=(1, 2))
    sum_yy = jnp.sum(weight_y * ycoord, axis=(1, 2))
    normal = jnp.stack(
        [
            jnp.stack([sum_w, sum_x, sum_y], -1),
            jnp.stack([sum_x, sum_xx, sum_xy], -1),
            jnp.stack([sum_y, sum_xy, sum_yy], -1),
        ],
        1,
    )
    moments = jnp.stack(
        [
            jnp.sum(pixel_weight * difference, axis=(1, 2)),
            jnp.sum(weight_x * difference, axis=(1, 2)),
            jnp.sum(weight_y * difference, axis=(1, 2)),
        ],
        -1,
    )
    normal, moments = lax.psum((normal, moments), ("row", "col"))
    plane_fit = solve_three(normal, moments)
    row_coord = centred(row_pos * tile_len + jnp.arange(tile_len, dtype=jnp.int32), height)
    background = (
        plane_fit[:, 0, None, None]
        + plane_fit[:, 1, None, None] * xcoord[None, None, :]
        + plane_fit[:, 2, None, None] * row_coord[None, :, None]
    )
    corrected = (matched - background).astype(jnp.bfloat16)
    choose = warp_index[:, 0, 0, :]
    row_maps = jnp.take(resample_bank, choose[:, 0], axis=0)
    col_maps = jnp.take(resample_bank, choose[:, 1], axis=0)
    halfway = jnp.einsum(
        "eij,ejk->eik", row_maps, corrected, preferred_element_type=jnp.float32
    ).astype(jnp.bfloat16)
    warped = jnp.einsum(
        "eik,elk->eil", halfway, col_maps, preferred_element_type=jnp.float32
    ).astype(jnp.bfloat16)
    listed = destinations[:, 0, 0, :]
    how_many = counts[:, 0, 0]
    usable = jnp.arange(MAXD, dtype=jnp.int32)[None, :] < how_many[:, None]
    owners = jnp.arange(visit_count, dtype=jnp.int32)
    member = jnp.any(usable[:, :, None] & (listed[:, :, None] == owners[None, None, :]), axis=1)
    tile_weight = weights[:, 0, 0]
    nothing = jnp.zeros((), jnp.bfloat16)
    picked = jnp.where(member, tile_weight[:, None], nothing)
    partial_sum = jnp.einsum("ev,eij->vij", picked, warped, preferred_element_type=jnp.float32)
    partial_weight = jnp.sum(picked.astype(jnp.float32), axis=0)
    numerator, denominator = (
        lax.psum_scatter(
            partial_sum.astype(jnp.bfloat16), "visit", scatter_dimension=0, tiled=True
        ).astype(jnp.float32),
        lax.psum_scatter(
            partial_weight.astype(jnp.bfloat16), "visit", scatter_dimension=0, tiled=True
        ).astype(jnp.float32),
    )
    coadd_patch = numerator / denominator[:, None, None]
    return (coadd_patch, plane_fit)


def solution(mesh):
    in_specs = (
        P("visit", "row", "col"),
        P("visit", None),
        P(),
        P("visit", "row", "col"),
        P(),
        P("visit", "row", "col", None),
        P("visit", "row", "col", None),
        P("visit", "row", "col"),
    )
    out_specs = (P("visit", "row", "col"), P("visit", None))
    return jax.shard_map(shards, mesh=mesh, in_specs=in_specs, out_specs=out_specs, check_vma=False)
```

profile of v0, /device:TPU:0, one launch (start us, length us, event | category | flops | bytes accessed | tf_op | source)
XLA Modules:
  0.0 194.2 jit_solution(17051824752516389986)
XLA Ops:
  9.1 2.4 %collective-permute-start = (bf16[4,16,512]{1,2,0:T(8,128)(2,1)}, bf16[4,16,512]{1,2,0:T(8,128)(2,1)S(1)}, u32[]{:S(2)}, u32[]{:S(2)}) collective-permute-start(bf16[4,16,512]{1,2,0:T(8,128)(2,1)} %copy.60), channel_id=1, source_target_pairs={{0,4},{1,5},{2,6},{3,7},{8,12},{9,13},{10,14},{11,15},{16,20},{17,... | collective-permute-start | bytes 196616 | tf_op jit(solution)/shard_map/ppermute | solution.py:21
  12.5 1.4 collective-permute-start.1
  13.9 4.2 %copy.62 = bf16[4,512,512]{1,2,0:T(8,128)(2,1)} copy(bf16[4,512,512]{2,1,0:T(8,128)(2,1)} %param.10) | data formatting | bytes 4194304 | tf_op args[0]
  19.9 2.9 %copy.63 = bf16[4,512,512]{2,0,1:T(4,128)(2,1)} copy(bf16[4,512,512]{2,1,0:T(8,128)(2,1)S(1)} %copy-done) | data formatting | bytes 4194304 | tf_op args[0]
  23.3 1.9 gather_fusion.1
  25.2 17.3 %all_gather.3 = bf16[16,32,512]{2,1,0:T(8,128)(2,1)S(1)} all-gather(bf16[4,32,512]{2,1,0:T(8,128)(2,1)S(1)} %copy.64), channel_id=1, replica_groups=mesh['visit'=4,'row'=2,'col'=4] {'visit'}, dimensions={0}, use_global_device_ids=true | all-gather | bytes 655360 | tf_op jit(solution)/shard_map/all_gather | solution.py:93
  42.6 4.8 %gather_fusion.3 = bf16[4,512,512]{2,1,0:T(8,128)(2,1)} fusion(bf16[12,512,512]{2,1,0:T(8,128)(2,1)} %param.14, s32[1024]{0:T(1024)S(1)} %get-tuple-element.65), kind=kCustom, calls=%fused_computation.clone | custom fusion | bytes 4194320 | tf_op jit(solution)/shard_map/jit(_take)/gather | solution.py:136
  47.4 5.0 %gather_fusion.4 = bf16[4,512,512]{2,1,0:T(8,128)(2,1)} fusion(bf16[12,512,512]{2,1,0:T(8,128)(2,1)} %param.14, s32[1024]{0:T(1024)S(1)} %get-tuple-element.64), kind=kCustom, calls=%fused_computation.1.clone | custom fusion | bytes 4194320 | tf_op jit(solution)/shard_map/jit(_take)/gather | solution.py:137
  54.1 3.4 %collective-permute-start.2 = (bf16[4,544,16]{1,2,0:T(8,128)(2,1)S(1)}, bf16[4,544,16]{1,2,0:T(8,128)(2,1)S(1)}, u32[]{:S(2)}, u32[]{:S(2)}) collective-permute-start(bf16[4,544,16]{1,2,0:T(8,128)(2,1)S(1)} %get-tuple-element.49), channel_id=1, source_target_pairs={{0,1},{1,2},{2,3},{4,5},{5,6},{6,7},{8,9},{9,10},{10,11},{12,13},{... | collective-permute-start | bytes 208904 | tf_op jit(solution)/shard_map/ppermute | solution.py:21
  57.5 1.5 collective-permute-start.3
  59.6 4.2 %collective-permute-done.3 = bf16[4,544,16]{1,2,0:T(8,128)(2,1)S(1)} collective-permute-done((bf16[4,544,16]{1,2,0:T(8,128)(2,1)S(1)}, bf16[4,544,16]{1,2,0:T(8,128)(2,1)S(1)}, u32[]{:S(2)}, u32[]{:S(2)}) %collective-permute-start.3) | collective-permute-done | bytes 69664 | tf_op jit(solution)/shard_map/ppermute | solution.py:22
  63.8 7.6 %fusion.2 = f32[4,512,512]{2,1,0:T(8,128)} fusion(f32[]{:T(128)} %exponential_reduce_fusion.1, bf16[4,544,16]{1,2,0:T(8,128)(2,1)S(1)} %collective-permute-done.3, bf16[4,16,512]{1,2,0:T(8,128)(2,1)} %collective-permute-done.1, bf16[4,512,512]{1,2,0:T(8,128)(2,1)S(1)} %copy-done.1, bf16[4,16,512]{1,2,0:T(8,128)(2,1)S(1)} %collective-permute-done, ...), kind=kOutput, calls=%fused_computation.10 | convolution fusion | flops 2372083712 | bytes 6561796 | tf_op jit(solution)/shard_map/eil,ml->eim/dot_general | solution.py:79
  71.4 7.7 %fusion = f32[4,512,512]{2,1,0:T(8,128)} fusion(f32[]{:T(128)} %exponential_reduce_fusion, bf16[4,544,16]{1,2,0:T(8,128)(2,1)S(1)} %collective-permute-done.3, bf16[4,16,512]{1,2,0:T(8,128)(2,1)} %collective-permute-done.1, bf16[4,512,512]{1,2,0:T(8,128)(2,1)S(1)} %copy-done.1, bf16[4,16,512]{1,2,0:T(8,128)(2,1)S(1)} %collective-permute-done, ...), kind=kOutput, calls=%fused_computation.8 | convolution fusion | flops 2372083712 | bytes 6561796 | tf_op jit(solution)/shard_map/eil,ml->eim/dot_general | solution.py:79
  79.1 9.8 %multiply_add_fusion = f32[4,512,512]{2,1,0:T(8,128)} fusion(f32[4,512,512]{2,1,0:T(8,128)} %fusion, f32[4,512,512]{2,1,0:T(8,128)} %fusion.2, f32[4]{0:T(128)S(1)} %get-tuple-element.30, f32[4]{0:T(128)S(1)} %get-tuple-element.31, f32[4]{0:T(128)S(1)} %get-tuple-element.29, f32[]{:T(128)} %exponential_reduce_fusion.2, ...), kind=kOutput, calls=%fused_computation.6 | convolution fusion | flops 2377326592 | bytes 14950452 | tf_op jit(solution)/shard_map/eil,ml->eim/dot_general | solution.py:79
  88.9 6.8 %copy.65 = f32[4,512,512]{2,0,1:T(4,128)} copy(f32[4,512,512]{2,1,0:T(8,128)} %multiply_add_fusion) | data formatting | bytes 8388608 | tf_op jit(solution)/shard_map/add | solution.py:80
  95.7 1.9 gather_fusion.2
  98.5 27.4 %all-reduce.2 = (f32[4,3,3]{1,2,0:T(4,128)S(1)}, f32[4,3]{0,1:T(4,128)S(1)}) all-reduce(f32[4,3,3]{1,2,0:T(4,128)S(1)} %pad_maximum_fusion.4, f32[4,3]{0,1:T(4,128)S(1)} %pad_maximum_fusion.5), channel_id=1, replica_groups=mesh['visit'=4,'row'=2,'col'=4] {'row','col'}, use_global_device_ids=true, to_apply=%region_16.18 | all-reduce | flops 48 | bytes 384 | tf_op jit(solution)/shard_map/psum | solution.py:126
  128.1 6.7 %fusion.22 = bf16[4,512,512]{2,1,0:T(8,128)(2,1)} fusion(bf16[4,512,512]{2,1,0:T(8,128)(2,1)} %gather_fusion.4, pred[4]{0:T(512)(128)(4,1)S(1)} %get-tuple-element.59, f32[4,512,512]{2,1,0:T(8,128)} %multiply_add_fusion, bf16[4,512,512]{2,1,0:T(8,128)(2,1)S(1)} %copy-done.2, f32[4,512]{1,0:T(4,128)S(1)} %get-tuple-element.67, ...), kind=kOutput, calls=%fused_computation.28 | convolution fusion | flops 2154823680 | bytes 10502152 | tf_op jit(solution)/shard_map/eik,elk->eil/dot_general | solution.py:141
  134.8 4.0 %fusion.27 = bf16[4,512,512]{2,0,1:T(4,128)(2,1)S(1)} fusion(bf16[4,512,512]{2,1,0:T(8,128)(2,1)} %fusion.22, pred[4,4]{1,0:T(4,128)(4,1)S(1)} %fusion.79, bf16[4]{0:T(256)(128)(2,1)S(1)} %bitcast.139), kind=kOutput, calls=%fused_computation.29 | convolution fusion | flops 9437200 | bytes 4194328 | tf_op jit(solution)/shard_map/ev,eij->vij/dot_general | solution.py:152
  138.8 1.8 copy.79
  140.6 11.6 %all-reduce.1 = bf16[4]{0:T(256)(128)(2,1)S(1)} all-reduce(bf16[4]{0:T(256)(128)(2,1)S(1)} %select_reduce_fusion.2), channel_id=3, replica_groups=mesh['visit'=4,'row'=2,'col'=4] {'visit'}, use_global_device_ids=true, to_apply=%region_21.23.clone | all-reduce | flops 4 | bytes 16
  152.8 1.2 dynamic-slice.1
  155.4 29.8 %reduce-scatter.2.cloned.1.call-done = bf16[1,512,512]{2,1,0:T(8,128)(2,1)} async-done(((bf16[4,512,512]{2,1,0:T(8,128)(2,1)}), bf16[1,512,512]{2,1,0:T(8,128)(2,1)}) %reduce-scatter.2.cloned.1.call-update) | async-done | bytes 524304 | tf_op jit(solution)/shard_map/reduce_scatter | solution.py:155
  185.2 2.2 %convert_divide_fusion = f32[1,512,512]{2,1,0:T(8,128)} fusion(bf16[1,512,512]{2,1,0:T(8,128)(2,1)} %reduce-scatter.2.cloned.1.call-done, f32[]{:T(128)S(6)} %convert.2), kind=kLoop, calls=%fused_computation.40 | loop fusion | flops 524288 | bytes 1572868 | tf_op jit(solution)/shard_map/div | solution.py:162
  (79 shorter events, 12.1 us)
Async XLA Ops:
  7.2 178.1 %reduce-scatter.2.cloned.1.call-start = ((), (), s32[]{:S(2)}) async-start(), calls=%async_computation.1 | async-start | bytes 2621440 | tf_op jit(solution)/shard_map/reduce_scatter | solution.py:155
  9.1 44.1 %collective-permute-start = (bf16[4,16,512]{1,2,0:T(8,128)(2,1)}, bf16[4,16,512]{1,2,0:T(8,128)(2,1)S(1)}, u32[]{:S(2)}, u32[]{:S(2)}) collective-permute-start(bf16[4,16,512]{1,2,0:T(8,128)(2,1)} %copy.60), channel_id=1, source_target_pairs={{0,4},{1,5},{2,6},{3,7},{8,12},{9,13},{10,14},{11,15},{16,20},{17,... | collective-permute-start | bytes 196616 | tf_op jit(solution)/shard_map/ppermute | solution.py:21
  12.5 7.4 %copy-start = (bf16[4,512,512]{2,1,0:T(8,128)(2,1)S(1)}, bf16[4,512,512]{2,1,0:T(8,128)(2,1)}, u32[]{:S(2)}) copy-start(bf16[4,512,512]{2,1,0:T(8,128)(2,1)} %param.10) | copy-start | bytes 6291460
  12.5 40.7 %collective-permute-start.1 = (bf16[4,16,512]{1,2,0:T(8,128)(2,1)}, bf16[4,16,512]{1,2,0:T(8,128)(2,1)}, u32[]{:S(2)}, u32[]{:S(2)}) collective-permute-start(bf16[4,16,512]{1,2,0:T(8,128)(2,1)} %copy.61), channel_id=1, source_target_pairs={{4,0},{5,1},{6,2},{7,3},{12,8},{13,9},{14,10},{15,11},{20,16},{21,... | collective-permute-start | bytes 196616 | tf_op jit(solution)/shard_map/ppermute | solution.py:22
  19.9 2.9 %copy-start.5 = (s32[8,3]{0,1:T(4,128)S(1)}, s32[8,3]{0,1:T(4,128)}, u32[]{:S(2)}) copy-start(s32[8,3]{0,1:T(4,128)} %param.12) | copy-start | bytes 292
  19.9 3.2 %copy-start.3 = (f32[4,3]{1,0:T(4,128)S(1)}, f32[4,3]{1,0:T(4,128)}, u32[]{:S(2)}) copy-start(f32[4,3]{1,0:T(4,128)} %param.11) | copy-start | bytes 148
  22.8 19.8 %copy-start.6 = (s32[4,1,1,2]{0,3,2,1:T(2,128)S(1)}, s32[4,1,1,2]{0,3,2,1:T(2,128)}, u32[]{:S(2)}) copy-start(s32[4,1,1,2]{0,3,2,1:T(2,128)} %param.15) | copy-start | bytes 100
  47.4 5.0 %copy-start.7 = (s32[4,1,1]{0,2,1:T(1,128)S(1)}, s32[4,1,1]{0,2,1:T(1,128)}, u32[]{:S(2)}) copy-start(s32[4,1,1]{0,2,1:T(1,128)} %param.17) | copy-start | bytes 52
  47.4 5.6 %copy-start.4 = (s32[4,1,1,4]{3,2,1,0:T(1,128)S(1)}, s32[4,1,1,4]{3,2,1,0:T(1,128)}, u32[]{:S(2)}) copy-start(s32[4,1,1,4]{3,2,1,0:T(1,128)} %param.16) | copy-start | bytes 196
  47.4 5.8 %copy-start.1 = (bf16[4,512,512]{1,2,0:T(8,128)(2,1)S(1)}, bf16[4,512,512]{1,2,0:T(8,128)(2,1)}, u32[]{:S(2)}) copy-start(bf16[4,512,512]{1,2,0:T(8,128)(2,1)} %copy.62) | copy-start | bytes 6291460
  54.1 5.6 %collective-permute-start.2 = (bf16[4,544,16]{1,2,0:T(8,128)(2,1)S(1)}, bf16[4,544,16]{1,2,0:T(8,128)(2,1)S(1)}, u32[]{:S(2)}, u32[]{:S(2)}) collective-permute-start(bf16[4,544,16]{1,2,0:T(8,128)(2,1)S(1)} %get-tuple-element.49), channel_id=1, source_target_pairs={{0,1},{1,2},{2,3},{4,5},{5,6},{6,7},{8,9},{9,10},{10,11},{12,13},{... | collective-permute-start | bytes 208904 | tf_op jit(solution)/shard_map/ppermute | solution.py:21
  57.5 6.3 %collective-permute-start.3 = (bf16[4,544,16]{1,2,0:T(8,128)(2,1)S(1)}, bf16[4,544,16]{1,2,0:T(8,128)(2,1)S(1)}, u32[]{:S(2)}, u32[]{:S(2)}) collective-permute-start(bf16[4,544,16]{1,2,0:T(8,128)(2,1)S(1)} %get-tuple-element.50), channel_id=1, source_target_pairs={{1,0},{2,1},{3,2},{5,4},{6,5},{7,6},{9,8},{10,9},{11,10},{13,12},{... | collective-permute-start | bytes 208904 | tf_op jit(solution)/shard_map/ppermute | solution.py:22
  95.7 32.4 %copy-start.2 = (bf16[4,512,512]{2,1,0:T(8,128)(2,1)S(1)}, bf16[4,512,512]{2,1,0:T(8,128)(2,1)}, u32[]{:S(2)}) copy-start(bf16[4,512,512]{2,1,0:T(8,128)(2,1)} %gather_fusion.3) | copy-start | bytes 6291460
  128.1 6.7 %copy-start.8 = (bf16[4,1,1]{0,2,1:T(2,128)(2,1)S(1)}, bf16[4,1,1]{0,2,1:T(2,128)(2,1)}, u32[]{:S(2)}) copy-start(bf16[4,1,1]{0,2,1:T(2,128)(2,1)} %param.13) | copy-start | bytes 28
  140.5 11.7 %copy-start.9 = (u32[32]{0:T(128)S(1)}, u32[32]{0:T(128)}, u32[]{:S(2)}) copy-start(u32[32]{0:T(128)} %constant.184) | copy-start | bytes 388
Sparse Core Ops, SparseCore 0:
  140.7 44.5 reduce-scatter.1
where the time goes:
time: 195 us; the launch traced here: 194 us
  blocking collectives  56.3 us (29%)
  local copies, waits for them, and re-layouts  36.1 us (19%)
  matrix products  35.7 us (18%)
  waiting for transfers between devices  34.7 us (18%)
  between operations  14.9 us (8%)
  starting transfers between devices  8.7 us (4%)
  other arithmetic  7.86 us (4%)
    reduce_scatter x1, waiting for transfers between devices, shards(): lax.psum_scatter(partial_sum.astype(jnp.bfloat16), 'visit', scatter_dimen...  29.8 us
    psum x1, blocking collectives, shards(): normal, moments = lax.psum((normal, moments), ('row', 'col'))  27.4 us
    dot_general x3, matrix products, shards(): jnp.einsum('eil,ml->eim', across, table, preferred_element_type=jnp.float32)  25.1 us
    all_gather x1, blocking collectives, shards(): everyone = lax.all_gather(own_strip, 'visit', axis=0, tiled=True)  17.3 us
    unnamed x1, blocking collectives  11.6 us
    unnamed x25, local copies, waits for them, and re-layouts  9.58 us
    add x1, local copies, waits for them, and re-layouts, shards(): matched = matched + coeffs[:, kernel, None, None] * smoothed  6.81 us
    dot_general x1, matrix products, shards(): jnp.einsum('eik,elk->eil', halfway, col_maps, preferred_element_type=jnp....  6.68 us
  transfers between devices with their start and end apart: 5, of which 3 were waited for; matrix products, arithmetic and copies ran while one was open for 13% of the time, Pallas kernels for 0%

commit v1 on v0

--- a/solution.py
+++ b/solution.py
@@ -52,6 +52,29 @@
         ..., 0, 0
     ]
     return jnp.stack([upper_low, upper_mid, upper_top], -1)
+
+
+def butterfly_sum(values, axes):
+    for axis, size in axes:
+        if size & (size - 1) == 0:
+            bit = 1
+            while bit < size:
+                pairs = [(i, i ^ bit) for i in range(size)]
+                values = jax.tree.map(lambda v: v + lax.ppermute(v, axis, pairs), values)
+                bit *= 2
+        else:
+            position = lax.axis_index(axis)
+            def gathered(v):
+                parts = [v]
+                for shift in range(1, size):
+                    pairs = [(i, (i + shift) % size) for i in range(size)]
+                    parts.append(lax.ppermute(v, axis, pairs))
+                stacked = jnp.stack(parts, 0)
+                order = (position - jnp.arange(size)) % size
+                canonical = jnp.zeros_like(stacked).at[order].set(stacked)
+                return jnp.sum(canonical, axis=0)
+            values = jax.tree.map(gathered, values)
+    return values
 
 
 def rows_from(source, anchor):
@@ -90,8 +113,33 @@
     )
     offset = jnp.sum(jnp.where(hit_first | hit_second, offsets[None, :], 0), axis=1)
     own_strip = jax.vmap(rows_from)(images, offset)
-    everyone = lax.all_gather(own_strip, "visit", axis=0, tiled=True)
-    theirs = jnp.take(everyone, partner, axis=0).astype(jnp.float32)
+    listed = destinations[:, 0, 0, :]
+    how_many = counts[:, 0, 0]
+    usable = jnp.arange(MAXD, dtype=jnp.int32)[None, :] < how_many[:, None]
+    owners = jnp.arange(visit_count, dtype=jnp.int32)
+    member = jnp.any(usable[:, :, None] & (listed[:, :, None] == owners[None, None, :]), axis=1)
+    tile_weight = weights[:, 0, 0]
+    nothing = jnp.zeros((), jnp.bfloat16)
+    picked = jnp.where(member, tile_weight[:, None], nothing)
+    strip_rows_n = exp_dev * STRIP
+    extra = -(-(exp_dev * visit_count) // tile_len)
+    extra = -(-extra // 16) * 16
+    tail = jnp.zeros((extra * tile_len,), jnp.bfloat16)
+    tail = tail.at[: exp_dev * visit_count].set(picked.reshape(-1)).reshape(extra, tile_len)
+    payload = jnp.concatenate([own_strip.reshape(strip_rows_n, tile_len), tail], axis=0)
+    received = [payload]
+    for shift in range(1, visit_count):
+        pairs = [(i, (i + shift) % visit_count) for i in range(visit_count)]
+        received.append(lax.ppermute(payload, "visit", pairs))
+    stacked = jnp.stack(received, 0)
+    strips_all = stacked[:, :strip_rows_n].reshape(visit_count * exp_dev, STRIP, tile_len)
+    picked_all = stacked[:, strip_rows_n:].reshape(visit_count, -1)[:, : exp_dev * visit_count]
+    picked_all = picked_all.reshape(visit_count, exp_dev, visit_count)
+    partner_visit = partner // exp_dev
+    slot = (visit_pos - partner_visit) % visit_count
+    theirs = jnp.take(strips_all, slot * exp_dev + partner % exp_dev, axis=0).astype(jnp.float32)
+    own_patch = jnp.take(picked_all, visit_pos, axis=2).astype(jnp.float32)
+    denominator = jnp.sum(own_patch).reshape(1)
     nearby = jax.vmap(rows_from)(matched, offset)
     difference = nearby - theirs
     pixel_weight = 1.0 / (1.0 + theirs * theirs)
@@ -123,7 +171,10 @@
         ],
         -1,
     )
-    normal, moments = lax.psum((normal, moments), ("row", "col"))
+    packed = jnp.concatenate([normal.reshape(exp_dev, 9), moments], axis=1)
+    packed = butterfly_sum(packed, (("row", row_count), ("col", col_count)))
+    normal = packed[:, :9].reshape(exp_dev, 3, 3)
+    moments = packed[:, 9:]
     plane_fit = solve_three(normal, moments)
     row_coord = centred(row_pos * tile_len + jnp.arange(tile_len, dtype=jnp.int32), height)
     background = (
@@ -133,32 +184,22 @@
     )
     corrected = (matched - background).astype(jnp.bfloat16)
     choose = warp_index[:, 0, 0, :]
-    row_maps = jnp.take(resample_bank, choose[:, 0], axis=0)
-    col_maps = jnp.take(resample_bank, choose[:, 1], axis=0)
+    row_maps = jnp.stack(
+        [lax.dynamic_index_in_dim(resample_bank, choose[e, 0], 0, False) for e in range(exp_dev)]
+    )
+    col_maps = jnp.stack(
+        [lax.dynamic_index_in_dim(resample_bank, choose[e, 1], 0, False) for e in range(exp_dev)]
+    )
     halfway = jnp.einsum(
         "eij,ejk->eik", row_maps, corrected, preferred_element_type=jnp.float32
     ).astype(jnp.bfloat16)
     warped = jnp.einsum(
         "eik,elk->eil", halfway, col_maps, preferred_element_type=jnp.float32
     ).astype(jnp.bfloat16)
-    listed = destinations[:, 0, 0, :]
-    how_many = counts[:, 0, 0]
-    usable = jnp.arange(MAXD, dtype=jnp.int32)[None, :] < how_many[:, None]
-    owners = jnp.arange(visit_count, dtype=jnp.int32)
-    member = jnp.any(usable[:, :, None] & (listed[:, :, None] == owners[None, None, :]), axis=1)
-    tile_weight = weights[:, 0, 0]
-    nothing = jnp.zeros((), jnp.bfloat16)
-    picked = jnp.where(member, tile_weight[:, None], nothing)
     partial_sum = jnp.einsum("ev,eij->vij", picked, warped, preferred_element_type=jnp.float32)
-    partial_weight = jnp.sum(picked.astype(jnp.float32), axis=0)
-    numerator, denominator = (
-        lax.psum_scatter(
-            partial_sum.astype(jnp.bfloat16), "visit", scatter_dimension=0, tiled=True
-        ).astype(jnp.float32),
-        lax.psum_scatter(
-            partial_weight.astype(jnp.bfloat16), "visit", scatter_dimension=0, tiled=True
-        ).astype(jnp.float32),
-    )
+    numerator = lax.psum_scatter(
+        partial_sum.astype(jnp.bfloat16), "visit", scatter_dimension=0, tiled=True
+    ).astype(jnp.float32)
     coadd_patch = numerator / denominator[:, None, None]
     return (coadd_patch, plane_fit)
 

time: 195 us -> 174 us (0.89)
  blocking collectives: 56.3 us -> 0 us
  waiting for transfers between devices: 34.7 us -> 50.3 us
  between operations: 14.9 us -> 29.2 us
  starting transfers between devices: 8.7 us -> 18.6 us
  local copies, waits for them, and re-layouts: 36.1 us -> 29.5 us
  other arithmetic: 7.86 us -> 9.99 us
    psum x1 -> x0, blocking collectives: 27.4 us -> none  [shards(): normal, moments = lax.psum((normal, moments), ('row', 'col'))]
    all_gather x1 -> x0, blocking collectives: 17.3 us -> none  [shards(): everyone = lax.all_gather(own_strip, 'visit', axis=0, tiled=True)]
    unnamed x1 -> x0, blocking collectives: 11.6 us -> none
    ppermute x0 -> x6, starting transfers between devices: none -> 11 us  [the longest x3 7.01 us: shards(): received.append(lax.ppermute(payload, 'visit', pairs))]
    reduce_scatter x1, waiting for transfers between devices: 29.8 us -> 40.3 us  [shards(): lax.psum_scatter(partial_sum.astype(jnp.bfloat16), 'visit', scatter_dimen...]
    gather x3 -> x1, local copies, waits for them, and re-layouts: 10.3 us -> 0.56 us  [shards(): jnp.take(strips_all, slot * exp_dev + partner % exp_dev, axis=0)]
    ppermute x0 -> x6, waiting for transfers between devices: none -> 4.81 us  [the longest x3 4.8 us: butterfly_sum(): values = jax.tree.map(lambda v: v + lax.ppermute(v, axis, pairs), values)]
    dynamic_slice x0 -> x1, local copies, waits for them, and re-layouts: none -> 4.43 us  [shards(): lax.dynamic_index_in_dim(resample_bank, choose[e, 0], 0, False)]
  transfers between devices with their start and end apart: 5 -> 11, of which waited for: 3 -> 6; matrix products, arithmetic and copies ran while one was open for 13% -> 28% of each run, Pallas kernels for 0% -> 0%
where the time goes in v1:
time: 174 us; the launch traced here: 173 us
  waiting for transfers between devices  50.3 us (29%)
  matrix products  35.9 us (21%)
  local copies, waits for them, and re-layouts  29.5 us (17%)
  between operations  29.2 us (17%)
  starting transfers between devices  18.6 us (11%)
  other arithmetic  9.99 us (6%)
    reduce_scatter x1, waiting for transfers between devices, shards(): lax.psum_scatter(partial_sum.astype(jnp.bfloat16), 'visit', scatter_dimen...  40.3 us
    dot_general x3, matrix products, shards(): jnp.einsum('eil,ml->eim', across, table, preferred_element_type=jnp.float32)  25.2 us
    unnamed x23, local copies, waits for them, and re-layouts  7.21 us
    ppermute x3, starting transfers between devices, shards(): received.append(lax.ppermute(payload, 'visit', pairs))  7.01 us
    add x1, local copies, waits for them, and re-layouts, shards(): matched = matched + coeffs[:, kernel, None, None] * smoothed  6.81 us
    dot_general x1, matrix products, shards(): jnp.einsum('eik,elk->eil', halfway, col_maps, preferred_element_type=jnp....  6.72 us
    ppermute x3, waiting for transfers between devices, butterfly_sum(): values = jax.tree.map(lambda v: v + lax.ppermute(v, axis, pairs), values)  4.8 us
    ppermute x2, starting transfers between devices, extended(): before = lax.ppermute(last, axis, up)  4.64 us
  transfers between devices with their start and end apart: 11, of which 6 were waited for; matrix products, arithmetic and copies ran while one was open for 28% of the time, Pallas kernels for 0%

profile of v1, /device:TPU:0, one launch (start us, length us, event | category | flops | bytes accessed | tf_op | source)
XLA Modules:
  0.0 173.4 jit_solution(14433761624073984131)
XLA Ops:
  8.3 4.7 %copy.99 = bf16[4,512,512]{2,0,1:T(4,128)(2,1)} copy(bf16[4,512,512]{2,1,0:T(8,128)(2,1)} %param.10) | data formatting | bytes 4194304 | tf_op args[0]
  13.0 1.9 %gather_fusion.1 = bf16[4,32,512]{2,0,1:T(4,128)(2,1)S(1)} fusion(bf16[4,512,512]{2,0,1:T(4,128)(2,1)} %copy.99, s32[4]{0:T(128)S(1)} %fusion.102), kind=kCustom, calls=%fused_computation.1 | custom fusion | bytes 262192 | tf_op jit(solution)/shard_map/vmap()/gather | solution.py:81
  15.3 3.1 %collective-permute-start.4 = (bf16[144,512]{1,0:T(8,128)(2,1)S(1)}, bf16[144,512]{1,0:T(8,128)(2,1)S(1)}, u32[]{:S(2)}, u32[]{:S(2)}) collective-permute-start(bf16[144,512]{1,0:T(8,128)(2,1)S(1)} %get-tuple-element.66), channel_id=1, source_target_pairs={{0,8},{8,16},{16,24},{24,0},{1,9},{9,17},{17,25},{25,1},{2,10},{10... | collective-permute-start | bytes 442376 | tf_op jit(solution)/shard_map/ppermute | solution.py:133
  18.4 2.6 %collective-permute-start.5 = (bf16[144,512]{1,0:T(8,128)(2,1)S(1)}, bf16[144,512]{1,0:T(8,128)(2,1)S(1)}, u32[]{:S(2)}, u32[]{:S(2)}) collective-permute-start(bf16[144,512]{1,0:T(8,128)(2,1)S(1)} %get-tuple-element.66), channel_id=1, source_target_pairs={{0,16},{8,24},{16,0},{24,8},{1,17},{9,25},{17,1},{25,9},{2,18},{10... | collective-permute-start | bytes 442376 | tf_op jit(solution)/shard_map/ppermute | solution.py:133
  21.0 1.4 collective-permute-start.6
  25.7 1.4 collective-permute-start.1
  27.1 2.4 %copy.98 = bf16[4,512,512]{1,2,0:T(8,128)(2,1)} copy(bf16[4,512,512]{2,1,0:T(8,128)(2,1)S(1)} %copy-done) | data formatting | bytes 4194304 | tf_op args[0]
  47.2 4.4 %constant_dynamic-slice_fusion.7 = (bf16[1,512,512]{2,1,0:T(8,128)(2,1)}, bf16[1,512,512]{2,1,0:T(8,128)(2,1)}, bf16[1,512,512]{2,1,0:T(8,128)(2,1)}, bf16[1,512...) fusion(bf16[12,512,512]{2,1,0:T(8,128)(2,1)} %param.14, ...), kind=kLoop, calls=%fused_computation.104 | loop fusion | bytes 8388640 | tf_op jit(solution)/shard_map/jit(dynamic_index_in_dim)/dynamic_slice | solution.py:188
  52.5 3.3 %collective-permute-start.2 = (bf16[4,544,16]{1,2,0:T(8,128)(2,1)S(1)}, bf16[4,544,16]{1,2,0:T(8,128)(2,1)S(1)}, u32[]{:S(2)}, u32[]{:S(2)}) collective-permute-start(bf16[4,544,16]{1,2,0:T(8,128)(2,1)S(1)} %get-tuple-element.61), channel_id=1, source_target_pairs={{0,1},{1,2},{2,3},{4,5},{5,6},{6,7},{8,9},{9,10},{10,11},{12,13},{... | collective-permute-start | bytes 208904 | tf_op jit(solution)/shard_map/ppermute | solution.py:21
  55.9 1.5 collective-permute-start.3
  57.9 4.6 %collective-permute-done.3 = bf16[4,544,16]{1,2,0:T(8,128)(2,1)} collective-permute-done((bf16[4,544,16]{1,2,0:T(8,128)(2,1)S(1)}, bf16[4,544,16]{1,2,0:T(8,128)(2,1)}, u32[]{:S(2)}, u32[]{:S(2)}) %collective-permute-start.3) | collective-permute-done | bytes 69664 | tf_op jit(solution)/shard_map/ppermute | solution.py:22
  62.5 7.7 %fusion.2 = f32[4,512,512]{2,1,0:T(8,128)} fusion(f32[]{:T(128)} %exponential_reduce_fusion.1, bf16[4,544,16]{1,2,0:T(8,128)(2,1)} %collective-permute-done.3, bf16[4,16,512]{1,2,0:T(8,128)(2,1)} %collective-permute-done.1, bf16[4,512,512]{1,2,0:T(8,128)(2,1)S(1)} %copy-done.1, bf16[4,16,512]{1,2,0:T(8,128)(2,1)S(1)} %collective-permute-done, ...), kind=kOutput, calls=%fused_computation.8 | convolution fusion | flops 2372083712 | bytes 6561796 | tf_op jit(solution)/shard_map/eil,ml->eim/dot_general | solution.py:102
  70.2 7.7 %fusion = f32[4,512,512]{2,1,0:T(8,128)} fusion(f32[]{:T(128)} %exponential_reduce_fusion, bf16[4,544,16]{1,2,0:T(8,128)(2,1)} %collective-permute-done.3, bf16[4,16,512]{1,2,0:T(8,128)(2,1)} %collective-permute-done.1, bf16[4,512,512]{1,2,0:T(8,128)(2,1)S(1)} %copy-done.1, bf16[4,16,512]{1,2,0:T(8,128)(2,1)S(1)} %collective-permute-done, ...), kind=kOutput, calls=%fused_computation.6 | convolution fusion | flops 2372083712 | bytes 6561796 | tf_op jit(solution)/shard_map/eil,ml->eim/dot_general | solution.py:102
  77.9 9.8 %multiply_add_fusion = f32[4,512,512]{2,1,0:T(8,128)} fusion(f32[4,512,512]{2,1,0:T(8,128)} %fusion, f32[4,512,512]{2,1,0:T(8,128)} %fusion.2, f32[4]{0:T(128)S(1)} %get-tuple-element.42, f32[4]{0:T(128)S(1)} %get-tuple-element.43, f32[4]{0:T(128)S(1)} %get-tuple-element.41, f32[]{:T(128)} %exponential_reduce_fusion.2, ...), kind=kOutput, calls=%fused_computation.4 | convolution fusion | flops 2377326592 | bytes 14950452 | tf_op jit(solution)/shard_map/eil,ml->eim/dot_general | solution.py:102
  87.7 6.8 %copy.105 = f32[4,512,512]{2,0,1:T(4,128)} copy(f32[4,512,512]{2,1,0:T(8,128)} %multiply_add_fusion) | data formatting | bytes 8388608 | tf_op jit(solution)/shard_map/add | solution.py:103
  94.5 1.9 %gather_fusion.2 = f32[4,32,512]{2,0,1:T(4,128)S(1)} fusion(f32[4,512,512]{2,0,1:T(4,128)} %copy.105, s32[4]{0:T(128)S(1)} %fusion.102), kind=kCustom, calls=%fused_computation.2 | custom fusion | bytes 524336 | tf_op jit(solution)/shard_map/vmap()/gather | solution.py:81
  99.8 2.4 %collective-permute-start.8 = (f32[4,12]{1,0:T(4,128)S(1)}, f32[4,12]{1,0:T(4,128)S(1)}, u32[]{:S(2)}, u32[]{:S(2)}) collective-permute-start(f32[4,12]{1,0:T(4,128)S(1)} %fusion.134), channel_id=1, source_target_pairs={{0,1},{1,0},{2,3},{3,2},{4,5},{5,4},{6,7},{7,6},{8,9},{9,8},{10,11... | collective-permute-start | bytes 584 | tf_op jit(solution)/shard_map/ppermute | solution.py:63
  102.2 1.6 collective-permute-done.8
  104.9 2.4 %collective-permute-done.9 = f32[4,12]{1,0:T(4,128)S(1)} collective-permute-done((f32[4,12]{1,0:T(4,128)S(1)}, f32[4,12]{1,0:T(4,128)S(1)}, u32[]{:S(2)}, u32[]{:S(2)}) %collective-permute-start.9) | collective-permute-done | bytes 224 | tf_op jit(solution)/shard_map/ppermute | solution.py:63
  109.4 6.7 %fusion.35 = bf16[4,512,512]{2,1,0:T(8,128)(2,1)} fusion(bf16[1,512,512]{2,1,0:T(8,128)(2,1)} %get-tuple-element.59, bf16[1,512,512]{2,1,0:T(8,128)(2,1)} %get-tuple-element.60, bf16[1,512,512]{2,1,0:T(8,128)(2,1)S(1)} %copy-done.3, bf16[1,512,512]{2,1,0:T(8,128)(2,1)S(1)} %copy-done.4, f32[4,512,512]{2,1,0:T(8,128)} %multiply_add_fusion, ...), kind=kOutput, calls=%fused_computation.37 | convolution fusion | flops 2159017984 | bytes 10502144 | tf_op jit(solution)/shard_map/eik,elk->eil/dot_general | solution.py:196
  116.1 4.0 %fusion.32 = bf16[4,512,512]{2,0,1:T(4,128)(2,1)S(1)} fusion(bf16[4,512,512]{2,1,0:T(8,128)(2,1)} %fusion.35, pred[4,4]{1,0:T(4,128)(4,1)S(1)} %fusion.87, bf16[4]{0:T(256)(128)(2,1)S(1)} %bitcast.142), kind=kOutput, calls=%fused_computation.36 | convolution fusion | flops 9437200 | bytes 4194328 | tf_op jit(solution)/shard_map/ev,eij->vij/dot_general | solution.py:199
  120.1 1.8 %copy.116 = bf16[4,512,512]{2,1,0:T(8,128)(2,1)} copy(bf16[4,512,512]{2,0,1:T(4,128)(2,1)S(1)} %fusion.32) | data formatting | bytes 4194304 | tf_op jit(solution)/shard_map/convert_element_type | solution.py:201
  123.5 40.3 %reduce-scatter.2.cloned.1.call-done = bf16[1,512,512]{2,1,0:T(8,128)(2,1)} async-done(((bf16[4,512,512]{2,1,0:T(8,128)(2,1)}), bf16[1,512,512]{2,1,0:T(8,128)(2,1)}) %reduce-scatter.2.cloned.1.call-update) | async-done | bytes 524304 | tf_op jit(solution)/shard_map/reduce_scatter | solution.py:200
  163.8 2.8 %convert_divide_fusion = f32[1,512,512]{2,1,0:T(8,128)} fusion(bf16[1,512,512]{2,1,0:T(8,128)(2,1)} %reduce-scatter.2.cloned.1.call-done, f32[]{:T(128)} %convert_reduce_fusion), kind=kLoop, calls=%fused_computation.47 | loop fusion | flops 524288 | bytes 1572868 | tf_op jit(solution)/shard_map/div | solution.py:203
  (99 shorter events, 17.1 us)
Async XLA Ops:
  7.2 156.6 %reduce-scatter.2.cloned.1.call-start = ((), (), s32[]{:S(2)}) async-start(), calls=%async_computation.1 | async-start | bytes 2621440 | tf_op jit(solution)/shard_map/reduce_scatter | solution.py:200
  8.2 6.7 %copy-start.9 = (s32[4,1,1]{0,2,1:T(1,128)S(1)}, s32[4,1,1]{0,2,1:T(1,128)}, u32[]{:S(2)}) copy-start(s32[4,1,1]{0,2,1:T(1,128)} %param.17) | copy-start | bytes 52
  8.2 6.7 %copy-start.7 = (s32[4,1,1,4]{3,2,1,0:T(1,128)S(1)}, s32[4,1,1,4]{3,2,1,0:T(1,128)}, u32[]{:S(2)}) copy-start(s32[4,1,1,4]{3,2,1,0:T(1,128)} %param.16) | copy-start | bytes 196
  8.2 6.8 %copy-start.8 = (bf16[4,1,1]{0,2,1:T(2,128)(2,1)S(1)}, bf16[4,1,1]{0,2,1:T(2,128)(2,1)}, u32[]{:S(2)}) copy-start(bf16[4,1,1]{0,2,1:T(2,128)(2,1)} %param.13) | copy-start | bytes 28
  8.3 14.1 %copy-start = (bf16[4,512,512]{2,1,0:T(8,128)(2,1)S(1)}, bf16[4,512,512]{2,1,0:T(8,128)(2,1)}, u32[]{:S(2)}) copy-start(bf16[4,512,512]{2,1,0:T(8,128)(2,1)} %param.10) | copy-start | bytes 6291460
  15.3 81.2 %collective-permute-start.4 = (bf16[144,512]{1,0:T(8,128)(2,1)S(1)}, bf16[144,512]{1,0:T(8,128)(2,1)S(1)}, u32[]{:S(2)}, u32[]{:S(2)}) collective-permute-start(bf16[144,512]{1,0:T(8,128)(2,1)S(1)} %get-tuple-element.66), channel_id=1, source_target_pairs={{0,8},{8,16},{16,24},{24,0},{1,9},{9,17},{17,25},{25,1},{2,10},{10... | collective-permute-start | bytes 442376 | tf_op jit(solution)/shard_map/ppermute | solution.py:133
  18.4 78.2 %collective-permute-start.5 = (bf16[144,512]{1,0:T(8,128)(2,1)S(1)}, bf16[144,512]{1,0:T(8,128)(2,1)S(1)}, u32[]{:S(2)}, u32[]{:S(2)}) collective-permute-start(bf16[144,512]{1,0:T(8,128)(2,1)S(1)} %get-tuple-element.66), channel_id=1, source_target_pairs={{0,16},{8,24},{16,0},{24,8},{1,17},{9,25},{17,1},{25,9},{2,18},{10... | collective-permute-start | bytes 442376 | tf_op jit(solution)/shard_map/ppermute | solution.py:133
  21.0 75.6 %collective-permute-start.6 = (bf16[144,512]{1,0:T(8,128)(2,1)S(1)}, bf16[144,512]{1,0:T(8,128)(2,1)S(1)}, u32[]{:S(2)}, u32[]{:S(2)}) collective-permute-start(bf16[144,512]{1,0:T(8,128)(2,1)S(1)} %get-tuple-element.66), channel_id=1, source_target_pairs={{0,24},{8,0},{16,8},{24,16},{1,25},{9,1},{17,9},{25,17},{2,26},{10... | collective-permute-start | bytes 442376 | tf_op jit(solution)/shard_map/ppermute | solution.py:133
  23.4 28.3 %collective-permute-start = (bf16[4,16,512]{1,2,0:T(8,128)(2,1)}, bf16[4,16,512]{1,2,0:T(8,128)(2,1)S(1)}, u32[]{:S(2)}, u32[]{:S(2)}) collective-permute-start(bf16[4,16,512]{1,2,0:T(8,128)(2,1)} %copy.96), channel_id=1, source_target_pairs={{0,4},{1,5},{2,6},{3,7},{8,12},{9,13},{10,14},{11,15},{16,20},{17,... | collective-permute-start | bytes 196616 | tf_op jit(solution)/shard_map/ppermute | solution.py:21
  25.7 5.7 %copy-start.6 = (s32[4,1,1,2]{0,3,2,1:T(2,128)S(1)}, s32[4,1,1,2]{0,3,2,1:T(2,128)}, u32[]{:S(2)}) copy-start(s32[4,1,1,2]{0,3,2,1:T(2,128)} %param.15) | copy-start | bytes 100
  25.7 16.3 %copy-start.5 = (f32[4,3]{1,0:T(4,128)S(1)}, f32[4,3]{1,0:T(4,128)}, u32[]{:S(2)}) copy-start(f32[4,3]{1,0:T(4,128)} %param.11) | copy-start | bytes 148
  25.7 26.0 %collective-permute-start.1 = (bf16[4,16,512]{1,2,0:T(8,128)(2,1)}, bf16[4,16,512]{1,2,0:T(8,128)(2,1)}, u32[]{:S(2)}, u32[]{:S(2)}) collective-permute-start(bf16[4,16,512]{1,2,0:T(8,128)(2,1)} %copy.97), channel_id=1, source_target_pairs={{4,0},{5,1},{6,2},{7,3},{12,8},{13,9},{14,10},{15,11},{20,16},{21,... | collective-permute-start | bytes 196616 | tf_op jit(solution)/shard_map/ppermute | solution.py:22
  47.2 4.5 %copy-start.1 = (bf16[4,512,512]{1,2,0:T(8,128)(2,1)S(1)}, bf16[4,512,512]{1,2,0:T(8,128)(2,1)}, u32[]{:S(2)}) copy-start(bf16[4,512,512]{1,2,0:T(8,128)(2,1)} %copy.98) | copy-start | bytes 6291460
  52.5 5.4 %collective-permute-start.2 = (bf16[4,544,16]{1,2,0:T(8,128)(2,1)S(1)}, bf16[4,544,16]{1,2,0:T(8,128)(2,1)S(1)}, u32[]{:S(2)}, u32[]{:S(2)}) collective-permute-start(bf16[4,544,16]{1,2,0:T(8,128)(2,1)S(1)} %get-tuple-element.61), channel_id=1, source_target_pairs={{0,1},{1,2},{2,3},{4,5},{5,6},{6,7},{8,9},{9,10},{10,11},{12,13},{... | collective-permute-start | bytes 208904 | tf_op jit(solution)/shard_map/ppermute | solution.py:21
  55.9 6.6 %collective-permute-start.3 = (bf16[4,544,16]{1,2,0:T(8,128)(2,1)S(1)}, bf16[4,544,16]{1,2,0:T(8,128)(2,1)}, u32[]{:S(2)}, u32[]{:S(2)}) collective-permute-start(bf16[4,544,16]{1,2,0:T(8,128)(2,1)S(1)} %get-tuple-element.62), channel_id=1, source_target_pairs={{1,0},{2,1},{3,2},{5,4},{6,5},{7,6},{9,8},{10,9},{11,10},{13,12},{... | collective-permute-start | bytes 208904 | tf_op jit(solution)/shard_map/ppermute | solution.py:22
  96.5 12.9 %copy-start.2 = (bf16[1,512,512]{2,1,0:T(8,128)(2,1)S(1)}, bf16[1,512,512]{2,1,0:T(8,128)(2,1)}, u32[]{:S(2)}) copy-start(bf16[1,512,512]{2,1,0:T(8,128)(2,1)} %get-tuple-element.53) | copy-start | bytes 1572868
  96.5 12.9 %copy-start.3 = (bf16[1,512,512]{2,1,0:T(8,128)(2,1)S(1)}, bf16[1,512,512]{2,1,0:T(8,128)(2,1)}, u32[]{:S(2)}) copy-start(bf16[1,512,512]{2,1,0:T(8,128)(2,1)} %get-tuple-element.54) | copy-start | bytes 1572868
  96.5 12.9 %copy-start.4 = (bf16[1,512,512]{2,1,0:T(8,128)(2,1)S(1)}, bf16[1,512,512]{2,1,0:T(8,128)(2,1)}, u32[]{:S(2)}) copy-start(bf16[1,512,512]{2,1,0:T(8,128)(2,1)} %get-tuple-element.55) | copy-start | bytes 1572868
  98.4 1.3 collective-permute-start.7
  99.8 4.0 %collective-permute-start.8 = (f32[4,12]{1,0:T(4,128)S(1)}, f32[4,12]{1,0:T(4,128)S(1)}, u32[]{:S(2)}, u32[]{:S(2)}) collective-permute-start(f32[4,12]{1,0:T(4,128)S(1)} %fusion.134), channel_id=1, source_target_pairs={{0,1},{1,0},{2,3},{3,2},{4,5},{5,4},{6,7},{7,6},{8,9},{9,8},{10,11... | collective-permute-start | bytes 584 | tf_op jit(solution)/shard_map/ppermute | solution.py:63
  103.8 3.6 %collective-permute-start.9 = (f32[4,12]{1,0:T(4,128)S(1)}, f32[4,12]{1,0:T(4,128)S(1)}, u32[]{:S(2)}, u32[]{:S(2)}) collective-permute-start(f32[4,12]{1,0:T(4,128)S(1)} %add.300), channel_id=1, source_target_pairs={{0,2},{1,3},{2,0},{3,1},{4,6},{5,7},{6,4},{7,5},{8,10},{9,11},{10,... | collective-permute-start | bytes 584 | tf_op jit(solution)/shard_map/ppermute | solution.py:63
Sparse Core Ops, SparseCore 0:
  122.0 41.7 reduce-scatter.1

commit v2 on v1

--- a/solution.py
+++ b/solution.py
@@ -93,14 +93,6 @@
     height = row_count * tile_len
     breadth = col_count * tile_len
     padded = extended(images, (("row", 1), ("col", 2)), HALO)
-    matched = jnp.zeros((exp_dev, tile_len, tile_len), jnp.float32)
-    for kernel in range(len(SIGMA_PARTS)):
-        table = band_table(tile_len, HALO, HALO * SIGMA_PARTS[kernel])
-        across = jnp.einsum(
-            "ij,ejl->eil", table, padded, preferred_element_type=jnp.float32
-        ).astype(jnp.bfloat16)
-        smoothed = jnp.einsum("eil,ml->eim", across, table, preferred_element_type=jnp.float32)
-        matched = matched + coeffs[:, kernel, None, None] * smoothed
     own_ids = visit_pos * exp_dev + jnp.arange(exp_dev, dtype=jnp.int32)
     first_col = pair_list[:, 0]
     second_col = pair_list[:, 1]
@@ -112,7 +104,7 @@
         axis=1,
     )
     offset = jnp.sum(jnp.where(hit_first | hit_second, offsets[None, :], 0), axis=1)
-    own_strip = jax.vmap(rows_from)(images, offset)
+    own_strip = jnp.stack([rows_from(images[e], offset[e]) for e in range(exp_dev)])
     listed = destinations[:, 0, 0, :]
     how_many = counts[:, 0, 0]
     usable = jnp.arange(MAXD, dtype=jnp.int32)[None, :] < how_many[:, None]
@@ -140,7 +132,27 @@
     theirs = jnp.take(strips_all, slot * exp_dev + partner % exp_dev, axis=0).astype(jnp.float32)
     own_patch = jnp.take(picked_all, visit_pos, axis=2).astype(jnp.float32)
     denominator = jnp.sum(own_patch).reshape(1)
-    nearby = jax.vmap(rows_from)(matched, offset)
+    tables = [band_table(tile_len, HALO, HALO * part) for part in SIGMA_PARTS]
+    window = STRIP + 2 * HALO
+    pieces = jnp.stack(
+        [lax.dynamic_slice_in_dim(padded[e], offset[e], window, 0) for e in range(exp_dev)]
+    )
+    nearby = jnp.zeros((exp_dev, STRIP, tile_len), jnp.float32)
+    for kernel in range(len(SIGMA_PARTS)):
+        table = tables[kernel]
+        across = jnp.einsum(
+            "ij,ejl->eil", table[:STRIP, :window], pieces, preferred_element_type=jnp.float32
+        ).astype(jnp.bfloat16)
+        smoothed = jnp.einsum("eil,ml->eim", across, table, preferred_element_type=jnp.float32)
+        nearby = nearby + coeffs[:, kernel, None, None] * smoothed
+    matched = jnp.zeros((exp_dev, tile_len, tile_len), jnp.float32)
+    for kernel in range(len(SIGMA_PARTS)):
+        table = tables[kernel]
+        across = jnp.einsum(
+            "ij,ejl->eil", table, padded, preferred_element_type=jnp.float32
+        ).astype(jnp.bfloat16)
+        smoothed = jnp.einsum("eil,ml->eim", across, table, preferred_element_type=jnp.float32)
+        matched = matched + coeffs[:, kernel, None, None] * smoothed
     difference = nearby - theirs
     pixel_weight = 1.0 / (1.0 + theirs * theirs)
     strip_rows = row_pos * tile_len + offset[:, None] + jnp.arange(STRIP, dtype=jnp.int32)[None, :]

time: 174 us -> 190 us (1.092)
  between operations: 29.2 us -> 42.4 us
  other arithmetic: 9.99 us -> 22.1 us
  local copies, waits for them, and re-layouts: 29.5 us -> 20.8 us
  waiting for transfers between devices: 50.3 us -> 44.1 us
  matrix products: 35.9 us -> 40.4 us
    dot_general x0 -> x2, matrix products: none -> 14.8 us  [the longest x1 10.5 us: shards(): jnp.einsum('eij,ejk->eik', row_maps, corrected, preferred_element_type=jn...]
    add x1 -> x0, local copies, waits for them, and re-layouts: 6.81 us -> none  [shards(): matched = matched + coeffs[:, kernel, None, None] * smoothed]
    convert_element_type x0 -> x3, other arithmetic: none -> 5.85 us  [band_table(): return jnp.where(jnp.abs(offset) <= width, values, 0.0).astype(jnp.bfloat16)]
    ppermute x3, waiting for transfers between devices: 4.8 us -> 0.01 us  [butterfly_sum(): values = jax.tree.map(lambda v: v + lax.ppermute(v, axis, pairs), values)]
    dot_general x3 -> x5, matrix products: 25.2 us -> 20.7 us  [shards(): jnp.einsum('eil,ml->eim', across, table, preferred_element_type=jnp.float32)]
    dot_general x1, matrix products: 6.72 us -> 2.89 us  [shards(): jnp.einsum('eik,elk->eil', halfway, col_maps, preferred_element_type=jnp....]
    gather x3 -> x0, local copies, waits for them, and re-layouts: 3.83 us -> none  [rows_from(): return lax.dynamic_slice_in_dim(source, anchor, STRIP, 0)]
    unnamed x23 -> x34, local copies, waits for them, and re-layouts: 7.21 us -> 4.21 us
  transfers between devices with their start and end apart: 11 -> 11, of which waited for: 6 -> 3; matrix products, arithmetic and copies ran while one was open for 28% -> 25% of each run, Pallas kernels for 0% -> 0%
where the time goes in v2:
time: 190 us; the launch traced here: 189 us
  waiting for transfers between devices  44.1 us (23%)
  between operations  42.4 us (22%)
  matrix products  40.4 us (21%)
  other arithmetic  22.1 us (12%)
  local copies, waits for them, and re-layouts  20.8 us (11%)
  starting transfers between devices  19.3 us (10%)
    reduce_scatter x1, waiting for transfers between devices, shards(): lax.psum_scatter(partial_sum.astype(jnp.bfloat16), 'visit', scatter_dimen...  39.5 us
    dot_general x5, matrix products, shards(): jnp.einsum('eil,ml->eim', across, table, preferred_element_type=jnp.float32)  20.7 us
    dot_general x1, matrix products, shards(): jnp.einsum('eij,ejk->eik', row_maps, corrected, preferred_element_type=jn...  10.5 us
    ppermute x3, starting transfers between devices, shards(): received.append(lax.ppermute(payload, 'visit', pairs))  7.86 us
    ppermute x2, starting transfers between devices, extended(): before = lax.ppermute(last, axis, up)  6.26 us
    convert_element_type x3, other arithmetic, band_table(): return jnp.where(jnp.abs(offset) <= width, values, 0.0).astype(jnp.bfloat16)  5.85 us
    dynamic_slice x1, local copies, waits for them, and re-layouts, shards(): lax.dynamic_index_in_dim(resample_bank, choose[e, 0], 0, False)  4.47 us
    dot_general x1, matrix products, shards(): jnp.einsum('ij,ejl->eil', table, padded, preferred_element_type=jnp.float32)  4.31 us
  transfers between devices with their start and end apart: 11, of which 3 were waited for; matrix products, arithmetic and copies ran while one was open for 25% of the time, Pallas kernels for 0%

profile of v2, /device:TPU:0, one launch (start us, length us, event | category | flops | bytes accessed | tf_op | source)
XLA Modules:
  0.0 189.1 jit_solution(12932408348202617450)
XLA Ops:
  21.3 4.0 %collective-permute-start.5 = (bf16[144,512]{1,0:T(8,128)(2,1)}, bf16[144,512]{1,0:T(8,128)(2,1)S(1)}, u32[]{:S(2)}, u32[]{:S(2)}) collective-permute-start(bf16[144,512]{1,0:T(8,128)(2,1)} %get-tuple-element.74), channel_id=1, source_target_pairs={{0,16},{8,24},{16,0},{24,8},{1,17},{9,25},{17,1},{25,9},{2,18},{10... | collective-permute-start | bytes 442376 | tf_op jit(solution)/shard_map/ppermute | solution.py:125
  26.9 2.2 %collective-permute-start.6 = (bf16[144,512]{1,0:T(8,128)(2,1)}, bf16[144,512]{1,0:T(8,128)(2,1)}, u32[]{:S(2)}, u32[]{:S(2)}) collective-permute-start(bf16[144,512]{1,0:T(8,128)(2,1)} %get-tuple-element.74), channel_id=1, source_target_pairs={{0,24},{8,0},{16,8},{24,16},{1,25},{9,1},{17,9},{25,17},{2,26},{10... | collective-permute-start | bytes 442376 | tf_op jit(solution)/shard_map/ppermute | solution.py:125
  33.3 3.1 %collective-permute-start = (bf16[4,16,512]{1,2,0:T(8,128)(2,1)}, bf16[4,16,512]{1,2,0:T(8,128)(2,1)S(1)}, u32[]{:S(2)}, u32[]{:S(2)}) collective-permute-start(bf16[4,16,512]{1,2,0:T(8,128)(2,1)} %copy.138), channel_id=1, source_target_pairs={{0,4},{1,5},{2,6},{3,7},{8,12},{9,13},{10,14},{11,15},{16,20},{17,... | collective-permute-start | bytes 196616 | tf_op jit(solution)/shard_map/ppermute | solution.py:21
  52.2 2.8 %copy.140 = bf16[4,512,512]{1,2,0:T(8,128)(2,1)S(1)} copy(bf16[4,512,512]{2,1,0:T(8,128)(2,1)} %param.10) | data formatting | bytes 4194304 | tf_op args[0]
  58.4 2.0 %select_convert_fusion = bf16[512,544]{0,1:T(8,128)(2,1)} fusion(f32[]{:T(128)} %exponential_reduce_fusion), kind=kLoop, calls=%fused_computation.48 | loop fusion | flops 3063808 | bytes 557060 | tf_op jit(solution)/shard_map/convert_element_type | solution.py:35
  60.4 1.9 %select_convert_fusion.1 = bf16[512,544]{0,1:T(8,128)(2,1)} fusion(f32[]{:T(128)} %exponential_reduce_fusion.1), kind=kLoop, calls=%fused_computation.49 | loop fusion | flops 3063808 | bytes 557060 | tf_op jit(solution)/shard_map/convert_element_type | solution.py:35
  62.3 1.9 %select_convert_fusion.2 = bf16[512,544]{0,1:T(8,128)(2,1)} fusion(f32[]{:T(128)} %exponential_reduce_fusion.2), kind=kLoop, calls=%fused_computation.50 | loop fusion | flops 3063808 | bytes 557060 | tf_op jit(solution)/shard_map/convert_element_type | solution.py:35
  69.3 4.5 %constant_dynamic-slice_fusion.16 = (bf16[1,512,512]{2,1,0:T(8,128)(2,1)}, bf16[1,512,512]{2,1,0:T(8,128)(2,1)}, bf16[1,512,512]{2,1,0:T(8,128)(2,1)}, bf16[1,51...) fusion(bf16[12,512,512]{2,1,0:T(8,128)(2,1)} %param.14, ...), kind=kLoop, calls=%fused_computation.111 | loop fusion | bytes 8388640 | tf_op jit(solution)/shard_map/jit(dynamic_index_in_dim)/dynamic_slice | solution.py:200
  73.9 3.2 %collective-permute-start.2 = (bf16[4,544,16]{1,2,0:T(8,128)(2,1)S(1)}, bf16[4,544,16]{1,2,0:T(8,128)(2,1)S(1)}, u32[]{:S(2)}, u32[]{:S(2)}) collective-permute-start(bf16[4,544,16]{1,2,0:T(8,128)(2,1)S(1)} %get-tuple-element.61), channel_id=1, source_target_pairs={{0,1},{1,2},{2,3},{4,5},{5,6},{6,7},{8,9},{9,10},{10,11},{12,13},{... | collective-permute-start | bytes 208904 | tf_op jit(solution)/shard_map/ppermute | solution.py:21
  79.2 4.3 %collective-permute-done.3 = bf16[4,544,16]{1,2,0:T(8,128)(2,1)S(1)} collective-permute-done((bf16[4,544,16]{1,2,0:T(8,128)(2,1)S(1)}, bf16[4,544,16]{1,2,0:T(8,128)(2,1)S(1)}, u32[]{:S(2)}, u32[]{:S(2)}) %collective-permute-start.3) | collective-permute-done | bytes 69664 | tf_op jit(solution)/shard_map/ppermute | solution.py:22
  83.5 2.0 %pad_maximum_fusion = bf16[4,544,544]{1,2,0:T(8,128)(2,1)S(1)} fusion(bf16[4,544,16]{1,2,0:T(8,128)(2,1)S(1)} %collective-permute-done.3, bf16[4,16,512]{1,2,0:T(8,128)(2,1)S(1)} %collective-permute-done.1, bf16[4,512,512]{1,2,0:T(8,128)(2,1)S(1)} %copy.140, bf16[4,16,512]{1,2,0:T(8,128)(2,1)S(1)} %collective-permute-done, ...), kind=kLoop, calls=%fused_computation.2 | loop fusion | flops 11837440 | bytes 4734976 | tf_op jit(solution)/shard_map/concatenate | solution.py:23
  87.4 2.2 %convolution_multiply_fusion.1 = f32[4,32,512]{2,1,0:T(8,128)S(1)} fusion(f32[]{:T(128)} %exponential_reduce_fusion.1, f32[4]{0:T(128)S(1)} %get-tuple-element.43, bf16[512,544]{0,1:T(8,128)(2,1)} %select_convert_fusion.1, bf16[1,64,544]{1,2,0:T(8,128)(2,1)S(1)} %get-tuple-element.106, bf16[1,64,544]{1,2,0:T(8,128)(2,1)S(1)} %get-tuple-element.107, ...), kind=kOutput, calls=%fused_computation.37 | convolution fusion | flops 83832832 | bytes 557584 | tf_op jit(solution)/shard_map/eil,ml->eim/dot_general | solution.py:146
  89.6 2.9 %fusion.44 = f32[4,32,512]{2,1,0:T(8,128)} fusion(f32[4,32,512]{2,1,0:T(8,128)S(1)} %convolution_multiply_fusion.1, f32[]{:T(128)} %exponential_reduce_fusion.2, f32[4]{0:T(128)S(1)} %get-tuple-element.42, bf16[512,544]{0,1:T(8,128)(2,1)} %select_convert_fusion.2, bf16[1,64,544]{1,2,0:T(8,128)(2,1)S(1)} %get-tuple-element.106, ...), kind=kOutput, calls=%fused_computation.39 | convolution fusion | flops 83898368 | bytes 819728 | tf_op jit(solution)/shard_map/eil,ml->eim/dot_general | solution.py:146
  94.7 3.0 %multiply_reduce_fusion.2 = (f32[4]{0:T(128)S(1)}, f32[4]{0:T(128)S(1)}, f32[4]{0:T(128)S(1)}, f32[4]{0:T(128)S(1)}, f32[4]{0:T(128)S(1)}, /*index=5*/f32[4]{0:T...) fusion(bf16[4,32,512]{2,1,0:T(8,128)(2,1)} %gather_fusion, pred[4]{0:T(512)(128)(4,1)} %compare_and_fusion, ...), kind=kOutput, calls=%fused_computation.69 | convolution fusion | flops 85405696 | bytes 762000 | tf_op jit(solution)/shard_map/eil,ml->eim/dot_general | solution.py:146
  98.5 6.3 %fusion = f32[4,512,512]{2,1,0:T(8,128)} fusion(bf16[4,544,544]{1,2,0:T(8,128)(2,1)S(1)} %copy-done.1, f32[]{:T(128)} %exponential_reduce_fusion), kind=kOutput, calls=%fused_computation.3 | convolution fusion | flops 2360246272 | bytes 6561796 | tf_op jit(solution)/shard_map/eil,ml->eim/dot_general | solution.py:154
  105.0 2.5 %collective-permute-start.8 = (f32[4,12]{1,0:T(4,128)S(1)}, f32[4,12]{1,0:T(4,128)S(1)}, u32[]{:S(2)}, u32[]{:S(2)}) collective-permute-start(f32[4,12]{1,0:T(4,128)S(1)} %fusion.132), channel_id=1, source_target_pairs={{0,1},{1,0},{2,3},{3,2},{4,5},{5,4},{6,7},{7,6},{8,9},{9,8},{10,11... | collective-permute-start | bytes 584 | tf_op jit(solution)/shard_map/ppermute | solution.py:63
  107.5 6.3 %fusion.2 = f32[4,512,512]{2,1,0:T(8,128)} fusion(bf16[4,544,544]{1,2,0:T(8,128)(2,1)S(1)} %copy-done.1, f32[]{:T(128)} %exponential_reduce_fusion.1), kind=kOutput, calls=%fused_computation.5 | convolution fusion | flops 2360246272 | bytes 6561796 | tf_op jit(solution)/shard_map/eil,ml->eim/dot_general | solution.py:154
  113.9 4.3 %fusion.59 = bf16[4,544,512]{2,1,0:T(8,128)(2,1)} fusion(bf16[4,544,544]{1,2,0:T(8,128)(2,1)S(1)} %copy-done.1, f32[]{:T(128)} %exponential_reduce_fusion.2), kind=kOutput, calls=%fused_computation.62 | convolution fusion | flops 1215217664 | bytes 4595716 | tf_op jit(solution)/shard_map/ij,ejl->eil/dot_general | solution.py:151
  120.4 10.5 %fusion.11 = bf16[4,512,512]{2,1,0:T(8,128)(2,1)} fusion(bf16[1,512,512]{2,1,0:T(8,128)(2,1)} %get-tuple-element.56, bf16[1,512,512]{2,1,0:T(8,128)(2,1)} %get-tuple-element.57, bf16[1,512,512]{2,1,0:T(8,128)(2,1)} %get-tuple-element.58, bf16[1,512,512]{2,1,0:T(8,128)(2,1)} %get-tuple-element.53, f32[4,512,512]{2,1,0:T(8,128)} %fusion, ...), kind=kOutput, calls=%fused_computation.12 | convolution fusion | flops 2229190656 | bytes 14827572 | tf_op jit(solution)/shard_map/eij,ejk->eik/dot_general | solution.py:205
  131.0 2.9 %fusion.33 = bf16[4,512,512]{2,1,0:T(8,128)(2,1)S(1)} fusion(bf16[1,512,512]{2,1,0:T(8,128)(2,1)S(1)} %copy-done.4, bf16[1,512,512]{2,1,0:T(8,128)(2,1)S(1)} %copy-done.5, bf16[1,512,512]{2,1,0:T(8,128)(2,1)S(1)} %copy-done.2, bf16[1,512,512]{2,1,0:T(8,128)(2,1)S(1)} %copy-done.3, bf16[4,512,512]{2,1,0:T(8,128)(2,1)} %fusion.11), kind=kOutput, calls=%fused_computation.32 | convolution fusion | flops 1077936128 | bytes 6291456 | tf_op jit(solution)/shard_map/eik,elk->eil/dot_general | solution.py:208
  133.9 2.0 %fusion.30 = bf16[4,512,512]{2,0,1:T(4,128)(2,1)S(1)} fusion(bf16[4,512,512]{2,1,0:T(8,128)(2,1)S(1)} %fusion.33, pred[4,4]{1,0:T(4,128)(4,1)S(1)} %fusion.65, bf16[4]{0:T(256)(128)(2,1)S(1)} %bitcast.180), kind=kOutput, calls=%fused_computation.31 | convolution fusion | flops 9437200 | bytes 4194328 | tf_op jit(solution)/shard_map/ev,eij->vij/dot_general | solution.py:211
  135.9 1.8 copy.160
  140.0 39.5 %reduce-scatter.2.cloned.1.call-done = bf16[1,512,512]{2,1,0:T(8,128)(2,1)} async-done(((bf16[4,512,512]{2,1,0:T(8,128)(2,1)}), bf16[1,512,512]{2,1,0:T(8,128)(2,1)}) %reduce-scatter.2.cloned.1.call-update) | async-done | bytes 524304 | tf_op jit(solution)/shard_map/reduce_scatter | solution.py:212
  179.5 2.8 %convert_divide_fusion = f32[1,512,512]{2,1,0:T(8,128)} fusion(bf16[1,512,512]{2,1,0:T(8,128)(2,1)} %reduce-scatter.2.cloned.1.call-done, f32[]{:T(128)} %convert_reduce_fusion), kind=kLoop, calls=%fused_computation.53 | loop fusion | flops 524288 | bytes 1572868 | tf_op jit(solution)/shard_map/div | solution.py:215
  (121 shorter events, 27.8 us)
Async XLA Ops:
  7.2 172.4 %reduce-scatter.2.cloned.1.call-start = ((), (), s32[]{:S(2)}) async-start(), calls=%async_computation.1 | async-start | bytes 2621440 | tf_op jit(solution)/shard_map/reduce_scatter | solution.py:212
  20.6 20.8 %copy-start.8 = (s32[4,1,1,2]{0,3,2,1:T(2,128)S(1)}, s32[4,1,1,2]{0,3,2,1:T(2,128)}, u32[]{:S(2)}) copy-start(s32[4,1,1,2]{0,3,2,1:T(2,128)} %param.15) | copy-start | bytes 100
  21.3 71.2 %collective-permute-start.5 = (bf16[144,512]{1,0:T(8,128)(2,1)}, bf16[144,512]{1,0:T(8,128)(2,1)S(1)}, u32[]{:S(2)}, u32[]{:S(2)}) collective-permute-start(bf16[144,512]{1,0:T(8,128)(2,1)} %get-tuple-element.74), channel_id=1, source_target_pairs={{0,16},{8,24},{16,0},{24,8},{1,17},{9,25},{17,1},{25,9},{2,18},{10... | collective-permute-start | bytes 442376 | tf_op jit(solution)/shard_map/ppermute | solution.py:125
  25.3 67.1 %collective-permute-start.4 = (bf16[144,512]{1,0:T(8,128)(2,1)}, bf16[144,512]{1,0:T(8,128)(2,1)}, u32[]{:S(2)}, u32[]{:S(2)}) collective-permute-start(bf16[144,512]{1,0:T(8,128)(2,1)} %get-tuple-element.74), channel_id=1, source_target_pairs={{0,8},{8,16},{16,24},{24,0},{1,9},{9,17},{17,25},{25,1},{2,10},{10... | collective-permute-start | bytes 442376 | tf_op jit(solution)/shard_map/ppermute | solution.py:125
  26.9 65.5 %collective-permute-start.6 = (bf16[144,512]{1,0:T(8,128)(2,1)}, bf16[144,512]{1,0:T(8,128)(2,1)}, u32[]{:S(2)}, u32[]{:S(2)}) collective-permute-start(bf16[144,512]{1,0:T(8,128)(2,1)} %get-tuple-element.74), channel_id=1, source_target_pairs={{0,24},{8,0},{16,8},{24,16},{1,25},{9,1},{17,9},{25,17},{2,26},{10... | collective-permute-start | bytes 442376 | tf_op jit(solution)/shard_map/ppermute | solution.py:125
  31.0 42.8 %collective-permute-start.1 = (bf16[4,16,512]{1,2,0:T(8,128)(2,1)}, bf16[4,16,512]{1,2,0:T(8,128)(2,1)S(1)}, u32[]{:S(2)}, u32[]{:S(2)}) collective-permute-start(bf16[4,16,512]{1,2,0:T(8,128)(2,1)} %copy.139), channel_id=1, source_target_pairs={{4,0},{5,1},{6,2},{7,3},{12,8},{13,9},{14,10},{15,11},{20,16},{21,... | collective-permute-start | bytes 196616 | tf_op jit(solution)/shard_map/ppermute | solution.py:22
  33.3 40.5 %collective-permute-start = (bf16[4,16,512]{1,2,0:T(8,128)(2,1)}, bf16[4,16,512]{1,2,0:T(8,128)(2,1)S(1)}, u32[]{:S(2)}, u32[]{:S(2)}) collective-permute-start(bf16[4,16,512]{1,2,0:T(8,128)(2,1)} %copy.138), channel_id=1, source_target_pairs={{0,4},{1,5},{2,6},{3,7},{8,12},{9,13},{10,14},{11,15},{16,20},{17,... | collective-permute-start | bytes 196616 | tf_op jit(solution)/shard_map/ppermute | solution.py:21
  55.7 31.6 %copy-start.13 = (f32[4]{0:T(128)}, f32[4]{0:T(128)S(1)}, u32[]{:S(2)}) copy-start(f32[4]{0:T(128)S(1)} %get-tuple-element.43) | copy-start | bytes 52
  55.7 33.8 %copy-start.11 = (f32[4]{0:T(128)}, f32[4]{0:T(128)S(1)}, u32[]{:S(2)}) copy-start(f32[4]{0:T(128)S(1)} %get-tuple-element.42) | copy-start | bytes 52
  73.9 5.2 %collective-permute-start.2 = (bf16[4,544,16]{1,2,0:T(8,128)(2,1)S(1)}, bf16[4,544,16]{1,2,0:T(8,128)(2,1)S(1)}, u32[]{:S(2)}, u32[]{:S(2)}) collective-permute-start(bf16[4,544,16]{1,2,0:T(8,128)(2,1)S(1)} %get-tuple-element.61), channel_id=1, source_target_pairs={{0,1},{1,2},{2,3},{4,5},{5,6},{6,7},{8,9},{9,10},{10,11},{12,13},{... | collective-permute-start | bytes 208904 | tf_op jit(solution)/shard_map/ppermute | solution.py:21
  77.1 6.3 %collective-permute-start.3 = (bf16[4,544,16]{1,2,0:T(8,128)(2,1)S(1)}, bf16[4,544,16]{1,2,0:T(8,128)(2,1)S(1)}, u32[]{:S(2)}, u32[]{:S(2)}) collective-permute-start(bf16[4,544,16]{1,2,0:T(8,128)(2,1)S(1)} %get-tuple-element.62), channel_id=1, source_target_pairs={{1,0},{2,1},{3,2},{5,4},{6,5},{7,6},{9,8},{10,9},{11,10},{13,12},{... | collective-permute-start | bytes 208904 | tf_op jit(solution)/shard_map/ppermute | solution.py:22
  94.7 3.8 %copy-start.1 = (bf16[4,544,544]{1,2,0:T(8,128)(2,1)S(1)}, bf16[4,544,544]{1,2,0:T(8,128)(2,1)}, u32[]{:S(2)}) copy-start(bf16[4,544,544]{1,2,0:T(8,128)(2,1)} %copy-done) | copy-start | bytes 7102468
  98.5 6.4 %collective-permute-start.7 = (f32[4,12]{1,0:T(4,128)S(1)}, f32[4,12]{1,0:T(4,128)S(1)}, u32[]{:S(2)}, u32[]{:S(2)}) collective-permute-start(f32[4,12]{1,0:T(4,128)S(1)} %pad_maximum_fusion.12), channel_id=1, source_target_pairs={{0,4},{4,0},{1,5},{5,1},{2,6},{6,2},{3,7},{7,3},{8,12},{12,8},{9,1... | collective-permute-start | bytes 584 | tf_op jit(solution)/shard_map/ppermute | solution.py:63
  105.0 8.9 %collective-permute-start.8 = (f32[4,12]{1,0:T(4,128)S(1)}, f32[4,12]{1,0:T(4,128)S(1)}, u32[]{:S(2)}, u32[]{:S(2)}) collective-permute-start(f32[4,12]{1,0:T(4,128)S(1)} %fusion.132), channel_id=1, source_target_pairs={{0,1},{1,0},{2,3},{3,2},{4,5},{5,4},{6,7},{7,6},{8,9},{9,8},{10,11... | collective-permute-start | bytes 584 | tf_op jit(solution)/shard_map/ppermute | solution.py:63
  113.8 5.8 %copy-start.15 = (pred[3,3]{1,0:T(4,128)(4,1)S(1)}, pred[3,3]{1,0:T(4,128)(4,1)}, u32[]{:S(2)}) copy-start(pred[3,3]{1,0:T(4,128)(4,1)} %iota_compare_fusion.1) | copy-start | bytes 31
  113.8 6.5 %copy-start.10 = (f32[4]{0:T(128)S(1)}, f32[4]{0:T(128)}, u32[]{:S(2)}) copy-start(f32[4]{0:T(128)} %get-tuple-element.41) | copy-start | bytes 52
  113.8 6.5 %copy-start.12 = (f32[4]{0:T(128)S(1)}, f32[4]{0:T(128)}, u32[]{:S(2)}) copy-start(f32[4]{0:T(128)} %copy-done.11) | copy-start | bytes 52
  113.8 6.5 %copy-start.14 = (f32[4]{0:T(128)S(1)}, f32[4]{0:T(128)}, u32[]{:S(2)}) copy-start(f32[4]{0:T(128)} %copy-done.13) | copy-start | bytes 52
  113.9 4.4 %collective-permute-start.9 = (f32[4,12]{1,0:T(4,128)S(1)}, f32[4,12]{1,0:T(4,128)S(1)}, u32[]{:S(2)}, u32[]{:S(2)}) collective-permute-start(f32[4,12]{1,0:T(4,128)S(1)} %add.326), channel_id=1, source_target_pairs={{0,2},{1,3},{2,0},{3,1},{4,6},{5,7},{6,4},{7,5},{8,10},{9,11},{10,... | collective-permute-start | bytes 584 | tf_op jit(solution)/shard_map/ppermute | solution.py:63
  120.4 10.6 %copy-start.2 = (bf16[1,512,512]{2,1,0:T(8,128)(2,1)S(1)}, bf16[1,512,512]{2,1,0:T(8,128)(2,1)}, u32[]{:S(2)}) copy-start(bf16[1,512,512]{2,1,0:T(8,128)(2,1)} %get-tuple-element.54) | copy-start | bytes 1572868
  120.4 10.6 %copy-start.3 = (bf16[1,512,512]{2,1,0:T(8,128)(2,1)S(1)}, bf16[1,512,512]{2,1,0:T(8,128)(2,1)}, u32[]{:S(2)}) copy-start(bf16[1,512,512]{2,1,0:T(8,128)(2,1)} %get-tuple-element.55) | copy-start | bytes 1572868
  120.4 10.6 %copy-start.4 = (bf16[1,512,512]{2,1,0:T(8,128)(2,1)S(1)}, bf16[1,512,512]{2,1,0:T(8,128)(2,1)}, u32[]{:S(2)}) copy-start(bf16[1,512,512]{2,1,0:T(8,128)(2,1)} %get-tuple-element.59) | copy-start | bytes 1572868
  120.4 10.6 %copy-start.5 = (bf16[1,512,512]{2,1,0:T(8,128)(2,1)S(1)}, bf16[1,512,512]{2,1,0:T(8,128)(2,1)}, u32[]{:S(2)}) copy-start(bf16[1,512,512]{2,1,0:T(8,128)(2,1)} %get-tuple-element.60) | copy-start | bytes 1572868
  131.0 2.9 %copy-start.9 = (bf16[4,1,1]{0,2,1:T(2,128)(2,1)S(1)}, bf16[4,1,1]{0,2,1:T(2,128)(2,1)}, u32[]{:S(2)}) copy-start(bf16[4,1,1]{0,2,1:T(2,128)(2,1)} %param.13) | copy-start | bytes 28
  (3 other events, 6.6 us)
Sparse Core Ops, SparseCore 0:
  137.8 41.6 reduce-scatter.1

commit v3 on v2

--- a/solution.py
+++ b/solution.py
@@ -2,6 +2,8 @@
 import jax.numpy as jnp
 from jax import lax
 from jax.sharding import PartitionSpec as P
+from jax.experimental import pallas as pl
+from jax.experimental.pallas import tpu as pltpu
 
 HALO = 16
 STRIP = 32
@@ -77,6 +79,48 @@
     return values
 
 
+def warp_body(idx_ref, plane_ref, xrow_ref, ycol_ref, matched_ref, rmap_ref, cmap_ref, out_ref):
+    e = pl.program_id(0)
+    background = (
+        plane_ref[e, 0] + plane_ref[e, 1] * xrow_ref[...]
+    ) + plane_ref[e, 2] * ycol_ref[...]
+    corrected = (matched_ref[0] - background).astype(jnp.bfloat16)
+    halfway = jnp.dot(rmap_ref[0], corrected, preferred_element_type=jnp.float32)
+    warped = lax.dot_general(
+        halfway.astype(jnp.bfloat16), cmap_ref[0], (((1,), (1,)), ((), ())),
+        preferred_element_type=jnp.float32,
+    )
+    out_ref[0] = warped.astype(jnp.bfloat16)
+
+
+def warp_tiles(choose, plane, xrow, ycol, matched, bank):
+    exp_dev, tile_len = matched.shape[0], matched.shape[1]
+    grid_spec = pltpu.PrefetchScalarGridSpec(
+        num_scalar_prefetch=1,
+        grid=(exp_dev,),
+        in_specs=[
+            pl.BlockSpec(memory_space=pltpu.SMEM),
+            pl.BlockSpec((1, tile_len), lambda e, idx: (0, 0)),
+            pl.BlockSpec((tile_len, 1), lambda e, idx: (0, 0)),
+            pl.BlockSpec((1, tile_len, tile_len), lambda e, idx: (e, 0, 0)),
+            pl.BlockSpec((1, tile_len, tile_len), lambda e, idx: (idx[e, 0], 0, 0)),
+            pl.BlockSpec((1, tile_len, tile_len), lambda e, idx: (idx[e, 1], 0, 0)),
+        ],
+        out_specs=pl.BlockSpec((1, tile_len, tile_len), lambda e, idx: (e, 0, 0)),
+    )
+    flops = exp_dev * 4 * tile_len ** 3
+    moved = exp_dev * tile_len * tile_len * (4 + 2 + 2 + 2)
+    return pl.pallas_call(
+        warp_body,
+        grid_spec=grid_spec,
+        out_shape=jax.ShapeDtypeStruct(matched.shape, jnp.bfloat16),
+        compiler_params=pltpu.CompilerParams(
+            dimension_semantics=("arbitrary",), vmem_limit_bytes=48 * 1024 * 1024
+        ),
+        cost_estimate=pl.CostEstimate(flops=flops, bytes_accessed=moved, transcendentals=0),
+    )(choose, plane, xrow, ycol, matched, bank, bank)
+
+
 def rows_from(source, anchor):
     return lax.dynamic_slice_in_dim(source, anchor, STRIP, 0)
 
@@ -104,7 +148,13 @@
         axis=1,
     )
     offset = jnp.sum(jnp.where(hit_first | hit_second, offsets[None, :], 0), axis=1)
-    own_strip = jnp.stack([rows_from(images[e], offset[e]) for e in range(exp_dev)])
+    pick_rows = (
+        lax.broadcasted_iota(jnp.int32, (exp_dev, STRIP, tile_len), 2)
+        == offset[:, None, None] + lax.broadcasted_iota(jnp.int32, (exp_dev, STRIP, tile_len), 1)
+    ).astype(jnp.bfloat16)
+    own_strip = jnp.einsum(
+        "esr,erl->esl", pick_rows, images, preferred_element_type=jnp.float32
+    ).astype(jnp.bfloat16)
     listed = destinations[:, 0, 0, :]
     how_many = counts[:, 0, 0]
     usable = jnp.arange(MAXD, dtype=jnp.int32)[None, :] < how_many[:, None]
@@ -129,19 +179,24 @@
     picked_all = picked_all.reshape(visit_count, exp_dev, visit_count)
     partner_visit = partner // exp_dev
     slot = (visit_pos - partner_visit) % visit_count
-    theirs = jnp.take(strips_all, slot * exp_dev + partner % exp_dev, axis=0).astype(jnp.float32)
+    source = slot * exp_dev + partner % exp_dev
+    choose_strip = (
+        lax.broadcasted_iota(jnp.int32, (exp_dev, visit_count * exp_dev), 1) == source[:, None]
+    ).astype(jnp.bfloat16)
+    theirs = jnp.einsum(
+        "ej,jsl->esl", choose_strip, strips_all, preferred_element_type=jnp.float32
+    )
     own_patch = jnp.take(picked_all, visit_pos, axis=2).astype(jnp.float32)
     denominator = jnp.sum(own_patch).reshape(1)
     tables = [band_table(tile_len, HALO, HALO * part) for part in SIGMA_PARTS]
-    window = STRIP + 2 * HALO
-    pieces = jnp.stack(
-        [lax.dynamic_slice_in_dim(padded[e], offset[e], window, 0) for e in range(exp_dev)]
-    )
     nearby = jnp.zeros((exp_dev, STRIP, tile_len), jnp.float32)
     for kernel in range(len(SIGMA_PARTS)):
         table = tables[kernel]
+        strip_table = jnp.einsum(
+            "esr,rj->esj", pick_rows, table, preferred_element_type=jnp.float32
+        ).astype(jnp.bfloat16)
         across = jnp.einsum(
-            "ij,ejl->eil", table[:STRIP, :window], pieces, preferred_element_type=jnp.float32
+            "esj,ejl->esl", strip_table, padded, preferred_element_type=jnp.float32
         ).astype(jnp.bfloat16)
         smoothed = jnp.einsum("eil,ml->eim", across, table, preferred_element_type=jnp.float32)
         nearby = nearby + coeffs[:, kernel, None, None] * smoothed
@@ -189,25 +244,11 @@
     moments = packed[:, 9:]
     plane_fit = solve_three(normal, moments)
     row_coord = centred(row_pos * tile_len + jnp.arange(tile_len, dtype=jnp.int32), height)
-    background = (
-        plane_fit[:, 0, None, None]
-        + plane_fit[:, 1, None, None] * xcoord[None, None, :]
-        + plane_fit[:, 2, None, None] * row_coord[None, :, None]
-    )
-    corrected = (matched - background).astype(jnp.bfloat16)
     choose = warp_index[:, 0, 0, :]
-    row_maps = jnp.stack(
-        [lax.dynamic_index_in_dim(resample_bank, choose[e, 0], 0, False) for e in range(exp_dev)]
-    )
-    col_maps = jnp.stack(
-        [lax.dynamic_index_in_dim(resample_bank, choose[e, 1], 0, False) for e in range(exp_dev)]
-    )
-    halfway = jnp.einsum(
-        "eij,ejk->eik", row_maps, corrected, preferred_element_type=jnp.float32
-    ).astype(jnp.bfloat16)
-    warped = jnp.einsum(
-        "eik,elk->eil", halfway, col_maps, preferred_element_type=jnp.float32
-    ).astype(jnp.bfloat16)
+    warped = warp_tiles(
+        choose, plane_fit, xcoord.reshape(1, tile_len), row_coord.reshape(tile_len, 1),
+        matched, resample_bank,
+    )
     partial_sum = jnp.einsum("ev,eij->vij", picked, warped, preferred_element_type=jnp.float32)
     numerator = lax.psum_scatter(
         partial_sum.astype(jnp.bfloat16), "visit", scatter_dimension=0, tiled=True

time: 190 us -> 164 us (0.86)
  between operations: 42.4 us -> 14.4 us
  matrix products: 40.4 us -> 57 us
  other arithmetic: 22.1 us -> 10.5 us
  local copies, waits for them, and re-layouts: 20.8 us -> 9.34 us
  Pallas kernels: 0 us -> 6.33 us
  starting transfers between devices: 19.3 us -> 22.5 us
    dot_general x5 -> x6, matrix products: 20.7 us -> 38.6 us  [shards(): jnp.einsum('eil,ml->eim', across, table, preferred_element_type=jnp.float32)]
    pallas_call x0 -> x1, Pallas kernels: none -> 6.33 us  [warp_tiles(): pl.pallas_call(warp_body, grid_spec=grid_spec, out_shape=jax.ShapeDtypeSt...]
    convert_element_type x3 -> x0, other arithmetic: 5.85 us -> none  [band_table(): return jnp.where(jnp.abs(offset) <= width, values, 0.0).astype(jnp.bfloat16)]
    dynamic_slice x5 -> x0, local copies, waits for them, and re-layouts: 4.85 us -> none  [the longest x1 4.47 us: shards(): lax.dynamic_index_in_dim(resample_bank, choose[e, 0], 0, False)]
    ppermute x2, waiting for transfers between devices: 4.3 us -> 0.01 us  [extended(): after = lax.ppermute(initial, axis, down)]
    slice x6 -> x1, local copies, waits for them, and re-layouts: 4.02 us -> 0.18 us  [shards(): nearby = nearby + coeffs[:, kernel, None, None] * smoothed]
    concatenate x1 -> x0, other arithmetic: 2.01 us -> none  [extended(): value = jnp.concatenate([before, value, after], axis=dim)]
    dot_general x3 -> x5, matrix products: 17.7 us -> 16.4 us  [the longest x3 13.4 us: shards(): jnp.einsum('esj,ejl->esl', strip_table, padded, preferred_element_type=jn...]
  transfers between devices with their start and end apart: 11 -> 11, of which waited for: 3 -> 2; matrix products, arithmetic and copies ran while one was open for 25% -> 35% of each run, Pallas kernels for 0% -> 0%
where the time goes in v3:
time: 164 us; the launch traced here: 163 us
  matrix products  57 us (35%)
  waiting for transfers between devices  42.8 us (26%)
  starting transfers between devices  22.5 us (14%)
  between operations  14.4 us (9%)
  other arithmetic  10.5 us (6%)
  local copies, waits for them, and re-layouts  9.34 us (6%)
  Pallas kernels  6.33 us (4%)
    reduce_scatter x1, waiting for transfers between devices, shards(): lax.psum_scatter(partial_sum.astype(jnp.bfloat16), 'visit', scatter_dimen...  40.9 us
    dot_general x6, matrix products, shards(): jnp.einsum('eil,ml->eim', across, table, preferred_element_type=jnp.float32)  38.6 us
    dot_general x3, matrix products, shards(): jnp.einsum('esj,ejl->esl', strip_table, padded, preferred_element_type=jn...  13.4 us
    ppermute x3, starting transfers between devices, shards(): received.append(lax.ppermute(payload, 'visit', pairs))  7.93 us
    ppermute x2, starting transfers between devices, extended(): before = lax.ppermute(last, axis, up)  7.76 us
    pallas_call x1, Pallas kernels, warp_tiles(): pl.pallas_call(warp_body, grid_spec=grid_spec, out_shape=jax.ShapeDtypeSt...  6.33 us
    ppermute x3, starting transfers between devices, butterfly_sum(): values = jax.tree.map(lambda v: v + lax.ppermute(v, axis, pairs), values)  4.23 us
    unnamed x25, local copies, waits for them, and re-layouts  3.86 us
  transfers between devices with their start and end apart: 11, of which 2 were waited for; matrix products, arithmetic and copies ran while one was open for 35% of the time, Pallas kernels for 0%

profile of v3, /device:TPU:0, one launch (start us, length us, event | category | flops | bytes accessed | tf_op | source)
XLA Modules:
  0.0 162.9 jit_solution(10342549337950484177)
XLA Ops:
  10.6 2.2 %convolution_convert_fusion.6 = bf16[4,32,512]{2,1,0:T(8,128)(2,1)S(1)} fusion(bf16[4,512,512]{2,1,0:T(8,128)(2,1)} %param.10, s32[4]{0:T(128)S(1)} %get-tuple-element.42), kind=kOutput, calls=%fused_computation.24 | convolution fusion | flops 67305472 | bytes 2228240 | tf_op jit(solution)/shard_map/esr,erl->esl/dot_general | solution.py:155
  12.9 4.1 %collective-permute-start.1 = (bf16[144,512]{1,0:T(8,128)(2,1)S(1)}, bf16[144,512]{1,0:T(8,128)(2,1)S(1)}, u32[]{:S(2)}, u32[]{:S(2)}) collective-permute-start(bf16[144,512]{1,0:T(8,128)(2,1)S(1)} %get-tuple-element.53), channel_id=1, source_target_pairs={{0,16},{8,24},{16,0},{24,8},{1,17},{9,25},{17,1},{25,9},{2,18},{10... | collective-permute-start | bytes 442376 | tf_op jit(solution)/shard_map/ppermute | solution.py:175
  17.0 1.6 collective-permute-start
  18.5 2.2 %collective-permute-start.2 = (bf16[144,512]{1,0:T(8,128)(2,1)S(1)}, bf16[144,512]{1,0:T(8,128)(2,1)S(1)}, u32[]{:S(2)}, u32[]{:S(2)}) collective-permute-start(bf16[144,512]{1,0:T(8,128)(2,1)S(1)} %get-tuple-element.53), channel_id=1, source_target_pairs={{0,24},{8,0},{16,8},{24,16},{1,25},{9,1},{17,9},{25,17},{2,26},{10... | collective-permute-start | bytes 442376 | tf_op jit(solution)/shard_map/ppermute | solution.py:175
  22.1 3.0 %collective-permute-start.3 = (bf16[4,16,512]{2,1,0:T(8,128)(2,1)S(1)}, bf16[4,16,512]{2,1,0:T(8,128)(2,1)S(1)}, u32[]{:S(2)}, u32[]{:S(2)}) collective-permute-start(bf16[4,16,512]{2,1,0:T(8,128)(2,1)S(1)} %get-tuple-element.49), channel_id=1, source_target_pairs={{0,4},{1,5},{2,6},{3,7},{8,12},{9,13},{10,14},{11,15},{16,20},{17,... | collective-permute-start | bytes 196616 | tf_op jit(solution)/shard_map/ppermute | solution.py:23
  27.8 1.4 copy-done.2
  31.2 4.7 %collective-permute-start.5 = (bf16[4,544,16]{1,2,0:T(8,128)(2,1)S(1)}, bf16[4,544,16]{1,2,0:T(8,128)(2,1)S(1)}, u32[]{:S(2)}, u32[]{:S(2)}) collective-permute-start(bf16[4,544,16]{1,2,0:T(8,128)(2,1)S(1)} %copy.137), channel_id=1, source_target_pairs={{0,1},{1,2},{2,3},{4,5},{5,6},{6,7},{8,9},{9,10},{10,11},{12,13},{... | collective-permute-start | bytes 208904 | tf_op jit(solution)/shard_map/ppermute | solution.py:23
  35.9 1.8 %collective-permute-done.5 = bf16[4,544,16]{1,2,0:T(8,128)(2,1)S(1)} collective-permute-done((bf16[4,544,16]{1,2,0:T(8,128)(2,1)S(1)}, bf16[4,544,16]{1,2,0:T(8,128)(2,1)S(1)}, u32[]{:S(2)}, u32[]{:S(2)}) %collective-permute-start.5) | collective-permute-done | bytes 69664 | tf_op jit(solution)/shard_map/ppermute | solution.py:23
  39.8 4.8 %convolution_convert_fusion.2 = bf16[4,32,544]{2,1,0:T(8,128)(2,1)} fusion(f32[]{:T(128)} %exponential_reduce_fusion.1, s32[4]{0:T(128)S(1)} %get-tuple-element.42, bf16[4,544,16]{2,1,0:T(8,128)(2,1)S(1)} %copy.140, bf16[4,544,512]{2,1,0:T(8,128)(2,1)} %copy-done.2, bf16[4,544,16]{2,1,0:T(8,128)(2,1)S(1)} %copy.139), kind=kOutput, calls=%fused_computation.20 | convolution fusion | flops 157499392 | bytes 2506772 | tf_op jit(solution)/shard_map/esj,ejl->esl/dot_general | solution.py:198
  44.5 3.0 %fusion.33 = f32[4,32,512]{2,1,0:T(8,128)} fusion(bf16[4,32,544]{2,1,0:T(8,128)(2,1)} %convolution_convert_fusion.2, f32[]{:T(128)} %exponential_reduce_fusion.1), kind=kOutput, calls=%fused_computation.36 | convolution fusion | flops 74366976 | bytes 401412 | tf_op jit(solution)/shard_map/eil,ml->eim/dot_general | solution.py:201
  47.5 4.4 %convolution_convert_fusion = bf16[4,32,544]{2,1,0:T(8,128)(2,1)} fusion(f32[]{:T(128)} %exponential_reduce_fusion, s32[4]{0:T(128)S(1)} %get-tuple-element.42, bf16[4,544,16]{2,1,0:T(8,128)(2,1)} %copy-done.5, bf16[4,544,512]{2,1,0:T(8,128)(2,1)S(1)} %copy-done.3, bf16[4,544,16]{2,1,0:T(8,128)(2,1)} %copy-done.4), kind=kOutput, calls=%fused_computation.18 | convolution fusion | flops 157499392 | bytes 2506772 | tf_op jit(solution)/shard_map/esj,ejl->esl/dot_general | solution.py:198
  51.9 2.9 %fusion.27 = f32[4,32,512]{2,1,0:T(8,128)} fusion(bf16[4,32,544]{2,1,0:T(8,128)(2,1)} %convolution_convert_fusion, f32[]{:T(128)} %exponential_reduce_fusion), kind=kOutput, calls=%fused_computation.35 | convolution fusion | flops 74366976 | bytes 401412 | tf_op jit(solution)/shard_map/eil,ml->eim/dot_general | solution.py:201
  54.8 4.3 %convolution_convert_fusion.4 = bf16[4,32,544]{2,1,0:T(8,128)(2,1)} fusion(f32[]{:T(128)} %exponential_reduce_fusion.2, s32[4]{0:T(128)S(1)} %get-tuple-element.42, bf16[4,544,16]{2,1,0:T(8,128)(2,1)} %copy-done.5, bf16[4,544,512]{2,1,0:T(8,128)(2,1)S(1)} %copy-done.3, bf16[4,544,16]{2,1,0:T(8,128)(2,1)} %copy-done.4), kind=kOutput, calls=%fused_computation.22 | convolution fusion | flops 157499392 | bytes 2506772 | tf_op jit(solution)/shard_map/esj,ejl->esl/dot_general | solution.py:198
  59.0 2.1 %fusion.39 = f32[4,32,512]{2,1,0:T(8,128)S(1)} fusion(bf16[4,32,544]{2,1,0:T(8,128)(2,1)} %convolution_convert_fusion.4, f32[]{:T(128)} %exponential_reduce_fusion.2), kind=kOutput, calls=%fused_computation.37 | convolution fusion | flops 74366976 | bytes 401412 | tf_op jit(solution)/shard_map/eil,ml->eim/dot_general | solution.py:201
  64.4 9.5 %fusion = f32[4,512,512]{2,1,0:T(8,128)} fusion(f32[]{:T(128)} %exponential_reduce_fusion, bf16[4,544,16]{2,1,0:T(8,128)(2,1)} %copy-done.5, bf16[4,544,512]{2,1,0:T(8,128)(2,1)S(1)} %copy-done.3, bf16[4,544,16]{2,1,0:T(8,128)(2,1)} %copy-done.4), kind=kOutput, calls=%fused_computation.2 | convolution fusion | flops 2367348736 | bytes 6561796 | tf_op jit(solution)/shard_map/eil,ml->eim/dot_general | solution.py:209
  73.9 2.4 %collective-permute-start.8 = (f32[4,12]{1,0:T(4,128)S(1)}, f32[4,12]{1,0:T(4,128)S(1)}, u32[]{:S(2)}, u32[]{:S(2)}) collective-permute-start(f32[4,12]{1,0:T(4,128)S(1)} %fusion.134), channel_id=1, source_target_pairs={{0,1},{1,0},{2,3},{3,2},{4,5},{5,4},{6,7},{7,6},{8,9},{9,8},{10,11... | collective-permute-start | bytes 584 | tf_op jit(solution)/shard_map/ppermute | solution.py:65
  76.3 9.2 %fusion.2 = f32[4,512,512]{2,1,0:T(8,128)} fusion(f32[]{:T(128)} %exponential_reduce_fusion.1, bf16[4,544,16]{2,1,0:T(8,128)(2,1)} %copy-done.5, bf16[4,544,512]{2,1,0:T(8,128)(2,1)S(1)} %copy-done.3, bf16[4,544,16]{2,1,0:T(8,128)(2,1)} %copy-done.4), kind=kOutput, calls=%fused_computation.4 | convolution fusion | flops 2367348736 | bytes 6561796 | tf_op jit(solution)/shard_map/eil,ml->eim/dot_general | solution.py:209
  85.5 1.8 %collective-permute-start.9 = (f32[4,12]{1,0:T(4,128)S(1)}, f32[4,12]{1,0:T(4,128)S(1)}, u32[]{:S(2)}, u32[]{:S(2)}) collective-permute-start(f32[4,12]{1,0:T(4,128)S(1)} %add.241), channel_id=1, source_target_pairs={{0,2},{1,3},{2,0},{3,1},{4,6},{5,7},{6,4},{7,5},{8,10},{9,11},{10,... | collective-permute-start | bytes 584 | tf_op jit(solution)/shard_map/ppermute | solution.py:65
  87.3 12.0 %multiply_add_fusion.matched_ref = f32[4,512,512]{2,1,0:T(8,128)} fusion(f32[4,512,512]{2,1,0:T(8,128)} %fusion, f32[4,512,512]{2,1,0:T(8,128)} %fusion.2, f32[4]{0:T(128)S(1)} %get-tuple-element.39, f32[4]{0:T(128)S(1)} %get-tuple-element.40, f32[4]{0:T(128)S(1)} %get-tuple-element.38, f32[]{:T(128)} %exponential_reduce_fusion.2, ...), kind=kOutput, calls=%fused_computation | convolution fusion | flops 2372591616 | bytes 14950452 | tf_op jit(solution)/shard_map/eil,ml->eim/dot_general | solution.py:209
  101.4 6.3 %shard_map.95 = bf16[4,512,512]{2,1,0:T(8,128)(2,1)S(1)} custom-call(s32[4,2]{1,0:T(4,128)S(1)} %copy.163.idx_ref, f32[4,3]{1,0:T(4,128)S(1)} %pad_maximum_fusion.8.plane_ref, f32[1,512]{1,0:T(1,128)S(1)} %multiply_add_fusion.2.xrow_ref, f32[512,1]{1,0:T(8,128)S(1)} %multiply_add_fusion.1.ycol_ref, f32[4,512,512]{2,1,0:T(8,128)} %multiply_add_fusion.matched_ref, ...), custom_call_target="tpu_custom_call" | custom-call | flops 2147483648 | bytes 10485760 | tf_op jit(solution)/shard_map/pallas_call | solution.py:113
  107.8 2.0 %fusion.13 = bf16[4,512,512]{2,0,1:T(4,128)(2,1)S(1)} fusion(bf16[4,512,512]{2,1,0:T(8,128)(2,1)S(1)} %shard_map.95, pred[4,4]{1,0:T(4,128)(4,1)S(1)} %fusion.57, bf16[4]{0:T(256)(128)(2,1)S(1)} %bitcast.123), kind=kOutput, calls=%fused_computation.13 | convolution fusion | flops 9437200 | bytes 4194328 | tf_op jit(solution)/shard_map/ev,eij->vij/dot_general | solution.py:252
  109.8 1.8 %copy.166 = bf16[4,512,512]{2,1,0:T(8,128)(2,1)} copy(bf16[4,512,512]{2,0,1:T(4,128)(2,1)S(1)} %fusion.13) | data formatting | bytes 4194304 | tf_op jit(solution)/shard_map/convert_element_type | solution.py:254
  112.4 40.9 %reduce-scatter.2.cloned.1.call-done = bf16[1,512,512]{2,1,0:T(8,128)(2,1)} async-done(((bf16[4,512,512]{2,1,0:T(8,128)(2,1)}), bf16[1,512,512]{2,1,0:T(8,128)(2,1)}) %reduce-scatter.2.cloned.1.call-update) | async-done | bytes 524304 | tf_op jit(solution)/shard_map/reduce_scatter | solution.py:253
  153.3 2.8 %convert_divide_fusion = f32[1,512,512]{2,1,0:T(8,128)} fusion(bf16[1,512,512]{2,1,0:T(8,128)(2,1)} %reduce-scatter.2.cloned.1.call-done, f32[]{:T(128)} %convert_reduce_fusion), kind=kLoop, calls=%fused_computation.30 | loop fusion | flops 524288 | bytes 1572868 | tf_op jit(solution)/shard_map/div | solution.py:256
  (100 shorter events, 17.4 us)
Async XLA Ops:
  7.2 146.1 %reduce-scatter.2.cloned.1.call-start = ((), (), s32[]{:S(2)}) async-start(), calls=%async_computation.1 | async-start | bytes 2621440 | tf_op jit(solution)/shard_map/reduce_scatter | solution.py:253
  10.6 10.2 %copy-start.1 = (bf16[4,512,512]{2,1,0:T(8,128)(2,1)S(1)}, bf16[4,512,512]{2,1,0:T(8,128)(2,1)}, u32[]{:S(2)}) copy-start(bf16[4,512,512]{2,1,0:T(8,128)(2,1)} %param.10) | copy-start | bytes 6291460
  10.6 16.5 %copy-start.6 = (f32[4,3]{1,0:T(4,128)S(1)}, f32[4,3]{1,0:T(4,128)}, u32[]{:S(2)}) copy-start(f32[4,3]{1,0:T(4,128)} %param.11) | copy-start | bytes 148
  10.6 16.8 %copy-start.7 = (s32[4,1,1,2]{0,3,2,1:T(2,128)S(1)}, s32[4,1,1,2]{0,3,2,1:T(2,128)}, u32[]{:S(2)}) copy-start(s32[4,1,1,2]{0,3,2,1:T(2,128)} %param.15) | copy-start | bytes 100
  12.9 48.3 %collective-permute-start.1 = (bf16[144,512]{1,0:T(8,128)(2,1)S(1)}, bf16[144,512]{1,0:T(8,128)(2,1)S(1)}, u32[]{:S(2)}, u32[]{:S(2)}) collective-permute-start(bf16[144,512]{1,0:T(8,128)(2,1)S(1)} %get-tuple-element.53), channel_id=1, source_target_pairs={{0,16},{8,24},{16,0},{24,8},{1,17},{9,25},{17,1},{25,9},{2,18},{10... | collective-permute-start | bytes 442376 | tf_op jit(solution)/shard_map/ppermute | solution.py:175
  17.0 44.2 %collective-permute-start = (bf16[144,512]{1,0:T(8,128)(2,1)S(1)}, bf16[144,512]{1,0:T(8,128)(2,1)S(1)}, u32[]{:S(2)}, u32[]{:S(2)}) collective-permute-start(bf16[144,512]{1,0:T(8,128)(2,1)S(1)} %get-tuple-element.53), channel_id=1, source_target_pairs={{0,8},{8,16},{16,24},{24,0},{1,9},{9,17},{17,25},{25,1},{2,10},{10... | collective-permute-start | bytes 442376 | tf_op jit(solution)/shard_map/ppermute | solution.py:175
  18.5 42.6 %collective-permute-start.2 = (bf16[144,512]{1,0:T(8,128)(2,1)S(1)}, bf16[144,512]{1,0:T(8,128)(2,1)S(1)}, u32[]{:S(2)}, u32[]{:S(2)}) collective-permute-start(bf16[144,512]{1,0:T(8,128)(2,1)S(1)} %get-tuple-element.53), channel_id=1, source_target_pairs={{0,24},{8,0},{16,8},{24,16},{1,25},{9,1},{17,9},{25,17},{2,26},{10... | collective-permute-start | bytes 442376 | tf_op jit(solution)/shard_map/ppermute | solution.py:175
  20.8 7.0 %collective-permute-start.4 = (bf16[4,16,512]{2,1,0:T(8,128)(2,1)S(1)}, bf16[4,16,512]{2,1,0:T(8,128)(2,1)S(1)}, u32[]{:S(2)}, u32[]{:S(2)}) collective-permute-start(bf16[4,16,512]{2,1,0:T(8,128)(2,1)S(1)} %get-tuple-element.48), channel_id=1, source_target_pairs={{4,0},{5,1},{6,2},{7,3},{12,8},{13,9},{14,10},{15,11},{20,16},{21,... | collective-permute-start | bytes 196616 | tf_op jit(solution)/shard_map/ppermute | solution.py:24
  22.1 5.5 %collective-permute-start.3 = (bf16[4,16,512]{2,1,0:T(8,128)(2,1)S(1)}, bf16[4,16,512]{2,1,0:T(8,128)(2,1)S(1)}, u32[]{:S(2)}, u32[]{:S(2)}) collective-permute-start(bf16[4,16,512]{2,1,0:T(8,128)(2,1)S(1)} %get-tuple-element.49), channel_id=1, source_target_pairs={{0,4},{1,5},{2,6},{3,7},{8,12},{9,13},{10,14},{11,15},{16,20},{17,... | collective-permute-start | bytes 196616 | tf_op jit(solution)/shard_map/ppermute | solution.py:23
  27.8 1.4 copy-start.2
  29.9 8.2 %collective-permute-start.6 = (bf16[4,544,16]{1,2,0:T(8,128)(2,1)S(1)}, bf16[4,544,16]{1,2,0:T(8,128)(2,1)S(1)}, u32[]{:S(2)}, u32[]{:S(2)}) collective-permute-start(bf16[4,544,16]{1,2,0:T(8,128)(2,1)S(1)} %copy.138), channel_id=1, source_target_pairs={{1,0},{2,1},{3,2},{5,4},{6,5},{7,6},{9,8},{10,9},{11,10},{13,12},{... | collective-permute-start | bytes 208904 | tf_op jit(solution)/shard_map/ppermute | solution.py:24
  31.2 6.6 %collective-permute-start.5 = (bf16[4,544,16]{1,2,0:T(8,128)(2,1)S(1)}, bf16[4,544,16]{1,2,0:T(8,128)(2,1)S(1)}, u32[]{:S(2)}, u32[]{:S(2)}) collective-permute-start(bf16[4,544,16]{1,2,0:T(8,128)(2,1)S(1)} %copy.137), channel_id=1, source_target_pairs={{0,1},{1,2},{2,3},{4,5},{5,6},{6,7},{8,9},{9,10},{10,11},{12,13},{... | collective-permute-start | bytes 208904 | tf_op jit(solution)/shard_map/ppermute | solution.py:23
  38.1 0.9 copy-start.4
  38.9 0.8 copy-start.5
  44.5 3.0 %copy-start.3 = (bf16[4,544,512]{2,1,0:T(8,128)(2,1)S(1)}, bf16[4,544,512]{2,1,0:T(8,128)(2,1)}, u32[]{:S(2)}) copy-start(bf16[4,544,512]{2,1,0:T(8,128)(2,1)} %copy-done.2) | copy-start | bytes 6684676
  61.2 1.0 copy-start.9
  61.2 1.0 copy-start.10
  64.4 9.5 %collective-permute-start.7 = (f32[4,12]{1,0:T(4,128)S(1)}, f32[4,12]{1,0:T(4,128)S(1)}, u32[]{:S(2)}, u32[]{:S(2)}) collective-permute-start(f32[4,12]{1,0:T(4,128)S(1)} %pad_maximum_fusion.7), channel_id=1, source_target_pairs={{0,4},{4,0},{1,5},{5,1},{2,6},{6,2},{3,7},{7,3},{8,12},{12,8},{9,1... | collective-permute-start | bytes 584 | tf_op jit(solution)/shard_map/ppermute | solution.py:65
  73.9 11.6 %collective-permute-start.8 = (f32[4,12]{1,0:T(4,128)S(1)}, f32[4,12]{1,0:T(4,128)S(1)}, u32[]{:S(2)}, u32[]{:S(2)}) collective-permute-start(f32[4,12]{1,0:T(4,128)S(1)} %fusion.134), channel_id=1, source_target_pairs={{0,1},{1,0},{2,3},{3,2},{4,5},{5,4},{6,7},{7,6},{8,9},{9,8},{10,11... | collective-permute-start | bytes 584 | tf_op jit(solution)/shard_map/ppermute | solution.py:65
  85.5 13.9 %collective-permute-start.9 = (f32[4,12]{1,0:T(4,128)S(1)}, f32[4,12]{1,0:T(4,128)S(1)}, u32[]{:S(2)}, u32[]{:S(2)}) collective-permute-start(f32[4,12]{1,0:T(4,128)S(1)} %add.241), channel_id=1, source_target_pairs={{0,2},{1,3},{2,0},{3,1},{4,6},{5,7},{6,4},{7,5},{8,10},{9,11},{10,... | collective-permute-start | bytes 584 | tf_op jit(solution)/shard_map/ppermute | solution.py:65
  101.4 6.3 %copy-start = (f32[4,3]{1,0:T(4,128)}, f32[4,3]{1,0:T(4,128)S(1)}, u32[]{:S(2)}) copy-start(f32[4,3]{1,0:T(4,128)S(1)} %pad_maximum_fusion.8.plane_ref) | copy-start | bytes 148
  101.4 6.3 %copy-start.8 = (bf16[4,1,1]{0,2,1:T(2,128)(2,1)S(1)}, bf16[4,1,1]{0,2,1:T(2,128)(2,1)}, u32[]{:S(2)}) copy-start(bf16[4,1,1]{0,2,1:T(2,128)(2,1)} %param.13) | copy-start | bytes 28
Sparse Core Ops, SparseCore 0:
  111.7 41.5 reduce-scatter.1

commit v4 on v3

--- a/solution.py
+++ b/solution.py
@@ -77,6 +77,50 @@
                 return jnp.sum(canonical, axis=0)
             values = jax.tree.map(gathered, values)
     return values
+
+
+def conv_body(coef_ref, vt_ref, ht_ref, padded_ref, out_ref):
+    e = pl.program_id(0)
+    image = padded_ref[0]
+    total = None
+    for kernel in range(len(SIGMA_PARTS)):
+        across = jnp.dot(vt_ref[0, kernel], image, preferred_element_type=jnp.float32)
+        smoothed = lax.dot_general(
+            across.astype(jnp.bfloat16), ht_ref[kernel], (((1,), (1,)), ((), ())),
+            preferred_element_type=jnp.float32,
+        )
+        term = coef_ref[e, kernel] * smoothed
+        total = term if total is None else total + term
+    out_ref[0] = total
+
+
+def conv_tiles(coeffs, vtables, htables, padded, per_exposure):
+    exp_dev, wide = padded.shape[0], padded.shape[1]
+    nk, out_rows = vtables.shape[-3], vtables.shape[-2]
+    tile_len = htables.shape[1]
+    if per_exposure:
+        vspec = pl.BlockSpec((1, nk, out_rows, wide), lambda e: (e, 0, 0, 0))
+    else:
+        vtables = vtables[None]
+        vspec = pl.BlockSpec((1, nk, out_rows, wide), lambda e: (0, 0, 0, 0))
+    flops = exp_dev * nk * 2 * out_rows * wide * (wide + tile_len)
+    moved = exp_dev * wide * wide * 2 + exp_dev * out_rows * tile_len * 4
+    return pl.pallas_call(
+        conv_body,
+        grid=(exp_dev,),
+        in_specs=[
+            pl.BlockSpec(memory_space=pltpu.SMEM),
+            vspec,
+            pl.BlockSpec((nk, tile_len, wide), lambda e: (0, 0, 0)),
+            pl.BlockSpec((1, wide, wide), lambda e: (e, 0, 0)),
+        ],
+        out_specs=pl.BlockSpec((1, out_rows, tile_len), lambda e: (e, 0, 0)),
+        out_shape=jax.ShapeDtypeStruct((exp_dev, out_rows, tile_len), jnp.float32),
+        compiler_params=pltpu.CompilerParams(
+            dimension_semantics=("arbitrary",), vmem_limit_bytes=48 * 1024 * 1024
+        ),
+        cost_estimate=pl.CostEstimate(flops=flops, bytes_accessed=moved, transcendentals=0),
+    )(coeffs, vtables, htables, padded)
 
 
 def warp_body(idx_ref, plane_ref, xrow_ref, ycol_ref, matched_ref, rmap_ref, cmap_ref, out_ref):
@@ -189,25 +233,12 @@
     own_patch = jnp.take(picked_all, visit_pos, axis=2).astype(jnp.float32)
     denominator = jnp.sum(own_patch).reshape(1)
     tables = [band_table(tile_len, HALO, HALO * part) for part in SIGMA_PARTS]
-    nearby = jnp.zeros((exp_dev, STRIP, tile_len), jnp.float32)
-    for kernel in range(len(SIGMA_PARTS)):
-        table = tables[kernel]
-        strip_table = jnp.einsum(
-            "esr,rj->esj", pick_rows, table, preferred_element_type=jnp.float32
-        ).astype(jnp.bfloat16)
-        across = jnp.einsum(
-            "esj,ejl->esl", strip_table, padded, preferred_element_type=jnp.float32
-        ).astype(jnp.bfloat16)
-        smoothed = jnp.einsum("eil,ml->eim", across, table, preferred_element_type=jnp.float32)
-        nearby = nearby + coeffs[:, kernel, None, None] * smoothed
-    matched = jnp.zeros((exp_dev, tile_len, tile_len), jnp.float32)
-    for kernel in range(len(SIGMA_PARTS)):
-        table = tables[kernel]
-        across = jnp.einsum(
-            "ij,ejl->eil", table, padded, preferred_element_type=jnp.float32
-        ).astype(jnp.bfloat16)
-        smoothed = jnp.einsum("eil,ml->eim", across, table, preferred_element_type=jnp.float32)
-        matched = matched + coeffs[:, kernel, None, None] * smoothed
+    stacked_tables = jnp.stack(tables)
+    strip_tables = jnp.einsum(
+        "esr,krj->eksj", pick_rows, stacked_tables, preferred_element_type=jnp.float32
+    ).astype(jnp.bfloat16)
+    nearby = conv_tiles(coeffs, strip_tables, stacked_tables, padded, True)
+    matched = conv_tiles(coeffs, stacked_tables, stacked_tables, padded, False)
     difference = nearby - theirs
     pixel_weight = 1.0 / (1.0 + theirs * theirs)
     strip_rows = row_pos * tile_len + offset[:, None] + jnp.arange(STRIP, dtype=jnp.int32)[None, :]

time: 164 us -> 144 us (0.88)
  matrix products: 57 us -> 4.98 us
  Pallas kernels: 6.33 us -> 26.2 us
  other arithmetic: 10.5 us -> 20.2 us
  waiting for transfers between devices: 42.8 us -> 49.4 us
  starting transfers between devices: 22.5 us -> 18.6 us
    dot_general x9 -> x1, matrix products: 52 us -> 0.49 us  [shards(): jnp.einsum('esr,krj->eksj', pick_rows, stacked_tables, preferred_element_...]
    pallas_call x0 -> x2, Pallas kernels: none -> 19.9 us  [conv_tiles(): pl.pallas_call(conv_body, grid=(exp_dev,), in_specs=[pl.BlockSpec(memory_...]
    ppermute x2, waiting for transfers between devices: 0.01 us -> 4.34 us  [extended(): after = lax.ppermute(initial, axis, down)]
    concatenate x0 -> x1, other arithmetic: none -> 3.53 us  [extended(): value = jnp.concatenate([before, value, after], axis=dim)]
    convert_element_type x0 -> x2, other arithmetic: none -> 3.43 us  [band_table(): return jnp.where(jnp.abs(offset) <= width, values, 0.0).astype(jnp.bfloat16)]
    ppermute x3, waiting for transfers between devices: 0.01 us -> 2.6 us  [butterfly_sum(): values = jax.tree.map(lambda v: v + lax.ppermute(v, axis, pairs), values)]
    ppermute x2, starting transfers between devices: 7.76 us -> 5.3 us  [extended(): before = lax.ppermute(last, axis, up)]
    broadcast_in_dim x0 -> x1, other arithmetic: none -> 2.28 us  [conv_tiles(): vtables = vtables[None]]
  transfers between devices with their start and end apart: 11 -> 11, of which waited for: 2 -> 5; matrix products, arithmetic and copies ran while one was open for 35% -> 11% of each run, Pallas kernels for 0% -> 14%
where the time goes in v4:
time: 144 us
  waiting for transfers between devices  49.4 us (34%)
  Pallas kernels  26.2 us (18%)
  other arithmetic  20.2 us (14%)
  starting transfers between devices  18.6 us (13%)
  between operations  14.4 us (10%)
  local copies, waits for them, and re-layouts  9.79 us (7%)
  matrix products  4.98 us (3%)
    reduce_scatter x1, waiting for transfers between devices, shards(): lax.psum_scatter(partial_sum.astype(jnp.bfloat16), 'visit', scatter_dimen...  41.5 us
    pallas_call x2, Pallas kernels, conv_tiles(): pl.pallas_call(conv_body, grid=(exp_dev,), in_specs=[pl.BlockSpec(memory_...  19.9 us
    ppermute x3, starting transfers between devices, shards(): received.append(lax.ppermute(payload, 'visit', pairs))  6.96 us
    pallas_call x1, Pallas kernels, warp_tiles(): pl.pallas_call(warp_body, grid_spec=grid_spec, out_shape=jax.ShapeDtypeSt...  6.33 us
    ppermute x2, starting transfers between devices, extended(): before = lax.ppermute(last, axis, up)  5.3 us
    ppermute x2, waiting for transfers between devices, extended(): after = lax.ppermute(initial, axis, down)  4.34 us
    unnamed x23, local copies, waits for them, and re-layouts  4 us
    ppermute x3, starting transfers between devices, butterfly_sum(): values = jax.tree.map(lambda v: v + lax.ppermute(v, axis, pairs), values)  3.55 us
  transfers between devices with their start and end apart: 11, of which 5 were waited for; matrix products, arithmetic and copies ran while one was open for 11% of the time, Pallas kernels for 14%

profile of v4, /device:TPU:0, one launch (start us, length us, event | category | flops | bytes accessed | tf_op | source)
XLA Modules:
  0.0 143.5 jit_solution(13439060257333093910)
XLA Ops:
  10.6 2.1 %convolution_convert_fusion = bf16[4,32,512]{2,1,0:T(8,128)(2,1)S(1)} fusion(bf16[4,512,512]{2,1,0:T(8,128)(2,1)} %param.10, s32[4]{0:T(128)S(1)} %get-tuple-element.39), kind=kOutput, calls=%fused_computation.15 | convolution fusion | flops 67305472 | bytes 2228240 | tf_op jit(solution)/shard_map/esr,erl->esl/dot_general | solution.py:199
  13.4 3.0 %collective-permute-start = (bf16[144,512]{1,0:T(8,128)(2,1)}, bf16[144,512]{1,0:T(8,128)(2,1)S(1)}, u32[]{:S(2)}, u32[]{:S(2)}) collective-permute-start(bf16[144,512]{1,0:T(8,128)(2,1)} %get-tuple-element.50), channel_id=1, source_target_pairs={{0,8},{8,16},{16,24},{24,0},{1,9},{9,17},{17,25},{25,1},{2,10},{10... | collective-permute-start | bytes 442376 | tf_op jit(solution)/shard_map/ppermute | solution.py:219
  16.4 2.6 %collective-permute-start.1 = (bf16[144,512]{1,0:T(8,128)(2,1)}, bf16[144,512]{1,0:T(8,128)(2,1)S(1)}, u32[]{:S(2)}, u32[]{:S(2)}) collective-permute-start(bf16[144,512]{1,0:T(8,128)(2,1)} %get-tuple-element.50), channel_id=1, source_target_pairs={{0,16},{8,24},{16,0},{24,8},{1,17},{9,25},{17,1},{25,9},{2,18},{10... | collective-permute-start | bytes 442376 | tf_op jit(solution)/shard_map/ppermute | solution.py:219
  19.0 1.3 collective-permute-start.2
  21.0 1.9 %collective-permute-start.3 = (bf16[4,16,512]{2,1,0:T(8,128)(2,1)}, bf16[4,16,512]{2,1,0:T(8,128)(2,1)}, u32[]{:S(2)}, u32[]{:S(2)}) collective-permute-start(bf16[4,16,512]{2,1,0:T(8,128)(2,1)} %get-tuple-element.46), channel_id=1, source_target_pairs={{0,4},{1,5},{2,6},{3,7},{8,12},{9,13},{10,14},{11,15},{16,20},{17,... | collective-permute-start | bytes 196616 | tf_op jit(solution)/shard_map/ppermute | solution.py:23
  22.9 1.3 collective-permute-start.4
  26.1 1.3 select_convert_fusion.2
  27.4 2.1 %select_convert_fusion = (bf16[1,512,544]{2,1,0:T(8,128)(2,1)S(1)}, bf16[1,512,544]{2,1,0:T(8,128)(2,1)S(1)}) fusion(f32[]{:T(128)} %exponential_reduce_fusion, f32[]{:T(128)} %exponential_reduce_fusion.1), kind=kLoop, calls=%fused_computation.8 | loop fusion | flops 4177920 | bytes 1114120 | tf_op jit(solution)/shard_map/convert_element_type | solution.py:37
  30.1 2.3 %fusion.32 = (bf16[1,3,512,544]{3,2,1,0:T(8,128)(2,1)}, bf16[3,512,544]{2,1,0:T(8,128)(2,1)}) fusion(bf16[1,512,544]{2,1,0:T(8,128)(2,1)S(1)} %get-tuple-element.65, bf16[1,512,544]{2,1,0:T(8,128)(2,1)S(1)} %get-tuple-element.66, bf16[1,512,544]{2,1,0:T(8,128)(2,1)S(1)} %select_convert_fusion.2), kind=kLoop, calls=%fused_computation.99 | loop fusion | flops 1671168 | bytes 5013504 | tf_op jit(solution)/shard_map/broadcast_in_dim | solution.py:104
  33.6 1.4 copy-done.7
  35.4 3.4 %collective-permute-start.5 = (bf16[4,544,16]{1,2,0:T(8,128)(2,1)S(1)}, bf16[4,544,16]{1,2,0:T(8,128)(2,1)S(1)}, u32[]{:S(2)}, u32[]{:S(2)}) collective-permute-start(bf16[4,544,16]{1,2,0:T(8,128)(2,1)S(1)} %copy.142), channel_id=1, source_target_pairs={{0,1},{1,2},{2,3},{4,5},{5,6},{6,7},{8,9},{9,10},{10,11},{12,13},{... | collective-permute-start | bytes 208904 | tf_op jit(solution)/shard_map/ppermute | solution.py:23
  39.1 1.5 %collective-permute-start.6 = (bf16[4,544,16]{1,2,0:T(8,128)(2,1)S(1)}, bf16[4,544,16]{1,2,0:T(8,128)(2,1)S(1)}, u32[]{:S(2)}, u32[]{:S(2)}) collective-permute-start(bf16[4,544,16]{1,2,0:T(8,128)(2,1)S(1)} %copy.143), channel_id=1, source_target_pairs={{1,0},{2,1},{3,2},{5,4},{6,5},{7,6},{9,8},{10,9},{11,10},{13,12},{... | collective-permute-start | bytes 208904 | tf_op jit(solution)/shard_map/ppermute | solution.py:24
  41.8 4.3 %collective-permute-done.6 = bf16[4,544,16]{1,2,0:T(8,128)(2,1)S(1)} collective-permute-done((bf16[4,544,16]{1,2,0:T(8,128)(2,1)S(1)}, bf16[4,544,16]{1,2,0:T(8,128)(2,1)S(1)}, u32[]{:S(2)}, u32[]{:S(2)}) %collective-permute-start.6) | collective-permute-done | bytes 69664 | tf_op jit(solution)/shard_map/ppermute | solution.py:24
  46.5 3.5 %pad_maximum_fusion.padded_ref = bf16[4,544,544]{2,1,0:T(8,128)(2,1)S(1)} fusion(bf16[4,544,16]{2,1,0:T(8,128)(2,1)S(1)} %copy.145, bf16[4,544,512]{2,1,0:T(8,128)(2,1)} %copy-done.7, bf16[4,544,16]{2,1,0:T(8,128)(2,1)S(1)} %copy.144), kind=kLoop, calls=%fused_computation | loop fusion | flops 7102464 | bytes 4734976 | tf_op jit(solution)/shard_map/concatenate | solution.py:25
  50.1 5.1 %shard_map.95 = f32[4,32,512]{2,1,0:T(8,128)S(1)} custom-call(f32[4,3]{1,0:T(4,128)S(1)} %copy-done.5, bf16[4,3,32,544]{3,2,1,0:T(8,128)(2,1)S(1)} %fusion.10.vt_ref, bf16[3,512,544]{2,1,0:T(8,128)(2,1)S(1)} %copy-done.1, bf16[4,544,544]{2,1,0:T(8,128)(2,1)S(1)} %pad_maximum_fusion.padded_ref), custom_call_target="tpu_custom_call" | custom-call | flops 441188352 | bytes 2629632 | tf_op jit(solution)/shard_map/pallas_call | solution.py:108
  58.1 2.4 %collective-permute-start.8 = (f32[4,12]{1,0:T(4,128)S(1)}, f32[4,12]{1,0:T(4,128)S(1)}, u32[]{:S(2)}, u32[]{:S(2)}) collective-permute-start(f32[4,12]{1,0:T(4,128)S(1)} %fusion.36), channel_id=1, source_target_pairs={{0,1},{1,0},{2,3},{3,2},{4,5},{5,4},{6,7},{7,6},{8,9},{9,8},{10,11... | collective-permute-start | bytes 584 | tf_op jit(solution)/shard_map/ppermute | solution.py:65
  60.6 1.5 %collective-permute-done.8 = f32[4,12]{1,0:T(4,128)S(1)} collective-permute-done((f32[4,12]{1,0:T(4,128)S(1)}, f32[4,12]{1,0:T(4,128)S(1)}, u32[]{:S(2)}, u32[]{:S(2)}) %collective-permute-start.8) | collective-permute-done | bytes 224 | tf_op jit(solution)/shard_map/ppermute | solution.py:65
  63.2 1.5 %copy-done.3 = bf16[1,3,512,544]{3,2,1,0:T(8,128)(2,1)S(1)} copy-done((bf16[1,3,512,544]{3,2,1,0:T(8,128)(2,1)S(1)}, bf16[1,3,512,544]{3,2,1,0:T(8,128)(2,1)}, u32[]{:S(2)}) %copy-start.3) | copy-done | bytes 1671192
  64.7 14.8 %shard_map.96.matched_ref = f32[4,512,512]{2,1,0:T(8,128)} custom-call(f32[4,3]{1,0:T(4,128)S(1)} %copy-done.5, bf16[1,3,512,544]{3,2,1,0:T(8,128)(2,1)S(1)} %copy-done.3, bf16[3,512,544]{2,1,0:T(8,128)(2,1)S(1)} %copy-done.2, bf16[4,544,544]{2,1,0:T(8,128)(2,1)} %copy-done), custom_call_target="tpu_custom_call" | custom-call | flops 7059013632 | bytes 6561792 | tf_op jit(solution)/shard_map/pallas_call | solution.py:108
  81.4 6.3 %shard_map.97 = bf16[4,512,512]{2,1,0:T(8,128)(2,1)S(1)} custom-call(s32[4,2]{1,0:T(4,128)S(1)} %copy.163.idx_ref, f32[4,3]{1,0:T(4,128)S(1)} %pad_maximum_fusion.9.plane_ref, f32[1,512]{1,0:T(1,128)S(1)} %multiply_add_fusion.1.xrow_ref, f32[512,1]{1,0:T(8,128)S(1)} %multiply_add_fusion.ycol_ref, f32[4,512,512]{2,1,0:T(8,128)} %shard_map.96.matched_ref, ...), custom_call_target="tpu_custom_call" | custom-call | flops 2147483648 | bytes 10485760 | tf_op jit(solution)/shard_map/pallas_call | solution.py:157
  87.7 2.0 %fusion.4 = bf16[4,512,512]{2,0,1:T(4,128)(2,1)S(1)} fusion(bf16[4,512,512]{2,1,0:T(8,128)(2,1)S(1)} %shard_map.97, pred[4,4]{1,0:T(4,128)(4,1)S(1)} %fusion.21, bf16[4]{0:T(256)(128)(2,1)S(1)} %bitcast.102), kind=kOutput, calls=%fused_computation.7 | convolution fusion | flops 9437200 | bytes 4194328 | tf_op jit(solution)/shard_map/ev,eij->vij/dot_general | solution.py:283
  89.8 1.8 %copy.166 = bf16[4,512,512]{2,1,0:T(8,128)(2,1)} copy(bf16[4,512,512]{2,0,1:T(4,128)(2,1)S(1)} %fusion.4) | data formatting | bytes 4194304 | tf_op jit(solution)/shard_map/convert_element_type | solution.py:285
  92.4 41.5 %reduce-scatter.2.cloned.1.call-done = bf16[1,512,512]{2,1,0:T(8,128)(2,1)} async-done(((bf16[4,512,512]{2,1,0:T(8,128)(2,1)}), bf16[1,512,512]{2,1,0:T(8,128)(2,1)}) %reduce-scatter.2.cloned.1.call-update) | async-done | bytes 524304 | tf_op jit(solution)/shard_map/reduce_scatter | solution.py:284
  133.9 2.8 %convert_divide_fusion = f32[1,512,512]{2,1,0:T(8,128)} fusion(bf16[1,512,512]{2,1,0:T(8,128)(2,1)} %reduce-scatter.2.cloned.1.call-done, f32[]{:T(128)} %convert_reduce_fusion), kind=kLoop, calls=%fused_computation.16 | loop fusion | flops 524288 | bytes 1572868 | tf_op jit(solution)/shard_map/div | solution.py:287
  (94 shorter events, 17.5 us)
Async XLA Ops:
  7.2 13.2 %copy-start.6 = (bf16[4,512,512]{2,1,0:T(8,128)(2,1)S(1)}, bf16[4,512,512]{2,1,0:T(8,128)(2,1)}, u32[]{:S(2)}) copy-start(bf16[4,512,512]{2,1,0:T(8,128)(2,1)} %param.10) | copy-start | bytes 6291460
  7.2 126.7 %reduce-scatter.2.cloned.1.call-start = ((), (), s32[]{:S(2)}) async-start(), calls=%async_computation.1 | async-start | bytes 2621440 | tf_op jit(solution)/shard_map/reduce_scatter | solution.py:284
  13.4 41.7 %collective-permute-start = (bf16[144,512]{1,0:T(8,128)(2,1)}, bf16[144,512]{1,0:T(8,128)(2,1)S(1)}, u32[]{:S(2)}, u32[]{:S(2)}) collective-permute-start(bf16[144,512]{1,0:T(8,128)(2,1)} %get-tuple-element.50), channel_id=1, source_target_pairs={{0,8},{8,16},{16,24},{24,0},{1,9},{9,17},{17,25},{25,1},{2,10},{10... | collective-permute-start | bytes 442376 | tf_op jit(solution)/shard_map/ppermute | solution.py:219
  16.4 38.7 %collective-permute-start.1 = (bf16[144,512]{1,0:T(8,128)(2,1)}, bf16[144,512]{1,0:T(8,128)(2,1)S(1)}, u32[]{:S(2)}, u32[]{:S(2)}) collective-permute-start(bf16[144,512]{1,0:T(8,128)(2,1)} %get-tuple-element.50), channel_id=1, source_target_pairs={{0,16},{8,24},{16,0},{24,8},{1,17},{9,25},{17,1},{25,9},{2,18},{10... | collective-permute-start | bytes 442376 | tf_op jit(solution)/shard_map/ppermute | solution.py:219
  19.0 36.1 %collective-permute-start.2 = (bf16[144,512]{1,0:T(8,128)(2,1)}, bf16[144,512]{1,0:T(8,128)(2,1)S(1)}, u32[]{:S(2)}, u32[]{:S(2)}) collective-permute-start(bf16[144,512]{1,0:T(8,128)(2,1)} %get-tuple-element.50), channel_id=1, source_target_pairs={{0,24},{8,0},{16,8},{24,16},{1,25},{9,1},{17,9},{25,17},{2,26},{10... | collective-permute-start | bytes 442376 | tf_op jit(solution)/shard_map/ppermute | solution.py:219
  21.0 11.5 %collective-permute-start.3 = (bf16[4,16,512]{2,1,0:T(8,128)(2,1)}, bf16[4,16,512]{2,1,0:T(8,128)(2,1)}, u32[]{:S(2)}, u32[]{:S(2)}) collective-permute-start(bf16[4,16,512]{2,1,0:T(8,128)(2,1)} %get-tuple-element.46), channel_id=1, source_target_pairs={{0,4},{1,5},{2,6},{3,7},{8,12},{9,13},{10,14},{11,15},{16,20},{17,... | collective-permute-start | bytes 196616 | tf_op jit(solution)/shard_map/ppermute | solution.py:23
  22.9 10.6 %collective-permute-start.4 = (bf16[4,16,512]{2,1,0:T(8,128)(2,1)}, bf16[4,16,512]{2,1,0:T(8,128)(2,1)S(1)}, u32[]{:S(2)}, u32[]{:S(2)}) collective-permute-start(bf16[4,16,512]{2,1,0:T(8,128)(2,1)} %get-tuple-element.45), channel_id=1, source_target_pairs={{4,0},{5,1},{6,2},{7,3},{12,8},{13,9},{14,10},{15,11},{20,16},{21,... | collective-permute-start | bytes 196616 | tf_op jit(solution)/shard_map/ppermute | solution.py:24
  33.6 1.4 copy-start.7
  35.4 6.1 %collective-permute-start.5 = (bf16[4,544,16]{1,2,0:T(8,128)(2,1)S(1)}, bf16[4,544,16]{1,2,0:T(8,128)(2,1)S(1)}, u32[]{:S(2)}, u32[]{:S(2)}) collective-permute-start(bf16[4,544,16]{1,2,0:T(8,128)(2,1)S(1)} %copy.142), channel_id=1, source_target_pairs={{0,1},{1,2},{2,3},{4,5},{5,6},{6,7},{8,9},{9,10},{10,11},{12,13},{... | collective-permute-start | bytes 208904 | tf_op jit(solution)/shard_map/ppermute | solution.py:23
  39.1 7.1 %collective-permute-start.6 = (bf16[4,544,16]{1,2,0:T(8,128)(2,1)S(1)}, bf16[4,544,16]{1,2,0:T(8,128)(2,1)S(1)}, u32[]{:S(2)}, u32[]{:S(2)}) collective-permute-start(bf16[4,544,16]{1,2,0:T(8,128)(2,1)S(1)} %copy.143), channel_id=1, source_target_pairs={{1,0},{2,1},{3,2},{5,4},{6,5},{7,6},{9,8},{10,9},{11,10},{13,12},{... | collective-permute-start | bytes 208904 | tf_op jit(solution)/shard_map/ppermute | solution.py:24
  46.5 3.6 %copy-start.1 = (bf16[3,512,544]{2,1,0:T(8,128)(2,1)S(1)}, bf16[3,512,544]{2,1,0:T(8,128)(2,1)}, u32[]{:S(2)}) copy-start(bf16[3,512,544]{2,1,0:T(8,128)(2,1)} %get-tuple-element.48.ht_ref) | copy-start | bytes 5013508
  46.5 3.6 %copy-start.5 = (f32[4,3]{1,0:T(4,128)S(1)}, f32[4,3]{1,0:T(4,128)}, u32[]{:S(2)}) copy-start(f32[4,3]{1,0:T(4,128)} %coef_ref.3) | copy-start | bytes 148
  50.0 5.1 %copy-start = (bf16[4,544,544]{2,1,0:T(8,128)(2,1)}, bf16[4,544,544]{2,1,0:T(8,128)(2,1)S(1)}, u32[]{:S(2)}) copy-start(bf16[4,544,544]{2,1,0:T(8,128)(2,1)S(1)} %pad_maximum_fusion.padded_ref) | copy-start | bytes 7102468
  55.1 5.3 %copy-start.8 = (s32[4,1,1,2]{0,3,2,1:T(2,128)S(1)}, s32[4,1,1,2]{0,3,2,1:T(2,128)}, u32[]{:S(2)}) copy-start(s32[4,1,1,2]{0,3,2,1:T(2,128)} %param.15) | copy-start | bytes 100
  55.1 8.0 %copy-start.2 = (bf16[3,512,544]{2,1,0:T(8,128)(2,1)S(1)}, bf16[3,512,544]{2,1,0:T(8,128)(2,1)}, u32[]{:S(2)}) copy-start(bf16[3,512,544]{2,1,0:T(8,128)(2,1)} %get-tuple-element.48.ht_ref) | copy-start | bytes 5013508
  56.8 1.2 collective-permute-start.7
  58.1 4.0 %collective-permute-start.8 = (f32[4,12]{1,0:T(4,128)S(1)}, f32[4,12]{1,0:T(4,128)S(1)}, u32[]{:S(2)}, u32[]{:S(2)}) collective-permute-start(f32[4,12]{1,0:T(4,128)S(1)} %fusion.36), channel_id=1, source_target_pairs={{0,1},{1,0},{2,3},{3,2},{4,5},{5,4},{6,7},{7,6},{8,9},{9,8},{10,11... | collective-permute-start | bytes 584 | tf_op jit(solution)/shard_map/ppermute | solution.py:65
  62.0 17.5 %collective-permute-start.9 = (f32[4,12]{1,0:T(4,128)S(1)}, f32[4,12]{1,0:T(4,128)S(1)}, u32[]{:S(2)}, u32[]{:S(2)}) collective-permute-start(f32[4,12]{1,0:T(4,128)S(1)} %add.242), channel_id=1, source_target_pairs={{0,2},{1,3},{2,0},{3,1},{4,6},{5,7},{6,4},{7,5},{8,10},{9,11},{10,... | collective-permute-start | bytes 584 | tf_op jit(solution)/shard_map/ppermute | solution.py:65
  63.2 1.5 %copy-start.3 = (bf16[1,3,512,544]{3,2,1,0:T(8,128)(2,1)S(1)}, bf16[1,3,512,544]{3,2,1,0:T(8,128)(2,1)}, u32[]{:S(2)}) copy-start(bf16[1,3,512,544]{3,2,1,0:T(8,128)(2,1)} %get-tuple-element.47.vt_ref) | copy-start | bytes 5013508
  81.4 6.3 %copy-start.4 = (f32[4,3]{1,0:T(4,128)}, f32[4,3]{1,0:T(4,128)S(1)}, u32[]{:S(2)}) copy-start(f32[4,3]{1,0:T(4,128)S(1)} %pad_maximum_fusion.9.plane_ref) | copy-start | bytes 148
  81.4 6.4 %copy-start.9 = (bf16[4,1,1]{0,2,1:T(2,128)(2,1)S(1)}, bf16[4,1,1]{0,2,1:T(2,128)(2,1)}, u32[]{:S(2)}) copy-start(bf16[4,1,1]{0,2,1:T(2,128)(2,1)} %param.13) | copy-start | bytes 28
Sparse Core Ops, SparseCore 0:
  91.7 42.2 reduce-scatter.1

commit v5 on v4

--- a/solution.py
+++ b/solution.py
@@ -16,12 +16,20 @@
 def extended(value, sides, width):
     for axis, dim in sides:
         devices, length = (lax.axis_size(axis), value.shape[dim])
-        up = [(i, (i + 1) % devices) for i in range(devices - 1)]
-        down = [(j, i) for i, j in up]
         last = lax.slice_in_dim(value, length - width, length, axis=dim)
         initial = lax.slice_in_dim(value, 0, width, axis=dim)
-        before = lax.ppermute(last, axis, up)
-        after = lax.ppermute(initial, axis, down)
+        if devices == 2:
+            position = lax.axis_index(axis)
+            facing = jnp.where(position == 0, last, initial)
+            arrived = lax.ppermute(facing, axis, [(0, 1), (1, 0)])
+            empty = jnp.zeros_like(arrived)
+            before = jnp.where(position == 1, arrived, empty)
+            after = jnp.where(position == 0, arrived, empty)
+        else:
+            up = [(i, (i + 1) % devices) for i in range(devices - 1)]
+            down = [(j, i) for i, j in up]
+            before = lax.ppermute(last, axis, up)
+            after = lax.ppermute(initial, axis, down)
         value = jnp.concatenate([before, value, after], axis=dim)
     return value
 
@@ -180,7 +188,7 @@
     visit_pos = lax.axis_index("visit")
     height = row_count * tile_len
     breadth = col_count * tile_len
-    padded = extended(images, (("row", 1), ("col", 2)), HALO)
+    padded = extended(images, (("col", 2), ("row", 1)), HALO)
     own_ids = visit_pos * exp_dev + jnp.arange(exp_dev, dtype=jnp.int32)
     first_col = pair_list[:, 0]
     second_col = pair_list[:, 1]
@@ -232,8 +240,7 @@
     )
     own_patch = jnp.take(picked_all, visit_pos, axis=2).astype(jnp.float32)
     denominator = jnp.sum(own_patch).reshape(1)
-    tables = [band_table(tile_len, HALO, HALO * part) for part in SIGMA_PARTS]
-    stacked_tables = jnp.stack(tables)
+    stacked_tables = jnp.stack([band_table(tile_len, HALO, HALO * part) for part in SIGMA_PARTS])
     strip_tables = jnp.einsum(
         "esr,krj->eksj", pick_rows, stacked_tables, preferred_element_type=jnp.float32
     ).astype(jnp.bfloat16)

time: 144 us -> 149 us (1.035)
  waiting for transfers between devices: 49.4 us -> 57.8 us
  starting transfers between devices: 18.6 us -> 15.1 us
  local copies, waits for them, and re-layouts: 9.79 us -> 7.29 us
  other arithmetic: 20.2 us -> 22.6 us
    ppermute x2 -> x1, waiting for transfers between devices: 4.34 us -> 13.2 us  [extended(): after = lax.ppermute(initial, axis, down)]
    ppermute x3, starting transfers between devices: 3.55 us -> 1.66 us  [butterfly_sum(): values = jax.tree.map(lambda v: v + lax.ppermute(v, axis, pairs), values)]
    unnamed x23 -> x25, local copies, waits for them, and re-layouts: 4 us -> 2.52 us
    ppermute x2 -> x1, starting transfers between devices: 5.3 us -> 4.19 us  [extended(): before = lax.ppermute(last, axis, up)]
  transfers between devices with their start and end apart: 11 -> 10, of which waited for: 5 -> 6; matrix products, arithmetic and copies ran while one was open for 11% -> 10% of each run, Pallas kernels for 14% -> 13%
where the time goes in v5:
time: 149 us; the launch traced here: 148 us
  waiting for transfers between devices  57.8 us (39%)
  Pallas kernels  26.2 us (18%)
  other arithmetic  22.6 us (15%)
  starting transfers between devices  15.1 us (10%)
  between operations  14.4 us (10%)
  local copies, waits for them, and re-layouts  7.29 us (5%)
  matrix products  4.96 us (3%)
    reduce_scatter x1, waiting for transfers between devices, shards(): lax.psum_scatter(partial_sum.astype(jnp.bfloat16), 'visit', scatter_dimen...  40.1 us
    pallas_call x2, Pallas kernels, conv_tiles(): pl.pallas_call(conv_body, grid=(exp_dev,), in_specs=[pl.BlockSpec(memory_...  19.8 us
    ppermute x1, waiting for transfers between devices, extended(): after = lax.ppermute(initial, axis, down)  13.2 us
    ppermute x3, starting transfers between devices, shards(): received.append(lax.ppermute(payload, 'visit', pairs))  7.86 us
    pallas_call x1, Pallas kernels, warp_tiles(): pl.pallas_call(warp_body, grid_spec=grid_spec, out_shape=jax.ShapeDtypeSt...  6.47 us
    ppermute x1, starting transfers between devices, extended(): before = lax.ppermute(last, axis, up)  4.19 us
    convert_element_type x2, other arithmetic, band_table(): return jnp.where(jnp.abs(offset) <= width, values, 0.0).astype(jnp.bfloat16)  3.41 us
    concatenate x1, other arithmetic, extended(): value = jnp.concatenate([before, value, after], axis=dim)  3 us
  transfers between devices with their start and end apart: 10, of which 6 were waited for; matrix products, arithmetic and copies ran while one was open for 10% of the time, Pallas kernels for 13%

profile of v5, /device:TPU:0, one launch (start us, length us, event | category | flops | bytes accessed | tf_op | source)
XLA Modules:
  0.0 148.4 jit_solution(1112992081007771815)
XLA Ops:
  10.7 2.1 %convolution_convert_fusion = bf16[4,32,512]{2,1,0:T(8,128)(2,1)S(1)} fusion(bf16[4,512,512]{2,1,0:T(8,128)(2,1)} %param.10, s32[4]{0:T(128)S(1)} %get-tuple-element.39), kind=kOutput, calls=%fused_computation.15 | convolution fusion | flops 67305472 | bytes 2228240 | tf_op jit(solution)/shard_map/esr,erl->esl/dot_general | solution.py:207
  13.5 4.0 %collective-permute-start.1 = (bf16[144,512]{1,0:T(8,128)(2,1)S(1)}, bf16[144,512]{1,0:T(8,128)(2,1)}, u32[]{:S(2)}, u32[]{:S(2)}) collective-permute-start(bf16[144,512]{1,0:T(8,128)(2,1)S(1)} %get-tuple-element.48), channel_id=1, source_target_pairs={{0,16},{8,24},{16,0},{24,8},{1,17},{9,25},{17,1},{25,9},{2,18},{10... | collective-permute-start | bytes 442376 | tf_op jit(solution)/shard_map/ppermute | solution.py:227
  17.5 1.6 %collective-permute-start = (bf16[144,512]{1,0:T(8,128)(2,1)S(1)}, bf16[144,512]{1,0:T(8,128)(2,1)}, u32[]{:S(2)}, u32[]{:S(2)}) collective-permute-start(bf16[144,512]{1,0:T(8,128)(2,1)S(1)} %get-tuple-element.48), channel_id=1, source_target_pairs={{0,8},{8,16},{16,24},{24,0},{1,9},{9,17},{17,25},{25,1},{2,10},{10... | collective-permute-start | bytes 442376 | tf_op jit(solution)/shard_map/ppermute | solution.py:227
  19.1 2.2 %collective-permute-start.2 = (bf16[144,512]{1,0:T(8,128)(2,1)S(1)}, bf16[144,512]{1,0:T(8,128)(2,1)}, u32[]{:S(2)}, u32[]{:S(2)}) collective-permute-start(bf16[144,512]{1,0:T(8,128)(2,1)S(1)} %get-tuple-element.48), channel_id=1, source_target_pairs={{0,24},{8,0},{16,8},{24,16},{1,25},{9,1},{17,9},{25,17},{2,26},{10... | collective-permute-start | bytes 442376 | tf_op jit(solution)/shard_map/ppermute | solution.py:227
  22.4 4.2 %collective-permute-start.3 = (bf16[4,512,16]{2,1,0:T(8,128)(2,1)}, bf16[4,512,16]{2,1,0:T(8,128)(2,1)}, u32[]{:S(2)}, u32[]{:S(2)}) collective-permute-start(bf16[4,512,16]{2,1,0:T(8,128)(2,1)} %get-tuple-element.43), channel_id=1, source_target_pairs={{0,1},{1,2},{2,3},{4,5},{5,6},{6,7},{8,9},{9,10},{10,11},{12,13},{... | collective-permute-start | bytes 196616 | tf_op jit(solution)/shard_map/ppermute | solution.py:31
  26.6 1.3 collective-permute-start.4
  29.8 1.3 select_convert_fusion.2
  31.1 2.1 %select_convert_fusion = (bf16[1,512,544]{2,1,0:T(8,128)(2,1)S(1)}, bf16[1,512,544]{2,1,0:T(8,128)(2,1)S(1)}) fusion(f32[]{:T(128)} %exponential_reduce_fusion, f32[]{:T(128)} %exponential_reduce_fusion.1), kind=kLoop, calls=%fused_computation.8 | loop fusion | flops 4177920 | bytes 1114120 | tf_op jit(solution)/shard_map/convert_element_type | solution.py:45
  33.7 2.3 %fusion.33 = (bf16[1,3,512,544]{3,2,1,0:T(8,128)(2,1)}, bf16[3,512,544]{2,1,0:T(8,128)(2,1)}) fusion(bf16[1,512,544]{2,1,0:T(8,128)(2,1)S(1)} %get-tuple-element.63, bf16[1,512,544]{2,1,0:T(8,128)(2,1)S(1)} %get-tuple-element.64, bf16[1,512,544]{2,1,0:T(8,128)(2,1)S(1)} %select_convert_fusion.2), kind=kLoop, calls=%fused_computation.101 | loop fusion | flops 1671168 | bytes 5013504 | tf_op jit(solution)/shard_map/broadcast_in_dim | solution.py:112
  36.4 13.2 %collective-permute-done.4 = bf16[4,512,16]{2,1,0:T(8,128)(2,1)} collective-permute-done((bf16[4,512,16]{2,1,0:T(8,128)(2,1)S(1)}, bf16[4,512,16]{2,1,0:T(8,128)(2,1)}, u32[]{:S(2)}, u32[]{:S(2)}) %collective-permute-start.4) | collective-permute-done | bytes 65568 | tf_op jit(solution)/shard_map/ppermute | solution.py:32
  50.6 1.3 collective-permute-done.5
  51.9 3.0 %pad_maximum_fusion.padded_ref = bf16[4,544,544]{2,1,0:T(8,128)(2,1)S(1)} fusion(bf16[4,16,544]{2,1,0:T(8,128)(2,1)S(1)} %get-tuple-element.50, bf16[4,512,16]{2,1,0:T(8,128)(2,1)} %collective-permute-done.4, bf16[4,512,512]{2,1,0:T(8,128)(2,1)S(1)} %copy-done.7, bf16[4,512,16]{2,1,0:T(8,128)(2,1)} %collective-permute-done.3, ...), kind=kLoop, calls=%fused_computation | loop fusion | flops 11837440 | bytes 4734976 | tf_op jit(solution)/shard_map/concatenate | solution.py:33
  54.9 5.1 %shard_map.95 = f32[4,32,512]{2,1,0:T(8,128)S(1)} custom-call(f32[4,3]{1,0:T(4,128)S(1)} %copy-done.5, bf16[4,3,32,544]{3,2,1,0:T(8,128)(2,1)S(1)} %fusion.10.vt_ref, bf16[3,512,544]{2,1,0:T(8,128)(2,1)S(1)} %copy-done.1, bf16[4,544,544]{2,1,0:T(8,128)(2,1)S(1)} %pad_maximum_fusion.padded_ref), custom_call_target="tpu_custom_call" | custom-call | flops 441188352 | bytes 2629632 | tf_op jit(solution)/shard_map/pallas_call | solution.py:116
  60.1 1.3 pad_maximum_fusion.2
  64.2 1.5 %collective-permute-start.7 = (f32[4,12]{1,0:T(4,128)S(1)}, f32[4,12]{1,0:T(4,128)S(1)}, u32[]{:S(2)}, u32[]{:S(2)}) collective-permute-start(f32[4,12]{1,0:T(4,128)S(1)} %fusion.36), channel_id=1, source_target_pairs={{0,1},{1,0},{2,3},{3,2},{4,5},{5,4},{6,7},{7,6},{8,9},{9,8},{10,11... | collective-permute-start | bytes 584 | tf_op jit(solution)/shard_map/ppermute | solution.py:73
  65.8 2.0 %collective-permute-done.7 = f32[4,12]{1,0:T(4,128)S(1)} collective-permute-done((f32[4,12]{1,0:T(4,128)S(1)}, f32[4,12]{1,0:T(4,128)S(1)}, u32[]{:S(2)}, u32[]{:S(2)}) %collective-permute-start.7) | collective-permute-done | bytes 224 | tf_op jit(solution)/shard_map/ppermute | solution.py:73
  67.8 1.5 %copy-done.3 = bf16[1,3,512,544]{3,2,1,0:T(8,128)(2,1)S(1)} copy-done((bf16[1,3,512,544]{3,2,1,0:T(8,128)(2,1)S(1)}, bf16[1,3,512,544]{3,2,1,0:T(8,128)(2,1)}, u32[]{:S(2)}) %copy-start.3) | copy-done | bytes 1671192
  69.3 14.7 %shard_map.96.matched_ref = f32[4,512,512]{2,1,0:T(8,128)} custom-call(f32[4,3]{1,0:T(4,128)S(1)} %copy-done.5, bf16[1,3,512,544]{3,2,1,0:T(8,128)(2,1)S(1)} %copy-done.3, bf16[3,512,544]{2,1,0:T(8,128)(2,1)S(1)} %copy-done.2, bf16[4,544,544]{2,1,0:T(8,128)(2,1)} %copy-done), custom_call_target="tpu_custom_call" | custom-call | flops 7059013632 | bytes 6561792 | tf_op jit(solution)/shard_map/pallas_call | solution.py:116
  84.2 1.1 custom-call.4
  85.9 6.5 %shard_map.97 = bf16[4,512,512]{2,1,0:T(8,128)(2,1)S(1)} custom-call(s32[4,2]{1,0:T(4,128)S(1)} %copy.151.idx_ref, f32[4,3]{1,0:T(4,128)S(1)} %pad_maximum_fusion.11.plane_ref, f32[1,512]{1,0:T(1,128)S(1)} %multiply_add_fusion.1.xrow_ref, f32[512,1]{1,0:T(8,128)S(1)} %multiply_add_fusion.ycol_ref, f32[4,512,512]{2,1,0:T(8,128)} %shard_map.96.matched_ref, ...), custom_call_target="tpu_custom_call" | custom-call | flops 2147483648 | bytes 10485760 | tf_op jit(solution)/shard_map/pallas_call | solution.py:165
  92.4 2.0 %fusion.4 = bf16[4,512,512]{2,0,1:T(4,128)(2,1)S(1)} fusion(bf16[4,512,512]{2,1,0:T(8,128)(2,1)S(1)} %shard_map.97, pred[4,4]{1,0:T(4,128)(4,1)S(1)} %fusion.22, bf16[4]{0:T(256)(128)(2,1)S(1)} %bitcast.96), kind=kOutput, calls=%fused_computation.7 | convolution fusion | flops 9437200 | bytes 4194328 | tf_op jit(solution)/shard_map/ev,eij->vij/dot_general | solution.py:290
  94.4 1.8 %copy.154 = bf16[4,512,512]{2,1,0:T(8,128)(2,1)} copy(bf16[4,512,512]{2,0,1:T(4,128)(2,1)S(1)} %fusion.4) | data formatting | bytes 4194304 | tf_op jit(solution)/shard_map/convert_element_type | solution.py:292
  98.6 40.1 %reduce-scatter.2.cloned.1.call-done = bf16[1,512,512]{2,1,0:T(8,128)(2,1)} async-done(((bf16[4,512,512]{2,1,0:T(8,128)(2,1)}), bf16[1,512,512]{2,1,0:T(8,128)(2,1)}) %reduce-scatter.2.cloned.1.call-update) | async-done | bytes 524304 | tf_op jit(solution)/shard_map/reduce_scatter | solution.py:291
  138.7 2.8 %convert_divide_fusion = f32[1,512,512]{2,1,0:T(8,128)} fusion(bf16[1,512,512]{2,1,0:T(8,128)(2,1)} %reduce-scatter.2.cloned.1.call-done, f32[]{:T(128)} %convert_reduce_fusion), kind=kLoop, calls=%fused_computation.16 | loop fusion | flops 524288 | bytes 1572868 | tf_op jit(solution)/shard_map/div | solution.py:294
  (91 shorter events, 15.2 us)
Async XLA Ops:
  7.2 14.2 %copy-start.6 = (bf16[4,512,512]{2,1,0:T(8,128)(2,1)S(1)}, bf16[4,512,512]{2,1,0:T(8,128)(2,1)}, u32[]{:S(2)}) copy-start(bf16[4,512,512]{2,1,0:T(8,128)(2,1)} %param.10) | copy-start | bytes 6291460
  7.2 131.6 %reduce-scatter.2.cloned.1.call-start = ((), (), s32[]{:S(2)}) async-start(), calls=%async_computation.1 | async-start | bytes 2621440 | tf_op jit(solution)/shard_map/reduce_scatter | solution.py:291
  13.5 46.6 %collective-permute-start.1 = (bf16[144,512]{1,0:T(8,128)(2,1)S(1)}, bf16[144,512]{1,0:T(8,128)(2,1)}, u32[]{:S(2)}, u32[]{:S(2)}) collective-permute-start(bf16[144,512]{1,0:T(8,128)(2,1)S(1)} %get-tuple-element.48), channel_id=1, source_target_pairs={{0,16},{8,24},{16,0},{24,8},{1,17},{9,25},{17,1},{25,9},{2,18},{10... | collective-permute-start | bytes 442376 | tf_op jit(solution)/shard_map/ppermute | solution.py:227
  17.5 42.5 %collective-permute-start = (bf16[144,512]{1,0:T(8,128)(2,1)S(1)}, bf16[144,512]{1,0:T(8,128)(2,1)}, u32[]{:S(2)}, u32[]{:S(2)}) collective-permute-start(bf16[144,512]{1,0:T(8,128)(2,1)S(1)} %get-tuple-element.48), channel_id=1, source_target_pairs={{0,8},{8,16},{16,24},{24,0},{1,9},{9,17},{17,25},{25,1},{2,10},{10... | collective-permute-start | bytes 442376 | tf_op jit(solution)/shard_map/ppermute | solution.py:227
  19.1 41.0 %collective-permute-start.2 = (bf16[144,512]{1,0:T(8,128)(2,1)S(1)}, bf16[144,512]{1,0:T(8,128)(2,1)}, u32[]{:S(2)}, u32[]{:S(2)}) collective-permute-start(bf16[144,512]{1,0:T(8,128)(2,1)S(1)} %get-tuple-element.48), channel_id=1, source_target_pairs={{0,24},{8,0},{16,8},{24,16},{1,25},{9,1},{17,9},{25,17},{2,26},{10... | collective-permute-start | bytes 442376 | tf_op jit(solution)/shard_map/ppermute | solution.py:227
  22.4 14.0 %collective-permute-start.3 = (bf16[4,512,16]{2,1,0:T(8,128)(2,1)}, bf16[4,512,16]{2,1,0:T(8,128)(2,1)}, u32[]{:S(2)}, u32[]{:S(2)}) collective-permute-start(bf16[4,512,16]{2,1,0:T(8,128)(2,1)} %get-tuple-element.43), channel_id=1, source_target_pairs={{0,1},{1,2},{2,3},{4,5},{5,6},{6,7},{8,9},{9,10},{10,11},{12,13},{... | collective-permute-start | bytes 196616 | tf_op jit(solution)/shard_map/ppermute | solution.py:31
  26.6 23.0 %collective-permute-start.4 = (bf16[4,512,16]{2,1,0:T(8,128)(2,1)S(1)}, bf16[4,512,16]{2,1,0:T(8,128)(2,1)}, u32[]{:S(2)}, u32[]{:S(2)}) collective-permute-start(bf16[4,512,16]{2,1,0:T(8,128)(2,1)S(1)} %get-tuple-element.44), channel_id=1, source_target_pairs={{1,0},{2,1},{3,2},{5,4},{6,5},{7,6},{9,8},{10,9},{11,10},{13,12},{... | collective-permute-start | bytes 196616 | tf_op jit(solution)/shard_map/ppermute | solution.py:32
  36.0 15.8 %copy-start.7 = (bf16[4,512,512]{2,1,0:T(8,128)(2,1)S(1)}, bf16[4,512,512]{2,1,0:T(8,128)(2,1)}, u32[]{:S(2)}) copy-start(bf16[4,512,512]{2,1,0:T(8,128)(2,1)} %param.10) | copy-start | bytes 6291460
  50.5 1.3 collective-permute-start.5
  51.9 3.0 %copy-start.1 = (bf16[3,512,544]{2,1,0:T(8,128)(2,1)S(1)}, bf16[3,512,544]{2,1,0:T(8,128)(2,1)}, u32[]{:S(2)}) copy-start(bf16[3,512,544]{2,1,0:T(8,128)(2,1)} %get-tuple-element.46.ht_ref) | copy-start | bytes 5013508
  51.9 3.0 %copy-start.5 = (f32[4,3]{1,0:T(4,128)S(1)}, f32[4,3]{1,0:T(4,128)}, u32[]{:S(2)}) copy-start(f32[4,3]{1,0:T(4,128)} %coef_ref.3) | copy-start | bytes 148
  54.9 5.1 %copy-start = (bf16[4,544,544]{2,1,0:T(8,128)(2,1)}, bf16[4,544,544]{2,1,0:T(8,128)(2,1)S(1)}, u32[]{:S(2)}) copy-start(bf16[4,544,544]{2,1,0:T(8,128)(2,1)S(1)} %pad_maximum_fusion.padded_ref) | copy-start | bytes 7102468
  54.9 5.1 %copy-start.8 = (bf16[1,144,512]{2,1,0:T(8,128)(2,1)S(1)}, bf16[1,144,512]{2,1,0:T(8,128)(2,1)}, u32[]{:S(2)}) copy-start(bf16[1,144,512]{2,1,0:T(8,128)(2,1)} %get-tuple-element.47) | copy-start | bytes 442372
  60.0 5.6 %copy-start.10 = (s32[4,1,1,2]{0,3,2,1:T(2,128)S(1)}, s32[4,1,1,2]{0,3,2,1:T(2,128)}, u32[]{:S(2)}) copy-start(s32[4,1,1,2]{0,3,2,1:T(2,128)} %param.15) | copy-start | bytes 100
  60.0 7.7 %copy-start.2 = (bf16[3,512,544]{2,1,0:T(8,128)(2,1)S(1)}, bf16[3,512,544]{2,1,0:T(8,128)(2,1)}, u32[]{:S(2)}) copy-start(bf16[3,512,544]{2,1,0:T(8,128)(2,1)} %get-tuple-element.46.ht_ref) | copy-start | bytes 5013508
  62.9 1.2 collective-permute-start.6
  64.2 3.6 %collective-permute-start.7 = (f32[4,12]{1,0:T(4,128)S(1)}, f32[4,12]{1,0:T(4,128)S(1)}, u32[]{:S(2)}, u32[]{:S(2)}) collective-permute-start(f32[4,12]{1,0:T(4,128)S(1)} %fusion.36), channel_id=1, source_target_pairs={{0,1},{1,0},{2,3},{3,2},{4,5},{5,4},{6,7},{7,6},{8,9},{9,8},{10,11... | collective-permute-start | bytes 584 | tf_op jit(solution)/shard_map/ppermute | solution.py:73
  67.7 16.3 %collective-permute-start.8 = (f32[4,12]{1,0:T(4,128)S(1)}, f32[4,12]{1,0:T(4,128)S(1)}, u32[]{:S(2)}, u32[]{:S(2)}) collective-permute-start(f32[4,12]{1,0:T(4,128)S(1)} %add.242), channel_id=1, source_target_pairs={{0,2},{1,3},{2,0},{3,1},{4,6},{5,7},{6,4},{7,5},{8,10},{9,11},{10,... | collective-permute-start | bytes 584 | tf_op jit(solution)/shard_map/ppermute | solution.py:73
  67.8 1.5 %copy-start.3 = (bf16[1,3,512,544]{3,2,1,0:T(8,128)(2,1)S(1)}, bf16[1,3,512,544]{3,2,1,0:T(8,128)(2,1)}, u32[]{:S(2)}) copy-start(bf16[1,3,512,544]{3,2,1,0:T(8,128)(2,1)} %get-tuple-element.45.vt_ref) | copy-start | bytes 5013508
  85.9 6.5 %copy-start.4 = (f32[4,3]{1,0:T(4,128)}, f32[4,3]{1,0:T(4,128)S(1)}, u32[]{:S(2)}) copy-start(f32[4,3]{1,0:T(4,128)S(1)} %pad_maximum_fusion.11.plane_ref) | copy-start | bytes 148
  85.9 6.5 %copy-start.11 = (bf16[4,1,1]{0,2,1:T(2,128)(2,1)S(1)}, bf16[4,1,1]{0,2,1:T(2,128)(2,1)}, u32[]{:S(2)}) copy-start(bf16[4,1,1]{0,2,1:T(2,128)(2,1)} %param.13) | copy-start | bytes 28
  96.1 0.9 copy-start.9
Sparse Core Ops, SparseCore 0:
  96.3 42.4 reduce-scatter.1

commit v6 on v5

--- a/solution.py
+++ b/solution.py
@@ -18,6 +18,12 @@
         devices, length = (lax.axis_size(axis), value.shape[dim])
         last = lax.slice_in_dim(value, length - width, length, axis=dim)
         initial = lax.slice_in_dim(value, 0, width, axis=dim)
+        minor = dim == value.ndim - 1
+        if minor:
+            flat = value.shape[:-2] + (-1,)
+            turned = jnp.swapaxes(last, -1, -2).shape
+            last = jnp.swapaxes(last, -1, -2).reshape(flat)
+            initial = jnp.swapaxes(initial, -1, -2).reshape(flat)
         if devices == 2:
             position = lax.axis_index(axis)
             facing = jnp.where(position == 0, last, initial)
@@ -30,6 +36,9 @@
             down = [(j, i) for i, j in up]
             before = lax.ppermute(last, axis, up)
             after = lax.ppermute(initial, axis, down)
+        if minor:
+            before = jnp.swapaxes(before.reshape(turned), -1, -2)
+            after = jnp.swapaxes(after.reshape(turned), -1, -2)
         value = jnp.concatenate([before, value, after], axis=dim)
     return value
 

time: 149 us -> 137 us (0.919)
  waiting for transfers between devices: 57.8 us -> 44.3 us
  starting transfers between devices: 15.1 us -> 17.5 us
    ppermute x1, waiting for transfers between devices: 13.2 us -> 0.01 us  [extended(): after = lax.ppermute(initial, axis, down)]
    ppermute x3, starting transfers between devices: 1.66 us -> 3.7 us  [butterfly_sum(): values = jax.tree.map(lambda v: v + lax.ppermute(v, axis, pairs), values)]
  transfers between devices with their start and end apart: 10 -> 10, of which waited for: 6 -> 4; matrix products, arithmetic and copies ran while one was open for 10% -> 11% of each run, Pallas kernels for 13% -> 14%
where the time goes in v6:
time: 137 us; the launch traced here: 136 us
  waiting for transfers between devices  44.3 us (32%)
  Pallas kernels  26.1 us (19%)
  other arithmetic  21.6 us (16%)
  starting transfers between devices  17.5 us (13%)
  between operations  14.4 us (11%)
  local copies, waits for them, and re-layouts  7.44 us (5%)
  matrix products  4.98 us (4%)
    reduce_scatter x1, waiting for transfers between devices, shards(): lax.psum_scatter(partial_sum.astype(jnp.bfloat16), 'visit', scatter_dimen...  40.6 us
    pallas_call x2, Pallas kernels, conv_tiles(): pl.pallas_call(conv_body, grid=(exp_dev,), in_specs=[pl.BlockSpec(memory_...  19.8 us
    ppermute x3, starting transfers between devices, shards(): received.append(lax.ppermute(payload, 'visit', pairs))  7.86 us
    pallas_call x1, Pallas kernels, warp_tiles(): pl.pallas_call(warp_body, grid_spec=grid_spec, out_shape=jax.ShapeDtypeSt...  6.34 us
    ppermute x1, starting transfers between devices, extended(): before = lax.ppermute(last, axis, up)  4.55 us
    ppermute x3, starting transfers between devices, butterfly_sum(): values = jax.tree.map(lambda v: v + lax.ppermute(v, axis, pairs), values)  3.7 us
    convert_element_type x2, other arithmetic, band_table(): return jnp.where(jnp.abs(offset) <= width, values, 0.0).astype(jnp.bfloat16)  3.45 us
    div x1, other arithmetic, shards(): coadd_patch = numerator / denominator[:, None, None]  2.77 us
  transfers between devices with their start and end apart: 10, of which 4 were waited for; matrix products, arithmetic and copies ran while one was open for 11% of the time, Pallas kernels for 14%

profile of v6, /device:TPU:0, one launch (start us, length us, event | category | flops | bytes accessed | tf_op | source)
XLA Modules:
  0.0 136.4 jit_solution(5676949910547084417)
XLA Ops:
  10.7 2.1 %convolution_convert_fusion = bf16[4,32,512]{2,1,0:T(8,128)(2,1)S(1)} fusion(bf16[4,512,512]{2,1,0:T(8,128)(2,1)} %param.10, s32[4]{0:T(128)S(1)} %get-tuple-element.39), kind=kOutput, calls=%fused_computation.15 | convolution fusion | flops 67305472 | bytes 2228240 | tf_op jit(solution)/shard_map/esr,erl->esl/dot_general | solution.py:216
  13.5 4.0 %collective-permute-start.1 = (bf16[144,512]{1,0:T(8,128)(2,1)}, bf16[144,512]{1,0:T(8,128)(2,1)}, u32[]{:S(2)}, u32[]{:S(2)}) collective-permute-start(bf16[144,512]{1,0:T(8,128)(2,1)} %get-tuple-element.48), channel_id=1, source_target_pairs={{0,16},{8,24},{16,0},{24,8},{1,17},{9,25},{17,1},{25,9},{2,18},{10... | collective-permute-start | bytes 442376 | tf_op jit(solution)/shard_map/ppermute | solution.py:236
  17.6 1.6 %collective-permute-start = (bf16[144,512]{1,0:T(8,128)(2,1)}, bf16[144,512]{1,0:T(8,128)(2,1)}, u32[]{:S(2)}, u32[]{:S(2)}) collective-permute-start(bf16[144,512]{1,0:T(8,128)(2,1)} %get-tuple-element.48), channel_id=1, source_target_pairs={{0,8},{8,16},{16,24},{24,0},{1,9},{9,17},{17,25},{25,1},{2,10},{10... | collective-permute-start | bytes 442376 | tf_op jit(solution)/shard_map/ppermute | solution.py:236
  19.1 2.2 %collective-permute-start.2 = (bf16[144,512]{1,0:T(8,128)(2,1)}, bf16[144,512]{1,0:T(8,128)(2,1)}, u32[]{:S(2)}, u32[]{:S(2)}) collective-permute-start(bf16[144,512]{1,0:T(8,128)(2,1)} %get-tuple-element.48), channel_id=1, source_target_pairs={{0,24},{8,0},{16,8},{24,16},{1,25},{9,1},{17,9},{25,17},{2,26},{10... | collective-permute-start | bytes 442376 | tf_op jit(solution)/shard_map/ppermute | solution.py:236
  21.9 1.3 collective-permute-start.4
  23.5 4.5 %collective-permute-start.3 = (bf16[4,8192]{1,0:T(4,128)(2,1)S(1)}, bf16[4,8192]{1,0:T(4,128)(2,1)S(1)}, u32[]{:S(2)}, u32[]{:S(2)}) collective-permute-start(bf16[4,8192]{1,0:T(4,128)(2,1)S(1)} %bitcast.102), channel_id=1, source_target_pairs={{0,1},{1,2},{2,3},{4,5},{5,6},{6,7},{8,9},{9,10},{10,11},{12,13},{... | collective-permute-start | bytes 196616 | tf_op jit(solution)/shard_map/ppermute | solution.py:37
  30.0 1.3 select_convert_fusion.2
  31.2 2.2 %select_convert_fusion = (bf16[1,512,544]{2,1,0:T(8,128)(2,1)S(1)}, bf16[1,512,544]{2,1,0:T(8,128)(2,1)S(1)}) fusion(f32[]{:T(128)} %exponential_reduce_fusion, f32[]{:T(128)} %exponential_reduce_fusion.1), kind=kLoop, calls=%fused_computation.8 | loop fusion | flops 4177920 | bytes 1114120 | tf_op jit(solution)/shard_map/convert_element_type | solution.py:54
  33.9 2.3 %fusion.33 = (bf16[1,3,512,544]{3,2,1,0:T(8,128)(2,1)}, bf16[3,512,544]{2,1,0:T(8,128)(2,1)}) fusion(bf16[1,512,544]{2,1,0:T(8,128)(2,1)S(1)} %get-tuple-element.63, bf16[1,512,544]{2,1,0:T(8,128)(2,1)S(1)} %get-tuple-element.64, bf16[1,512,544]{2,1,0:T(8,128)(2,1)S(1)} %select_convert_fusion.2), kind=kLoop, calls=%fused_computation.105 | loop fusion | flops 1671168 | bytes 5013504 | tf_op jit(solution)/shard_map/broadcast_in_dim | solution.py:121
  38.8 1.3 collective-permute-done.5
  40.1 1.8 %pad_maximum_fusion.padded_ref = bf16[4,544,544]{2,1,0:T(8,128)(2,1)S(1)} fusion(bf16[4,16,544]{2,1,0:T(8,128)(2,1)S(1)} %get-tuple-element.50, bf16[4,512,16]{2,1,0:T(8,128)(2,1)S(1)} %bitcast.92, bf16[4,512,512]{2,1,0:T(8,128)(2,1)S(1)} %copy-done.7, bf16[4,512,16]{2,1,0:T(8,128)(2,1)S(1)} %bitcast.90, bf16[4,16,544]{2,1,0:T(8,128)(2,1)S(1)} %get-tuple-element.49), kind=kLoop, calls=%fused_computation | loop fusion | flops 11837440 | bytes 4734976 | tf_op jit(solution)/shard_map/concatenate | solution.py:42
  42.0 5.1 %shard_map.95 = f32[4,32,512]{2,1,0:T(8,128)S(1)} custom-call(f32[4,3]{1,0:T(4,128)S(1)} %copy-done.5, bf16[4,3,32,544]{3,2,1,0:T(8,128)(2,1)S(1)} %fusion.10.vt_ref, bf16[3,512,544]{2,1,0:T(8,128)(2,1)S(1)} %copy-done.1, bf16[4,544,544]{2,1,0:T(8,128)(2,1)S(1)} %pad_maximum_fusion.padded_ref), custom_call_target="tpu_custom_call" | custom-call | flops 441188352 | bytes 2629632 | tf_op jit(solution)/shard_map/pallas_call | solution.py:125
  47.1 1.3 pad_maximum_fusion.2
  51.2 2.4 %collective-permute-start.7 = (f32[4,12]{1,0:T(4,128)S(1)}, f32[4,12]{1,0:T(4,128)S(1)}, u32[]{:S(2)}, u32[]{:S(2)}) collective-permute-start(f32[4,12]{1,0:T(4,128)S(1)} %fusion.35), channel_id=1, source_target_pairs={{0,1},{1,0},{2,3},{3,2},{4,5},{5,4},{6,7},{7,6},{8,9},{9,8},{10,11... | collective-permute-start | bytes 584 | tf_op jit(solution)/shard_map/ppermute | solution.py:82
  53.7 1.5 %collective-permute-done.7 = f32[4,12]{1,0:T(4,128)S(1)} collective-permute-done((f32[4,12]{1,0:T(4,128)S(1)}, f32[4,12]{1,0:T(4,128)S(1)}, u32[]{:S(2)}, u32[]{:S(2)}) %collective-permute-start.7) | collective-permute-done | bytes 224 | tf_op jit(solution)/shard_map/ppermute | solution.py:82
  55.2 1.1 collective-permute-start.8
  56.3 1.5 %copy-done.3 = bf16[1,3,512,544]{3,2,1,0:T(8,128)(2,1)S(1)} copy-done((bf16[1,3,512,544]{3,2,1,0:T(8,128)(2,1)S(1)}, bf16[1,3,512,544]{3,2,1,0:T(8,128)(2,1)}, u32[]{:S(2)}) %copy-start.3) | copy-done | bytes 1671192
  57.9 14.7 %shard_map.96.matched_ref = f32[4,512,512]{2,1,0:T(8,128)} custom-call(f32[4,3]{1,0:T(4,128)S(1)} %copy-done.5, bf16[1,3,512,544]{3,2,1,0:T(8,128)(2,1)S(1)} %copy-done.3, bf16[3,512,544]{2,1,0:T(8,128)(2,1)S(1)} %copy-done.2, bf16[4,544,544]{2,1,0:T(8,128)(2,1)} %copy-done), custom_call_target="tpu_custom_call" | custom-call | flops 7059013632 | bytes 6561792 | tf_op jit(solution)/shard_map/pallas_call | solution.py:125
  72.8 1.1 custom-call.4
  74.4 6.3 %shard_map.97 = bf16[4,512,512]{2,1,0:T(8,128)(2,1)S(1)} custom-call(s32[4,2]{1,0:T(4,128)S(1)} %copy.167.idx_ref, f32[4,3]{1,0:T(4,128)S(1)} %pad_maximum_fusion.11.plane_ref, f32[1,512]{1,0:T(1,128)S(1)} %multiply_add_fusion.1.xrow_ref, f32[512,1]{1,0:T(8,128)S(1)} %multiply_add_fusion.ycol_ref, f32[4,512,512]{2,1,0:T(8,128)} %shard_map.96.matched_ref, ...), custom_call_target="tpu_custom_call" | custom-call | flops 2147483648 | bytes 10485760 | tf_op jit(solution)/shard_map/pallas_call | solution.py:174
  80.8 2.0 %fusion.4 = bf16[4,512,512]{2,0,1:T(4,128)(2,1)S(1)} fusion(bf16[4,512,512]{2,1,0:T(8,128)(2,1)S(1)} %shard_map.97, pred[4,4]{1,0:T(4,128)(4,1)S(1)} %fusion.22, bf16[4]{0:T(256)(128)(2,1)S(1)} %bitcast.126), kind=kOutput, calls=%fused_computation.7 | convolution fusion | flops 9437200 | bytes 4194328 | tf_op jit(solution)/shard_map/ev,eij->vij/dot_general | solution.py:299
  82.8 1.8 %copy.170 = bf16[4,512,512]{2,1,0:T(8,128)(2,1)} copy(bf16[4,512,512]{2,0,1:T(4,128)(2,1)S(1)} %fusion.4) | data formatting | bytes 4194304 | tf_op jit(solution)/shard_map/convert_element_type | solution.py:301
  86.2 40.6 %reduce-scatter.2.cloned.1.call-done = bf16[1,512,512]{2,1,0:T(8,128)(2,1)} async-done(((bf16[4,512,512]{2,1,0:T(8,128)(2,1)}), bf16[1,512,512]{2,1,0:T(8,128)(2,1)}) %reduce-scatter.2.cloned.1.call-update) | async-done | bytes 524304 | tf_op jit(solution)/shard_map/reduce_scatter | solution.py:300
  126.8 2.8 %convert_divide_fusion = f32[1,512,512]{2,1,0:T(8,128)} fusion(bf16[1,512,512]{2,1,0:T(8,128)(2,1)} %reduce-scatter.2.cloned.1.call-done, f32[]{:T(128)} %convert_reduce_fusion), kind=kLoop, calls=%fused_computation.16 | loop fusion | flops 524288 | bytes 1572868 | tf_op jit(solution)/shard_map/div | solution.py:303
  (99 shorter events, 15.2 us)
Async XLA Ops:
  7.2 14.2 %copy-start.6 = (bf16[4,512,512]{2,1,0:T(8,128)(2,1)S(1)}, bf16[4,512,512]{2,1,0:T(8,128)(2,1)}, u32[]{:S(2)}) copy-start(bf16[4,512,512]{2,1,0:T(8,128)(2,1)} %param.10) | copy-start | bytes 6291460
  7.2 119.6 %reduce-scatter.2.cloned.1.call-start = ((), (), s32[]{:S(2)}) async-start(), calls=%async_computation.1 | async-start | bytes 2621440 | tf_op jit(solution)/shard_map/reduce_scatter | solution.py:300
  13.5 33.5 %collective-permute-start.1 = (bf16[144,512]{1,0:T(8,128)(2,1)}, bf16[144,512]{1,0:T(8,128)(2,1)}, u32[]{:S(2)}, u32[]{:S(2)}) collective-permute-start(bf16[144,512]{1,0:T(8,128)(2,1)} %get-tuple-element.48), channel_id=1, source_target_pairs={{0,16},{8,24},{16,0},{24,8},{1,17},{9,25},{17,1},{25,9},{2,18},{10... | collective-permute-start | bytes 442376 | tf_op jit(solution)/shard_map/ppermute | solution.py:236
  17.6 29.5 %collective-permute-start = (bf16[144,512]{1,0:T(8,128)(2,1)}, bf16[144,512]{1,0:T(8,128)(2,1)}, u32[]{:S(2)}, u32[]{:S(2)}) collective-permute-start(bf16[144,512]{1,0:T(8,128)(2,1)} %get-tuple-element.48), channel_id=1, source_target_pairs={{0,8},{8,16},{16,24},{24,0},{1,9},{9,17},{17,25},{25,1},{2,10},{10... | collective-permute-start | bytes 442376 | tf_op jit(solution)/shard_map/ppermute | solution.py:236
  19.1 28.0 %collective-permute-start.2 = (bf16[144,512]{1,0:T(8,128)(2,1)}, bf16[144,512]{1,0:T(8,128)(2,1)}, u32[]{:S(2)}, u32[]{:S(2)}) collective-permute-start(bf16[144,512]{1,0:T(8,128)(2,1)} %get-tuple-element.48), channel_id=1, source_target_pairs={{0,24},{8,0},{16,8},{24,16},{1,25},{9,1},{17,9},{25,17},{2,26},{10... | collective-permute-start | bytes 442376 | tf_op jit(solution)/shard_map/ppermute | solution.py:236
  21.9 14.4 %collective-permute-start.4 = (bf16[4,8192]{1,0:T(4,128)(2,1)S(1)}, bf16[4,8192]{1,0:T(4,128)(2,1)S(1)}, u32[]{:S(2)}, u32[]{:S(2)}) collective-permute-start(bf16[4,8192]{1,0:T(4,128)(2,1)S(1)} %bitcast.100), channel_id=1, source_target_pairs={{1,0},{2,1},{3,2},{5,4},{6,5},{7,6},{9,8},{10,9},{11,10},{13,12},{... | collective-permute-start | bytes 196616 | tf_op jit(solution)/shard_map/ppermute | solution.py:38
  23.5 12.9 %collective-permute-start.3 = (bf16[4,8192]{1,0:T(4,128)(2,1)S(1)}, bf16[4,8192]{1,0:T(4,128)(2,1)S(1)}, u32[]{:S(2)}, u32[]{:S(2)}) collective-permute-start(bf16[4,8192]{1,0:T(4,128)(2,1)S(1)} %bitcast.102), channel_id=1, source_target_pairs={{0,1},{1,2},{2,3},{4,5},{5,6},{6,7},{8,9},{9,10},{10,11},{12,13},{... | collective-permute-start | bytes 196616 | tf_op jit(solution)/shard_map/ppermute | solution.py:37
  37.7 2.4 %copy-start.7 = (bf16[4,512,512]{2,1,0:T(8,128)(2,1)S(1)}, bf16[4,512,512]{2,1,0:T(8,128)(2,1)}, u32[]{:S(2)}) copy-start(bf16[4,512,512]{2,1,0:T(8,128)(2,1)} %param.10) | copy-start | bytes 6291460
  37.7 2.4 %copy-start.8 = (bf16[4,16,512]{1,2,0:T(8,128)(2,1)S(1)}, bf16[4,16,512]{1,2,0:T(8,128)(2,1)}, u32[]{:S(2)}) copy-start(bf16[4,16,512]{1,2,0:T(8,128)(2,1)} %copy.149) | copy-start | bytes 196612
  38.7 1.3 collective-permute-start.5
  40.1 1.9 %copy-start.1 = (bf16[3,512,544]{2,1,0:T(8,128)(2,1)S(1)}, bf16[3,512,544]{2,1,0:T(8,128)(2,1)}, u32[]{:S(2)}) copy-start(bf16[3,512,544]{2,1,0:T(8,128)(2,1)} %get-tuple-element.46.ht_ref) | copy-start | bytes 5013508
  40.1 1.9 %copy-start.5 = (f32[4,3]{1,0:T(4,128)S(1)}, f32[4,3]{1,0:T(4,128)}, u32[]{:S(2)}) copy-start(f32[4,3]{1,0:T(4,128)} %coef_ref.3) | copy-start | bytes 148
  42.0 5.1 %copy-start = (bf16[4,544,544]{2,1,0:T(8,128)(2,1)}, bf16[4,544,544]{2,1,0:T(8,128)(2,1)S(1)}, u32[]{:S(2)}) copy-start(bf16[4,544,544]{2,1,0:T(8,128)(2,1)S(1)} %pad_maximum_fusion.padded_ref) | copy-start | bytes 7102468
  42.0 5.1 %copy-start.9 = (bf16[1,144,512]{2,1,0:T(8,128)(2,1)S(1)}, bf16[1,144,512]{2,1,0:T(8,128)(2,1)}, u32[]{:S(2)}) copy-start(bf16[1,144,512]{2,1,0:T(8,128)(2,1)} %get-tuple-element.47) | copy-start | bytes 442372
  47.1 6.6 %copy-start.10 = (s32[4,1,1,2]{0,3,2,1:T(2,128)S(1)}, s32[4,1,1,2]{0,3,2,1:T(2,128)}, u32[]{:S(2)}) copy-start(s32[4,1,1,2]{0,3,2,1:T(2,128)} %param.15) | copy-start | bytes 100
  47.1 9.2 %copy-start.2 = (bf16[3,512,544]{2,1,0:T(8,128)(2,1)S(1)}, bf16[3,512,544]{2,1,0:T(8,128)(2,1)}, u32[]{:S(2)}) copy-start(bf16[3,512,544]{2,1,0:T(8,128)(2,1)} %get-tuple-element.46.ht_ref) | copy-start | bytes 5013508
  50.0 1.2 collective-permute-start.6
  51.2 4.0 %collective-permute-start.7 = (f32[4,12]{1,0:T(4,128)S(1)}, f32[4,12]{1,0:T(4,128)S(1)}, u32[]{:S(2)}, u32[]{:S(2)}) collective-permute-start(f32[4,12]{1,0:T(4,128)S(1)} %fusion.35), channel_id=1, source_target_pairs={{0,1},{1,0},{2,3},{3,2},{4,5},{5,4},{6,7},{7,6},{8,9},{9,8},{10,11... | collective-permute-start | bytes 584 | tf_op jit(solution)/shard_map/ppermute | solution.py:82
  55.2 17.4 %collective-permute-start.8 = (f32[4,12]{1,0:T(4,128)S(1)}, f32[4,12]{1,0:T(4,128)S(1)}, u32[]{:S(2)}, u32[]{:S(2)}) collective-permute-start(f32[4,12]{1,0:T(4,128)S(1)} %add.242), channel_id=1, source_target_pairs={{0,2},{1,3},{2,0},{3,1},{4,6},{5,7},{6,4},{7,5},{8,10},{9,11},{10,... | collective-permute-start | bytes 584 | tf_op jit(solution)/shard_map/ppermute | solution.py:82
  56.3 1.5 %copy-start.3 = (bf16[1,3,512,544]{3,2,1,0:T(8,128)(2,1)S(1)}, bf16[1,3,512,544]{3,2,1,0:T(8,128)(2,1)}, u32[]{:S(2)}) copy-start(bf16[1,3,512,544]{3,2,1,0:T(8,128)(2,1)} %get-tuple-element.45.vt_ref) | copy-start | bytes 5013508
  74.4 6.4 %copy-start.4 = (f32[4,3]{1,0:T(4,128)}, f32[4,3]{1,0:T(4,128)S(1)}, u32[]{:S(2)}) copy-start(f32[4,3]{1,0:T(4,128)S(1)} %pad_maximum_fusion.11.plane_ref) | copy-start | bytes 148
  74.4 6.4 %copy-start.11 = (bf16[4,1,1]{0,2,1:T(2,128)(2,1)S(1)}, bf16[4,1,1]{0,2,1:T(2,128)(2,1)}, u32[]{:S(2)}) copy-start(bf16[4,1,1]{0,2,1:T(2,128)(2,1)} %param.13) | copy-start | bytes 28
Sparse Core Ops, SparseCore 0:
  84.7 42.0 reduce-scatter.1

commit v7 on v6

--- a/solution.py
+++ b/solution.py
@@ -138,6 +138,55 @@
         ),
         cost_estimate=pl.CostEstimate(flops=flops, bytes_accessed=moved, transcendentals=0),
     )(coeffs, vtables, htables, padded)
+
+
+BLOCK = 128
+
+
+def band_body(coef_ref, blk_ref, padded_ref, out_ref):
+    e = pl.program_id(0)
+    tile_len = out_ref.shape[1]
+    total = None
+    for kernel in range(len(SIGMA_PARTS)):
+        block = blk_ref[kernel]
+        rows = [
+            jnp.dot(block, padded_ref[0, start:start + 2 * BLOCK, :], preferred_element_type=jnp.float32)
+            for start in range(0, tile_len, BLOCK)
+        ]
+        across = jnp.concatenate(rows, 0).astype(jnp.bfloat16)
+        cols = [
+            lax.dot_general(
+                across[:, start:start + 2 * BLOCK], block, (((1,), (1,)), ((), ())),
+                preferred_element_type=jnp.float32,
+            )
+            for start in range(0, tile_len, BLOCK)
+        ]
+        term = coef_ref[e, kernel] * jnp.concatenate(cols, 1)
+        total = term if total is None else total + term
+    out_ref[0] = total
+
+
+def band_tiles(coeffs, blocks, padded, tile_len):
+    exp_dev, wide = padded.shape[0], padded.shape[1]
+    nk = blocks.shape[0]
+    steps = tile_len // BLOCK
+    flops = exp_dev * nk * steps * 2 * BLOCK * 2 * BLOCK * (wide + tile_len)
+    moved = exp_dev * wide * wide * 2 + exp_dev * tile_len * tile_len * 4
+    return pl.pallas_call(
+        band_body,
+        grid=(exp_dev,),
+        in_specs=[
+            pl.BlockSpec(memory_space=pltpu.SMEM),
+            pl.BlockSpec((nk, BLOCK, 2 * BLOCK), lambda e: (0, 0, 0)),
+            pl.BlockSpec((1, wide, wide), lambda e: (e, 0, 0)),
+        ],
+        out_specs=pl.BlockSpec((1, tile_len, tile_len), lambda e: (e, 0, 0)),
+        out_shape=jax.ShapeDtypeStruct((exp_dev, tile_len, tile_len), jnp.float32),
+        compiler_params=pltpu.CompilerParams(
+            dimension_semantics=("arbitrary",), vmem_limit_bytes=48 * 1024 * 1024
+        ),
+        cost_estimate=pl.CostEstimate(flops=flops, bytes_accessed=moved, transcendentals=0),
+    )(coeffs, blocks, padded)
 
 
 def warp_body(idx_ref, plane_ref, xrow_ref, ycol_ref, matched_ref, rmap_ref, cmap_ref, out_ref):
@@ -254,7 +303,10 @@
         "esr,krj->eksj", pick_rows, stacked_tables, preferred_element_type=jnp.float32
     ).astype(jnp.bfloat16)
     nearby = conv_tiles(coeffs, strip_tables, stacked_tables, padded, True)
-    matched = conv_tiles(coeffs, stacked_tables, stacked_tables, padded, False)
+    spare = 2 * BLOCK + tile_len - BLOCK - padded.shape[1]
+    roomy = jnp.pad(padded, ((0, 0), (0, spare), (0, spare)))
+    blocks = stacked_tables[:, :BLOCK, : 2 * BLOCK]
+    matched = band_tiles(coeffs, blocks, roomy, tile_len)
     difference = nearby - theirs
     pixel_weight = 1.0 / (1.0 + theirs * theirs)
     strip_rows = row_pos * tile_len + offset[:, None] + jnp.arange(STRIP, dtype=jnp.int32)[None, :]

time: 137 us -> 135 us (0.985)
  Pallas kernels: 26.1 us -> 19.5 us
  local copies, waits for them, and re-layouts: 7.44 us -> 12.7 us
  waiting for transfers between devices: 44.3 us -> 41.3 us
    pallas_call x2 -> x1, Pallas kernels: 19.8 us -> 5.05 us  [conv_tiles(): pl.pallas_call(conv_body, grid=(exp_dev,), in_specs=[pl.BlockSpec(memory_...]
    pallas_call x0 -> x1, Pallas kernels: none -> 8.15 us  [band_tiles(): pl.pallas_call(band_body, grid=(exp_dev,), in_specs=[pl.BlockSpec(memory_...]
    broadcast_in_dim x1 -> x0, other arithmetic: 2.28 us -> none  [conv_tiles(): vtables = vtables[None]]
    unnamed x29 -> x35, local copies, waits for them, and re-layouts: 1.8 us -> 4.08 us
    another operation x1 -> x2, other arithmetic: 0.08 us -> 1.71 us  [the longest x1 1.63 us: shards(): jnp.stack([band_table(tile_len, HALO, HALO * part) for part in SIGMA_PARTS])]
    reduce_scatter x1, waiting for transfers between devices: 40.6 us -> 39 us  [shards(): lax.psum_scatter(partial_sum.astype(jnp.bfloat16), 'visit', scatter_dimen...]
  transfers between devices with their start and end apart: 10 -> 10, of which waited for: 4 -> 3; matrix products, arithmetic and copies ran while one was open for 11% -> 17% of each run, Pallas kernels for 14% -> 10%
where the time goes in v7:
time: 135 us; the launch traced here: 134 us
  waiting for transfers between devices  41.3 us (31%)
  other arithmetic  22.9 us (17%)
  Pallas kernels  19.5 us (14%)
  starting transfers between devices  17.9 us (13%)
  between operations  14.4 us (11%)
  local copies, waits for them, and re-layouts  12.7 us (9%)
  matrix products  4.99 us (4%)
    reduce_scatter x1, waiting for transfers between devices, shards(): lax.psum_scatter(partial_sum.astype(jnp.bfloat16), 'visit', scatter_dimen...  39 us
    pallas_call x1, Pallas kernels, band_tiles(): pl.pallas_call(band_body, grid=(exp_dev,), in_specs=[pl.BlockSpec(memory_...  8.15 us
    ppermute x3, starting transfers between devices, shards(): received.append(lax.ppermute(payload, 'visit', pairs))  7.86 us
    pallas_call x1, Pallas kernels, warp_tiles(): pl.pallas_call(warp_body, grid_spec=grid_spec, out_shape=jax.ShapeDtypeSt...  6.34 us
    ppermute x1, starting transfers between devices, extended(): before = lax.ppermute(last, axis, up)  5.16 us
    pallas_call x1, Pallas kernels, conv_tiles(): pl.pallas_call(conv_body, grid=(exp_dev,), in_specs=[pl.BlockSpec(memory_...  5.05 us
    unnamed x35, local copies, waits for them, and re-layouts  4.08 us
    ppermute x3, starting transfers between devices, butterfly_sum(): values = jax.tree.map(lambda v: v + lax.ppermute(v, axis, pairs), values)  3.46 us
  transfers between devices with their start and end apart: 10, of which 3 were waited for; matrix products, arithmetic and copies ran while one was open for 17% of the time, Pallas kernels for 10%

profile of v7, /device:TPU:0, one launch (start us, length us, event | category | flops | bytes accessed | tf_op | source)
XLA Modules:
  0.0 133.7 jit_solution(2050868849867063216)
XLA Ops:
  10.7 2.1 %convolution_convert_fusion = bf16[4,32,512]{2,1,0:T(8,128)(2,1)S(1)} fusion(bf16[4,512,512]{2,1,0:T(8,128)(2,1)} %param.10, s32[4]{0:T(128)S(1)} %get-tuple-element.39), kind=kOutput, calls=%fused_computation.15 | convolution fusion | flops 67305472 | bytes 2228240 | tf_op jit(solution)/shard_map/esr,erl->esl/dot_general | solution.py:265
  13.6 4.0 %collective-permute-start.1 = (bf16[144,512]{1,0:T(8,128)(2,1)}, bf16[144,512]{1,0:T(8,128)(2,1)}, u32[]{:S(2)}, u32[]{:S(2)}) collective-permute-start(bf16[144,512]{1,0:T(8,128)(2,1)} %get-tuple-element.46), channel_id=1, source_target_pairs={{0,16},{8,24},{16,0},{24,8},{1,17},{9,25},{17,1},{25,9},{2,18},{10... | collective-permute-start | bytes 442376 | tf_op jit(solution)/shard_map/ppermute | solution.py:285
  17.6 1.6 %collective-permute-start = (bf16[144,512]{1,0:T(8,128)(2,1)}, bf16[144,512]{1,0:T(8,128)(2,1)}, u32[]{:S(2)}, u32[]{:S(2)}) collective-permute-start(bf16[144,512]{1,0:T(8,128)(2,1)} %get-tuple-element.46), channel_id=1, source_target_pairs={{0,8},{8,16},{16,24},{24,0},{1,9},{9,17},{17,25},{25,1},{2,10},{10... | collective-permute-start | bytes 442376 | tf_op jit(solution)/shard_map/ppermute | solution.py:285
  19.2 2.2 %collective-permute-start.2 = (bf16[144,512]{1,0:T(8,128)(2,1)}, bf16[144,512]{1,0:T(8,128)(2,1)}, u32[]{:S(2)}, u32[]{:S(2)}) collective-permute-start(bf16[144,512]{1,0:T(8,128)(2,1)} %get-tuple-element.46), channel_id=1, source_target_pairs={{0,24},{8,0},{16,8},{24,16},{1,25},{9,1},{17,9},{25,17},{2,26},{10... | collective-permute-start | bytes 442376 | tf_op jit(solution)/shard_map/ppermute | solution.py:285
  21.4 1.0 slice_bitcast_fusion.1
  22.5 1.2 copy.148
  24.4 1.3 collective-permute-start.4
  26.5 5.2 %collective-permute-start.3 = (bf16[4,8192]{1,0:T(4,128)(2,1)}, bf16[4,8192]{1,0:T(4,128)(2,1)}, u32[]{:S(2)}, u32[]{:S(2)}) collective-permute-start(bf16[4,8192]{1,0:T(4,128)(2,1)} %bitcast.49), channel_id=1, source_target_pairs={{0,1},{1,2},{2,3},{4,5},{5,6},{6,7},{8,9},{9,10},{10,11},{12,13},{... | collective-permute-start | bytes 196616 | tf_op jit(solution)/shard_map/ppermute | solution.py:37
  33.6 1.3 select_convert_fusion.2
  34.9 2.1 %select_convert_fusion = (bf16[1,512,544]{2,1,0:T(8,128)(2,1)S(1)}, bf16[1,512,544]{2,1,0:T(8,128)(2,1)S(1)}) fusion(f32[]{:T(128)} %exponential_reduce_fusion, f32[]{:T(128)} %exponential_reduce_fusion.1), kind=kLoop, calls=%fused_computation.8 | loop fusion | flops 4177920 | bytes 1114120 | tf_op jit(solution)/shard_map/convert_element_type | solution.py:54
  37.6 1.6 %pad_maximum_fusion.1.ht_ref = bf16[3,512,544]{2,1,0:T(8,128)(2,1)} fusion(bf16[1,512,544]{2,1,0:T(8,128)(2,1)S(1)} %get-tuple-element.61, bf16[1,512,544]{2,1,0:T(8,128)(2,1)S(1)} %get-tuple-element.62, bf16[1,512,544]{2,1,0:T(8,128)(2,1)S(1)} %select_convert_fusion.2), kind=kLoop, calls=%fused_computation.3 | loop fusion | flops 1671168 | bytes 3342336 | tf_op jit(solution)/shard_map/stack | solution.py:301
  45.3 2.9 %pad_maximum_fusion.padded_ref = bf16[4,544,544]{2,1,0:T(8,128)(2,1)S(1)} fusion(bf16[4,16,544]{2,1,0:T(8,128)(2,1)S(1)} %get-tuple-element.48, bf16[4,512,16]{2,1,0:T(8,128)(2,1)S(1)} %bitcast.90, bf16[4,512,512]{2,1,0:T(8,128)(2,1)S(1)} %copy-done.4, bf16[4,512,16]{2,1,0:T(8,128)(2,1)} %bitcast.88, bf16[4,16,544]{2,1,0:T(8,128)(2,1)S(1)} %get-tuple-element.47), kind=kLoop, calls=%fused_computation | loop fusion | flops 11837440 | bytes 4734976 | tf_op jit(solution)/shard_map/concatenate | solution.py:42
  48.2 5.0 %shard_map.95 = f32[4,32,512]{2,1,0:T(8,128)S(1)} custom-call(f32[4,3]{1,0:T(4,128)S(1)} %copy-done.2, bf16[4,3,32,544]{3,2,1,0:T(8,128)(2,1)S(1)} %fusion.10.vt_ref, bf16[3,512,544]{2,1,0:T(8,128)(2,1)S(1)} %copy-done, bf16[4,544,544]{2,1,0:T(8,128)(2,1)S(1)} %pad_maximum_fusion.padded_ref), custom_call_target="tpu_custom_call" | custom-call | flops 441188352 | bytes 2629632 | tf_op jit(solution)/shard_map/pallas_call | solution.py:125
  53.4 1.1 pad_maximum_fusion.2
  57.3 1.8 %collective-permute-start.7 = (f32[4,12]{1,0:T(4,128)S(1)}, f32[4,12]{1,0:T(4,128)S(1)}, u32[]{:S(2)}, u32[]{:S(2)}) collective-permute-start(f32[4,12]{1,0:T(4,128)S(1)} %fusion.34), channel_id=1, source_target_pairs={{0,1},{1,0},{2,3},{3,2},{4,5},{5,4},{6,7},{7,6},{8,9},{9,8},{10,11... | collective-permute-start | bytes 584 | tf_op jit(solution)/shard_map/ppermute | solution.py:82
  59.5 1.4 %collective-permute-done.7 = f32[4,12]{1,0:T(4,128)S(1)} collective-permute-done((f32[4,12]{1,0:T(4,128)S(1)}, f32[4,12]{1,0:T(4,128)S(1)}, u32[]{:S(2)}, u32[]{:S(2)}) %collective-permute-start.7) | collective-permute-done | bytes 224 | tf_op jit(solution)/shard_map/ppermute | solution.py:82
  60.9 1.5 %collective-permute-start.8 = (f32[4,12]{1,0:T(4,128)S(1)}, f32[4,12]{1,0:T(4,128)S(1)}, u32[]{:S(2)}, u32[]{:S(2)}) collective-permute-start(f32[4,12]{1,0:T(4,128)S(1)} %add.244), channel_id=1, source_target_pairs={{0,2},{1,3},{2,0},{3,1},{4,6},{5,7},{6,4},{7,5},{8,10},{9,11},{10,... | collective-permute-start | bytes 584 | tf_op jit(solution)/shard_map/ppermute | solution.py:82
  62.5 8.2 %shard_map.96.matched_ref = f32[4,512,512]{2,1,0:T(8,128)} custom-call(f32[4,3]{1,0:T(4,128)S(1)} %copy-done.2, bf16[3,128,256]{2,1,0:T(8,128)(2,1)S(1)} %slice.127.blk_ref, bf16[4,640,640]{2,1,0:T(8,128)(2,1)S(1)} %pad.7.padded_ref), custom_call_target="tpu_custom_call" | custom-call | flops 3623878656 | bytes 7471104 | tf_op jit(solution)/shard_map/pallas_call | solution.py:175
  70.8 1.1 custom-call.4
  72.5 6.3 %shard_map.97 = bf16[4,512,512]{2,1,0:T(8,128)(2,1)S(1)} custom-call(s32[4,2]{1,0:T(4,128)S(1)} %copy.167.idx_ref, f32[4,3]{1,0:T(4,128)S(1)} %pad_maximum_fusion.11.plane_ref, f32[1,512]{1,0:T(1,128)S(1)} %multiply_add_fusion.1.xrow_ref, f32[512,1]{1,0:T(8,128)S(1)} %multiply_add_fusion.ycol_ref, f32[4,512,512]{2,1,0:T(8,128)} %shard_map.96.matched_ref, ...), custom_call_target="tpu_custom_call" | custom-call | flops 2147483648 | bytes 10485760 | tf_op jit(solution)/shard_map/pallas_call | solution.py:223
  78.8 2.0 %fusion.4 = bf16[4,512,512]{2,0,1:T(4,128)(2,1)S(1)} fusion(bf16[4,512,512]{2,1,0:T(8,128)(2,1)S(1)} %shard_map.97, pred[4,4]{1,0:T(4,128)(4,1)S(1)} %copy-done.10, bf16[4]{0:T(256)(128)(2,1)S(1)} %bitcast.120), kind=kOutput, calls=%fused_computation.7 | convolution fusion | flops 9437200 | bytes 4194328 | tf_op jit(solution)/shard_map/ev,eij->vij/dot_general | solution.py:351
  80.8 1.8 %copy.170 = bf16[4,512,512]{2,1,0:T(8,128)(2,1)} copy(bf16[4,512,512]{2,0,1:T(4,128)(2,1)S(1)} %fusion.4) | data formatting | bytes 4194304 | tf_op jit(solution)/shard_map/convert_element_type | solution.py:353
  85.1 39.0 %reduce-scatter.2.cloned.1.call-done = bf16[1,512,512]{2,1,0:T(8,128)(2,1)} async-done(((bf16[4,512,512]{2,1,0:T(8,128)(2,1)}), bf16[1,512,512]{2,1,0:T(8,128)(2,1)}) %reduce-scatter.2.cloned.1.call-update) | async-done | bytes 524304 | tf_op jit(solution)/shard_map/reduce_scatter | solution.py:352
  124.1 2.8 %convert_divide_fusion = f32[1,512,512]{2,1,0:T(8,128)} fusion(bf16[1,512,512]{2,1,0:T(8,128)(2,1)} %reduce-scatter.2.cloned.1.call-done, f32[]{:T(128)} %convert_reduce_fusion), kind=kLoop, calls=%fused_computation.16 | loop fusion | flops 524288 | bytes 1572868 | tf_op jit(solution)/shard_map/div | solution.py:355
  (107 shorter events, 20.6 us)
Async XLA Ops:
  7.2 14.3 %copy-start.3 = (bf16[4,512,512]{2,1,0:T(8,128)(2,1)S(1)}, bf16[4,512,512]{2,1,0:T(8,128)(2,1)}, u32[]{:S(2)}) copy-start(bf16[4,512,512]{2,1,0:T(8,128)(2,1)} %param.10) | copy-start | bytes 6291460
  7.2 116.9 %reduce-scatter.2.cloned.1.call-start = ((), (), s32[]{:S(2)}) async-start(), calls=%async_computation.1 | async-start | bytes 2621440 | tf_op jit(solution)/shard_map/reduce_scatter | solution.py:352
  8.9 1.8 %copy-start.9 = (pred[4,4]{1,0:T(4,128)(4,1)}, pred[4,4]{1,0:T(4,128)(4,1)S(1)}, u32[]{:S(2)}) copy-start(pred[4,4]{1,0:T(4,128)(4,1)S(1)} %fusion.22) | copy-start | bytes 52
  13.6 39.8 %collective-permute-start.1 = (bf16[144,512]{1,0:T(8,128)(2,1)}, bf16[144,512]{1,0:T(8,128)(2,1)}, u32[]{:S(2)}, u32[]{:S(2)}) collective-permute-start(bf16[144,512]{1,0:T(8,128)(2,1)} %get-tuple-element.46), channel_id=1, source_target_pairs={{0,16},{8,24},{16,0},{24,8},{1,17},{9,25},{17,1},{25,9},{2,18},{10... | collective-permute-start | bytes 442376 | tf_op jit(solution)/shard_map/ppermute | solution.py:285
  17.6 35.7 %collective-permute-start = (bf16[144,512]{1,0:T(8,128)(2,1)}, bf16[144,512]{1,0:T(8,128)(2,1)}, u32[]{:S(2)}, u32[]{:S(2)}) collective-permute-start(bf16[144,512]{1,0:T(8,128)(2,1)} %get-tuple-element.46), channel_id=1, source_target_pairs={{0,8},{8,16},{16,24},{24,0},{1,9},{9,17},{17,25},{25,1},{2,10},{10... | collective-permute-start | bytes 442376 | tf_op jit(solution)/shard_map/ppermute | solution.py:285
  19.2 34.2 %collective-permute-start.2 = (bf16[144,512]{1,0:T(8,128)(2,1)}, bf16[144,512]{1,0:T(8,128)(2,1)}, u32[]{:S(2)}, u32[]{:S(2)}) collective-permute-start(bf16[144,512]{1,0:T(8,128)(2,1)} %get-tuple-element.46), channel_id=1, source_target_pairs={{0,24},{8,0},{16,8},{24,16},{1,25},{9,1},{17,9},{25,17},{2,26},{10... | collective-permute-start | bytes 442376 | tf_op jit(solution)/shard_map/ppermute | solution.py:285
  24.4 15.5 %collective-permute-start.4 = (bf16[4,8192]{1,0:T(4,128)(2,1)}, bf16[4,8192]{1,0:T(4,128)(2,1)}, u32[]{:S(2)}, u32[]{:S(2)}) collective-permute-start(bf16[4,8192]{1,0:T(4,128)(2,1)} %bitcast.53), channel_id=1, source_target_pairs={{1,0},{2,1},{3,2},{5,4},{6,5},{7,6},{9,8},{10,9},{11,10},{13,12},{... | collective-permute-start | bytes 196616 | tf_op jit(solution)/shard_map/ppermute | solution.py:38
  26.5 14.2 %collective-permute-start.3 = (bf16[4,8192]{1,0:T(4,128)(2,1)}, bf16[4,8192]{1,0:T(4,128)(2,1)}, u32[]{:S(2)}, u32[]{:S(2)}) collective-permute-start(bf16[4,8192]{1,0:T(4,128)(2,1)} %bitcast.49), channel_id=1, source_target_pairs={{0,1},{1,2},{2,3},{4,5},{5,6},{6,7},{8,9},{9,10},{10,11},{12,13},{... | collective-permute-start | bytes 196616 | tf_op jit(solution)/shard_map/ppermute | solution.py:37
  41.8 3.4 %copy-start.5 = (bf16[4,16,512]{1,2,0:T(8,128)(2,1)}, bf16[4,16,512]{1,2,0:T(8,128)(2,1)S(1)}, u32[]{:S(2)}) copy-start(bf16[4,16,512]{1,2,0:T(8,128)(2,1)S(1)} %copy.147) | copy-start | bytes 196612
  42.8 2.4 %copy-start.4 = (bf16[4,512,512]{2,1,0:T(8,128)(2,1)S(1)}, bf16[4,512,512]{2,1,0:T(8,128)(2,1)}, u32[]{:S(2)}) copy-start(bf16[4,512,512]{2,1,0:T(8,128)(2,1)} %param.10) | copy-start | bytes 6291460
  42.8 2.4 %copy-start.6 = (bf16[4,16,512]{1,2,0:T(8,128)(2,1)S(1)}, bf16[4,16,512]{1,2,0:T(8,128)(2,1)}, u32[]{:S(2)}) copy-start(bf16[4,16,512]{1,2,0:T(8,128)(2,1)} %copy.149) | copy-start | bytes 196612
  43.9 1.3 %collective-permute-start.5 = (bf16[4,16,544]{2,1,0:T(8,128)(2,1)S(1)}, bf16[4,16,544]{2,1,0:T(8,128)(2,1)S(1)}, u32[]{:S(2)}, u32[]{:S(2)}) collective-permute-start(bf16[4,16,544]{2,1,0:T(8,128)(2,1)S(1)} %fusion.19), channel_id=1, source_target_pairs={{0,4},{4,0},{1,5},{5,1},{2,6},{6,2},{3,7},{7,3},{8,12},{12,8},{9,1... | collective-permute-start | bytes 208904 | tf_op jit(solution)/shard_map/ppermute | solution.py:30
  45.3 2.9 %copy-start = (bf16[3,512,544]{2,1,0:T(8,128)(2,1)S(1)}, bf16[3,512,544]{2,1,0:T(8,128)(2,1)}, u32[]{:S(2)}) copy-start(bf16[3,512,544]{2,1,0:T(8,128)(2,1)} %pad_maximum_fusion.1.ht_ref) | copy-start | bytes 5013508
  45.3 2.9 %copy-start.2 = (f32[4,3]{1,0:T(4,128)S(1)}, f32[4,3]{1,0:T(4,128)}, u32[]{:S(2)}) copy-start(f32[4,3]{1,0:T(4,128)} %coef_ref.3) | copy-start | bytes 148
  48.2 5.1 %copy-start.7 = (bf16[1,144,512]{2,1,0:T(8,128)(2,1)S(1)}, bf16[1,144,512]{2,1,0:T(8,128)(2,1)}, u32[]{:S(2)}) copy-start(bf16[1,144,512]{2,1,0:T(8,128)(2,1)} %get-tuple-element.45) | copy-start | bytes 442372
  53.3 1.2 copy-start.14
  53.4 5.8 %copy-start.11 = (s32[4,1,1,2]{0,3,2,1:T(2,128)S(1)}, s32[4,1,1,2]{0,3,2,1:T(2,128)}, u32[]{:S(2)}) copy-start(s32[4,1,1,2]{0,3,2,1:T(2,128)} %param.15) | copy-start | bytes 100
  56.1 1.2 collective-permute-start.6
  57.3 3.6 %collective-permute-start.7 = (f32[4,12]{1,0:T(4,128)S(1)}, f32[4,12]{1,0:T(4,128)S(1)}, u32[]{:S(2)}, u32[]{:S(2)}) collective-permute-start(f32[4,12]{1,0:T(4,128)S(1)} %fusion.34), channel_id=1, source_target_pairs={{0,1},{1,0},{2,3},{3,2},{4,5},{5,4},{6,7},{7,6},{8,9},{9,8},{10,11... | collective-permute-start | bytes 584 | tf_op jit(solution)/shard_map/ppermute | solution.py:82
  60.9 11.2 %copy-start.12 = (pred[3,3]{1,0:T(4,128)(4,1)S(1)}, pred[3,3]{1,0:T(4,128)(4,1)}, u32[]{:S(2)}) copy-start(pred[3,3]{1,0:T(4,128)(4,1)} %iota_compare_fusion.2) | copy-start | bytes 31
  60.9 9.7 %collective-permute-start.8 = (f32[4,12]{1,0:T(4,128)S(1)}, f32[4,12]{1,0:T(4,128)S(1)}, u32[]{:S(2)}, u32[]{:S(2)}) collective-permute-start(f32[4,12]{1,0:T(4,128)S(1)} %add.244), channel_id=1, source_target_pairs={{0,2},{1,3},{2,0},{3,1},{4,6},{5,7},{6,4},{7,5},{8,10},{9,11},{10,... | collective-permute-start | bytes 584 | tf_op jit(solution)/shard_map/ppermute | solution.py:82
  72.4 6.4 %copy-start.1 = (f32[4,3]{1,0:T(4,128)}, f32[4,3]{1,0:T(4,128)S(1)}, u32[]{:S(2)}) copy-start(f32[4,3]{1,0:T(4,128)S(1)} %pad_maximum_fusion.11.plane_ref) | copy-start | bytes 148
  72.4 6.4 %copy-start.10 = (pred[4,4]{1,0:T(4,128)(4,1)S(1)}, pred[4,4]{1,0:T(4,128)(4,1)}, u32[]{:S(2)}) copy-start(pred[4,4]{1,0:T(4,128)(4,1)} %copy-done.9) | copy-start | bytes 52
  72.4 6.4 %copy-start.13 = (bf16[4,1,1]{0,2,1:T(2,128)(2,1)S(1)}, bf16[4,1,1]{0,2,1:T(2,128)(2,1)}, u32[]{:S(2)}) copy-start(bf16[4,1,1]{0,2,1:T(2,128)(2,1)} %param.13) | copy-start | bytes 28
  (1 other events, 0.9 us)
Sparse Core Ops, SparseCore 0:
  82.7 41.3 reduce-scatter.1

commit v8 on v7

--- a/solution.py
+++ b/solution.py
@@ -43,6 +43,15 @@
     return value
 
 
+def band_values(offset, width, sigma):
+    spread = (jnp.arange(2 * width + 1) - width).astype(jnp.float32)
+    curve = jnp.exp(-spread * spread / (2.0 * sigma * sigma))
+    total = jnp.sum(curve)
+    offset = offset.astype(jnp.float32)
+    values = jnp.exp(-offset * offset / (2.0 * sigma * sigma)) / total
+    return jnp.where(jnp.abs(offset) <= width, values, 0.0).astype(jnp.bfloat16)
+
+
 def band_table(length, width, sigma):
     spread = (jnp.arange(2 * width + 1) - width).astype(jnp.float32)
     curve = jnp.exp(-spread * spread / (2.0 * sigma * sigma))
@@ -187,6 +196,50 @@
         ),
         cost_estimate=pl.CostEstimate(flops=flops, bytes_accessed=moved, transcendentals=0),
     )(coeffs, blocks, padded)
+
+
+def strip_body(coef_ref, st_ref, blk_ref, padded_ref, out_ref):
+    e = pl.program_id(0)
+    tile_len = out_ref.shape[2]
+    image = padded_ref[0]
+    total = None
+    for kernel in range(len(SIGMA_PARTS)):
+        block = blk_ref[kernel]
+        across = jnp.dot(st_ref[0, kernel], image, preferred_element_type=jnp.float32)
+        across = across.astype(jnp.bfloat16)
+        cols = [
+            lax.dot_general(
+                across[:, start:start + 2 * BLOCK], block, (((1,), (1,)), ((), ())),
+                preferred_element_type=jnp.float32,
+            )
+            for start in range(0, tile_len, BLOCK)
+        ]
+        term = coef_ref[e, kernel] * jnp.concatenate(cols, 1)
+        total = term if total is None else total + term
+    out_ref[0] = total
+
+
+def strip_tiles(coeffs, strip_tables, blocks, padded, tile_len):
+    exp_dev, wide = padded.shape[0], padded.shape[1]
+    nk, rows = strip_tables.shape[1], strip_tables.shape[2]
+    flops = exp_dev * nk * 2 * rows * (wide * wide + 2 * BLOCK * tile_len)
+    moved = exp_dev * wide * wide * 2 + exp_dev * rows * tile_len * 4
+    return pl.pallas_call(
+        strip_body,
+        grid=(exp_dev,),
+        in_specs=[
+            pl.BlockSpec(memory_space=pltpu.SMEM),
+            pl.BlockSpec((1, nk, rows, wide), lambda e: (e, 0, 0, 0)),
+            pl.BlockSpec((nk, BLOCK, 2 * BLOCK), lambda e: (0, 0, 0)),
+            pl.BlockSpec((1, wide, wide), lambda e: (e, 0, 0)),
+        ],
+        out_specs=pl.BlockSpec((1, rows, tile_len), lambda e: (e, 0, 0)),
+        out_shape=jax.ShapeDtypeStruct((exp_dev, rows, tile_len), jnp.float32),
+        compiler_params=pltpu.CompilerParams(
+            dimension_semantics=("arbitrary",), vmem_limit_bytes=48 * 1024 * 1024
+        ),
+        cost_estimate=pl.CostEstimate(flops=flops, bytes_accessed=moved, transcendentals=0),
+    )(coeffs, strip_tables, blocks, padded)
 
 
 def warp_body(idx_ref, plane_ref, xrow_ref, ycol_ref, matched_ref, rmap_ref, cmap_ref, out_ref):
@@ -298,14 +351,25 @@
     )
     own_patch = jnp.take(picked_all, visit_pos, axis=2).astype(jnp.float32)
     denominator = jnp.sum(own_patch).reshape(1)
-    stacked_tables = jnp.stack([band_table(tile_len, HALO, HALO * part) for part in SIGMA_PARTS])
-    strip_tables = jnp.einsum(
-        "esr,krj->eksj", pick_rows, stacked_tables, preferred_element_type=jnp.float32
-    ).astype(jnp.bfloat16)
-    nearby = conv_tiles(coeffs, strip_tables, stacked_tables, padded, True)
-    spare = 2 * BLOCK + tile_len - BLOCK - padded.shape[1]
+    spare = 2 * BLOCK + tile_len - BLOCK - (tile_len + 2 * HALO)
     roomy = jnp.pad(padded, ((0, 0), (0, spare), (0, spare)))
-    blocks = stacked_tables[:, :BLOCK, : 2 * BLOCK]
+    wide = roomy.shape[1]
+    block_offset = (
+        lax.broadcasted_iota(jnp.int32, (BLOCK, 2 * BLOCK), 1)
+        - lax.broadcasted_iota(jnp.int32, (BLOCK, 2 * BLOCK), 0)
+        - HALO
+    )
+    blocks = jnp.stack([band_values(block_offset, HALO, HALO * part) for part in SIGMA_PARTS])
+    strip_offset = (
+        lax.broadcasted_iota(jnp.int32, (exp_dev, STRIP, wide), 2)
+        - lax.broadcasted_iota(jnp.int32, (exp_dev, STRIP, wide), 1)
+        - offset[:, None, None]
+        - HALO
+    )
+    strip_tables = jnp.stack(
+        [band_values(strip_offset, HALO, HALO * part) for part in SIGMA_PARTS], 1
+    )
+    nearby = strip_tiles(coeffs, strip_tables, blocks, roomy, tile_len)
     matched = band_tiles(coeffs, blocks, roomy, tile_len)
     difference = nearby - theirs
     pixel_weight = 1.0 / (1.0 + theirs * theirs)

time: 135 us -> 144 us (1.067)
  other arithmetic: 22.9 us -> 32.3 us
  waiting for transfers between devices: 41.3 us -> 42.8 us
    another operation x3, local copies, waits for them, and re-layouts: 0.28 us -> 3.92 us  [shards(): jnp.stack([jnp.sum(pixel_weight * difference, axis=(1, 2)), jnp.sum(weigh...]
    concatenate x1, other arithmetic: 2.92 us -> 6.28 us  [extended(): value = jnp.concatenate([before, value, after], axis=dim)]
    unnamed x35 -> x37, local copies, waits for them, and re-layouts: 4.08 us -> 1.45 us
    reduce_scatter x1, waiting for transfers between devices: 39 us -> 40.5 us  [shards(): lax.psum_scatter(partial_sum.astype(jnp.bfloat16), 'visit', scatter_dimen...]
    convert_element_type x2 -> x3, other arithmetic: 3.41 us -> 4.45 us  [band_values(): return jnp.where(jnp.abs(offset) <= width, values, 0.0).astype(jnp.bfloat16)]
  transfers between devices with their start and end apart: 10 -> 10, of which waited for: 3 -> 4; matrix products, arithmetic and copies ran while one was open for 17% -> 14% of each run, Pallas kernels for 10% -> 9%
where the time goes in v8:
time: 144 us; the launch traced here: 143 us
  waiting for transfers between devices  42.8 us (30%)
  other arithmetic  32.3 us (22%)
  Pallas kernels  18.9 us (13%)
  starting transfers between devices  17.4 us (12%)
  between operations  14.5 us (10%)
  local copies, waits for them, and re-layouts  13 us (9%)
  matrix products  4.49 us (3%)
    reduce_scatter x1, waiting for transfers between devices, shards(): lax.psum_scatter(partial_sum.astype(jnp.bfloat16), 'visit', scatter_dimen...  40.5 us
    pallas_call x1, Pallas kernels, band_tiles(): pl.pallas_call(band_body, grid=(exp_dev,), in_specs=[pl.BlockSpec(memory_...  8.17 us
    ppermute x3, starting transfers between devices, shards(): received.append(lax.ppermute(payload, 'visit', pairs))  7.86 us
    pallas_call x1, Pallas kernels, warp_tiles(): pl.pallas_call(warp_body, grid_spec=grid_spec, out_shape=jax.ShapeDtypeSt...  6.34 us
    concatenate x1, other arithmetic, extended(): value = jnp.concatenate([before, value, after], axis=dim)  6.28 us
    ppermute x1, starting transfers between devices, extended(): before = lax.ppermute(last, axis, up)  4.55 us
    convert_element_type x3, other arithmetic, band_values(): return jnp.where(jnp.abs(offset) <= width, values, 0.0).astype(jnp.bfloat16)  4.45 us
    pallas_call x1, Pallas kernels, strip_tiles(): pl.pallas_call(strip_body, grid=(exp_dev,), in_specs=[pl.BlockSpec(memory...  4.37 us
  transfers between devices with their start and end apart: 10, of which 4 were waited for; matrix products, arithmetic and copies ran while one was open for 14% of the time, Pallas kernels for 9%

profile of v8, /device:TPU:0, one launch (start us, length us, event | category | flops | bytes accessed | tf_op | source)
XLA Modules:
  0.0 143.3 jit_solution(13660713817424957024)
XLA Ops:
  10.7 2.1 %convolution_convert_fusion = bf16[4,32,512]{2,1,0:T(8,128)(2,1)S(1)} fusion(bf16[4,512,512]{2,1,0:T(8,128)(2,1)} %param.10, s32[4]{0:T(128)S(1)} %get-tuple-element.39), kind=kOutput, calls=%fused_computation.20 | convolution fusion | flops 67305472 | bytes 2228240 | tf_op jit(solution)/shard_map/esr,erl->esl/dot_general | solution.py:318
  13.6 4.0 %collective-permute-start.1 = (bf16[144,512]{1,0:T(8,128)(2,1)}, bf16[144,512]{1,0:T(8,128)(2,1)}, u32[]{:S(2)}, u32[]{:S(2)}) collective-permute-start(bf16[144,512]{1,0:T(8,128)(2,1)} %get-tuple-element.46), channel_id=1, source_target_pairs={{0,16},{8,24},{16,0},{24,8},{1,17},{9,25},{17,1},{25,9},{2,18},{10... | collective-permute-start | bytes 442376 | tf_op jit(solution)/shard_map/ppermute | solution.py:338
  17.6 1.6 %collective-permute-start = (bf16[144,512]{1,0:T(8,128)(2,1)}, bf16[144,512]{1,0:T(8,128)(2,1)}, u32[]{:S(2)}, u32[]{:S(2)}) collective-permute-start(bf16[144,512]{1,0:T(8,128)(2,1)} %get-tuple-element.46), channel_id=1, source_target_pairs={{0,8},{8,16},{16,24},{24,0},{1,9},{9,17},{17,25},{25,1},{2,10},{10... | collective-permute-start | bytes 442376 | tf_op jit(solution)/shard_map/ppermute | solution.py:338
  19.2 2.2 %collective-permute-start.2 = (bf16[144,512]{1,0:T(8,128)(2,1)}, bf16[144,512]{1,0:T(8,128)(2,1)}, u32[]{:S(2)}, u32[]{:S(2)}) collective-permute-start(bf16[144,512]{1,0:T(8,128)(2,1)} %get-tuple-element.46), channel_id=1, source_target_pairs={{0,24},{8,0},{16,8},{24,16},{1,25},{9,1},{17,9},{25,17},{2,26},{10... | collective-permute-start | bytes 442376 | tf_op jit(solution)/shard_map/ppermute | solution.py:338
  21.9 1.3 collective-permute-start.4
  23.5 4.5 %collective-permute-start.3 = (bf16[4,8192]{1,0:T(4,128)(2,1)S(1)}, bf16[4,8192]{1,0:T(4,128)(2,1)S(1)}, u32[]{:S(2)}, u32[]{:S(2)}) collective-permute-start(bf16[4,8192]{1,0:T(4,128)(2,1)S(1)} %bitcast.86), channel_id=1, source_target_pairs={{0,1},{1,2},{2,3},{4,5},{5,6},{6,7},{8,9},{9,10},{10,11},{12,13},{... | collective-permute-start | bytes 196616 | tf_op jit(solution)/shard_map/ppermute | solution.py:37
  30.8 1.4 select_convert_fusion.3
  32.2 2.3 %select_convert_fusion.2 = (bf16[4,1,32,640]{3,2,1,0:T(8,128)(2,1)S(1)}, bf16[4,1,32,640]{3,2,1,0:T(8,128)(2,1)S(1)}, bf16[4,1,32,640]{3,2,1,0:T(8,128)(2,1)S(1)}) fusion(f32[]{:T(128)} %exponential_reduce_fusion.2, s32[4]{0:T(128)S(1)} %get-tuple-element.39, f32[]{:T(128)} %exponential_reduce_fusion, f32[]{:T(128)} %exponential_reduce_fusion.1), kind=kLoop, calls=%fused_computation.31 | loop fusion | flops 1638400 | bytes 491548 | tf_op jit(solution)/shard_map/convert_element_type | solution.py:52
  39.1 6.3 %fusion.8.padded_ref = bf16[4,640,640]{2,1,0:T(8,128)(2,1)S(1)} fusion(bf16[4,16,544]{2,1,0:T(8,128)(2,1)S(1)} %get-tuple-element.48, bf16[4,16,544]{2,1,0:T(8,128)(2,1)S(1)} %get-tuple-element.47, bf16[4,512,16]{2,1,0:T(8,128)(2,1)} %bitcast.76, bf16[4,512,512]{2,1,0:T(8,128)(2,1)S(1)} %copy-done.6, bf16[4,512,16]{2,1,0:T(8,128)(2,1)} %bitcast.74), kind=kLoop, calls=%fused_computation.10 | loop fusion | flops 37683200 | bytes 5644288 | tf_op jit(solution)/shard_map/concatenate | solution.py:42
  45.5 4.4 %shard_map.95 = f32[4,32,512]{2,1,0:T(8,128)S(1)} custom-call(f32[4,3]{1,0:T(4,128)S(1)} %copy-done.4, bf16[4,3,32,640]{3,2,1,0:T(8,128)(2,1)S(1)} %copy-done, bf16[3,128,256]{2,1,0:T(8,128)(2,1)S(1)} %copy-done.1, bf16[4,640,640]{2,1,0:T(8,128)(2,1)S(1)} %fusion.8.padded_ref), custom_call_target="tpu_custom_call" | custom-call | flops 415236096 | bytes 3538944 | tf_op jit(solution)/shard_map/pallas_call | solution.py:227
  49.9 1.1 pad_maximum_fusion
  52.5 1.3 copy.142
  53.8 1.3 copy.141
  55.1 1.3 copy.143
  56.4 1.3 pad_maximum_fusion.7
  57.7 1.3 copy.132
  63.9 2.4 %collective-permute-start.7 = (f32[4,12]{1,0:T(4,128)S(1)}, f32[4,12]{1,0:T(4,128)}, u32[]{:S(2)}, u32[]{:S(2)}) collective-permute-start(f32[4,12]{1,0:T(4,128)S(1)} %fusion.38), channel_id=1, source_target_pairs={{0,1},{1,0},{2,3},{3,2},{4,5},{5,4},{6,7},{7,6},{8,9},{9,8},{10,11... | collective-permute-start | bytes 584 | tf_op jit(solution)/shard_map/ppermute | solution.py:91
  68.6 1.1 collective-permute-start.8
  70.7 8.2 %shard_map.96.matched_ref = f32[4,512,512]{2,1,0:T(8,128)} custom-call(f32[4,3]{1,0:T(4,128)S(1)} %copy-done.4, bf16[3,128,256]{2,1,0:T(8,128)(2,1)S(1)} %copy-done.2, bf16[4,640,640]{2,1,0:T(8,128)(2,1)S(1)} %fusion.8.padded_ref), custom_call_target="tpu_custom_call" | custom-call | flops 3623878656 | bytes 7471104 | tf_op jit(solution)/shard_map/pallas_call | solution.py:184
  81.4 6.3 %shard_map.97 = bf16[4,512,512]{2,1,0:T(8,128)(2,1)S(1)} custom-call(s32[4,2]{1,0:T(4,128)S(1)} %copy.157.idx_ref, f32[4,3]{1,0:T(4,128)S(1)} %pad_maximum_fusion.11.plane_ref, f32[1,512]{1,0:T(1,128)S(1)} %multiply_add_fusion.1.xrow_ref, f32[512,1]{1,0:T(8,128)S(1)} %multiply_add_fusion.ycol_ref, f32[4,512,512]{2,1,0:T(8,128)} %shard_map.96.matched_ref, ...), custom_call_target="tpu_custom_call" | custom-call | flops 2147483648 | bytes 10485760 | tf_op jit(solution)/shard_map/pallas_call | solution.py:276
  87.7 2.0 %fusion.17 = bf16[4,512,512]{2,0,1:T(4,128)(2,1)S(1)} fusion(bf16[4,512,512]{2,1,0:T(8,128)(2,1)S(1)} %shard_map.97, pred[4,4]{1,0:T(4,128)(4,1)S(1)} %copy-done.12, bf16[4]{0:T(256)(128)(2,1)S(1)} %bitcast.110), kind=kOutput, calls=%fused_computation.19 | convolution fusion | flops 9437200 | bytes 4194328 | tf_op jit(solution)/shard_map/ev,eij->vij/dot_general | solution.py:415
  89.7 1.8 %copy.160 = bf16[4,512,512]{2,1,0:T(8,128)(2,1)} copy(bf16[4,512,512]{2,0,1:T(4,128)(2,1)S(1)} %fusion.17) | data formatting | bytes 4194304 | tf_op jit(solution)/shard_map/convert_element_type | solution.py:417
  93.1 40.5 %reduce-scatter.2.cloned.1.call-done = bf16[1,512,512]{2,1,0:T(8,128)(2,1)} async-done(((bf16[4,512,512]{2,1,0:T(8,128)(2,1)}), bf16[1,512,512]{2,1,0:T(8,128)(2,1)}) %reduce-scatter.2.cloned.1.call-update) | async-done | bytes 524304 | tf_op jit(solution)/shard_map/reduce_scatter | solution.py:416
  133.7 2.8 %convert_divide_fusion = f32[1,512,512]{2,1,0:T(8,128)} fusion(bf16[1,512,512]{2,1,0:T(8,128)(2,1)} %reduce-scatter.2.cloned.1.call-done, f32[]{:T(128)} %convert_reduce_fusion), kind=kLoop, calls=%fused_computation.21 | loop fusion | flops 524288 | bytes 1572868 | tf_op jit(solution)/shard_map/div | solution.py:419
  (108 shorter events, 25.9 us)
Async XLA Ops:
  7.2 14.3 %copy-start.5 = (bf16[4,512,512]{2,1,0:T(8,128)(2,1)S(1)}, bf16[4,512,512]{2,1,0:T(8,128)(2,1)}, u32[]{:S(2)}) copy-start(bf16[4,512,512]{2,1,0:T(8,128)(2,1)} %param.10) | copy-start | bytes 6291460
  7.2 126.5 %reduce-scatter.2.cloned.1.call-start = ((), (), s32[]{:S(2)}) async-start(), calls=%async_computation.1 | async-start | bytes 2621440 | tf_op jit(solution)/shard_map/reduce_scatter | solution.py:416
  8.9 1.6 %copy-start.11 = (pred[4,4]{1,0:T(4,128)(4,1)}, pred[4,4]{1,0:T(4,128)(4,1)S(1)}, u32[]{:S(2)}) copy-start(pred[4,4]{1,0:T(4,128)(4,1)S(1)} %fusion.26) | copy-start | bytes 52
  13.6 36.3 %collective-permute-start.1 = (bf16[144,512]{1,0:T(8,128)(2,1)}, bf16[144,512]{1,0:T(8,128)(2,1)}, u32[]{:S(2)}, u32[]{:S(2)}) collective-permute-start(bf16[144,512]{1,0:T(8,128)(2,1)} %get-tuple-element.46), channel_id=1, source_target_pairs={{0,16},{8,24},{16,0},{24,8},{1,17},{9,25},{17,1},{25,9},{2,18},{10... | collective-permute-start | bytes 442376 | tf_op jit(solution)/shard_map/ppermute | solution.py:338
  17.6 32.3 %collective-permute-start = (bf16[144,512]{1,0:T(8,128)(2,1)}, bf16[144,512]{1,0:T(8,128)(2,1)}, u32[]{:S(2)}, u32[]{:S(2)}) collective-permute-start(bf16[144,512]{1,0:T(8,128)(2,1)} %get-tuple-element.46), channel_id=1, source_target_pairs={{0,8},{8,16},{16,24},{24,0},{1,9},{9,17},{17,25},{25,1},{2,10},{10... | collective-permute-start | bytes 442376 | tf_op jit(solution)/shard_map/ppermute | solution.py:338
  19.2 30.7 %collective-permute-start.2 = (bf16[144,512]{1,0:T(8,128)(2,1)}, bf16[144,512]{1,0:T(8,128)(2,1)}, u32[]{:S(2)}, u32[]{:S(2)}) collective-permute-start(bf16[144,512]{1,0:T(8,128)(2,1)} %get-tuple-element.46), channel_id=1, source_target_pairs={{0,24},{8,0},{16,8},{24,16},{1,25},{9,1},{17,9},{25,17},{2,26},{10... | collective-permute-start | bytes 442376 | tf_op jit(solution)/shard_map/ppermute | solution.py:338
  21.9 14.8 %collective-permute-start.4 = (bf16[4,8192]{1,0:T(4,128)(2,1)S(1)}, bf16[4,8192]{1,0:T(4,128)(2,1)S(1)}, u32[]{:S(2)}, u32[]{:S(2)}) collective-permute-start(bf16[4,8192]{1,0:T(4,128)(2,1)S(1)} %bitcast.84), channel_id=1, source_target_pairs={{1,0},{2,1},{3,2},{5,4},{6,5},{7,6},{9,8},{10,9},{11,10},{13,12},{... | collective-permute-start | bytes 196616 | tf_op jit(solution)/shard_map/ppermute | solution.py:38
  23.5 13.2 %collective-permute-start.3 = (bf16[4,8192]{1,0:T(4,128)(2,1)S(1)}, bf16[4,8192]{1,0:T(4,128)(2,1)S(1)}, u32[]{:S(2)}, u32[]{:S(2)}) collective-permute-start(bf16[4,8192]{1,0:T(4,128)(2,1)S(1)} %bitcast.86), channel_id=1, source_target_pairs={{0,1},{1,2},{2,3},{4,5},{5,6},{6,7},{8,9},{9,10},{10,11},{12,13},{... | collective-permute-start | bytes 196616 | tf_op jit(solution)/shard_map/ppermute | solution.py:37
  37.0 1.8 %copy-start.7 = (bf16[4,16,512]{1,2,0:T(8,128)(2,1)}, bf16[4,16,512]{1,2,0:T(8,128)(2,1)S(1)}, u32[]{:S(2)}) copy-start(bf16[4,16,512]{1,2,0:T(8,128)(2,1)S(1)} %copy.137) | copy-start | bytes 196612
  37.3 1.8 %copy-start.6 = (bf16[4,512,512]{2,1,0:T(8,128)(2,1)S(1)}, bf16[4,512,512]{2,1,0:T(8,128)(2,1)}, u32[]{:S(2)}) copy-start(bf16[4,512,512]{2,1,0:T(8,128)(2,1)} %param.10) | copy-start | bytes 6291460
  37.5 1.3 collective-permute-start.5
  39.1 6.3 %copy-start = (bf16[4,3,32,640]{3,2,1,0:T(8,128)(2,1)S(1)}, bf16[4,3,32,640]{3,2,1,0:T(8,128)(2,1)}, u32[]{:S(2)}) copy-start(bf16[4,3,32,640]{3,2,1,0:T(8,128)(2,1)} %pad_maximum_fusion.1.st_ref) | copy-start | bytes 1474564
  39.1 6.3 %copy-start.1 = (bf16[3,128,256]{2,1,0:T(8,128)(2,1)S(1)}, bf16[3,128,256]{2,1,0:T(8,128)(2,1)}, u32[]{:S(2)}) copy-start(bf16[3,128,256]{2,1,0:T(8,128)(2,1)} %pad_maximum_fusion.2.blk_ref) | copy-start | bytes 589828
  39.1 6.3 %copy-start.4 = (f32[4,3]{1,0:T(4,128)S(1)}, f32[4,3]{1,0:T(4,128)}, u32[]{:S(2)}) copy-start(f32[4,3]{1,0:T(4,128)} %coef_ref.3) | copy-start | bytes 148
  45.5 4.4 %copy-start.9 = (bf16[1,144,512]{2,1,0:T(8,128)(2,1)S(1)}, bf16[1,144,512]{2,1,0:T(8,128)(2,1)}, u32[]{:S(2)}) copy-start(bf16[1,144,512]{2,1,0:T(8,128)(2,1)} %get-tuple-element.45) | copy-start | bytes 442372
  45.5 5.6 %copy-start.15 = (s32[4]{0:T(128)S(1)}, s32[4]{0:T(128)}, u32[]{:S(2)}) copy-start(s32[4]{0:T(128)} %fusion.33) | copy-start | bytes 52
  61.9 1.2 collective-permute-start.6
  63.9 4.1 %collective-permute-start.7 = (f32[4,12]{1,0:T(4,128)S(1)}, f32[4,12]{1,0:T(4,128)}, u32[]{:S(2)}, u32[]{:S(2)}) collective-permute-start(f32[4,12]{1,0:T(4,128)S(1)} %fusion.38), channel_id=1, source_target_pairs={{0,1},{1,0},{2,3},{3,2},{4,5},{5,4},{6,7},{7,6},{8,9},{9,8},{10,11... | collective-permute-start | bytes 584 | tf_op jit(solution)/shard_map/ppermute | solution.py:91
  68.6 10.3 %collective-permute-start.8 = (f32[4,12]{1,0:T(4,128)S(1)}, f32[4,12]{1,0:T(4,128)S(1)}, u32[]{:S(2)}, u32[]{:S(2)}) collective-permute-start(f32[4,12]{1,0:T(4,128)S(1)} %add.260), channel_id=1, source_target_pairs={{0,2},{1,3},{2,0},{3,1},{4,6},{5,7},{6,4},{7,5},{8,10},{9,11},{10,... | collective-permute-start | bytes 584 | tf_op jit(solution)/shard_map/ppermute | solution.py:91
  70.7 10.3 %copy-start.13 = (pred[3,3]{1,0:T(4,128)(4,1)S(1)}, pred[3,3]{1,0:T(4,128)(4,1)}, u32[]{:S(2)}) copy-start(pred[3,3]{1,0:T(4,128)(4,1)} %iota_compare_fusion.4) | copy-start | bytes 31
  81.3 6.4 %copy-start.3 = (f32[4,3]{1,0:T(4,128)}, f32[4,3]{1,0:T(4,128)S(1)}, u32[]{:S(2)}) copy-start(f32[4,3]{1,0:T(4,128)S(1)} %pad_maximum_fusion.11.plane_ref) | copy-start | bytes 148
  81.3 6.4 %copy-start.12 = (pred[4,4]{1,0:T(4,128)(4,1)S(1)}, pred[4,4]{1,0:T(4,128)(4,1)}, u32[]{:S(2)}) copy-start(pred[4,4]{1,0:T(4,128)(4,1)} %copy-done.11) | copy-start | bytes 52
  81.4 6.4 %copy-start.14 = (bf16[4,1,1]{0,2,1:T(2,128)(2,1)S(1)}, bf16[4,1,1]{0,2,1:T(2,128)(2,1)}, u32[]{:S(2)}) copy-start(bf16[4,1,1]{0,2,1:T(2,128)(2,1)} %param.13) | copy-start | bytes 28
  89.7 1.8 %copy-start.10 = (bf16[1,144,512]{2,1,0:T(8,128)(2,1)S(1)}, bf16[1,144,512]{2,1,0:T(8,128)(2,1)}, u32[]{:S(2)}) copy-start(bf16[1,144,512]{2,1,0:T(8,128)(2,1)} %get-tuple-element.45) | copy-start | bytes 442372
  (2 other events, 2.5 us)
Sparse Core Ops, SparseCore 0:
  91.6 41.9 reduce-scatter.1

commit v9 on v7

--- a/solution.py
+++ b/solution.py
@@ -189,7 +189,8 @@
     )(coeffs, blocks, padded)
 
 
-def warp_body(idx_ref, plane_ref, xrow_ref, ycol_ref, matched_ref, rmap_ref, cmap_ref, out_ref):
+def warp_body(idx_ref, plane_ref, pick_ref, xrow_ref, ycol_ref, matched_ref, rmap_ref, cmap_ref,
+              out_ref, acc_ref):
     e = pl.program_id(0)
     background = (
         plane_ref[e, 0] + plane_ref[e, 1] * xrow_ref[...]
@@ -200,15 +201,32 @@
         halfway.astype(jnp.bfloat16), cmap_ref[0], (((1,), (1,)), ((), ())),
         preferred_element_type=jnp.float32,
     )
-    out_ref[0] = warped.astype(jnp.bfloat16)
-
-
-def warp_tiles(choose, plane, xrow, ycol, matched, bank):
+    warped = warped.astype(jnp.bfloat16).astype(jnp.float32)
+    patches = acc_ref.shape[0]
+
+    @pl.when(e == 0)
+    def _():
+        for v in range(patches):
+            acc_ref[v] = pick_ref[e, v] * warped
+
+    @pl.when(e > 0)
+    def _():
+        for v in range(patches):
+            acc_ref[v] = acc_ref[v] + pick_ref[e, v] * warped
+
+    @pl.when(e == pl.num_programs(0) - 1)
+    def _():
+        out_ref[...] = acc_ref[...].astype(jnp.bfloat16)
+
+
+def warp_tiles(choose, plane, picked, xrow, ycol, matched, bank):
     exp_dev, tile_len = matched.shape[0], matched.shape[1]
+    patches = picked.shape[1]
     grid_spec = pltpu.PrefetchScalarGridSpec(
         num_scalar_prefetch=1,
         grid=(exp_dev,),
         in_specs=[
+            pl.BlockSpec(memory_space=pltpu.SMEM),
             pl.BlockSpec(memory_space=pltpu.SMEM),
             pl.BlockSpec((1, tile_len), lambda e, idx: (0, 0)),
             pl.BlockSpec((tile_len, 1), lambda e, idx: (0, 0)),
@@ -216,19 +234,21 @@
             pl.BlockSpec((1, tile_len, tile_len), lambda e, idx: (idx[e, 0], 0, 0)),
             pl.BlockSpec((1, tile_len, tile_len), lambda e, idx: (idx[e, 1], 0, 0)),
         ],
-        out_specs=pl.BlockSpec((1, tile_len, tile_len), lambda e, idx: (e, 0, 0)),
+        out_specs=pl.BlockSpec((patches, tile_len, tile_len), lambda e, idx: (0, 0, 0)),
+        scratch_shapes=[pltpu.VMEM((patches, tile_len, tile_len), jnp.float32)],
     )
     flops = exp_dev * 4 * tile_len ** 3
-    moved = exp_dev * tile_len * tile_len * (4 + 2 + 2 + 2)
+    moved = exp_dev * tile_len * tile_len * (4 + 2 + 2) + patches * tile_len * tile_len * 2
+    vmem = min(60 * 1024 * 1024, (16 + 3 * patches) * 1024 * 1024)
     return pl.pallas_call(
         warp_body,
         grid_spec=grid_spec,
-        out_shape=jax.ShapeDtypeStruct(matched.shape, jnp.bfloat16),
+        out_shape=jax.ShapeDtypeStruct((patches, tile_len, tile_len), jnp.bfloat16),
         compiler_params=pltpu.CompilerParams(
-            dimension_semantics=("arbitrary",), vmem_limit_bytes=48 * 1024 * 1024
+            dimension_semantics=("arbitrary",), vmem_limit_bytes=vmem
         ),
         cost_estimate=pl.CostEstimate(flops=flops, bytes_accessed=moved, transcendentals=0),
-    )(choose, plane, xrow, ycol, matched, bank, bank)
+    )(choose, plane, picked, xrow, ycol, matched, bank, bank)
 
 
 def rows_from(source, anchor):
@@ -344,13 +364,12 @@
     plane_fit = solve_three(normal, moments)
     row_coord = centred(row_pos * tile_len + jnp.arange(tile_len, dtype=jnp.int32), height)
     choose = warp_index[:, 0, 0, :]
-    warped = warp_tiles(
-        choose, plane_fit, xcoord.reshape(1, tile_len), row_coord.reshape(tile_len, 1),
-        matched, resample_bank,
-    )
-    partial_sum = jnp.einsum("ev,eij->vij", picked, warped, preferred_element_type=jnp.float32)
+    partial_sum = warp_tiles(
+        choose, plane_fit, picked.astype(jnp.float32), xcoord.reshape(1, tile_len),
+        row_coord.reshape(tile_len, 1), matched, resample_bank,
+    )
     numerator = lax.psum_scatter(
-        partial_sum.astype(jnp.bfloat16), "visit", scatter_dimension=0, tiled=True
+        partial_sum, "visit", scatter_dimension=0, tiled=True
     ).astype(jnp.float32)
     coadd_patch = numerator / denominator[:, None, None]
     return (coadd_patch, plane_fit)

time: 135 us -> 136 us (level)
  matrix products: 4.99 us -> 2.98 us
  local copies, waits for them, and re-layouts: 12.7 us -> 14.2 us
    unnamed x35, local copies, waits for them, and re-layouts: 4.08 us -> 9.06 us
    dot_general x1 -> x0, matrix products: 2 us -> none  [shards(): jnp.einsum('ev,eij->vij', picked, warped, preferred_element_type=jnp.floa...]
    convert_element_type x1 -> x0, local copies, waits for them, and re-layouts: 1.76 us -> none  [shards(): partial_sum.astype(jnp.bfloat16)]
  transfers between devices with their start and end apart: 10 -> 10, of which waited for: 3 -> 3; matrix products, arithmetic and copies ran while one was open for 17% -> 16% of each run, Pallas kernels for 10% -> 10%
where the time goes in v9:
time: 136 us; the launch traced here: 135 us
  waiting for transfers between devices  41.2 us (30%)
  other arithmetic  23.6 us (17%)
  Pallas kernels  20.8 us (15%)
  starting transfers between devices  17.9 us (13%)
  between operations  14.4 us (11%)
  local copies, waits for them, and re-layouts  14.2 us (10%)
  matrix products  2.98 us (2%)
    reduce_scatter x1, waiting for transfers between devices, shards(): lax.psum_scatter(partial_sum, 'visit', scatter_dimension=0, tiled=True)  39 us
    unnamed x35, local copies, waits for them, and re-layouts  9.06 us
    pallas_call x1, Pallas kernels, band_tiles(): pl.pallas_call(band_body, grid=(exp_dev,), in_specs=[pl.BlockSpec(memory_...  8.2 us
    ppermute x3, starting transfers between devices, shards(): received.append(lax.ppermute(payload, 'visit', pairs))  7.86 us
    pallas_call x1, Pallas kernels, warp_tiles(): pl.pallas_call(warp_body, grid_spec=grid_spec, out_shape=jax.ShapeDtypeSt...  7.51 us
    ppermute x1, starting transfers between devices, extended(): before = lax.ppermute(last, axis, up)  5.16 us
    pallas_call x1, Pallas kernels, conv_tiles(): pl.pallas_call(conv_body, grid=(exp_dev,), in_specs=[pl.BlockSpec(memory_...  5.05 us
    ppermute x3, starting transfers between devices, butterfly_sum(): values = jax.tree.map(lambda v: v + lax.ppermute(v, axis, pairs), values)  3.46 us
  transfers between devices with their start and end apart: 10, of which 3 were waited for; matrix products, arithmetic and copies ran while one was open for 16% of the time, Pallas kernels for 10%

profile of v9, /device:TPU:0, one launch (start us, length us, event | category | flops | bytes accessed | tf_op | source)
XLA Modules:
  0.0 135.0 jit_solution(16207564327701819664)
XLA Ops:
  10.7 2.1 %convolution_convert_fusion = bf16[4,32,512]{2,1,0:T(8,128)(2,1)S(1)} fusion(bf16[4,512,512]{2,1,0:T(8,128)(2,1)} %param.10, s32[4]{0:T(128)S(1)} %get-tuple-element.35), kind=kOutput, calls=%fused_computation.12 | convolution fusion | flops 67305472 | bytes 2228240 | tf_op jit(solution)/shard_map/esr,erl->esl/dot_general | solution.py:285
  13.5 4.0 %collective-permute-start.1 = (bf16[144,512]{1,0:T(8,128)(2,1)}, bf16[144,512]{1,0:T(8,128)(2,1)}, u32[]{:S(2)}, u32[]{:S(2)}) collective-permute-start(bf16[144,512]{1,0:T(8,128)(2,1)} %get-tuple-element.42), channel_id=1, source_target_pairs={{0,16},{8,24},{16,0},{24,8},{1,17},{9,25},{17,1},{25,9},{2,18},{10... | collective-permute-start | bytes 442376 | tf_op jit(solution)/shard_map/ppermute | solution.py:305
  17.6 1.6 %collective-permute-start = (bf16[144,512]{1,0:T(8,128)(2,1)}, bf16[144,512]{1,0:T(8,128)(2,1)}, u32[]{:S(2)}, u32[]{:S(2)}) collective-permute-start(bf16[144,512]{1,0:T(8,128)(2,1)} %get-tuple-element.42), channel_id=1, source_target_pairs={{0,8},{8,16},{16,24},{24,0},{1,9},{9,17},{17,25},{25,1},{2,10},{10... | collective-permute-start | bytes 442376 | tf_op jit(solution)/shard_map/ppermute | solution.py:305
  19.2 2.2 %collective-permute-start.2 = (bf16[144,512]{1,0:T(8,128)(2,1)}, bf16[144,512]{1,0:T(8,128)(2,1)}, u32[]{:S(2)}, u32[]{:S(2)}) collective-permute-start(bf16[144,512]{1,0:T(8,128)(2,1)} %get-tuple-element.42), channel_id=1, source_target_pairs={{0,24},{8,0},{16,8},{24,16},{1,25},{9,1},{17,9},{25,17},{2,26},{10... | collective-permute-start | bytes 442376 | tf_op jit(solution)/shard_map/ppermute | solution.py:305
  22.5 1.3 collective-permute-start.4
  24.7 5.2 %collective-permute-start.3 = (bf16[4,8192]{1,0:T(4,128)(2,1)}, bf16[4,8192]{1,0:T(4,128)(2,1)}, u32[]{:S(2)}, u32[]{:S(2)}) collective-permute-start(bf16[4,8192]{1,0:T(4,128)(2,1)} %bitcast.48), channel_id=1, source_target_pairs={{0,1},{1,2},{2,3},{4,5},{5,6},{6,7},{8,9},{9,10},{10,11},{12,13},{... | collective-permute-start | bytes 196616 | tf_op jit(solution)/shard_map/ppermute | solution.py:37
  31.8 1.3 select_convert_fusion.2
  33.1 2.1 %select_convert_fusion = (bf16[1,512,544]{2,1,0:T(8,128)(2,1)S(1)}, bf16[1,512,544]{2,1,0:T(8,128)(2,1)S(1)}) fusion(f32[]{:T(128)} %exponential_reduce_fusion, f32[]{:T(128)} %exponential_reduce_fusion.1), kind=kLoop, calls=%fused_computation.5 | loop fusion | flops 4177920 | bytes 1114120 | tf_op jit(solution)/shard_map/convert_element_type | solution.py:54
  35.8 1.6 %pad_maximum_fusion.1.ht_ref = bf16[3,512,544]{2,1,0:T(8,128)(2,1)} fusion(bf16[1,512,544]{2,1,0:T(8,128)(2,1)S(1)} %get-tuple-element.59, bf16[1,512,544]{2,1,0:T(8,128)(2,1)S(1)} %get-tuple-element.60, bf16[1,512,544]{2,1,0:T(8,128)(2,1)S(1)} %select_convert_fusion.2), kind=kLoop, calls=%fused_computation.1 | loop fusion | flops 1671168 | bytes 3342336 | tf_op jit(solution)/shard_map/stack | solution.py:321
  40.7 1.0 copy.107
  41.7 1.0 fusion.14
  44.1 2.9 %pad_maximum_fusion.padded_ref = bf16[4,544,544]{2,1,0:T(8,128)(2,1)S(1)} fusion(bf16[4,16,544]{2,1,0:T(8,128)(2,1)S(1)} %get-tuple-element.44, bf16[4,512,16]{2,1,0:T(8,128)(2,1)S(1)} %bitcast.87, bf16[4,512,512]{2,1,0:T(8,128)(2,1)S(1)} %copy-done.6, bf16[4,512,16]{2,1,0:T(8,128)(2,1)} %bitcast.85, bf16[4,16,544]{2,1,0:T(8,128)(2,1)S(1)} %get-tuple-element.43), kind=kLoop, calls=%fused_computation | loop fusion | flops 11837440 | bytes 4734976 | tf_op jit(solution)/shard_map/concatenate | solution.py:42
  47.1 5.1 %shard_map.95 = f32[4,32,512]{2,1,0:T(8,128)S(1)} custom-call(f32[4,3]{1,0:T(4,128)S(1)} %copy-done.4, bf16[4,3,32,544]{3,2,1,0:T(8,128)(2,1)S(1)} %fusion.5.vt_ref, bf16[3,512,544]{2,1,0:T(8,128)(2,1)S(1)} %copy-done.1, bf16[4,544,544]{2,1,0:T(8,128)(2,1)S(1)} %pad_maximum_fusion.padded_ref), custom_call_target="tpu_custom_call" | custom-call | flops 441188352 | bytes 2629632 | tf_op jit(solution)/shard_map/pallas_call | solution.py:125
  52.2 1.1 pad_maximum_fusion.2
  56.2 1.8 %collective-permute-start.7 = (f32[4,12]{1,0:T(4,128)S(1)}, f32[4,12]{1,0:T(4,128)S(1)}, u32[]{:S(2)}, u32[]{:S(2)}) collective-permute-start(f32[4,12]{1,0:T(4,128)S(1)} %fusion.29), channel_id=1, source_target_pairs={{0,1},{1,0},{2,3},{3,2},{4,5},{5,4},{6,7},{7,6},{8,9},{9,8},{10,11... | collective-permute-start | bytes 584 | tf_op jit(solution)/shard_map/ppermute | solution.py:82
  58.3 1.4 %collective-permute-done.7 = f32[4,12]{1,0:T(4,128)S(1)} collective-permute-done((f32[4,12]{1,0:T(4,128)S(1)}, f32[4,12]{1,0:T(4,128)S(1)}, u32[]{:S(2)}, u32[]{:S(2)}) %collective-permute-start.7) | collective-permute-done | bytes 224 | tf_op jit(solution)/shard_map/ppermute | solution.py:82
  59.8 1.5 %collective-permute-start.8 = (f32[4,12]{1,0:T(4,128)S(1)}, f32[4,12]{1,0:T(4,128)S(1)}, u32[]{:S(2)}, u32[]{:S(2)}) collective-permute-start(f32[4,12]{1,0:T(4,128)S(1)} %add.244), channel_id=1, source_target_pairs={{0,2},{1,3},{2,0},{3,1},{4,6},{5,7},{6,4},{7,5},{8,10},{9,11},{10,... | collective-permute-start | bytes 584 | tf_op jit(solution)/shard_map/ppermute | solution.py:82
  61.3 8.2 %shard_map.96.matched_ref = f32[4,512,512]{2,1,0:T(8,128)} custom-call(f32[4,3]{1,0:T(4,128)S(1)} %copy-done.4, bf16[3,128,256]{2,1,0:T(8,128)(2,1)S(1)} %slice.127.blk_ref, bf16[4,640,640]{2,1,0:T(8,128)(2,1)S(1)} %pad.7.padded_ref), custom_call_target="tpu_custom_call" | custom-call | flops 3623878656 | bytes 7471104 | tf_op jit(solution)/shard_map/pallas_call | solution.py:175
  69.7 1.1 custom-call.4
  71.3 2.8 %copy-done = bf16[12,512,512]{2,1,0:T(8,128)(2,1)S(1)} copy-done((bf16[12,512,512]{2,1,0:T(8,128)(2,1)S(1)}, bf16[12,512,512]{2,1,0:T(8,128)(2,1)}, u32[]{:S(2)}) %copy-start) | copy-done | bytes 6291480
  74.1 2.2 %copy-done.2 = f32[4,512,512]{2,1,0:T(8,128)S(1)} copy-done((f32[4,512,512]{2,1,0:T(8,128)S(1)}, f32[4,512,512]{2,1,0:T(8,128)}, u32[]{:S(2)}) %copy-start.2) | copy-done | bytes 4194328
  76.3 7.5 %shard_map.97 = bf16[4,512,512]{2,1,0:T(8,128)(2,1)} custom-call(s32[4,2]{1,0:T(4,128)S(1)} %copy.125.idx_ref, f32[4,3]{1,0:T(4,128)S(1)} %pad_maximum_fusion.11.plane_ref, f32[4,4]{1,0:T(4,128)S(1)} %get-tuple-element.54.pick_ref, f32[1,512]{1,0:T(1,128)S(1)} %multiply_add_fusion.1.xrow_ref, f32[512,1]{1,0:T(8,128)S(1)} %multiply_add_fusion.ycol_ref, ...), custom_call_target="tpu_custom_call" | custom-call | flops 2147483648 | bytes 10485760 | tf_op jit(solution)/shard_map/pallas_call | solution.py:243
  86.3 39.0 %reduce-scatter.2.cloned.1.call-done = bf16[1,512,512]{2,1,0:T(8,128)(2,1)} async-done(((bf16[4,512,512]{2,1,0:T(8,128)(2,1)}), bf16[1,512,512]{2,1,0:T(8,128)(2,1)}) %reduce-scatter.2.cloned.1.call-update) | async-done | bytes 524304 | tf_op jit(solution)/shard_map/reduce_scatter | solution.py:371
  125.4 2.8 %convert_divide_fusion = f32[1,512,512]{2,1,0:T(8,128)} fusion(bf16[1,512,512]{2,1,0:T(8,128)(2,1)} %reduce-scatter.2.cloned.1.call-done, f32[]{:T(128)} %convert_reduce_fusion), kind=kLoop, calls=%fused_computation.13 | loop fusion | flops 524288 | bytes 1572868 | tf_op jit(solution)/shard_map/div | solution.py:374
  (105 shorter events, 19.7 us)
Async XLA Ops:
  7.2 14.2 %copy-start.5 = (bf16[4,512,512]{2,1,0:T(8,128)(2,1)S(1)}, bf16[4,512,512]{2,1,0:T(8,128)(2,1)}, u32[]{:S(2)}) copy-start(bf16[4,512,512]{2,1,0:T(8,128)(2,1)} %param.10) | copy-start | bytes 6291460
  7.2 118.2 %reduce-scatter.2.cloned.1.call-start = ((), (), s32[]{:S(2)}) async-start(), calls=%async_computation.1 | async-start | bytes 2621440 | tf_op jit(solution)/shard_map/reduce_scatter | solution.py:371
  13.5 38.6 %collective-permute-start.1 = (bf16[144,512]{1,0:T(8,128)(2,1)}, bf16[144,512]{1,0:T(8,128)(2,1)}, u32[]{:S(2)}, u32[]{:S(2)}) collective-permute-start(bf16[144,512]{1,0:T(8,128)(2,1)} %get-tuple-element.42), channel_id=1, source_target_pairs={{0,16},{8,24},{16,0},{24,8},{1,17},{9,25},{17,1},{25,9},{2,18},{10... | collective-permute-start | bytes 442376 | tf_op jit(solution)/shard_map/ppermute | solution.py:305
  17.6 34.6 %collective-permute-start = (bf16[144,512]{1,0:T(8,128)(2,1)}, bf16[144,512]{1,0:T(8,128)(2,1)}, u32[]{:S(2)}, u32[]{:S(2)}) collective-permute-start(bf16[144,512]{1,0:T(8,128)(2,1)} %get-tuple-element.42), channel_id=1, source_target_pairs={{0,8},{8,16},{16,24},{24,0},{1,9},{9,17},{17,25},{25,1},{2,10},{10... | collective-permute-start | bytes 442376 | tf_op jit(solution)/shard_map/ppermute | solution.py:305
  19.2 33.0 %collective-permute-start.2 = (bf16[144,512]{1,0:T(8,128)(2,1)}, bf16[144,512]{1,0:T(8,128)(2,1)}, u32[]{:S(2)}, u32[]{:S(2)}) collective-permute-start(bf16[144,512]{1,0:T(8,128)(2,1)} %get-tuple-element.42), channel_id=1, source_target_pairs={{0,24},{8,0},{16,8},{24,16},{1,25},{9,1},{17,9},{25,17},{2,26},{10... | collective-permute-start | bytes 442376 | tf_op jit(solution)/shard_map/ppermute | solution.py:305
  22.5 16.1 %collective-permute-start.4 = (bf16[4,8192]{1,0:T(4,128)(2,1)}, bf16[4,8192]{1,0:T(4,128)(2,1)}, u32[]{:S(2)}, u32[]{:S(2)}) collective-permute-start(bf16[4,8192]{1,0:T(4,128)(2,1)} %bitcast.52), channel_id=1, source_target_pairs={{1,0},{2,1},{3,2},{5,4},{6,5},{7,6},{9,8},{10,9},{11,10},{13,12},{... | collective-permute-start | bytes 196616 | tf_op jit(solution)/shard_map/ppermute | solution.py:38
  24.7 14.8 %collective-permute-start.3 = (bf16[4,8192]{1,0:T(4,128)(2,1)}, bf16[4,8192]{1,0:T(4,128)(2,1)}, u32[]{:S(2)}, u32[]{:S(2)}) collective-permute-start(bf16[4,8192]{1,0:T(4,128)(2,1)} %bitcast.48), channel_id=1, source_target_pairs={{0,1},{1,2},{2,3},{4,5},{5,6},{6,7},{8,9},{9,10},{10,11},{12,13},{... | collective-permute-start | bytes 196616 | tf_op jit(solution)/shard_map/ppermute | solution.py:37
  40.7 3.4 %copy-start.7 = (bf16[4,16,512]{1,2,0:T(8,128)(2,1)}, bf16[4,16,512]{1,2,0:T(8,128)(2,1)S(1)}, u32[]{:S(2)}) copy-start(bf16[4,16,512]{1,2,0:T(8,128)(2,1)S(1)} %copy.105) | copy-start | bytes 196612
  41.7 2.4 %copy-start.6 = (bf16[4,512,512]{2,1,0:T(8,128)(2,1)S(1)}, bf16[4,512,512]{2,1,0:T(8,128)(2,1)}, u32[]{:S(2)}) copy-start(bf16[4,512,512]{2,1,0:T(8,128)(2,1)} %param.10) | copy-start | bytes 6291460
  41.7 2.4 %copy-start.8 = (bf16[4,16,512]{1,2,0:T(8,128)(2,1)S(1)}, bf16[4,16,512]{1,2,0:T(8,128)(2,1)}, u32[]{:S(2)}) copy-start(bf16[4,16,512]{1,2,0:T(8,128)(2,1)} %copy.107) | copy-start | bytes 196612
  42.7 1.3 collective-permute-start.5
  44.1 2.9 %copy-start.1 = (bf16[3,512,544]{2,1,0:T(8,128)(2,1)S(1)}, bf16[3,512,544]{2,1,0:T(8,128)(2,1)}, u32[]{:S(2)}) copy-start(bf16[3,512,544]{2,1,0:T(8,128)(2,1)} %pad_maximum_fusion.1.ht_ref) | copy-start | bytes 5013508
  44.1 2.9 %copy-start.4 = (f32[4,3]{1,0:T(4,128)S(1)}, f32[4,3]{1,0:T(4,128)}, u32[]{:S(2)}) copy-start(f32[4,3]{1,0:T(4,128)} %coef_ref.3) | copy-start | bytes 148
  47.1 5.1 %copy-start.9 = (bf16[1,144,512]{2,1,0:T(8,128)(2,1)S(1)}, bf16[1,144,512]{2,1,0:T(8,128)(2,1)}, u32[]{:S(2)}) copy-start(bf16[1,144,512]{2,1,0:T(8,128)(2,1)} %get-tuple-element.41) | copy-start | bytes 442372
  52.1 1.3 copy-start.14
  52.1 1.7 %copy-start.11 = (f32[512]{0:T(512)S(1)}, f32[512]{0:T(512)}, u32[]{:S(2)}) copy-start(f32[512]{0:T(512)} %multiply_add_fusion.3) | copy-start | bytes 6148
  52.2 5.8 %copy-start.12 = (s32[4,1,1,2]{0,3,2,1:T(2,128)S(1)}, s32[4,1,1,2]{0,3,2,1:T(2,128)}, u32[]{:S(2)}) copy-start(s32[4,1,1,2]{0,3,2,1:T(2,128)} %param.15) | copy-start | bytes 100
  54.9 1.2 collective-permute-start.6
  56.2 3.6 %collective-permute-start.7 = (f32[4,12]{1,0:T(4,128)S(1)}, f32[4,12]{1,0:T(4,128)S(1)}, u32[]{:S(2)}, u32[]{:S(2)}) collective-permute-start(f32[4,12]{1,0:T(4,128)S(1)} %fusion.29), channel_id=1, source_target_pairs={{0,1},{1,0},{2,3},{3,2},{4,5},{5,4},{6,7},{7,6},{8,9},{9,8},{10,11... | collective-permute-start | bytes 584 | tf_op jit(solution)/shard_map/ppermute | solution.py:82
  59.8 11.2 %copy-start.13 = (pred[3,3]{1,0:T(4,128)(4,1)S(1)}, pred[3,3]{1,0:T(4,128)(4,1)}, u32[]{:S(2)}) copy-start(pred[3,3]{1,0:T(4,128)(4,1)} %iota_compare_fusion.2) | copy-start | bytes 31
  59.8 9.7 %collective-permute-start.8 = (f32[4,12]{1,0:T(4,128)S(1)}, f32[4,12]{1,0:T(4,128)S(1)}, u32[]{:S(2)}, u32[]{:S(2)}) collective-permute-start(f32[4,12]{1,0:T(4,128)S(1)} %add.244), channel_id=1, source_target_pairs={{0,2},{1,3},{2,0},{3,1},{4,6},{5,7},{6,4},{7,5},{8,10},{9,11},{10,... | collective-permute-start | bytes 584 | tf_op jit(solution)/shard_map/ppermute | solution.py:82
  71.3 12.5 %copy-start.3 = (f32[4,3]{1,0:T(4,128)}, f32[4,3]{1,0:T(4,128)S(1)}, u32[]{:S(2)}) copy-start(f32[4,3]{1,0:T(4,128)S(1)} %pad_maximum_fusion.11.plane_ref) | copy-start | bytes 148
  71.3 2.8 %copy-start = (bf16[12,512,512]{2,1,0:T(8,128)(2,1)S(1)}, bf16[12,512,512]{2,1,0:T(8,128)(2,1)}, u32[]{:S(2)}) copy-start(bf16[12,512,512]{2,1,0:T(8,128)(2,1)} %cmap_ref.1) | copy-start | bytes 18874372
  74.1 2.2 %copy-start.2 = (f32[4,512,512]{2,1,0:T(8,128)S(1)}, f32[4,512,512]{2,1,0:T(8,128)}, u32[]{:S(2)}) copy-start(f32[4,512,512]{2,1,0:T(8,128)} %shard_map.96.matched_ref) | copy-start | bytes 12582916
  (1 other events, 0.9 us)
Sparse Core Ops, SparseCore 0:
  84.0 41.3 reduce-scatter.1

commit v10 on v9

--- a/solution.py
+++ b/solution.py
@@ -239,7 +239,7 @@
     )
     flops = exp_dev * 4 * tile_len ** 3
     moved = exp_dev * tile_len * tile_len * (4 + 2 + 2) + patches * tile_len * tile_len * 2
-    vmem = min(60 * 1024 * 1024, (16 + 3 * patches) * 1024 * 1024)
+    vmem = 60 * 1024 * 1024
     return pl.pallas_call(
         warp_body,
         grid_spec=grid_spec,

time: 136 us -> 133 us (0.978)
  local copies, waits for them, and re-layouts: 14.2 us -> 8.19 us
  Pallas kernels: 20.8 us -> 22.3 us
    unnamed x35 -> x19, local copies, waits for them, and re-layouts: 9.06 us -> 2.55 us
    pallas_call x1, Pallas kernels: 7.51 us -> 9.16 us  [warp_tiles(): pl.pallas_call(warp_body, grid_spec=grid_spec, out_shape=jax.ShapeDtypeSt...]
  transfers between devices with their start and end apart: 10 -> 10, of which waited for: 3 -> 4; matrix products, arithmetic and copies ran while one was open for 16% -> 16% of each run, Pallas kernels for 10% -> 10%
where the time goes in v10:
time: 133 us; the launch traced here: 132 us
  waiting for transfers between devices  42.1 us (32%)
  other arithmetic  24.4 us (18%)
  Pallas kernels  22.3 us (17%)
  starting transfers between devices  17.9 us (13%)
  between operations  14.3 us (11%)
  local copies, waits for them, and re-layouts  8.19 us (6%)
  matrix products  2.98 us (2%)
    reduce_scatter x1, waiting for transfers between devices, shards(): lax.psum_scatter(partial_sum, 'visit', scatter_dimension=0, tiled=True)  39.9 us
    pallas_call x1, Pallas kernels, warp_tiles(): pl.pallas_call(warp_body, grid_spec=grid_spec, out_shape=jax.ShapeDtypeSt...  9.16 us
    pallas_call x1, Pallas kernels, band_tiles(): pl.pallas_call(band_body, grid=(exp_dev,), in_specs=[pl.BlockSpec(memory_...  8.09 us
    ppermute x3, starting transfers between devices, shards(): received.append(lax.ppermute(payload, 'visit', pairs))  7.86 us
    ppermute x1, starting transfers between devices, extended(): before = lax.ppermute(last, axis, up)  5.16 us
    pallas_call x1, Pallas kernels, conv_tiles(): pl.pallas_call(conv_body, grid=(exp_dev,), in_specs=[pl.BlockSpec(memory_...  5.05 us
    ppermute x3, starting transfers between devices, butterfly_sum(): values = jax.tree.map(lambda v: v + lax.ppermute(v, axis, pairs), values)  3.45 us
    convert_element_type x2, other arithmetic, band_table(): return jnp.where(jnp.abs(offset) <= width, values, 0.0).astype(jnp.bfloat16)  3.39 us
  transfers between devices with their start and end apart: 10, of which 4 were waited for; matrix products, arithmetic and copies ran while one was open for 16% of the time, Pallas kernels for 10%

profile of v10, /device:TPU:0, one launch (start us, length us, event | category | flops | bytes accessed | tf_op | source)
XLA Modules:
  0.0 132.2 jit_solution(8477156260712883705)
XLA Ops:
  9.7 1.3 fusion.26
  11.3 2.1 %convolution_convert_fusion = bf16[4,32,512]{2,1,0:T(8,128)(2,1)S(1)} fusion(bf16[4,512,512]{2,1,0:T(8,128)(2,1)} %param.10, s32[4]{0:T(128)S(1)} %get-tuple-element.35), kind=kOutput, calls=%fused_computation.12 | convolution fusion | flops 67305472 | bytes 2228240 | tf_op jit(solution)/shard_map/esr,erl->esl/dot_general | solution.py:285
  14.1 4.0 %collective-permute-start.1 = (bf16[144,512]{1,0:T(8,128)(2,1)}, bf16[144,512]{1,0:T(8,128)(2,1)}, u32[]{:S(2)}, u32[]{:S(2)}) collective-permute-start(bf16[144,512]{1,0:T(8,128)(2,1)} %get-tuple-element.42), channel_id=1, source_target_pairs={{0,16},{8,24},{16,0},{24,8},{1,17},{9,25},{17,1},{25,9},{2,18},{10... | collective-permute-start | bytes 442376 | tf_op jit(solution)/shard_map/ppermute | solution.py:305
  18.1 1.6 %collective-permute-start = (bf16[144,512]{1,0:T(8,128)(2,1)}, bf16[144,512]{1,0:T(8,128)(2,1)}, u32[]{:S(2)}, u32[]{:S(2)}) collective-permute-start(bf16[144,512]{1,0:T(8,128)(2,1)} %get-tuple-element.42), channel_id=1, source_target_pairs={{0,8},{8,16},{16,24},{24,0},{1,9},{9,17},{17,25},{25,1},{2,10},{10... | collective-permute-start | bytes 442376 | tf_op jit(solution)/shard_map/ppermute | solution.py:305
  19.7 2.2 %collective-permute-start.2 = (bf16[144,512]{1,0:T(8,128)(2,1)}, bf16[144,512]{1,0:T(8,128)(2,1)}, u32[]{:S(2)}, u32[]{:S(2)}) collective-permute-start(bf16[144,512]{1,0:T(8,128)(2,1)} %get-tuple-element.42), channel_id=1, source_target_pairs={{0,24},{8,0},{16,8},{24,16},{1,25},{9,1},{17,9},{25,17},{2,26},{10... | collective-permute-start | bytes 442376 | tf_op jit(solution)/shard_map/ppermute | solution.py:305
  22.4 1.3 collective-permute-start.4
  24.6 5.2 %collective-permute-start.3 = (bf16[4,8192]{1,0:T(4,128)(2,1)}, bf16[4,8192]{1,0:T(4,128)(2,1)}, u32[]{:S(2)}, u32[]{:S(2)}) collective-permute-start(bf16[4,8192]{1,0:T(4,128)(2,1)} %bitcast.48), channel_id=1, source_target_pairs={{0,1},{1,2},{2,3},{4,5},{5,6},{6,7},{8,9},{9,10},{10,11},{12,13},{... | collective-permute-start | bytes 196616 | tf_op jit(solution)/shard_map/ppermute | solution.py:37
  32.4 1.3 select_convert_fusion.2
  33.7 2.1 %select_convert_fusion = (bf16[1,512,544]{2,1,0:T(8,128)(2,1)S(1)}, bf16[1,512,544]{2,1,0:T(8,128)(2,1)S(1)}) fusion(f32[]{:T(128)} %exponential_reduce_fusion, f32[]{:T(128)} %exponential_reduce_fusion.1), kind=kLoop, calls=%fused_computation.5 | loop fusion | flops 4177920 | bytes 1114120 | tf_op jit(solution)/shard_map/convert_element_type | solution.py:54
  36.3 1.6 %pad_maximum_fusion.1.ht_ref = bf16[3,512,544]{2,1,0:T(8,128)(2,1)} fusion(bf16[1,512,544]{2,1,0:T(8,128)(2,1)S(1)} %get-tuple-element.59, bf16[1,512,544]{2,1,0:T(8,128)(2,1)S(1)} %get-tuple-element.60, bf16[1,512,544]{2,1,0:T(8,128)(2,1)S(1)} %select_convert_fusion.2), kind=kLoop, calls=%fused_computation.1 | loop fusion | flops 1671168 | bytes 3342336 | tf_op jit(solution)/shard_map/stack | solution.py:321
  40.7 1.0 copy.107
  41.7 1.0 fusion.14
  42.8 1.3 collective-permute-done.5
  44.1 2.9 %pad_maximum_fusion.padded_ref = bf16[4,544,544]{2,1,0:T(8,128)(2,1)S(1)} fusion(bf16[4,16,544]{2,1,0:T(8,128)(2,1)S(1)} %get-tuple-element.44, bf16[4,512,16]{2,1,0:T(8,128)(2,1)S(1)} %bitcast.87, bf16[4,512,512]{2,1,0:T(8,128)(2,1)S(1)} %copy-done.3, bf16[4,512,16]{2,1,0:T(8,128)(2,1)} %bitcast.85, bf16[4,16,544]{2,1,0:T(8,128)(2,1)S(1)} %get-tuple-element.43), kind=kLoop, calls=%fused_computation | loop fusion | flops 11837440 | bytes 4734976 | tf_op jit(solution)/shard_map/concatenate | solution.py:42
  47.0 5.1 %shard_map.95 = f32[4,32,512]{2,1,0:T(8,128)S(1)} custom-call(f32[4,3]{1,0:T(4,128)S(1)} %copy-done.1, bf16[4,3,32,544]{3,2,1,0:T(8,128)(2,1)S(1)} %fusion.5.vt_ref, bf16[3,512,544]{2,1,0:T(8,128)(2,1)S(1)} %copy-done, bf16[4,544,544]{2,1,0:T(8,128)(2,1)S(1)} %pad_maximum_fusion.padded_ref), custom_call_target="tpu_custom_call" | custom-call | flops 441188352 | bytes 2629632 | tf_op jit(solution)/shard_map/pallas_call | solution.py:125
  52.1 1.1 pad_maximum_fusion.2
  55.0 0.9 slice.127.blk_ref
  56.1 1.8 %collective-permute-start.7 = (f32[4,12]{1,0:T(4,128)S(1)}, f32[4,12]{1,0:T(4,128)S(1)}, u32[]{:S(2)}, u32[]{:S(2)}) collective-permute-start(f32[4,12]{1,0:T(4,128)S(1)} %fusion.29), channel_id=1, source_target_pairs={{0,1},{1,0},{2,3},{3,2},{4,5},{5,4},{6,7},{7,6},{8,9},{9,8},{10,11... | collective-permute-start | bytes 584 | tf_op jit(solution)/shard_map/ppermute | solution.py:82
  59.7 1.5 %collective-permute-start.8 = (f32[4,12]{1,0:T(4,128)S(1)}, f32[4,12]{1,0:T(4,128)S(1)}, u32[]{:S(2)}, u32[]{:S(2)}) collective-permute-start(f32[4,12]{1,0:T(4,128)S(1)} %add.244), channel_id=1, source_target_pairs={{0,2},{1,3},{2,0},{3,1},{4,6},{5,7},{6,4},{7,5},{8,10},{9,11},{10,... | collective-permute-start | bytes 584 | tf_op jit(solution)/shard_map/ppermute | solution.py:82
  61.2 8.1 %shard_map.96.matched_ref = f32[4,512,512]{2,1,0:T(8,128)} custom-call(f32[4,3]{1,0:T(4,128)S(1)} %copy-done.1, bf16[3,128,256]{2,1,0:T(8,128)(2,1)S(1)} %slice.127.blk_ref, bf16[4,640,640]{2,1,0:T(8,128)(2,1)S(1)} %pad.7.padded_ref), custom_call_target="tpu_custom_call" | custom-call | flops 3623878656 | bytes 7471104 | tf_op jit(solution)/shard_map/pallas_call | solution.py:175
  69.5 1.1 custom-call.4
  71.7 9.2 %shard_map.97 = bf16[4,512,512]{2,1,0:T(8,128)(2,1)} custom-call(s32[4,2]{1,0:T(4,128)} %copy.125.idx_ref, f32[4,3]{1,0:T(4,128)} %pad_maximum_fusion.11.plane_ref, f32[4,4]{1,0:T(4,128)} %get-tuple-element.54.pick_ref, f32[1,512]{1,0:T(1,128)} %multiply_add_fusion.1.xrow_ref, f32[512,1]{1,0:T(8,128)} %multiply_add_fusion.ycol_ref, ...), custom_call_target="tpu_custom_call" | custom-call | flops 2147483648 | bytes 10485760 | tf_op jit(solution)/shard_map/pallas_call | solution.py:243
  82.6 39.9 %reduce-scatter.2.cloned.1.call-done = bf16[1,512,512]{2,1,0:T(8,128)(2,1)} async-done(((bf16[4,512,512]{2,1,0:T(8,128)(2,1)}), bf16[1,512,512]{2,1,0:T(8,128)(2,1)}) %reduce-scatter.2.cloned.1.call-update) | async-done | bytes 524304 | tf_op jit(solution)/shard_map/reduce_scatter | solution.py:371
  122.5 2.8 %convert_divide_fusion = f32[1,512,512]{2,1,0:T(8,128)} fusion(bf16[1,512,512]{2,1,0:T(8,128)(2,1)} %reduce-scatter.2.cloned.1.call-done, f32[]{:T(128)} %convert_reduce_fusion), kind=kLoop, calls=%fused_computation.13 | loop fusion | flops 524288 | bytes 1572868 | tf_op jit(solution)/shard_map/div | solution.py:374
  (89 shorter events, 17.4 us)
Async XLA Ops:
  7.2 14.8 %copy-start.2 = (bf16[4,512,512]{2,1,0:T(8,128)(2,1)S(1)}, bf16[4,512,512]{2,1,0:T(8,128)(2,1)}, u32[]{:S(2)}) copy-start(bf16[4,512,512]{2,1,0:T(8,128)(2,1)} %param.10) | copy-start | bytes 6291460
  7.2 115.3 %reduce-scatter.2.cloned.1.call-start = ((), (), s32[]{:S(2)}) async-start(), calls=%async_computation.1 | async-start | bytes 2621440 | tf_op jit(solution)/shard_map/reduce_scatter | solution.py:371
  14.1 38.0 %collective-permute-start.1 = (bf16[144,512]{1,0:T(8,128)(2,1)}, bf16[144,512]{1,0:T(8,128)(2,1)}, u32[]{:S(2)}, u32[]{:S(2)}) collective-permute-start(bf16[144,512]{1,0:T(8,128)(2,1)} %get-tuple-element.42), channel_id=1, source_target_pairs={{0,16},{8,24},{16,0},{24,8},{1,17},{9,25},{17,1},{25,9},{2,18},{10... | collective-permute-start | bytes 442376 | tf_op jit(solution)/shard_map/ppermute | solution.py:305
  18.1 34.0 %collective-permute-start = (bf16[144,512]{1,0:T(8,128)(2,1)}, bf16[144,512]{1,0:T(8,128)(2,1)}, u32[]{:S(2)}, u32[]{:S(2)}) collective-permute-start(bf16[144,512]{1,0:T(8,128)(2,1)} %get-tuple-element.42), channel_id=1, source_target_pairs={{0,8},{8,16},{16,24},{24,0},{1,9},{9,17},{17,25},{25,1},{2,10},{10... | collective-permute-start | bytes 442376 | tf_op jit(solution)/shard_map/ppermute | solution.py:305
  19.7 32.4 %collective-permute-start.2 = (bf16[144,512]{1,0:T(8,128)(2,1)}, bf16[144,512]{1,0:T(8,128)(2,1)}, u32[]{:S(2)}, u32[]{:S(2)}) collective-permute-start(bf16[144,512]{1,0:T(8,128)(2,1)} %get-tuple-element.42), channel_id=1, source_target_pairs={{0,24},{8,0},{16,8},{24,16},{1,25},{9,1},{17,9},{25,17},{2,26},{10... | collective-permute-start | bytes 442376 | tf_op jit(solution)/shard_map/ppermute | solution.py:305
  22.4 16.2 %collective-permute-start.4 = (bf16[4,8192]{1,0:T(4,128)(2,1)S(1)}, bf16[4,8192]{1,0:T(4,128)(2,1)}, u32[]{:S(2)}, u32[]{:S(2)}) collective-permute-start(bf16[4,8192]{1,0:T(4,128)(2,1)S(1)} %bitcast.95), channel_id=1, source_target_pairs={{1,0},{2,1},{3,2},{5,4},{6,5},{7,6},{9,8},{10,9},{11,10},{13,12},{... | collective-permute-start | bytes 196616 | tf_op jit(solution)/shard_map/ppermute | solution.py:38
  24.6 14.9 %collective-permute-start.3 = (bf16[4,8192]{1,0:T(4,128)(2,1)}, bf16[4,8192]{1,0:T(4,128)(2,1)}, u32[]{:S(2)}, u32[]{:S(2)}) collective-permute-start(bf16[4,8192]{1,0:T(4,128)(2,1)} %bitcast.48), channel_id=1, source_target_pairs={{0,1},{1,2},{2,3},{4,5},{5,6},{6,7},{8,9},{9,10},{10,11},{12,13},{... | collective-permute-start | bytes 196616 | tf_op jit(solution)/shard_map/ppermute | solution.py:37
  40.6 3.4 %copy-start.4 = (bf16[4,16,512]{1,2,0:T(8,128)(2,1)}, bf16[4,16,512]{1,2,0:T(8,128)(2,1)S(1)}, u32[]{:S(2)}) copy-start(bf16[4,16,512]{1,2,0:T(8,128)(2,1)S(1)} %copy.105) | copy-start | bytes 196612
  41.7 2.4 %copy-start.3 = (bf16[4,512,512]{2,1,0:T(8,128)(2,1)S(1)}, bf16[4,512,512]{2,1,0:T(8,128)(2,1)}, u32[]{:S(2)}) copy-start(bf16[4,512,512]{2,1,0:T(8,128)(2,1)} %param.10) | copy-start | bytes 6291460
  41.7 2.4 %copy-start.5 = (bf16[4,16,512]{1,2,0:T(8,128)(2,1)S(1)}, bf16[4,16,512]{1,2,0:T(8,128)(2,1)}, u32[]{:S(2)}) copy-start(bf16[4,16,512]{1,2,0:T(8,128)(2,1)} %copy.107) | copy-start | bytes 196612
  42.7 1.3 %collective-permute-start.5 = (bf16[4,16,544]{2,1,0:T(8,128)(2,1)S(1)}, bf16[4,16,544]{2,1,0:T(8,128)(2,1)S(1)}, u32[]{:S(2)}, u32[]{:S(2)}) collective-permute-start(bf16[4,16,544]{2,1,0:T(8,128)(2,1)S(1)} %fusion.14), channel_id=1, source_target_pairs={{0,4},{4,0},{1,5},{5,1},{2,6},{6,2},{3,7},{7,3},{8,12},{12,8},{9,1... | collective-permute-start | bytes 208904 | tf_op jit(solution)/shard_map/ppermute | solution.py:30
  44.1 3.0 %copy-start = (bf16[3,512,544]{2,1,0:T(8,128)(2,1)S(1)}, bf16[3,512,544]{2,1,0:T(8,128)(2,1)}, u32[]{:S(2)}) copy-start(bf16[3,512,544]{2,1,0:T(8,128)(2,1)} %pad_maximum_fusion.1.ht_ref) | copy-start | bytes 5013508
  44.1 3.0 %copy-start.1 = (f32[4,3]{1,0:T(4,128)S(1)}, f32[4,3]{1,0:T(4,128)}, u32[]{:S(2)}) copy-start(f32[4,3]{1,0:T(4,128)} %coef_ref.3) | copy-start | bytes 148
  52.1 5.7 %copy-start.6 = (s32[4,1,1,2]{0,3,2,1:T(2,128)S(1)}, s32[4,1,1,2]{0,3,2,1:T(2,128)}, u32[]{:S(2)}) copy-start(s32[4,1,1,2]{0,3,2,1:T(2,128)} %param.15) | copy-start | bytes 100
  54.8 1.2 collective-permute-start.6
  56.1 3.6 %collective-permute-start.7 = (f32[4,12]{1,0:T(4,128)S(1)}, f32[4,12]{1,0:T(4,128)S(1)}, u32[]{:S(2)}, u32[]{:S(2)}) collective-permute-start(f32[4,12]{1,0:T(4,128)S(1)} %fusion.29), channel_id=1, source_target_pairs={{0,1},{1,0},{2,3},{3,2},{4,5},{5,4},{6,7},{7,6},{8,9},{9,8},{10,11... | collective-permute-start | bytes 584 | tf_op jit(solution)/shard_map/ppermute | solution.py:82
  59.7 9.6 %collective-permute-start.8 = (f32[4,12]{1,0:T(4,128)S(1)}, f32[4,12]{1,0:T(4,128)S(1)}, u32[]{:S(2)}, u32[]{:S(2)}) collective-permute-start(f32[4,12]{1,0:T(4,128)S(1)} %add.244), channel_id=1, source_target_pairs={{0,2},{1,3},{2,0},{3,1},{4,6},{5,7},{6,4},{7,5},{8,10},{9,11},{10,... | collective-permute-start | bytes 584 | tf_op jit(solution)/shard_map/ppermute | solution.py:82
Sparse Core Ops, SparseCore 0:
  81.0 41.4 reduce-scatter.1

commit v11 on v10

--- a/solution.py
+++ b/solution.py
@@ -1,3 +1,5 @@
+import functools
+
 import jax
 import jax.numpy as jnp
 from jax import lax
@@ -143,8 +145,9 @@
 BLOCK = 128
 
 
-def band_body(coef_ref, blk_ref, padded_ref, out_ref):
-    e = pl.program_id(0)
+def band_body(first, coef_ref, blk_ref, padded_ref, *rest):
+    out_ref = rest[-1]
+    e = pl.program_id(0) + first
     tile_len = out_ref.shape[1]
     total = None
     for kernel in range(len(SIGMA_PARTS)):
@@ -166,27 +169,35 @@
     out_ref[0] = total
 
 
-def band_tiles(coeffs, blocks, padded, tile_len):
+def band_tiles(coeffs, blocks, padded, tile_len, first, count, into):
     exp_dev, wide = padded.shape[0], padded.shape[1]
     nk = blocks.shape[0]
     steps = tile_len // BLOCK
-    flops = exp_dev * nk * steps * 2 * BLOCK * 2 * BLOCK * (wide + tile_len)
-    moved = exp_dev * wide * wide * 2 + exp_dev * tile_len * tile_len * 4
+    flops = count * nk * steps * 2 * BLOCK * 2 * BLOCK * (wide + tile_len)
+    moved = count * wide * wide * 2 + count * tile_len * tile_len * 4
+    in_specs = [
+        pl.BlockSpec(memory_space=pltpu.SMEM),
+        pl.BlockSpec((nk, BLOCK, 2 * BLOCK), lambda e: (0, 0, 0)),
+        pl.BlockSpec((1, wide, wide), lambda e: (e + first, 0, 0)),
+    ]
+    operands = [coeffs, blocks, padded]
+    aliases = {}
+    if into is not None:
+        in_specs.append(pl.BlockSpec(memory_space=pl.ANY))
+        operands.append(into)
+        aliases = {3: 0}
     return pl.pallas_call(
-        band_body,
-        grid=(exp_dev,),
-        in_specs=[
-            pl.BlockSpec(memory_space=pltpu.SMEM),
-            pl.BlockSpec((nk, BLOCK, 2 * BLOCK), lambda e: (0, 0, 0)),
-            pl.BlockSpec((1, wide, wide), lambda e: (e, 0, 0)),
-        ],
-        out_specs=pl.BlockSpec((1, tile_len, tile_len), lambda e: (e, 0, 0)),
+        functools.partial(band_body, first),
+        grid=(count,),
+        in_specs=in_specs,
+        out_specs=pl.BlockSpec((1, tile_len, tile_len), lambda e: (e + first, 0, 0)),
         out_shape=jax.ShapeDtypeStruct((exp_dev, tile_len, tile_len), jnp.float32),
+        input_output_aliases=aliases,
         compiler_params=pltpu.CompilerParams(
             dimension_semantics=("arbitrary",), vmem_limit_bytes=48 * 1024 * 1024
         ),
         cost_estimate=pl.CostEstimate(flops=flops, bytes_accessed=moved, transcendentals=0),
-    )(coeffs, blocks, padded)
+    )(*operands)
 
 
 def warp_body(idx_ref, plane_ref, pick_ref, xrow_ref, ycol_ref, matched_ref, rmap_ref, cmap_ref,
@@ -326,7 +337,9 @@
     spare = 2 * BLOCK + tile_len - BLOCK - padded.shape[1]
     roomy = jnp.pad(padded, ((0, 0), (0, spare), (0, spare)))
     blocks = stacked_tables[:, :BLOCK, : 2 * BLOCK]
-    matched = band_tiles(coeffs, blocks, roomy, tile_len)
+    half = exp_dev // 2
+    matched = band_tiles(coeffs, blocks, roomy, tile_len, 0, half, None)
+    matched = band_tiles(coeffs, blocks, roomy, tile_len, half, exp_dev - half, matched)
     difference = nearby - theirs
     pixel_weight = 1.0 / (1.0 + theirs * theirs)
     strip_rows = row_pos * tile_len + offset[:, None] + jnp.arange(STRIP, dtype=jnp.int32)[None, :]

time: 133 us -> 130 us (0.977)
  Pallas kernels: 22.3 us -> 24.3 us
  waiting for transfers between devices: 42.1 us -> 40.3 us
  local copies, waits for them, and re-layouts: 8.19 us -> 6.67 us
  starting transfers between devices: 17.9 us -> 16.4 us
    pallas_call x1 -> x2, Pallas kernels: 8.09 us -> 9.68 us  [band_tiles(): pl.pallas_call(functools.partial(band_body, first), grid=(count,), in_spe...]
    ppermute x3, starting transfers between devices: 3.45 us -> 1.95 us  [butterfly_sum(): values = jax.tree.map(lambda v: v + lax.ppermute(v, axis, pairs), values)]
  transfers between devices with their start and end apart: 10 -> 10, of which waited for: 4 -> 3; matrix products, arithmetic and copies ran while one was open for 16% -> 14% of each run, Pallas kernels for 10% -> 11%
where the time goes in v11:
time: 130 us; the launch traced here: 129 us
  waiting for transfers between devices  40.3 us (31%)
  Pallas kernels  24.3 us (19%)
  other arithmetic  24.1 us (19%)
  starting transfers between devices  16.4 us (13%)
  between operations  14.4 us (11%)
  local copies, waits for them, and re-layouts  6.67 us (5%)
  matrix products  2.98 us (2%)
    reduce_scatter x1, waiting for transfers between devices, shards(): lax.psum_scatter(partial_sum, 'visit', scatter_dimension=0, tiled=True)  38.9 us
    pallas_call x2, Pallas kernels, band_tiles(): pl.pallas_call(functools.partial(band_body, first), grid=(count,), in_spe...  9.68 us
    pallas_call x1, Pallas kernels, warp_tiles(): pl.pallas_call(warp_body, grid_spec=grid_spec, out_shape=jax.ShapeDtypeSt...  9.56 us
    ppermute x3, starting transfers between devices, shards(): received.append(lax.ppermute(payload, 'visit', pairs))  7.86 us
    ppermute x1, starting transfers between devices, extended(): before = lax.ppermute(last, axis, up)  5.17 us
    pallas_call x1, Pallas kernels, conv_tiles(): pl.pallas_call(conv_body, grid=(exp_dev,), in_specs=[pl.BlockSpec(memory_...  5.05 us
    convert_element_type x2, other arithmetic, band_table(): return jnp.where(jnp.abs(offset) <= width, values, 0.0).astype(jnp.bfloat16)  3.49 us
    concatenate x1, other arithmetic, extended(): value = jnp.concatenate([before, value, after], axis=dim)  2.92 us
  transfers between devices with their start and end apart: 10, of which 3 were waited for; matrix products, arithmetic and copies ran while one was open for 14% of the time, Pallas kernels for 11%

profile of v11, /device:TPU:0, one launch (start us, length us, event | category | flops | bytes accessed | tf_op | source)
XLA Modules:
  0.0 129.0 jit_solution(6468281012012709241)
XLA Ops:
  7.2 0.9 iota_compare_fusion.3
  9.7 1.3 %fusion.26 = (f32[4,4]{1,0:T(4,128)}, bf16[4,4]{1,0:T(4,128)(2,1)S(1)}) fusion(pred[4,4]{1,0:T(4,128)(4,1)S(1)} %fusion.17, bf16[4]{0:T(256)(128)(2,1)} %bitcast.119), kind=kLoop, calls=%fused_computation.100 | loop fusion | flops 32 | bytes 120 | tf_op jit(solution)/shard_map/convert_element_type | solution.py:381
  11.3 2.1 %convolution_convert_fusion = bf16[4,32,512]{2,1,0:T(8,128)(2,1)S(1)} fusion(bf16[4,512,512]{2,1,0:T(8,128)(2,1)} %param.10, s32[4]{0:T(128)S(1)} %get-tuple-element.35), kind=kOutput, calls=%fused_computation.12 | convolution fusion | flops 67305472 | bytes 2228240 | tf_op jit(solution)/shard_map/esr,erl->esl/dot_general | solution.py:296
  14.1 4.0 %collective-permute-start.1 = (bf16[144,512]{1,0:T(8,128)(2,1)}, bf16[144,512]{1,0:T(8,128)(2,1)}, u32[]{:S(2)}, u32[]{:S(2)}) collective-permute-start(bf16[144,512]{1,0:T(8,128)(2,1)} %get-tuple-element.42), channel_id=1, source_target_pairs={{0,16},{8,24},{16,0},{24,8},{1,17},{9,25},{17,1},{25,9},{2,18},{10... | collective-permute-start | bytes 442376 | tf_op jit(solution)/shard_map/ppermute | solution.py:316
  18.2 1.6 %collective-permute-start = (bf16[144,512]{1,0:T(8,128)(2,1)}, bf16[144,512]{1,0:T(8,128)(2,1)}, u32[]{:S(2)}, u32[]{:S(2)}) collective-permute-start(bf16[144,512]{1,0:T(8,128)(2,1)} %get-tuple-element.42), channel_id=1, source_target_pairs={{0,8},{8,16},{16,24},{24,0},{1,9},{9,17},{17,25},{25,1},{2,10},{10... | collective-permute-start | bytes 442376 | tf_op jit(solution)/shard_map/ppermute | solution.py:316
  19.8 2.2 %collective-permute-start.2 = (bf16[144,512]{1,0:T(8,128)(2,1)}, bf16[144,512]{1,0:T(8,128)(2,1)}, u32[]{:S(2)}, u32[]{:S(2)}) collective-permute-start(bf16[144,512]{1,0:T(8,128)(2,1)} %get-tuple-element.42), channel_id=1, source_target_pairs={{0,24},{8,0},{16,8},{24,16},{1,25},{9,1},{17,9},{25,17},{2,26},{10... | collective-permute-start | bytes 442376 | tf_op jit(solution)/shard_map/ppermute | solution.py:316
  22.5 1.3 %collective-permute-start.4 = (bf16[4,8192]{1,0:T(4,128)(2,1)S(1)}, bf16[4,8192]{1,0:T(4,128)(2,1)S(1)}, u32[]{:S(2)}, u32[]{:S(2)}) collective-permute-start(bf16[4,8192]{1,0:T(4,128)(2,1)S(1)} %bitcast.95), channel_id=1, source_target_pairs={{1,0},{2,1},{3,2},{5,4},{6,5},{7,6},{9,8},{10,9},{11,10},{13,12},{... | collective-permute-start | bytes 196616 | tf_op jit(solution)/shard_map/ppermute | solution.py:40
  24.0 5.2 %collective-permute-start.3 = (bf16[4,8192]{1,0:T(4,128)(2,1)S(1)}, bf16[4,8192]{1,0:T(4,128)(2,1)}, u32[]{:S(2)}, u32[]{:S(2)}) collective-permute-start(bf16[4,8192]{1,0:T(4,128)(2,1)S(1)} %bitcast.97), channel_id=1, source_target_pairs={{0,1},{1,2},{2,3},{4,5},{5,6},{6,7},{8,9},{9,10},{10,11},{12,13},{... | collective-permute-start | bytes 196616 | tf_op jit(solution)/shard_map/ppermute | solution.py:39
  32.5 1.3 %select_convert_fusion.2 = bf16[1,512,544]{2,1,0:T(8,128)(2,1)S(1)} fusion(f32[]{:T(128)} %exponential_reduce_fusion.2), kind=kLoop, calls=%fused_computation.7 | loop fusion | flops 3063808 | bytes 557060 | tf_op jit(solution)/shard_map/convert_element_type | solution.py:56
  33.8 2.2 %select_convert_fusion = (bf16[1,512,544]{2,1,0:T(8,128)(2,1)S(1)}, bf16[1,512,544]{2,1,0:T(8,128)(2,1)S(1)}) fusion(f32[]{:T(128)} %exponential_reduce_fusion, f32[]{:T(128)} %exponential_reduce_fusion.1), kind=kLoop, calls=%fused_computation.5 | loop fusion | flops 4177920 | bytes 1114120 | tf_op jit(solution)/shard_map/convert_element_type | solution.py:56
  38.8 1.0 copy.108
  39.8 1.2 fusion.14
  41.0 1.3 collective-permute-done.5
  42.4 2.9 %pad_maximum_fusion.padded_ref = bf16[4,544,544]{2,1,0:T(8,128)(2,1)S(1)} fusion(bf16[4,16,544]{2,1,0:T(8,128)(2,1)S(1)} %get-tuple-element.44, bf16[4,512,16]{2,1,0:T(8,128)(2,1)S(1)} %bitcast.87, bf16[4,512,512]{2,1,0:T(8,128)(2,1)S(1)} %copy-done.4, bf16[4,512,16]{2,1,0:T(8,128)(2,1)} %bitcast.85, bf16[4,16,544]{2,1,0:T(8,128)(2,1)S(1)} %get-tuple-element.43), kind=kLoop, calls=%fused_computation | loop fusion | flops 11837440 | bytes 4734976 | tf_op jit(solution)/shard_map/concatenate | solution.py:44
  45.3 5.0 %shard_map.95 = f32[4,32,512]{2,1,0:T(8,128)S(1)} custom-call(f32[4,3]{1,0:T(4,128)S(1)} %copy-done.2, bf16[4,3,32,544]{3,2,1,0:T(8,128)(2,1)S(1)} %fusion.5.vt_ref, bf16[3,512,544]{2,1,0:T(8,128)(2,1)S(1)} %copy-done.1, bf16[4,544,544]{2,1,0:T(8,128)(2,1)S(1)} %pad_maximum_fusion.padded_ref), custom_call_target="tpu_custom_call" | custom-call | flops 441188352 | bytes 2629632 | tf_op jit(solution)/shard_map/pallas_call | solution.py:127
  50.5 1.1 pad_maximum_fusion.2
  54.4 1.8 %collective-permute-start.7 = (f32[4,12]{1,0:T(4,128)S(1)}, f32[4,12]{1,0:T(4,128)S(1)}, u32[]{:S(2)}, u32[]{:S(2)}) collective-permute-start(f32[4,12]{1,0:T(4,128)S(1)} %fusion.29), channel_id=1, source_target_pairs={{0,1},{1,0},{2,3},{3,2},{4,5},{5,4},{6,7},{7,6},{8,9},{9,8},{10,11... | collective-permute-start | bytes 584 | tf_op jit(solution)/shard_map/ppermute | solution.py:84
  56.2 4.9 %shard_map.96.rest_0_ = f32[4,512,512]{2,1,0:T(8,128)} custom-call(f32[4,3]{1,0:T(4,128)S(1)} %copy-done.2, bf16[3,128,256]{2,1,0:T(8,128)(2,1)S(1)} %slice.127.blk_ref, bf16[4,640,640]{2,1,0:T(8,128)(2,1)S(1)} %pad.7.padded_ref), custom_call_target="tpu_custom_call" | custom-call | flops 1811939328 | bytes 3735552 | tf_op jit(solution)/shard_map/pallas_call | solution.py:189
  61.1 4.8 %shard_map.97.matched_ref = f32[4,512,512]{2,1,0:T(8,128)} custom-call(f32[4,3]{1,0:T(4,128)S(1)} %copy-done.2, bf16[3,128,256]{2,1,0:T(8,128)(2,1)S(1)} %slice.127.blk_ref, bf16[4,640,640]{2,1,0:T(8,128)(2,1)S(1)} %pad.7.padded_ref, f32[4,512,512]{2,1,0:T(8,128)} %shard_map.96.rest_0_), custom_call_target="tpu_custom_call", output_to_operand_aliasing={{}: (3, {})} | custom-call | flops 1811939328 | bytes 3735552 | tf_op jit(solution)/shard_map/pallas_call | solution.py:189
  66.1 1.1 custom-call.4
  68.3 9.6 %shard_map.98 = bf16[4,512,512]{2,1,0:T(8,128)(2,1)} custom-call(s32[4,2]{1,0:T(4,128)} %copy.126.idx_ref, f32[4,3]{1,0:T(4,128)} %pad_maximum_fusion.11.plane_ref, f32[4,4]{1,0:T(4,128)} %get-tuple-element.54.pick_ref, f32[1,512]{1,0:T(1,128)} %multiply_add_fusion.1.xrow_ref, f32[512,1]{1,0:T(8,128)} %multiply_add_fusion.ycol_ref, ...), custom_call_target="tpu_custom_call" | custom-call | flops 2147483648 | bytes 10485760 | tf_op jit(solution)/shard_map/pallas_call | solution.py:254
  77.9 0.9 copy-done.8
  80.4 38.9 %reduce-scatter.2.cloned.1.call-done = bf16[1,512,512]{2,1,0:T(8,128)(2,1)} async-done(((bf16[4,512,512]{2,1,0:T(8,128)(2,1)}), bf16[1,512,512]{2,1,0:T(8,128)(2,1)}) %reduce-scatter.2.cloned.1.call-update) | async-done | bytes 524304 | tf_op jit(solution)/shard_map/reduce_scatter | solution.py:384
  119.4 2.8 %convert_divide_fusion = f32[1,512,512]{2,1,0:T(8,128)} fusion(bf16[1,512,512]{2,1,0:T(8,128)(2,1)} %reduce-scatter.2.cloned.1.call-done, f32[]{:T(128)} %convert_reduce_fusion), kind=kLoop, calls=%fused_computation.13 | loop fusion | flops 524288 | bytes 1572868 | tf_op jit(solution)/shard_map/div | solution.py:387
  (98 shorter events, 15.2 us)
Async XLA Ops:
  7.2 14.8 %copy-start.3 = (bf16[4,512,512]{2,1,0:T(8,128)(2,1)S(1)}, bf16[4,512,512]{2,1,0:T(8,128)(2,1)}, u32[]{:S(2)}) copy-start(bf16[4,512,512]{2,1,0:T(8,128)(2,1)} %param.10) | copy-start | bytes 6291460
  7.2 112.2 %reduce-scatter.2.cloned.1.call-start = ((), (), s32[]{:S(2)}) async-start(), calls=%async_computation.1 | async-start | bytes 2621440 | tf_op jit(solution)/shard_map/reduce_scatter | solution.py:384
  14.1 36.3 %collective-permute-start.1 = (bf16[144,512]{1,0:T(8,128)(2,1)}, bf16[144,512]{1,0:T(8,128)(2,1)}, u32[]{:S(2)}, u32[]{:S(2)}) collective-permute-start(bf16[144,512]{1,0:T(8,128)(2,1)} %get-tuple-element.42), channel_id=1, source_target_pairs={{0,16},{8,24},{16,0},{24,8},{1,17},{9,25},{17,1},{25,9},{2,18},{10... | collective-permute-start | bytes 442376 | tf_op jit(solution)/shard_map/ppermute | solution.py:316
  18.2 32.2 %collective-permute-start = (bf16[144,512]{1,0:T(8,128)(2,1)}, bf16[144,512]{1,0:T(8,128)(2,1)}, u32[]{:S(2)}, u32[]{:S(2)}) collective-permute-start(bf16[144,512]{1,0:T(8,128)(2,1)} %get-tuple-element.42), channel_id=1, source_target_pairs={{0,8},{8,16},{16,24},{24,0},{1,9},{9,17},{17,25},{25,1},{2,10},{10... | collective-permute-start | bytes 442376 | tf_op jit(solution)/shard_map/ppermute | solution.py:316
  19.8 30.7 %collective-permute-start.2 = (bf16[144,512]{1,0:T(8,128)(2,1)}, bf16[144,512]{1,0:T(8,128)(2,1)}, u32[]{:S(2)}, u32[]{:S(2)}) collective-permute-start(bf16[144,512]{1,0:T(8,128)(2,1)} %get-tuple-element.42), channel_id=1, source_target_pairs={{0,24},{8,0},{16,8},{24,16},{1,25},{9,1},{17,9},{25,17},{2,26},{10... | collective-permute-start | bytes 442376 | tf_op jit(solution)/shard_map/ppermute | solution.py:316
  22.5 15.1 %collective-permute-start.4 = (bf16[4,8192]{1,0:T(4,128)(2,1)S(1)}, bf16[4,8192]{1,0:T(4,128)(2,1)S(1)}, u32[]{:S(2)}, u32[]{:S(2)}) collective-permute-start(bf16[4,8192]{1,0:T(4,128)(2,1)S(1)} %bitcast.95), channel_id=1, source_target_pairs={{1,0},{2,1},{3,2},{5,4},{6,5},{7,6},{9,8},{10,9},{11,10},{13,12},{... | collective-permute-start | bytes 196616 | tf_op jit(solution)/shard_map/ppermute | solution.py:40
  24.0 13.6 %collective-permute-start.3 = (bf16[4,8192]{1,0:T(4,128)(2,1)S(1)}, bf16[4,8192]{1,0:T(4,128)(2,1)}, u32[]{:S(2)}, u32[]{:S(2)}) collective-permute-start(bf16[4,8192]{1,0:T(4,128)(2,1)S(1)} %bitcast.97), channel_id=1, source_target_pairs={{0,1},{1,2},{2,3},{4,5},{5,6},{6,7},{8,9},{9,10},{10,11},{12,13},{... | collective-permute-start | bytes 196616 | tf_op jit(solution)/shard_map/ppermute | solution.py:39
  36.9 4.1 %copy-start = (bf16[3,512,544]{2,1,0:T(8,128)(2,1)}, bf16[3,512,544]{2,1,0:T(8,128)(2,1)S(1)}, u32[]{:S(2)}) copy-start(bf16[3,512,544]{2,1,0:T(8,128)(2,1)S(1)} %pad_maximum_fusion.1.ht_ref) | copy-start | bytes 5013508
  38.7 3.6 %copy-start.5 = (bf16[4,16,512]{1,2,0:T(8,128)(2,1)}, bf16[4,16,512]{1,2,0:T(8,128)(2,1)S(1)}, u32[]{:S(2)}) copy-start(bf16[4,16,512]{1,2,0:T(8,128)(2,1)S(1)} %copy.106) | copy-start | bytes 196612
  39.8 2.6 %copy-start.4 = (bf16[4,512,512]{2,1,0:T(8,128)(2,1)S(1)}, bf16[4,512,512]{2,1,0:T(8,128)(2,1)}, u32[]{:S(2)}) copy-start(bf16[4,512,512]{2,1,0:T(8,128)(2,1)} %param.10) | copy-start | bytes 6291460
  39.8 2.6 %copy-start.6 = (bf16[4,16,512]{1,2,0:T(8,128)(2,1)S(1)}, bf16[4,16,512]{1,2,0:T(8,128)(2,1)}, u32[]{:S(2)}) copy-start(bf16[4,16,512]{1,2,0:T(8,128)(2,1)} %copy.108) | copy-start | bytes 196612
  41.0 1.3 %collective-permute-start.5 = (bf16[4,16,544]{2,1,0:T(8,128)(2,1)S(1)}, bf16[4,16,544]{2,1,0:T(8,128)(2,1)S(1)}, u32[]{:S(2)}, u32[]{:S(2)}) collective-permute-start(bf16[4,16,544]{2,1,0:T(8,128)(2,1)S(1)} %fusion.14), channel_id=1, source_target_pairs={{0,4},{4,0},{1,5},{5,1},{2,6},{6,2},{3,7},{7,3},{8,12},{12,8},{9,1... | collective-permute-start | bytes 208904 | tf_op jit(solution)/shard_map/ppermute | solution.py:32
  42.4 3.0 %copy-start.1 = (bf16[3,512,544]{2,1,0:T(8,128)(2,1)S(1)}, bf16[3,512,544]{2,1,0:T(8,128)(2,1)}, u32[]{:S(2)}) copy-start(bf16[3,512,544]{2,1,0:T(8,128)(2,1)} %copy-done) | copy-start | bytes 5013508
  42.4 3.0 %copy-start.2 = (f32[4,3]{1,0:T(4,128)S(1)}, f32[4,3]{1,0:T(4,128)}, u32[]{:S(2)}) copy-start(f32[4,3]{1,0:T(4,128)} %coef_ref.5) | copy-start | bytes 148
  45.3 5.1 %copy-start.7 = (bf16[1,144,512]{2,1,0:T(8,128)(2,1)S(1)}, bf16[1,144,512]{2,1,0:T(8,128)(2,1)}, u32[]{:S(2)}) copy-start(bf16[1,144,512]{2,1,0:T(8,128)(2,1)} %get-tuple-element.41) | copy-start | bytes 442372
  50.4 1.2 copy-start.10
  50.4 2.9 %copy-start.9 = (s32[4,1,1,2]{0,3,2,1:T(2,128)S(1)}, s32[4,1,1,2]{0,3,2,1:T(2,128)}, u32[]{:S(2)}) copy-start(s32[4,1,1,2]{0,3,2,1:T(2,128)} %param.15) | copy-start | bytes 100
  53.2 1.2 collective-permute-start.6
  54.4 6.6 %collective-permute-start.7 = (f32[4,12]{1,0:T(4,128)S(1)}, f32[4,12]{1,0:T(4,128)S(1)}, u32[]{:S(2)}, u32[]{:S(2)}) collective-permute-start(f32[4,12]{1,0:T(4,128)S(1)} %fusion.29), channel_id=1, source_target_pairs={{0,1},{1,0},{2,3},{3,2},{4,5},{5,4},{6,7},{7,6},{8,9},{9,8},{10,11... | collective-permute-start | bytes 584 | tf_op jit(solution)/shard_map/ppermute | solution.py:84
  61.0 4.8 %collective-permute-start.8 = (f32[4,12]{1,0:T(4,128)S(1)}, f32[4,12]{1,0:T(4,128)S(1)}, u32[]{:S(2)}, u32[]{:S(2)}) collective-permute-start(f32[4,12]{1,0:T(4,128)S(1)} %add.244), channel_id=1, source_target_pairs={{0,2},{1,3},{2,0},{3,1},{4,6},{5,7},{6,4},{7,5},{8,10},{9,11},{10,... | collective-permute-start | bytes 584 | tf_op jit(solution)/shard_map/ppermute | solution.py:84
  77.9 0.9 copy-start.8
Sparse Core Ops, SparseCore 0:
  78.0 41.2 reduce-scatter.1

commit v12 on v11

--- a/solution.py
+++ b/solution.py
@@ -2,6 +2,8 @@
 
 import jax
 import jax.numpy as jnp
+import ml_dtypes
+import numpy as np
 from jax import lax
 from jax.sharding import PartitionSpec as P
 from jax.experimental import pallas as pl
@@ -45,6 +47,16 @@
     return value
 
 
+def toeplitz_block(size, width, sigma):
+    spread = (np.arange(2 * width + 1) - width).astype(np.float32)
+    scale = np.float32(2.0) * np.float32(sigma) * np.float32(sigma)
+    total = np.float32(np.exp(-spread * spread / scale).astype(np.float32).sum(dtype=np.float32))
+    offset = (np.arange(size)[None, :] - np.arange(size)[:, None] - width).astype(np.float32)
+    values = (np.exp(-offset * offset / scale).astype(np.float32) / total).astype(np.float32)
+    values = np.where(np.abs(offset) <= width, values, np.float32(0.0))
+    return values.astype(ml_dtypes.bfloat16)
+
+
 def band_table(length, width, sigma):
     spread = (jnp.arange(2 * width + 1) - width).astype(jnp.float32)
     curve = jnp.exp(-spread * spread / (2.0 * sigma * sigma))
@@ -145,13 +157,69 @@
 BLOCK = 128
 
 
+def strip_body(off_ref, coef_ref, tb_ref, padded_ref, out_ref):
+    e = pl.program_id(0)
+    rows, tile_len = out_ref.shape[1], out_ref.shape[2]
+    anchor = off_ref[e]
+    base = (anchor // BLOCK) * BLOCK
+    shift = anchor - base
+    window = padded_ref[0, pl.ds(pl.multiple_of(base, BLOCK), 2 * BLOCK), :]
+    pick = (
+        lax.broadcasted_iota(jnp.int32, (rows, 2 * BLOCK), 1)
+        == lax.broadcasted_iota(jnp.int32, (rows, 2 * BLOCK), 0) + shift
+    ).astype(jnp.bfloat16)
+    total = None
+    for kernel in range(len(SIGMA_PARTS)):
+        table = tb_ref[kernel]
+        strip_rows = jnp.dot(pick, table, preferred_element_type=jnp.float32).astype(jnp.bfloat16)
+        across = jnp.dot(strip_rows, window, preferred_element_type=jnp.float32)
+        across = across.astype(jnp.bfloat16)
+        block = table[:BLOCK]
+        cols = [
+            lax.dot_general(
+                across[:, start:start + 2 * BLOCK], block, (((1,), (1,)), ((), ())),
+                preferred_element_type=jnp.float32,
+            )
+            for start in range(0, tile_len, BLOCK)
+        ]
+        term = coef_ref[e, kernel] * jnp.concatenate(cols, 1)
+        total = term if total is None else total + term
+    out_ref[0] = total
+
+
+def strip_tiles(offset, coeffs, tb, padded, tile_len):
+    exp_dev, wide = padded.shape[0], padded.shape[1]
+    nk = tb.shape[0]
+    grid_spec = pltpu.PrefetchScalarGridSpec(
+        num_scalar_prefetch=1,
+        grid=(exp_dev,),
+        in_specs=[
+            pl.BlockSpec(memory_space=pltpu.SMEM),
+            pl.BlockSpec((nk, 2 * BLOCK, 2 * BLOCK), lambda e, off: (0, 0, 0)),
+            pl.BlockSpec((1, wide, wide), lambda e, off: (e, 0, 0)),
+        ],
+        out_specs=pl.BlockSpec((1, STRIP, tile_len), lambda e, off: (e, 0, 0)),
+    )
+    flops = exp_dev * nk * 2 * STRIP * 2 * BLOCK * (2 * BLOCK + wide + tile_len)
+    moved = exp_dev * wide * wide * 2 + exp_dev * STRIP * tile_len * 4
+    return pl.pallas_call(
+        strip_body,
+        grid_spec=grid_spec,
+        out_shape=jax.ShapeDtypeStruct((exp_dev, STRIP, tile_len), jnp.float32),
+        compiler_params=pltpu.CompilerParams(
+            dimension_semantics=("arbitrary",), vmem_limit_bytes=48 * 1024 * 1024
+        ),
+        cost_estimate=pl.CostEstimate(flops=flops, bytes_accessed=moved, transcendentals=0),
+    )(offset, coeffs, tb, padded)
+
+
 def band_body(first, coef_ref, blk_ref, padded_ref, *rest):
     out_ref = rest[-1]
     e = pl.program_id(0) + first
     tile_len = out_ref.shape[1]
     total = None
     for kernel in range(len(SIGMA_PARTS)):
-        block = blk_ref[kernel]
+        block = blk_ref[kernel][:BLOCK]
         rows = [
             jnp.dot(block, padded_ref[0, start:start + 2 * BLOCK, :], preferred_element_type=jnp.float32)
             for start in range(0, tile_len, BLOCK)
@@ -177,7 +245,7 @@
     moved = count * wide * wide * 2 + count * tile_len * tile_len * 4
     in_specs = [
         pl.BlockSpec(memory_space=pltpu.SMEM),
-        pl.BlockSpec((nk, BLOCK, 2 * BLOCK), lambda e: (0, 0, 0)),
+        pl.BlockSpec((nk, 2 * BLOCK, 2 * BLOCK), lambda e: (0, 0, 0)),
         pl.BlockSpec((1, wide, wide), lambda e: (e + first, 0, 0)),
     ]
     operands = [coeffs, blocks, padded]
@@ -329,14 +397,12 @@
     )
     own_patch = jnp.take(picked_all, visit_pos, axis=2).astype(jnp.float32)
     denominator = jnp.sum(own_patch).reshape(1)
-    stacked_tables = jnp.stack([band_table(tile_len, HALO, HALO * part) for part in SIGMA_PARTS])
-    strip_tables = jnp.einsum(
-        "esr,krj->eksj", pick_rows, stacked_tables, preferred_element_type=jnp.float32
-    ).astype(jnp.bfloat16)
-    nearby = conv_tiles(coeffs, strip_tables, stacked_tables, padded, True)
     spare = 2 * BLOCK + tile_len - BLOCK - padded.shape[1]
     roomy = jnp.pad(padded, ((0, 0), (0, spare), (0, spare)))
-    blocks = stacked_tables[:, :BLOCK, : 2 * BLOCK]
+    blocks = jnp.asarray(
+        np.stack([toeplitz_block(2 * BLOCK, HALO, HALO * part) for part in SIGMA_PARTS])
+    )
+    nearby = strip_tiles(offset, coeffs, blocks, roomy, tile_len)
     half = exp_dev // 2
     matched = band_tiles(coeffs, blocks, roomy, tile_len, 0, half, None)
     matched = band_tiles(coeffs, blocks, roomy, tile_len, half, exp_dev - half, matched)

time: 130 us -> 127 us (0.977)
  other arithmetic: 24.1 us -> 19.9 us
  waiting for transfers between devices: 40.3 us -> 42.7 us
  starting transfers between devices: 16.4 us -> 18 us
  local copies, waits for them, and re-layouts: 6.67 us -> 5.17 us
    convert_element_type x2 -> x0, other arithmetic: 3.49 us -> none  [band_table(): return jnp.where(jnp.abs(offset) <= width, values, 0.0).astype(jnp.bfloat16)]
    concatenate x1, other arithmetic: 2.92 us -> 6.26 us  [extended(): value = jnp.concatenate([before, value, after], axis=dim)]
    ppermute x3, starting transfers between devices: 1.95 us -> 4.22 us  [butterfly_sum(): values = jax.tree.map(lambda v: v + lax.ppermute(v, axis, pairs), values)]
    reduce_sum x3 -> x0, other arithmetic: 1.91 us -> none  [band_table(): total = jnp.sum(curve)]
    reduce_scatter x1, waiting for transfers between devices: 38.9 us -> 40.6 us  [shards(): lax.psum_scatter(partial_sum, 'visit', scatter_dimension=0, tiled=True)]
  transfers between devices with their start and end apart: 10 -> 10, of which waited for: 3 -> 4; matrix products, arithmetic and copies ran while one was open for 14% -> 9% of each run, Pallas kernels for 11% -> 12%
where the time goes in v12:
time: 127 us
  waiting for transfers between devices  42.7 us (34%)
  Pallas kernels  24.3 us (19%)
  other arithmetic  19.9 us (16%)
  starting transfers between devices  18 us (14%)
  between operations  14.3 us (11%)
  local copies, waits for them, and re-layouts  5.17 us (4%)
  matrix products  2.49 us (2%)
    reduce_scatter x1, waiting for transfers between devices, shards(): lax.psum_scatter(partial_sum, 'visit', scatter_dimension=0, tiled=True)  40.6 us
    pallas_call x2, Pallas kernels, band_tiles(): pl.pallas_call(functools.partial(band_body, first), grid=(count,), in_spe...  9.66 us
    pallas_call x1, Pallas kernels, warp_tiles(): pl.pallas_call(warp_body, grid_spec=grid_spec, out_shape=jax.ShapeDtypeSt...  9.21 us
    ppermute x3, starting transfers between devices, shards(): received.append(lax.ppermute(payload, 'visit', pairs))  7.86 us
    concatenate x1, other arithmetic, extended(): value = jnp.concatenate([before, value, after], axis=dim)  6.26 us
    pallas_call x1, Pallas kernels, strip_tiles(): pl.pallas_call(strip_body, grid_spec=grid_spec, out_shape=jax.ShapeDtypeS...  5.43 us
    ppermute x1, starting transfers between devices, extended(): before = lax.ppermute(last, axis, up)  4.55 us
    ppermute x3, starting transfers between devices, butterfly_sum(): values = jax.tree.map(lambda v: v + lax.ppermute(v, axis, pairs), values)  4.22 us
  transfers between devices with their start and end apart: 10, of which 4 were waited for; matrix products, arithmetic and copies ran while one was open for 9% of the time, Pallas kernels for 12%

profile of v12, /device:TPU:0, one launch (start us, length us, event | category | flops | bytes accessed | tf_op | source)
XLA Modules:
  0.0 127.0 jit_solution(4456893640399713319)
XLA Ops:
  7.2 0.9 iota_compare_fusion.5
  8.1 0.8 slice_bitcast_fusion.2
  8.9 0.8 fusion.21
  9.7 1.3 %fusion.30 = (f32[4,4]{1,0:T(4,128)}, bf16[4,4]{1,0:T(4,128)(2,1)S(1)}) fusion(pred[4,4]{1,0:T(4,128)(4,1)S(1)} %fusion.21, bf16[4]{0:T(256)(128)(2,1)} %bitcast.106), kind=kLoop, calls=%fused_computation.99 | loop fusion | flops 32 | bytes 120 | tf_op jit(solution)/shard_map/convert_element_type | solution.py:447
  11.3 2.1 %convolution_convert_fusion = bf16[4,32,512]{2,1,0:T(8,128)(2,1)S(1)} fusion(bf16[4,512,512]{2,1,0:T(8,128)(2,1)} %param.11, s32[4]{0:T(128)S(1)} %get-tuple-element.35.off_ref), kind=kOutput, calls=%fused_computation.17 | convolution fusion | flops 67305472 | bytes 2228240 | tf_op jit(solution)/shard_map/esr,erl->esl/dot_general | solution.py:364
  14.1 4.0 %collective-permute-start.1 = (bf16[144,512]{1,0:T(8,128)(2,1)}, bf16[144,512]{1,0:T(8,128)(2,1)}, u32[]{:S(2)}, u32[]{:S(2)}) collective-permute-start(bf16[144,512]{1,0:T(8,128)(2,1)} %get-tuple-element.42), channel_id=1, source_target_pairs={{0,16},{8,24},{16,0},{24,8},{1,17},{9,25},{17,1},{25,9},{2,18},{10... | collective-permute-start | bytes 442376 | tf_op jit(solution)/shard_map/ppermute | solution.py:384
  18.1 1.6 %collective-permute-start = (bf16[144,512]{1,0:T(8,128)(2,1)}, bf16[144,512]{1,0:T(8,128)(2,1)}, u32[]{:S(2)}, u32[]{:S(2)}) collective-permute-start(bf16[144,512]{1,0:T(8,128)(2,1)} %get-tuple-element.42), channel_id=1, source_target_pairs={{0,8},{8,16},{16,24},{24,0},{1,9},{9,17},{17,25},{25,1},{2,10},{10... | collective-permute-start | bytes 442376 | tf_op jit(solution)/shard_map/ppermute | solution.py:384
  19.7 2.2 %collective-permute-start.2 = (bf16[144,512]{1,0:T(8,128)(2,1)}, bf16[144,512]{1,0:T(8,128)(2,1)}, u32[]{:S(2)}, u32[]{:S(2)}) collective-permute-start(bf16[144,512]{1,0:T(8,128)(2,1)} %get-tuple-element.42), channel_id=1, source_target_pairs={{0,24},{8,0},{16,8},{24,16},{1,25},{9,1},{17,9},{25,17},{2,26},{10... | collective-permute-start | bytes 442376 | tf_op jit(solution)/shard_map/ppermute | solution.py:384
  22.4 1.3 %collective-permute-start.4 = (bf16[4,8192]{1,0:T(4,128)(2,1)S(1)}, bf16[4,8192]{1,0:T(4,128)(2,1)S(1)}, u32[]{:S(2)}, u32[]{:S(2)}) collective-permute-start(bf16[4,8192]{1,0:T(4,128)(2,1)S(1)} %bitcast.81), channel_id=1, source_target_pairs={{1,0},{2,1},{3,2},{5,4},{6,5},{7,6},{9,8},{10,9},{11,10},{13,12},{... | collective-permute-start | bytes 196616 | tf_op jit(solution)/shard_map/ppermute | solution.py:42
  24.0 4.5 %collective-permute-start.3 = (bf16[4,8192]{1,0:T(4,128)(2,1)S(1)}, bf16[4,8192]{1,0:T(4,128)(2,1)S(1)}, u32[]{:S(2)}, u32[]{:S(2)}) collective-permute-start(bf16[4,8192]{1,0:T(4,128)(2,1)S(1)} %bitcast.83), channel_id=1, source_target_pairs={{0,1},{1,2},{2,3},{4,5},{5,6},{6,7},{8,9},{9,10},{10,11},{12,13},{... | collective-permute-start | bytes 196616 | tf_op jit(solution)/shard_map/ppermute | solution.py:41
  31.2 1.3 collective-permute-done.5
  32.8 6.3 %fusion.8.padded_ref = bf16[4,640,640]{2,1,0:T(8,128)(2,1)S(1)} fusion(bf16[4,16,544]{2,1,0:T(8,128)(2,1)S(1)} %get-tuple-element.44, bf16[4,16,544]{2,1,0:T(8,128)(2,1)S(1)} %get-tuple-element.43, bf16[4,512,16]{2,1,0:T(8,128)(2,1)} %bitcast.73, bf16[4,512,512]{2,1,0:T(8,128)(2,1)S(1)} %copy-done.4, bf16[4,512,16]{2,1,0:T(8,128)(2,1)} %bitcast.71), kind=kLoop, calls=%fused_computation.10 | loop fusion | flops 37683200 | bytes 5644288 | tf_op jit(solution)/shard_map/concatenate | solution.py:46
  39.1 5.4 %shard_map.104 = f32[4,32,512]{2,1,0:T(8,128)S(1)} custom-call(s32[4]{0:T(128)S(1)} %get-tuple-element.35.off_ref, f32[4,3]{1,0:T(4,128)S(1)} %copy-done.2, bf16[3,256,256]{2,1,0:T(8,128)(2,1)S(1)} %copy-done, bf16[4,640,640]{2,1,0:T(8,128)(2,1)S(1)} %fusion.8.padded_ref), custom_call_target="tpu_custom_call" | custom-call | flops 276824064 | bytes 3538944 | tf_op jit(solution)/shard_map/pallas_call | solution.py:205
  44.6 1.1 pad_maximum_fusion
  48.5 2.4 %collective-permute-start.7 = (f32[4,12]{1,0:T(4,128)S(1)}, f32[4,12]{1,0:T(4,128)S(1)}, u32[]{:S(2)}, u32[]{:S(2)}) collective-permute-start(f32[4,12]{1,0:T(4,128)S(1)} %fusion.33), channel_id=1, source_target_pairs={{0,1},{1,0},{2,3},{3,2},{4,5},{5,4},{6,7},{7,6},{8,9},{9,8},{10,11... | collective-permute-start | bytes 584 | tf_op jit(solution)/shard_map/ppermute | solution.py:96
  50.9 1.0 copy-done.1
  51.9 4.8 %shard_map.105.rest_0_ = f32[4,512,512]{2,1,0:T(8,128)} custom-call(f32[4,3]{1,0:T(4,128)S(1)} %copy-done.2, bf16[3,256,256]{2,1,0:T(8,128)(2,1)S(1)} %copy-done.1, bf16[4,640,640]{2,1,0:T(8,128)(2,1)S(1)} %fusion.8.padded_ref), custom_call_target="tpu_custom_call" | custom-call | flops 1811939328 | bytes 3735552 | tf_op jit(solution)/shard_map/pallas_call | solution.py:257
  56.8 1.8 %collective-permute-start.8 = (f32[4,12]{1,0:T(4,128)S(1)}, f32[4,12]{1,0:T(4,128)S(1)}, u32[]{:S(2)}, u32[]{:S(2)}) collective-permute-start(f32[4,12]{1,0:T(4,128)S(1)} %add.227), channel_id=1, source_target_pairs={{0,2},{1,3},{2,0},{3,1},{4,6},{5,7},{6,4},{7,5},{8,10},{9,11},{10,... | collective-permute-start | bytes 584 | tf_op jit(solution)/shard_map/ppermute | solution.py:96
  58.6 4.8 %shard_map.106.matched_ref = f32[4,512,512]{2,1,0:T(8,128)} custom-call(f32[4,3]{1,0:T(4,128)S(1)} %copy-done.2, bf16[3,256,256]{2,1,0:T(8,128)(2,1)S(1)} %copy-done.1, bf16[4,640,640]{2,1,0:T(8,128)(2,1)S(1)} %fusion.8.padded_ref, f32[4,512,512]{2,1,0:T(8,128)} %shard_map.105.rest_0_), custom_call_target="tpu_custom_call", output_to_operand_aliasing={{}: (3, {})} | custom-call | flops 1811939328 | bytes 3735552 | tf_op jit(solution)/shard_map/pallas_call | solution.py:257
  63.6 1.1 custom-call.4
  65.8 9.2 %shard_map.107 = bf16[4,512,512]{2,1,0:T(8,128)(2,1)} custom-call(s32[4,2]{1,0:T(4,128)} %copy.119.idx_ref, f32[4,3]{1,0:T(4,128)} %pad_maximum_fusion.9.plane_ref, f32[4,4]{1,0:T(4,128)} %get-tuple-element.54.pick_ref, f32[1,512]{1,0:T(1,128)} %multiply_add_fusion.1.xrow_ref, f32[512,1]{1,0:T(8,128)} %multiply_add_fusion.ycol_ref, ...), custom_call_target="tpu_custom_call" | custom-call | flops 2147483648 | bytes 10485760 | tf_op jit(solution)/shard_map/pallas_call | solution.py:322
  76.0 0.8 convert_reduce_fusion
  76.7 40.6 %reduce-scatter.2.cloned.1.call-done = bf16[1,512,512]{2,1,0:T(8,128)(2,1)} async-done(((bf16[4,512,512]{2,1,0:T(8,128)(2,1)}), bf16[1,512,512]{2,1,0:T(8,128)(2,1)}) %reduce-scatter.2.cloned.1.call-update) | async-done | bytes 524304 | tf_op jit(solution)/shard_map/reduce_scatter | solution.py:450
  117.3 2.8 %convert_divide_fusion = f32[1,512,512]{2,1,0:T(8,128)} fusion(bf16[1,512,512]{2,1,0:T(8,128)(2,1)} %reduce-scatter.2.cloned.1.call-done, f32[]{:T(128)} %convert_reduce_fusion), kind=kLoop, calls=%fused_computation.18 | loop fusion | flops 524288 | bytes 1572868 | tf_op jit(solution)/shard_map/div | solution.py:453
  (83 shorter events, 9.7 us)
Async XLA Ops:
  7.2 14.8 %copy-start.3 = (bf16[4,512,512]{2,1,0:T(8,128)(2,1)S(1)}, bf16[4,512,512]{2,1,0:T(8,128)(2,1)}, u32[]{:S(2)}) copy-start(bf16[4,512,512]{2,1,0:T(8,128)(2,1)} %param.11) | copy-start | bytes 6291460
  7.2 110.1 %reduce-scatter.2.cloned.1.call-start = ((), (), s32[]{:S(2)}) async-start(), calls=%async_computation.1 | async-start | bytes 2621440 | tf_op jit(solution)/shard_map/reduce_scatter | solution.py:450
  14.1 30.5 %collective-permute-start.1 = (bf16[144,512]{1,0:T(8,128)(2,1)}, bf16[144,512]{1,0:T(8,128)(2,1)}, u32[]{:S(2)}, u32[]{:S(2)}) collective-permute-start(bf16[144,512]{1,0:T(8,128)(2,1)} %get-tuple-element.42), channel_id=1, source_target_pairs={{0,16},{8,24},{16,0},{24,8},{1,17},{9,25},{17,1},{25,9},{2,18},{10... | collective-permute-start | bytes 442376 | tf_op jit(solution)/shard_map/ppermute | solution.py:384
  18.1 26.4 %collective-permute-start = (bf16[144,512]{1,0:T(8,128)(2,1)}, bf16[144,512]{1,0:T(8,128)(2,1)}, u32[]{:S(2)}, u32[]{:S(2)}) collective-permute-start(bf16[144,512]{1,0:T(8,128)(2,1)} %get-tuple-element.42), channel_id=1, source_target_pairs={{0,8},{8,16},{16,24},{24,0},{1,9},{9,17},{17,25},{25,1},{2,10},{10... | collective-permute-start | bytes 442376 | tf_op jit(solution)/shard_map/ppermute | solution.py:384
  19.7 24.9 %collective-permute-start.2 = (bf16[144,512]{1,0:T(8,128)(2,1)}, bf16[144,512]{1,0:T(8,128)(2,1)}, u32[]{:S(2)}, u32[]{:S(2)}) collective-permute-start(bf16[144,512]{1,0:T(8,128)(2,1)} %get-tuple-element.42), channel_id=1, source_target_pairs={{0,24},{8,0},{16,8},{24,16},{1,25},{9,1},{17,9},{25,17},{2,26},{10... | collective-permute-start | bytes 442376 | tf_op jit(solution)/shard_map/ppermute | solution.py:384
  22.4 7.6 %collective-permute-start.4 = (bf16[4,8192]{1,0:T(4,128)(2,1)S(1)}, bf16[4,8192]{1,0:T(4,128)(2,1)S(1)}, u32[]{:S(2)}, u32[]{:S(2)}) collective-permute-start(bf16[4,8192]{1,0:T(4,128)(2,1)S(1)} %bitcast.81), channel_id=1, source_target_pairs={{1,0},{2,1},{3,2},{5,4},{6,5},{7,6},{9,8},{10,9},{11,10},{13,12},{... | collective-permute-start | bytes 196616 | tf_op jit(solution)/shard_map/ppermute | solution.py:42
  24.0 6.4 %collective-permute-start.3 = (bf16[4,8192]{1,0:T(4,128)(2,1)S(1)}, bf16[4,8192]{1,0:T(4,128)(2,1)S(1)}, u32[]{:S(2)}, u32[]{:S(2)}) collective-permute-start(bf16[4,8192]{1,0:T(4,128)(2,1)S(1)} %bitcast.83), channel_id=1, source_target_pairs={{0,1},{1,2},{2,3},{4,5},{5,6},{6,7},{8,9},{9,10},{10,11},{12,13},{... | collective-permute-start | bytes 196616 | tf_op jit(solution)/shard_map/ppermute | solution.py:41
  30.7 1.8 %copy-start.5 = (bf16[4,16,512]{1,2,0:T(8,128)(2,1)}, bf16[4,16,512]{1,2,0:T(8,128)(2,1)S(1)}, u32[]{:S(2)}) copy-start(bf16[4,16,512]{1,2,0:T(8,128)(2,1)S(1)} %copy.99) | copy-start | bytes 196612
  31.0 1.5 %copy-start.6 = (bf16[4,16,512]{1,2,0:T(8,128)(2,1)}, bf16[4,16,512]{1,2,0:T(8,128)(2,1)S(1)}, u32[]{:S(2)}) copy-start(bf16[4,16,512]{1,2,0:T(8,128)(2,1)S(1)} %copy.101) | copy-start | bytes 196612
  31.0 1.8 %copy-start.4 = (bf16[4,512,512]{2,1,0:T(8,128)(2,1)S(1)}, bf16[4,512,512]{2,1,0:T(8,128)(2,1)}, u32[]{:S(2)}) copy-start(bf16[4,512,512]{2,1,0:T(8,128)(2,1)} %param.11) | copy-start | bytes 6291460
  31.2 1.3 %collective-permute-start.5 = (bf16[4,16,544]{2,1,0:T(8,128)(2,1)S(1)}, bf16[4,16,544]{2,1,0:T(8,128)(2,1)S(1)}, u32[]{:S(2)}, u32[]{:S(2)}) collective-permute-start(bf16[4,16,544]{2,1,0:T(8,128)(2,1)S(1)} %fusion.18), channel_id=1, source_target_pairs={{0,4},{4,0},{1,5},{5,1},{2,6},{6,2},{3,7},{7,3},{8,12},{12,8},{9,1... | collective-permute-start | bytes 208904 | tf_op jit(solution)/shard_map/ppermute | solution.py:34
  32.8 6.3 %copy-start = (bf16[3,256,256]{2,1,0:T(8,128)(2,1)S(1)}, bf16[3,256,256]{2,1,0:T(8,128)(2,1)}, u32[]{:S(2)}) copy-start(bf16[3,256,256]{2,1,0:T(8,128)(2,1)} %constant.159.clone.tb_ref.blk_ref) | copy-start | bytes 1179652
  32.8 6.3 %copy-start.2 = (f32[4,3]{1,0:T(4,128)S(1)}, f32[4,3]{1,0:T(4,128)}, u32[]{:S(2)}) copy-start(f32[4,3]{1,0:T(4,128)} %coef_ref.5) | copy-start | bytes 148
  39.1 8.2 %copy-start.7 = (s32[4,1,1,2]{0,3,2,1:T(2,128)S(1)}, s32[4,1,1,2]{0,3,2,1:T(2,128)}, u32[]{:S(2)}) copy-start(s32[4,1,1,2]{0,3,2,1:T(2,128)} %param.16) | copy-start | bytes 100
  47.3 1.2 collective-permute-start.6
  48.5 8.2 %collective-permute-start.7 = (f32[4,12]{1,0:T(4,128)S(1)}, f32[4,12]{1,0:T(4,128)S(1)}, u32[]{:S(2)}, u32[]{:S(2)}) collective-permute-start(f32[4,12]{1,0:T(4,128)S(1)} %fusion.33), channel_id=1, source_target_pairs={{0,1},{1,0},{2,3},{3,2},{4,5},{5,4},{6,7},{7,6},{8,9},{9,8},{10,11... | collective-permute-start | bytes 584 | tf_op jit(solution)/shard_map/ppermute | solution.py:96
  50.9 1.0 copy-start.1
  56.8 6.6 %collective-permute-start.8 = (f32[4,12]{1,0:T(4,128)S(1)}, f32[4,12]{1,0:T(4,128)S(1)}, u32[]{:S(2)}, u32[]{:S(2)}) collective-permute-start(f32[4,12]{1,0:T(4,128)S(1)} %add.227), channel_id=1, source_target_pairs={{0,2},{1,3},{2,0},{3,1},{4,6},{5,7},{6,4},{7,5},{8,10},{9,11},{10,... | collective-permute-start | bytes 584 | tf_op jit(solution)/shard_map/ppermute | solution.py:96
Sparse Core Ops, SparseCore 0:
  75.2 42.0 reduce-scatter.1

commit v13 on v12

--- a/solution.py
+++ b/solution.py
@@ -160,10 +160,12 @@
 def strip_body(off_ref, coef_ref, tb_ref, padded_ref, out_ref):
     e = pl.program_id(0)
     rows, tile_len = out_ref.shape[1], out_ref.shape[2]
+    wide = padded_ref.shape[1]
+    windows = [(start, min(2 * BLOCK, wide - start)) for start in range(0, tile_len, BLOCK)]
     anchor = off_ref[e]
-    base = (anchor // BLOCK) * BLOCK
+    base = jnp.minimum((anchor // BLOCK) * BLOCK, wide - 2 * BLOCK)
     shift = anchor - base
-    window = padded_ref[0, pl.ds(pl.multiple_of(base, BLOCK), 2 * BLOCK), :]
+    window = padded_ref[0, pl.ds(pl.multiple_of(base, 16), 2 * BLOCK), :]
     pick = (
         lax.broadcasted_iota(jnp.int32, (rows, 2 * BLOCK), 1)
         == lax.broadcasted_iota(jnp.int32, (rows, 2 * BLOCK), 0) + shift
@@ -177,10 +179,10 @@
         block = table[:BLOCK]
         cols = [
             lax.dot_general(
-                across[:, start:start + 2 * BLOCK], block, (((1,), (1,)), ((), ())),
+                across[:, start:start + reach], block[:, :reach], (((1,), (1,)), ((), ())),
                 preferred_element_type=jnp.float32,
             )
-            for start in range(0, tile_len, BLOCK)
+            for start, reach in windows
         ]
         term = coef_ref[e, kernel] * jnp.concatenate(cols, 1)
         total = term if total is None else total + term
@@ -217,20 +219,25 @@
     out_ref = rest[-1]
     e = pl.program_id(0) + first
     tile_len = out_ref.shape[1]
+    wide = padded_ref.shape[1]
+    windows = [(start, min(2 * BLOCK, wide - start)) for start in range(0, tile_len, BLOCK)]
     total = None
     for kernel in range(len(SIGMA_PARTS)):
         block = blk_ref[kernel][:BLOCK]
         rows = [
-            jnp.dot(block, padded_ref[0, start:start + 2 * BLOCK, :], preferred_element_type=jnp.float32)
-            for start in range(0, tile_len, BLOCK)
+            jnp.dot(
+                block[:, :reach], padded_ref[0, start:start + reach, :],
+                preferred_element_type=jnp.float32,
+            )
+            for start, reach in windows
         ]
         across = jnp.concatenate(rows, 0).astype(jnp.bfloat16)
         cols = [
             lax.dot_general(
-                across[:, start:start + 2 * BLOCK], block, (((1,), (1,)), ((), ())),
+                across[:, start:start + reach], block[:, :reach], (((1,), (1,)), ((), ())),
                 preferred_element_type=jnp.float32,
             )
-            for start in range(0, tile_len, BLOCK)
+            for start, reach in windows
         ]
         term = coef_ref[e, kernel] * jnp.concatenate(cols, 1)
         total = term if total is None else total + term
@@ -397,8 +404,7 @@
     )
     own_patch = jnp.take(picked_all, visit_pos, axis=2).astype(jnp.float32)
     denominator = jnp.sum(own_patch).reshape(1)
-    spare = 2 * BLOCK + tile_len - BLOCK - padded.shape[1]
-    roomy = jnp.pad(padded, ((0, 0), (0, spare), (0, spare)))
+    roomy = padded
     blocks = jnp.asarray(
         np.stack([toeplitz_block(2 * BLOCK, HALO, HALO * part) for part in SIGMA_PARTS])
     )

time: 127 us -> 123 us (0.969)
  other arithmetic: 19.9 us -> 17.5 us
    concatenate x1, other arithmetic: 6.26 us -> 2.9 us  [extended(): value = jnp.concatenate([before, value, after], axis=dim)]
  transfers between devices with their start and end apart: 10 -> 10, of which waited for: 4 -> 3; matrix products, arithmetic and copies ran while one was open for 9% -> 7% of each run, Pallas kernels for 12% -> 12%
where the time goes in v13:
time: 123 us; the launch traced here: 122 us
  waiting for transfers between devices  41.7 us (34%)
  Pallas kernels  24.5 us (20%)
  other arithmetic  17.5 us (14%)
  starting transfers between devices  17.4 us (14%)
  between operations  14.4 us (12%)
  local copies, waits for them, and re-layouts  4.19 us (3%)
  matrix products  2.49 us (2%)
    reduce_scatter x1, waiting for transfers between devices, shards(): lax.psum_scatter(partial_sum, 'visit', scatter_dimension=0, tiled=True)  39.9 us
    pallas_call x2, Pallas kernels, band_tiles(): pl.pallas_call(functools.partial(band_body, first), grid=(count,), in_spe...  9.66 us
    pallas_call x1, Pallas kernels, warp_tiles(): pl.pallas_call(warp_body, grid_spec=grid_spec, out_shape=jax.ShapeDtypeSt...  9.45 us
    ppermute x3, starting transfers between devices, shards(): received.append(lax.ppermute(payload, 'visit', pairs))  7.86 us
    pallas_call x1, Pallas kernels, strip_tiles(): pl.pallas_call(strip_body, grid_spec=grid_spec, out_shape=jax.ShapeDtypeS...  5.43 us
    ppermute x1, starting transfers between devices, extended(): before = lax.ppermute(last, axis, up)  4.55 us
    ppermute x3, starting transfers between devices, butterfly_sum(): values = jax.tree.map(lambda v: v + lax.ppermute(v, axis, pairs), values)  3.64 us
    concatenate x1, other arithmetic, extended(): value = jnp.concatenate([before, value, after], axis=dim)  2.9 us
  transfers between devices with their start and end apart: 10, of which 3 were waited for; matrix products, arithmetic and copies ran while one was open for 7% of the time, Pallas kernels for 12%

profile of v13, /device:TPU:0, one launch (start us, length us, event | category | flops | bytes accessed | tf_op | source)
XLA Modules:
  0.0 122.2 jit_solution(1934162949560801144)
XLA Ops:
  7.2 0.9 iota_compare_fusion.3
  8.1 0.8 slice_bitcast_fusion.2
  8.9 0.8 fusion.6
  9.7 1.3 %fusion.15 = (f32[4,4]{1,0:T(4,128)}, bf16[4,4]{1,0:T(4,128)(2,1)S(1)}) fusion(pred[4,4]{1,0:T(4,128)(4,1)S(1)} %fusion.6, bf16[4]{0:T(256)(128)(2,1)} %bitcast.108), kind=kLoop, calls=%fused_computation.83 | loop fusion | flops 32 | bytes 120 | tf_op jit(solution)/shard_map/convert_element_type | solution.py:453
  11.3 2.1 %convolution_convert_fusion = bf16[4,32,512]{2,1,0:T(8,128)(2,1)S(1)} fusion(bf16[4,512,512]{2,1,0:T(8,128)(2,1)} %param.11, s32[4]{0:T(128)S(1)} %get-tuple-element.35.off_ref), kind=kOutput, calls=%fused_computation.1 | convolution fusion | flops 67305472 | bytes 2228240 | tf_op jit(solution)/shard_map/esr,erl->esl/dot_general | solution.py:371
  14.1 4.0 %collective-permute-start.1 = (bf16[144,512]{1,0:T(8,128)(2,1)}, bf16[144,512]{1,0:T(8,128)(2,1)S(1)}, u32[]{:S(2)}, u32[]{:S(2)}) collective-permute-start(bf16[144,512]{1,0:T(8,128)(2,1)} %get-tuple-element.42), channel_id=1, source_target_pairs={{0,16},{8,24},{16,0},{24,8},{1,17},{9,25},{17,1},{25,9},{2,18},{10... | collective-permute-start | bytes 442376 | tf_op jit(solution)/shard_map/ppermute | solution.py:391
  18.1 1.6 %collective-permute-start = (bf16[144,512]{1,0:T(8,128)(2,1)}, bf16[144,512]{1,0:T(8,128)(2,1)}, u32[]{:S(2)}, u32[]{:S(2)}) collective-permute-start(bf16[144,512]{1,0:T(8,128)(2,1)} %get-tuple-element.42), channel_id=1, source_target_pairs={{0,8},{8,16},{16,24},{24,0},{1,9},{9,17},{17,25},{25,1},{2,10},{10... | collective-permute-start | bytes 442376 | tf_op jit(solution)/shard_map/ppermute | solution.py:391
  19.7 2.2 %collective-permute-start.2 = (bf16[144,512]{1,0:T(8,128)(2,1)}, bf16[144,512]{1,0:T(8,128)(2,1)}, u32[]{:S(2)}, u32[]{:S(2)}) collective-permute-start(bf16[144,512]{1,0:T(8,128)(2,1)} %get-tuple-element.42), channel_id=1, source_target_pairs={{0,24},{8,0},{16,8},{24,16},{1,25},{9,1},{17,9},{25,17},{2,26},{10... | collective-permute-start | bytes 442376 | tf_op jit(solution)/shard_map/ppermute | solution.py:391
  22.4 1.3 %collective-permute-start.4 = (bf16[4,8192]{1,0:T(4,128)(2,1)S(1)}, bf16[4,8192]{1,0:T(4,128)(2,1)S(1)}, u32[]{:S(2)}, u32[]{:S(2)}) collective-permute-start(bf16[4,8192]{1,0:T(4,128)(2,1)S(1)} %bitcast.83), channel_id=1, source_target_pairs={{1,0},{2,1},{3,2},{5,4},{6,5},{7,6},{9,8},{10,9},{11,10},{13,12},{... | collective-permute-start | bytes 196616 | tf_op jit(solution)/shard_map/ppermute | solution.py:42
  24.0 4.5 %collective-permute-start.3 = (bf16[4,8192]{1,0:T(4,128)(2,1)S(1)}, bf16[4,8192]{1,0:T(4,128)(2,1)S(1)}, u32[]{:S(2)}, u32[]{:S(2)}) collective-permute-start(bf16[4,8192]{1,0:T(4,128)(2,1)S(1)} %bitcast.85), channel_id=1, source_target_pairs={{0,1},{1,2},{2,3},{4,5},{5,6},{6,7},{8,9},{9,10},{10,11},{12,13},{... | collective-permute-start | bytes 196616 | tf_op jit(solution)/shard_map/ppermute | solution.py:41
  29.1 0.8 multiply_add_fusion.ycol_ref
  31.9 1.3 %collective-permute-done.5 = bf16[4,16,544]{2,1,0:T(8,128)(2,1)S(1)} collective-permute-done((bf16[4,16,544]{2,1,0:T(8,128)(2,1)S(1)}, bf16[4,16,544]{2,1,0:T(8,128)(2,1)S(1)}, u32[]{:S(2)}, u32[]{:S(2)}) %collective-permute-start.5) | collective-permute-done | bytes 69664 | tf_op jit(solution)/shard_map/ppermute | solution.py:34
  33.5 2.9 %pad_maximum_fusion.padded_ref = bf16[4,544,544]{2,1,0:T(8,128)(2,1)S(1)} fusion(bf16[4,16,544]{2,1,0:T(8,128)(2,1)S(1)} %get-tuple-element.44, bf16[4,512,16]{2,1,0:T(8,128)(2,1)} %bitcast.73, bf16[4,512,512]{2,1,0:T(8,128)(2,1)S(1)} %copy-done.3, bf16[4,512,16]{2,1,0:T(8,128)(2,1)} %bitcast.71, bf16[4,16,544]{2,1,0:T(8,128)(2,1)S(1)} %get-tuple-element.43), kind=kLoop, calls=%fused_computation | loop fusion | flops 11837440 | bytes 4734976 | tf_op jit(solution)/shard_map/concatenate | solution.py:46
  36.4 5.4 %shard_map.104 = f32[4,32,512]{2,1,0:T(8,128)S(1)} custom-call(s32[4]{0:T(128)S(1)} %get-tuple-element.35.off_ref, f32[4,3]{1,0:T(4,128)S(1)} %copy-done.1, bf16[3,256,256]{2,1,0:T(8,128)(2,1)S(1)} %copy-done, bf16[4,544,544]{2,1,0:T(8,128)(2,1)S(1)} %pad_maximum_fusion.padded_ref), custom_call_target="tpu_custom_call" | custom-call | flops 257949696 | bytes 2629632 | tf_op jit(solution)/shard_map/pallas_call | solution.py:207
  41.9 1.1 pad_maximum_fusion.1
  45.8 2.4 %collective-permute-start.7 = (f32[4,12]{1,0:T(4,128)S(1)}, f32[4,12]{1,0:T(4,128)S(1)}, u32[]{:S(2)}, u32[]{:S(2)}) collective-permute-start(f32[4,12]{1,0:T(4,128)S(1)} %fusion.18), channel_id=1, source_target_pairs={{0,1},{1,0},{2,3},{3,2},{4,5},{5,4},{6,7},{7,6},{8,9},{9,8},{10,11... | collective-permute-start | bytes 584 | tf_op jit(solution)/shard_map/ppermute | solution.py:96
  48.2 4.9 %shard_map.105.rest_0_ = f32[4,512,512]{2,1,0:T(8,128)} custom-call(f32[4,3]{1,0:T(4,128)S(1)} %copy-done.1, bf16[3,256,256]{2,1,0:T(8,128)(2,1)S(1)} %copy-done, bf16[4,544,544]{2,1,0:T(8,128)(2,1)S(1)} %pad_maximum_fusion.padded_ref), custom_call_target="tpu_custom_call" | custom-call | flops 1660944384 | bytes 3280896 | tf_op jit(solution)/shard_map/pallas_call | solution.py:264
  53.0 1.2 %collective-permute-start.8 = (f32[4,12]{1,0:T(4,128)S(1)}, f32[4,12]{1,0:T(4,128)S(1)}, u32[]{:S(2)}, u32[]{:S(2)}) collective-permute-start(f32[4,12]{1,0:T(4,128)S(1)} %add.225), channel_id=1, source_target_pairs={{0,2},{1,3},{2,0},{3,1},{4,6},{5,7},{6,4},{7,5},{8,10},{9,11},{10,... | collective-permute-start | bytes 584 | tf_op jit(solution)/shard_map/ppermute | solution.py:96
  54.3 4.8 %shard_map.106.matched_ref = f32[4,512,512]{2,1,0:T(8,128)} custom-call(f32[4,3]{1,0:T(4,128)S(1)} %copy-done.1, bf16[3,256,256]{2,1,0:T(8,128)(2,1)S(1)} %copy-done, bf16[4,544,544]{2,1,0:T(8,128)(2,1)S(1)} %pad_maximum_fusion.padded_ref, f32[4,512,512]{2,1,0:T(8,128)} %shard_map.105.rest_0_), custom_call_target="tpu_custom_call", output_to_operand_aliasing={{}: (3, {})} | custom-call | flops 1660944384 | bytes 3280896 | tf_op jit(solution)/shard_map/pallas_call | solution.py:264
  59.3 1.1 custom-call.4
  61.5 9.4 %shard_map.107 = bf16[4,512,512]{2,1,0:T(8,128)(2,1)} custom-call(s32[4,2]{1,0:T(4,128)} %copy.119.idx_ref, f32[4,3]{1,0:T(4,128)} %pad_maximum_fusion.10.plane_ref, f32[4,4]{1,0:T(4,128)} %get-tuple-element.54.pick_ref, f32[1,512]{1,0:T(1,128)} %multiply_add_fusion.1.xrow_ref, f32[512,1]{1,0:T(8,128)} %multiply_add_fusion.ycol_ref, ...), custom_call_target="tpu_custom_call" | custom-call | flops 2147483648 | bytes 10485760 | tf_op jit(solution)/shard_map/pallas_call | solution.py:329
  71.9 0.8 convert_reduce_fusion
  72.6 39.9 %reduce-scatter.2.cloned.1.call-done = bf16[1,512,512]{2,1,0:T(8,128)(2,1)} async-done(((bf16[4,512,512]{2,1,0:T(8,128)(2,1)}), bf16[1,512,512]{2,1,0:T(8,128)(2,1)}) %reduce-scatter.2.cloned.1.call-update) | async-done | bytes 524304 | tf_op jit(solution)/shard_map/reduce_scatter | solution.py:456
  112.5 2.8 %convert_divide_fusion = f32[1,512,512]{2,1,0:T(8,128)} fusion(bf16[1,512,512]{2,1,0:T(8,128)(2,1)} %reduce-scatter.2.cloned.1.call-done, f32[]{:T(128)} %convert_reduce_fusion), kind=kLoop, calls=%fused_computation.2 | loop fusion | flops 524288 | bytes 1572868 | tf_op jit(solution)/shard_map/div | solution.py:459
  (85 shorter events, 9.6 us)
Async XLA Ops:
  7.2 14.8 %copy-start.2 = (bf16[4,512,512]{2,1,0:T(8,128)(2,1)S(1)}, bf16[4,512,512]{2,1,0:T(8,128)(2,1)}, u32[]{:S(2)}) copy-start(bf16[4,512,512]{2,1,0:T(8,128)(2,1)} %param.11) | copy-start | bytes 6291460
  7.2 105.4 %reduce-scatter.2.cloned.1.call-start = ((), (), s32[]{:S(2)}) async-start(), calls=%async_computation.1 | async-start | bytes 2621440 | tf_op jit(solution)/shard_map/reduce_scatter | solution.py:456
  14.1 27.8 %collective-permute-start.1 = (bf16[144,512]{1,0:T(8,128)(2,1)}, bf16[144,512]{1,0:T(8,128)(2,1)S(1)}, u32[]{:S(2)}, u32[]{:S(2)}) collective-permute-start(bf16[144,512]{1,0:T(8,128)(2,1)} %get-tuple-element.42), channel_id=1, source_target_pairs={{0,16},{8,24},{16,0},{24,8},{1,17},{9,25},{17,1},{25,9},{2,18},{10... | collective-permute-start | bytes 442376 | tf_op jit(solution)/shard_map/ppermute | solution.py:391
  18.1 23.8 %collective-permute-start = (bf16[144,512]{1,0:T(8,128)(2,1)}, bf16[144,512]{1,0:T(8,128)(2,1)}, u32[]{:S(2)}, u32[]{:S(2)}) collective-permute-start(bf16[144,512]{1,0:T(8,128)(2,1)} %get-tuple-element.42), channel_id=1, source_target_pairs={{0,8},{8,16},{16,24},{24,0},{1,9},{9,17},{17,25},{25,1},{2,10},{10... | collective-permute-start | bytes 442376 | tf_op jit(solution)/shard_map/ppermute | solution.py:391
  19.7 22.2 %collective-permute-start.2 = (bf16[144,512]{1,0:T(8,128)(2,1)}, bf16[144,512]{1,0:T(8,128)(2,1)}, u32[]{:S(2)}, u32[]{:S(2)}) collective-permute-start(bf16[144,512]{1,0:T(8,128)(2,1)} %get-tuple-element.42), channel_id=1, source_target_pairs={{0,24},{8,0},{16,8},{24,16},{1,25},{9,1},{17,9},{25,17},{2,26},{10... | collective-permute-start | bytes 442376 | tf_op jit(solution)/shard_map/ppermute | solution.py:391
  22.4 8.6 %collective-permute-start.4 = (bf16[4,8192]{1,0:T(4,128)(2,1)S(1)}, bf16[4,8192]{1,0:T(4,128)(2,1)S(1)}, u32[]{:S(2)}, u32[]{:S(2)}) collective-permute-start(bf16[4,8192]{1,0:T(4,128)(2,1)S(1)} %bitcast.83), channel_id=1, source_target_pairs={{1,0},{2,1},{3,2},{5,4},{6,5},{7,6},{9,8},{10,9},{11,10},{13,12},{... | collective-permute-start | bytes 196616 | tf_op jit(solution)/shard_map/ppermute | solution.py:42
  24.0 7.1 %collective-permute-start.3 = (bf16[4,8192]{1,0:T(4,128)(2,1)S(1)}, bf16[4,8192]{1,0:T(4,128)(2,1)S(1)}, u32[]{:S(2)}, u32[]{:S(2)}) collective-permute-start(bf16[4,8192]{1,0:T(4,128)(2,1)S(1)} %bitcast.85), channel_id=1, source_target_pairs={{0,1},{1,2},{2,3},{4,5},{5,6},{6,7},{8,9},{9,10},{10,11},{12,13},{... | collective-permute-start | bytes 196616 | tf_op jit(solution)/shard_map/ppermute | solution.py:41
  31.4 1.8 %copy-start.4 = (bf16[4,16,512]{1,2,0:T(8,128)(2,1)}, bf16[4,16,512]{1,2,0:T(8,128)(2,1)S(1)}, u32[]{:S(2)}) copy-start(bf16[4,16,512]{1,2,0:T(8,128)(2,1)S(1)} %copy.99) | copy-start | bytes 196612
  31.7 1.5 %copy-start.5 = (bf16[4,16,512]{1,2,0:T(8,128)(2,1)}, bf16[4,16,512]{1,2,0:T(8,128)(2,1)S(1)}, u32[]{:S(2)}) copy-start(bf16[4,16,512]{1,2,0:T(8,128)(2,1)S(1)} %copy.101) | copy-start | bytes 196612
  31.7 1.8 %copy-start.3 = (bf16[4,512,512]{2,1,0:T(8,128)(2,1)S(1)}, bf16[4,512,512]{2,1,0:T(8,128)(2,1)}, u32[]{:S(2)}) copy-start(bf16[4,512,512]{2,1,0:T(8,128)(2,1)} %param.11) | copy-start | bytes 6291460
  31.8 1.3 %collective-permute-start.5 = (bf16[4,16,544]{2,1,0:T(8,128)(2,1)S(1)}, bf16[4,16,544]{2,1,0:T(8,128)(2,1)S(1)}, u32[]{:S(2)}, u32[]{:S(2)}) collective-permute-start(bf16[4,16,544]{2,1,0:T(8,128)(2,1)S(1)} %fusion.3), channel_id=1, source_target_pairs={{0,4},{4,0},{1,5},{5,1},{2,6},{6,2},{3,7},{7,3},{8,12},{12,8},{9,1... | collective-permute-start | bytes 208904 | tf_op jit(solution)/shard_map/ppermute | solution.py:34
  33.5 2.9 %copy-start = (bf16[3,256,256]{2,1,0:T(8,128)(2,1)S(1)}, bf16[3,256,256]{2,1,0:T(8,128)(2,1)}, u32[]{:S(2)}) copy-start(bf16[3,256,256]{2,1,0:T(8,128)(2,1)} %constant.158.clone.tb_ref.blk_ref) | copy-start | bytes 1179652
  33.5 2.9 %copy-start.1 = (f32[4,3]{1,0:T(4,128)S(1)}, f32[4,3]{1,0:T(4,128)}, u32[]{:S(2)}) copy-start(f32[4,3]{1,0:T(4,128)} %coef_ref.5) | copy-start | bytes 148
  36.4 6.6 %copy-start.8 = (s32[4]{0:T(128)S(1)}, s32[4]{0:T(128)}, u32[]{:S(2)}) copy-start(s32[4]{0:T(128)} %fusion.12) | copy-start | bytes 52
  36.4 8.1 %copy-start.6 = (s32[4,1,1,2]{0,3,2,1:T(2,128)S(1)}, s32[4,1,1,2]{0,3,2,1:T(2,128)}, u32[]{:S(2)}) copy-start(s32[4,1,1,2]{0,3,2,1:T(2,128)} %param.16) | copy-start | bytes 100
  44.5 1.2 collective-permute-start.6
  45.8 7.3 %collective-permute-start.7 = (f32[4,12]{1,0:T(4,128)S(1)}, f32[4,12]{1,0:T(4,128)S(1)}, u32[]{:S(2)}, u32[]{:S(2)}) collective-permute-start(f32[4,12]{1,0:T(4,128)S(1)} %fusion.18), channel_id=1, source_target_pairs={{0,1},{1,0},{2,3},{3,2},{4,5},{5,4},{6,7},{7,6},{8,9},{9,8},{10,11... | collective-permute-start | bytes 584 | tf_op jit(solution)/shard_map/ppermute | solution.py:96
  53.0 7.6 %copy-start.7 = (pred[3,3]{1,0:T(4,128)(4,1)S(1)}, pred[3,3]{1,0:T(4,128)(4,1)}, u32[]{:S(2)}) copy-start(pred[3,3]{1,0:T(4,128)(4,1)} %iota_compare_fusion.2) | copy-start | bytes 31
  53.0 6.0 %collective-permute-start.8 = (f32[4,12]{1,0:T(4,128)S(1)}, f32[4,12]{1,0:T(4,128)S(1)}, u32[]{:S(2)}, u32[]{:S(2)}) collective-permute-start(f32[4,12]{1,0:T(4,128)S(1)} %add.225), channel_id=1, source_target_pairs={{0,2},{1,3},{2,0},{3,1},{4,6},{5,7},{6,4},{7,5},{8,10},{9,11},{10,... | collective-permute-start | bytes 584 | tf_op jit(solution)/shard_map/ppermute | solution.py:96
Sparse Core Ops, SparseCore 0:
  71.1 41.4 reduce-scatter.1

commit v14 on v13

--- a/solution.py
+++ b/solution.py
@@ -335,6 +335,18 @@
         ),
         cost_estimate=pl.CostEstimate(flops=flops, bytes_accessed=moved, transcendentals=0),
     )(choose, plane, picked, xrow, ycol, matched, bank, bank)
+
+
+def ring_scatter(parts, axis, size, position):
+    ring = [(i, (i + 1) % size) for i in range(size)]
+    travelling = None
+    for step in range(size - 1):
+        block = (position - step - 1) % size
+        own = lax.dynamic_index_in_dim(parts, block, 0, False).astype(jnp.float32)
+        outgoing = own if travelling is None else travelling + own
+        travelling = lax.ppermute(outgoing.astype(jnp.bfloat16), axis, ring).astype(jnp.float32)
+    own = lax.dynamic_index_in_dim(parts, position, 0, False).astype(jnp.float32)
+    return own if travelling is None else travelling + own
 
 
 def rows_from(source, anchor):
@@ -453,9 +465,7 @@
         choose, plane_fit, picked.astype(jnp.float32), xcoord.reshape(1, tile_len),
         row_coord.reshape(tile_len, 1), matched, resample_bank,
     )
-    numerator = lax.psum_scatter(
-        partial_sum, "visit", scatter_dimension=0, tiled=True
-    ).astype(jnp.float32)
+    numerator = ring_scatter(partial_sum, "visit", visit_count, visit_pos)[None]
     coadd_patch = numerator / denominator[:, None, None]
     return (coadd_patch, plane_fit)
 

time: 123 us -> 113 us (0.919)
  between operations: 14.4 us -> 1.09 us
  waiting for transfers between devices: 41.7 us -> 43.9 us
    ppermute x0 -> x3, waiting for transfers between devices: none -> 42.2 us  [ring_scatter(): lax.ppermute(outgoing.astype(jnp.bfloat16), axis, ring).astype(jnp.float32)]
    reduce_scatter x1 -> x0, waiting for transfers between devices: 39.9 us -> none  [shards(): lax.psum_scatter(partial_sum, 'visit', scatter_dimension=0, tiled=True)]
    convert_element_type x0 -> x2, other arithmetic: none -> 1.31 us  [ring_scatter(): outgoing.astype(jnp.bfloat16)]
  transfers between devices with their start and end apart: 10 -> 12, of which waited for: 3 -> 5; matrix products, arithmetic and copies ran while one was open for 7% -> 8% of each run, Pallas kernels for 12% -> 13%
where the time goes in v14:
time: 113 us
  waiting for transfers between devices  43.9 us (39%)
  Pallas kernels  24.3 us (22%)
  other arithmetic  17.8 us (16%)
  starting transfers between devices  17.6 us (16%)
  local copies, waits for them, and re-layouts  5.42 us (5%)
  matrix products  2.49 us (2%)
    ppermute x3, waiting for transfers between devices, ring_scatter(): lax.ppermute(outgoing.astype(jnp.bfloat16), axis, ring).astype(jnp.float32)  42.2 us
    pallas_call x2, Pallas kernels, band_tiles(): pl.pallas_call(functools.partial(band_body, first), grid=(count,), in_spe...  9.66 us
    pallas_call x1, Pallas kernels, warp_tiles(): pl.pallas_call(warp_body, grid_spec=grid_spec, out_shape=jax.ShapeDtypeSt...  9.21 us
    ppermute x3, starting transfers between devices, shards(): received.append(lax.ppermute(payload, 'visit', pairs))  7.86 us
    pallas_call x1, Pallas kernels, strip_tiles(): pl.pallas_call(strip_body, grid_spec=grid_spec, out_shape=jax.ShapeDtypeS...  5.43 us
    ppermute x1, starting transfers between devices, extended(): before = lax.ppermute(last, axis, up)  4.55 us
    ppermute x3, starting transfers between devices, butterfly_sum(): values = jax.tree.map(lambda v: v + lax.ppermute(v, axis, pairs), values)  3.61 us
    concatenate x1, other arithmetic, extended(): value = jnp.concatenate([before, value, after], axis=dim)  2.9 us
  transfers between devices with their start and end apart: 12, of which 5 were waited for; matrix products, arithmetic and copies ran while one was open for 8% of the time, Pallas kernels for 13%

profile of v14, /device:TPU:0, one launch (start us, length us, event | category | flops | bytes accessed | tf_op | source)
XLA Modules:
  0.0 112.6 jit_solution(2764595242720481407)
XLA Ops:
  0.7 0.9 iota_compare_fusion.3
  3.1 1.3 %fusion.19 = (f32[4,4]{1,0:T(4,128)}, bf16[4,4]{1,0:T(4,128)(2,1)S(1)}) fusion(pred[4,4]{1,0:T(4,128)(4,1)S(1)} %fusion.10, bf16[4]{0:T(256)(128)(2,1)} %bitcast.121), kind=kLoop, calls=%fused_computation.90 | loop fusion | flops 32 | bytes 120 | tf_op jit(solution)/shard_map/convert_element_type | solution.py:465
  4.7 2.1 %convolution_convert_fusion = bf16[4,32,512]{2,1,0:T(8,128)(2,1)S(1)} fusion(bf16[4,512,512]{2,1,0:T(8,128)(2,1)} %param.11, s32[4]{0:T(128)S(1)} %get-tuple-element.35.off_ref), kind=kOutput, calls=%fused_computation.1 | convolution fusion | flops 67305472 | bytes 2228240 | tf_op jit(solution)/shard_map/esr,erl->esl/dot_general | solution.py:383
  7.5 4.0 %collective-permute-start.1 = (bf16[144,512]{1,0:T(8,128)(2,1)}, bf16[144,512]{1,0:T(8,128)(2,1)S(1)}, u32[]{:S(2)}, u32[]{:S(2)}) collective-permute-start(bf16[144,512]{1,0:T(8,128)(2,1)} %get-tuple-element.42), channel_id=1, source_target_pairs={{0,16},{8,24},{16,0},{24,8},{1,17},{9,25},{17,1},{25,9},{2,18},{10... | collective-permute-start | bytes 442376 | tf_op jit(solution)/shard_map/ppermute | solution.py:403
  11.5 1.6 %collective-permute-start = (bf16[144,512]{1,0:T(8,128)(2,1)}, bf16[144,512]{1,0:T(8,128)(2,1)}, u32[]{:S(2)}, u32[]{:S(2)}) collective-permute-start(bf16[144,512]{1,0:T(8,128)(2,1)} %get-tuple-element.42), channel_id=1, source_target_pairs={{0,8},{8,16},{16,24},{24,0},{1,9},{9,17},{17,25},{25,1},{2,10},{10... | collective-permute-start | bytes 442376 | tf_op jit(solution)/shard_map/ppermute | solution.py:403
  13.1 2.2 %collective-permute-start.2 = (bf16[144,512]{1,0:T(8,128)(2,1)}, bf16[144,512]{1,0:T(8,128)(2,1)}, u32[]{:S(2)}, u32[]{:S(2)}) collective-permute-start(bf16[144,512]{1,0:T(8,128)(2,1)} %get-tuple-element.42), channel_id=1, source_target_pairs={{0,24},{8,0},{16,8},{24,16},{1,25},{9,1},{17,9},{25,17},{2,26},{10... | collective-permute-start | bytes 442376 | tf_op jit(solution)/shard_map/ppermute | solution.py:403
  15.9 1.3 %collective-permute-start.4 = (bf16[4,8192]{1,0:T(4,128)(2,1)S(1)}, bf16[4,8192]{1,0:T(4,128)(2,1)S(1)}, u32[]{:S(2)}, u32[]{:S(2)}) collective-permute-start(bf16[4,8192]{1,0:T(4,128)(2,1)S(1)} %bitcast.96), channel_id=1, source_target_pairs={{1,0},{2,1},{3,2},{5,4},{6,5},{7,6},{9,8},{10,9},{11,10},{13,12},{... | collective-permute-start | bytes 196616 | tf_op jit(solution)/shard_map/ppermute | solution.py:42
  17.4 4.5 %collective-permute-start.3 = (bf16[4,8192]{1,0:T(4,128)(2,1)S(1)}, bf16[4,8192]{1,0:T(4,128)(2,1)S(1)}, u32[]{:S(2)}, u32[]{:S(2)}) collective-permute-start(bf16[4,8192]{1,0:T(4,128)(2,1)S(1)} %bitcast.98), channel_id=1, source_target_pairs={{0,1},{1,2},{2,3},{4,5},{5,6},{6,7},{8,9},{9,10},{10,11},{12,13},{... | collective-permute-start | bytes 196616 | tf_op jit(solution)/shard_map/ppermute | solution.py:41
  25.4 1.3 %collective-permute-done.5 = bf16[4,16,544]{2,1,0:T(8,128)(2,1)S(1)} collective-permute-done((bf16[4,16,544]{2,1,0:T(8,128)(2,1)S(1)}, bf16[4,16,544]{2,1,0:T(8,128)(2,1)S(1)}, u32[]{:S(2)}, u32[]{:S(2)}) %collective-permute-start.5) | collective-permute-done | bytes 69664 | tf_op jit(solution)/shard_map/ppermute | solution.py:34
  26.9 2.9 %pad_maximum_fusion.padded_ref = bf16[4,544,544]{2,1,0:T(8,128)(2,1)S(1)} fusion(bf16[4,16,544]{2,1,0:T(8,128)(2,1)S(1)} %get-tuple-element.44, bf16[4,512,16]{2,1,0:T(8,128)(2,1)} %bitcast.86, bf16[4,512,512]{2,1,0:T(8,128)(2,1)S(1)} %copy-done.3, bf16[4,512,16]{2,1,0:T(8,128)(2,1)} %bitcast.84, bf16[4,16,544]{2,1,0:T(8,128)(2,1)S(1)} %get-tuple-element.43), kind=kLoop, calls=%fused_computation | loop fusion | flops 11837440 | bytes 4734976 | tf_op jit(solution)/shard_map/concatenate | solution.py:46
  29.9 5.4 %shard_map.104 = f32[4,32,512]{2,1,0:T(8,128)S(1)} custom-call(s32[4]{0:T(128)S(1)} %get-tuple-element.35.off_ref, f32[4,3]{1,0:T(4,128)S(1)} %copy-done.1, bf16[3,256,256]{2,1,0:T(8,128)(2,1)S(1)} %copy-done, bf16[4,544,544]{2,1,0:T(8,128)(2,1)S(1)} %pad_maximum_fusion.padded_ref), custom_call_target="tpu_custom_call" | custom-call | flops 257949696 | bytes 2629632 | tf_op jit(solution)/shard_map/pallas_call | solution.py:207
  35.3 1.1 pad_maximum_fusion.1
  39.2 2.4 %collective-permute-start.7 = (f32[4,12]{1,0:T(4,128)S(1)}, f32[4,12]{1,0:T(4,128)S(1)}, u32[]{:S(2)}, u32[]{:S(2)}) collective-permute-start(f32[4,12]{1,0:T(4,128)S(1)} %fusion.22), channel_id=1, source_target_pairs={{0,1},{1,0},{2,3},{3,2},{4,5},{5,4},{6,7},{7,6},{8,9},{9,8},{10,11... | collective-permute-start | bytes 584 | tf_op jit(solution)/shard_map/ppermute | solution.py:96
  41.6 4.9 %shard_map.105.rest_0_ = f32[4,512,512]{2,1,0:T(8,128)} custom-call(f32[4,3]{1,0:T(4,128)S(1)} %copy-done.1, bf16[3,256,256]{2,1,0:T(8,128)(2,1)S(1)} %copy-done, bf16[4,544,544]{2,1,0:T(8,128)(2,1)S(1)} %pad_maximum_fusion.padded_ref), custom_call_target="tpu_custom_call" | custom-call | flops 1660944384 | bytes 3280896 | tf_op jit(solution)/shard_map/pallas_call | solution.py:264
  46.5 1.2 %collective-permute-start.8 = (f32[4,12]{1,0:T(4,128)S(1)}, f32[4,12]{1,0:T(4,128)S(1)}, u32[]{:S(2)}, u32[]{:S(2)}) collective-permute-start(f32[4,12]{1,0:T(4,128)S(1)} %add.261), channel_id=1, source_target_pairs={{0,2},{1,3},{2,0},{3,1},{4,6},{5,7},{6,4},{7,5},{8,10},{9,11},{10,... | collective-permute-start | bytes 584 | tf_op jit(solution)/shard_map/ppermute | solution.py:96
  47.7 4.8 %shard_map.106.matched_ref = f32[4,512,512]{2,1,0:T(8,128)} custom-call(f32[4,3]{1,0:T(4,128)S(1)} %copy-done.1, bf16[3,256,256]{2,1,0:T(8,128)(2,1)S(1)} %copy-done, bf16[4,544,544]{2,1,0:T(8,128)(2,1)S(1)} %pad_maximum_fusion.padded_ref, f32[4,512,512]{2,1,0:T(8,128)} %shard_map.105.rest_0_), custom_call_target="tpu_custom_call", output_to_operand_aliasing={{}: (3, {})} | custom-call | flops 1660944384 | bytes 3280896 | tf_op jit(solution)/shard_map/pallas_call | solution.py:264
  52.7 1.1 custom-call.4
  54.9 9.2 %shard_map.107 = bf16[4,512,512]{2,1,0:T(8,128)(2,1)} custom-call(s32[4,2]{1,0:T(4,128)} %copy.119.idx_ref, f32[4,3]{1,0:T(4,128)} %pad_maximum_fusion.10.plane_ref, f32[4,4]{1,0:T(4,128)} %get-tuple-element.54.pick_ref, f32[1,512]{1,0:T(1,128)} %multiply_add_fusion.1.xrow_ref, f32[512,1]{1,0:T(8,128)} %multiply_add_fusion.ycol_ref, ...), custom_call_target="tpu_custom_call" | custom-call | flops 2147483648 | bytes 10485760 | tf_op jit(solution)/shard_map/pallas_call | solution.py:329
  64.1 1.2 %dynamic-slice_bitcast_fusion = bf16[512,512]{1,0:T(8,128)(2,1)S(1)} fusion(bf16[4,512,512]{2,1,0:T(8,128)(2,1)} %shard_map.107, s32[]{:T(128)S(6)} %select_n.115), kind=kLoop, calls=%fused_computation.12 | loop fusion | bytes 1048580 | tf_op jit(solution)/shard_map/jit(dynamic_index_in_dim)/squeeze | solution.py:345
  65.5 15.5 %collective-permute-done.9 = bf16[512,512]{1,0:T(8,128)(2,1)S(1)} collective-permute-done((bf16[512,512]{1,0:T(8,128)(2,1)S(1)}, bf16[512,512]{1,0:T(8,128)(2,1)S(1)}, u32[]{:S(2)}, u32[]{:S(2)}) %collective-permute-start.9) | collective-permute-done | bytes 524320 | tf_op jit(solution)/shard_map/ppermute | solution.py:347
  80.9 1.2 %fusion.3 = bf16[512,512]{1,0:T(8,128)(2,1)S(1)} fusion(bf16[512,512]{1,0:T(8,128)(2,1)S(1)} %collective-permute-done.9, bf16[4,512,512]{2,1,0:T(8,128)(2,1)} %shard_map.107, s32[]{:T(128)S(6)} %select_n.117), kind=kLoop, calls=%fused_computation.8 | loop fusion | flops 1048576 | bytes 1572868 | tf_op jit(solution)/shard_map/convert_element_type | solution.py:347
  82.2 14.6 %collective-permute-done.10 = bf16[512,512]{1,0:T(8,128)(2,1)S(1)} collective-permute-done((bf16[512,512]{1,0:T(8,128)(2,1)S(1)}, bf16[512,512]{1,0:T(8,128)(2,1)S(1)}, u32[]{:S(2)}, u32[]{:S(2)}) %collective-permute-start.10) | collective-permute-done | bytes 524320 | tf_op jit(solution)/shard_map/ppermute | solution.py:347
  98.7 12.1 %collective-permute-done.11 = bf16[512,512]{1,0:T(8,128)(2,1)S(1)} collective-permute-done((bf16[512,512]{1,0:T(8,128)(2,1)S(1)}, bf16[512,512]{1,0:T(8,128)(2,1)S(1)}, u32[]{:S(2)}, u32[]{:S(2)}) %collective-permute-start.11) | collective-permute-done | bytes 524320 | tf_op jit(solution)/shard_map/ppermute | solution.py:347
  110.7 1.8 %fusion.1 = f32[1,512,512]{2,1,0:T(8,128)} fusion(bf16[512,512]{1,0:T(8,128)(2,1)S(1)} %collective-permute-done.11, f32[]{:T(128)} %convert_reduce_fusion, bf16[4,512,512]{2,1,0:T(8,128)(2,1)S(1)} %copy-done.4, s32[]{:T(128)S(6)} %select_n.120), kind=kLoop, calls=%fused_computation.4 | loop fusion | flops 1048576 | bytes 2097160 | tf_op jit(solution)/shard_map/div | solution.py:469
  (93 shorter events, 12.9 us)
Async XLA Ops:
  0.6 14.7 %copy-start.2 = (bf16[4,512,512]{2,1,0:T(8,128)(2,1)S(1)}, bf16[4,512,512]{2,1,0:T(8,128)(2,1)}, u32[]{:S(2)}) copy-start(bf16[4,512,512]{2,1,0:T(8,128)(2,1)} %param.11) | copy-start | bytes 6291460
  7.5 27.8 %collective-permute-start.1 = (bf16[144,512]{1,0:T(8,128)(2,1)}, bf16[144,512]{1,0:T(8,128)(2,1)S(1)}, u32[]{:S(2)}, u32[]{:S(2)}) collective-permute-start(bf16[144,512]{1,0:T(8,128)(2,1)} %get-tuple-element.42), channel_id=1, source_target_pairs={{0,16},{8,24},{16,0},{24,8},{1,17},{9,25},{17,1},{25,9},{2,18},{10... | collective-permute-start | bytes 442376 | tf_op jit(solution)/shard_map/ppermute | solution.py:403
  11.5 23.8 %collective-permute-start = (bf16[144,512]{1,0:T(8,128)(2,1)}, bf16[144,512]{1,0:T(8,128)(2,1)}, u32[]{:S(2)}, u32[]{:S(2)}) collective-permute-start(bf16[144,512]{1,0:T(8,128)(2,1)} %get-tuple-element.42), channel_id=1, source_target_pairs={{0,8},{8,16},{16,24},{24,0},{1,9},{9,17},{17,25},{25,1},{2,10},{10... | collective-permute-start | bytes 442376 | tf_op jit(solution)/shard_map/ppermute | solution.py:403
  13.1 22.2 %collective-permute-start.2 = (bf16[144,512]{1,0:T(8,128)(2,1)}, bf16[144,512]{1,0:T(8,128)(2,1)}, u32[]{:S(2)}, u32[]{:S(2)}) collective-permute-start(bf16[144,512]{1,0:T(8,128)(2,1)} %get-tuple-element.42), channel_id=1, source_target_pairs={{0,24},{8,0},{16,8},{24,16},{1,25},{9,1},{17,9},{25,17},{2,26},{10... | collective-permute-start | bytes 442376 | tf_op jit(solution)/shard_map/ppermute | solution.py:403
  15.9 8.6 %collective-permute-start.4 = (bf16[4,8192]{1,0:T(4,128)(2,1)S(1)}, bf16[4,8192]{1,0:T(4,128)(2,1)S(1)}, u32[]{:S(2)}, u32[]{:S(2)}) collective-permute-start(bf16[4,8192]{1,0:T(4,128)(2,1)S(1)} %bitcast.96), channel_id=1, source_target_pairs={{1,0},{2,1},{3,2},{5,4},{6,5},{7,6},{9,8},{10,9},{11,10},{13,12},{... | collective-permute-start | bytes 196616 | tf_op jit(solution)/shard_map/ppermute | solution.py:42
  17.4 7.1 %collective-permute-start.3 = (bf16[4,8192]{1,0:T(4,128)(2,1)S(1)}, bf16[4,8192]{1,0:T(4,128)(2,1)S(1)}, u32[]{:S(2)}, u32[]{:S(2)}) collective-permute-start(bf16[4,8192]{1,0:T(4,128)(2,1)S(1)} %bitcast.98), channel_id=1, source_target_pairs={{0,1},{1,2},{2,3},{4,5},{5,6},{6,7},{8,9},{9,10},{10,11},{12,13},{... | collective-permute-start | bytes 196616 | tf_op jit(solution)/shard_map/ppermute | solution.py:41
  24.8 1.8 %copy-start.5 = (bf16[4,16,512]{1,2,0:T(8,128)(2,1)}, bf16[4,16,512]{1,2,0:T(8,128)(2,1)S(1)}, u32[]{:S(2)}) copy-start(bf16[4,16,512]{1,2,0:T(8,128)(2,1)S(1)} %copy.99) | copy-start | bytes 196612
  25.1 1.5 %copy-start.6 = (bf16[4,16,512]{1,2,0:T(8,128)(2,1)}, bf16[4,16,512]{1,2,0:T(8,128)(2,1)S(1)}, u32[]{:S(2)}) copy-start(bf16[4,16,512]{1,2,0:T(8,128)(2,1)S(1)} %copy.101) | copy-start | bytes 196612
  25.1 1.8 %copy-start.3 = (bf16[4,512,512]{2,1,0:T(8,128)(2,1)S(1)}, bf16[4,512,512]{2,1,0:T(8,128)(2,1)}, u32[]{:S(2)}) copy-start(bf16[4,512,512]{2,1,0:T(8,128)(2,1)} %param.11) | copy-start | bytes 6291460
  25.3 1.3 %collective-permute-start.5 = (bf16[4,16,544]{2,1,0:T(8,128)(2,1)S(1)}, bf16[4,16,544]{2,1,0:T(8,128)(2,1)S(1)}, u32[]{:S(2)}, u32[]{:S(2)}) collective-permute-start(bf16[4,16,544]{2,1,0:T(8,128)(2,1)S(1)} %fusion.7), channel_id=1, source_target_pairs={{0,4},{4,0},{1,5},{5,1},{2,6},{6,2},{3,7},{7,3},{8,12},{12,8},{9,1... | collective-permute-start | bytes 208904 | tf_op jit(solution)/shard_map/ppermute | solution.py:34
  26.9 2.9 %copy-start = (bf16[3,256,256]{2,1,0:T(8,128)(2,1)S(1)}, bf16[3,256,256]{2,1,0:T(8,128)(2,1)}, u32[]{:S(2)}) copy-start(bf16[3,256,256]{2,1,0:T(8,128)(2,1)} %constant.191.clone.tb_ref.blk_ref) | copy-start | bytes 1179652
  26.9 2.9 %copy-start.1 = (f32[4,3]{1,0:T(4,128)S(1)}, f32[4,3]{1,0:T(4,128)}, u32[]{:S(2)}) copy-start(f32[4,3]{1,0:T(4,128)} %coef_ref.5) | copy-start | bytes 148
  29.8 6.6 %copy-start.9 = (s32[4]{0:T(128)S(1)}, s32[4]{0:T(128)}, u32[]{:S(2)}) copy-start(s32[4]{0:T(128)} %fusion.16) | copy-start | bytes 52
  29.9 8.1 %copy-start.7 = (s32[4,1,1,2]{0,3,2,1:T(2,128)S(1)}, s32[4,1,1,2]{0,3,2,1:T(2,128)}, u32[]{:S(2)}) copy-start(s32[4,1,1,2]{0,3,2,1:T(2,128)} %param.16) | copy-start | bytes 100
  38.0 1.2 %collective-permute-start.6 = (f32[4,12]{1,0:T(4,128)S(1)}, f32[4,12]{1,0:T(4,128)S(1)}, u32[]{:S(2)}, u32[]{:S(2)}) collective-permute-start(f32[4,12]{1,0:T(4,128)S(1)} %pad_maximum_fusion.9), channel_id=1, source_target_pairs={{0,4},{4,0},{1,5},{5,1},{2,6},{6,2},{3,7},{7,3},{8,12},{12,8},{9,1... | collective-permute-start | bytes 584 | tf_op jit(solution)/shard_map/ppermute | solution.py:96
  39.2 7.2 %collective-permute-start.7 = (f32[4,12]{1,0:T(4,128)S(1)}, f32[4,12]{1,0:T(4,128)S(1)}, u32[]{:S(2)}, u32[]{:S(2)}) collective-permute-start(f32[4,12]{1,0:T(4,128)S(1)} %fusion.22), channel_id=1, source_target_pairs={{0,1},{1,0},{2,3},{3,2},{4,5},{5,4},{6,7},{7,6},{8,9},{9,8},{10,11... | collective-permute-start | bytes 584 | tf_op jit(solution)/shard_map/ppermute | solution.py:96
  46.5 7.5 %copy-start.8 = (pred[3,3]{1,0:T(4,128)(4,1)S(1)}, pred[3,3]{1,0:T(4,128)(4,1)}, u32[]{:S(2)}) copy-start(pred[3,3]{1,0:T(4,128)(4,1)} %iota_compare_fusion.2) | copy-start | bytes 31
  46.5 6.0 %collective-permute-start.8 = (f32[4,12]{1,0:T(4,128)S(1)}, f32[4,12]{1,0:T(4,128)S(1)}, u32[]{:S(2)}, u32[]{:S(2)}) collective-permute-start(f32[4,12]{1,0:T(4,128)S(1)} %add.261), channel_id=1, source_target_pairs={{0,2},{1,3},{2,0},{3,1},{4,6},{5,7},{6,4},{7,5},{8,10},{9,11},{10,... | collective-permute-start | bytes 584 | tf_op jit(solution)/shard_map/ppermute | solution.py:96
  64.1 32.7 %copy-start.4 = (bf16[4,512,512]{2,1,0:T(8,128)(2,1)S(1)}, bf16[4,512,512]{2,1,0:T(8,128)(2,1)}, u32[]{:S(2)}) copy-start(bf16[4,512,512]{2,1,0:T(8,128)(2,1)} %shard_map.107) | copy-start | bytes 6291460
  65.4 15.6 %collective-permute-start.9 = (bf16[512,512]{1,0:T(8,128)(2,1)S(1)}, bf16[512,512]{1,0:T(8,128)(2,1)S(1)}, u32[]{:S(2)}, u32[]{:S(2)}) collective-permute-start(bf16[512,512]{1,0:T(8,128)(2,1)S(1)} %dynamic-slice_bitcast_fusion), channel_id=1, source_target_pairs={{0,8},{8,16},{16,24},{24,0},{1,9},{9,17},{17,25},{25,1},{2,10},{10... | collective-permute-start | bytes 1572872 | tf_op jit(solution)/shard_map/ppermute | solution.py:347
  82.1 14.7 %collective-permute-start.10 = (bf16[512,512]{1,0:T(8,128)(2,1)S(1)}, bf16[512,512]{1,0:T(8,128)(2,1)S(1)}, u32[]{:S(2)}, u32[]{:S(2)}) collective-permute-start(bf16[512,512]{1,0:T(8,128)(2,1)S(1)} %fusion.3), channel_id=1, source_target_pairs={{0,8},{8,16},{16,24},{24,0},{1,9},{9,17},{17,25},{25,1},{2,10},{10... | collective-permute-start | bytes 1572872 | tf_op jit(solution)/shard_map/ppermute | solution.py:347
  97.0 13.8 %collective-permute-start.11 = (bf16[512,512]{1,0:T(8,128)(2,1)S(1)}, bf16[512,512]{1,0:T(8,128)(2,1)S(1)}, u32[]{:S(2)}, u32[]{:S(2)}) collective-permute-start(bf16[512,512]{1,0:T(8,128)(2,1)S(1)} %fusion.2), channel_id=1, source_target_pairs={{0,8},{8,16},{16,24},{24,0},{1,9},{9,17},{17,25},{25,1},{2,10},{10... | collective-permute-start | bytes 1572872 | tf_op jit(solution)/shard_map/ppermute | solution.py:347

commit v15 on v14

--- a/solution.py
+++ b/solution.py
@@ -337,15 +337,14 @@
     )(choose, plane, picked, xrow, ycol, matched, bank, bank)
 
 
-def ring_scatter(parts, axis, size, position):
+def ring_scatter(parts, axis, size):
     ring = [(i, (i + 1) % size) for i in range(size)]
     travelling = None
     for step in range(size - 1):
-        block = (position - step - 1) % size
-        own = lax.dynamic_index_in_dim(parts, block, 0, False).astype(jnp.float32)
+        own = parts[step].astype(jnp.float32)
         outgoing = own if travelling is None else travelling + own
         travelling = lax.ppermute(outgoing.astype(jnp.bfloat16), axis, ring).astype(jnp.float32)
-    own = lax.dynamic_index_in_dim(parts, position, 0, False).astype(jnp.float32)
+    own = parts[size - 1].astype(jnp.float32)
     return own if travelling is None else travelling + own
 
 
@@ -461,11 +460,17 @@
     plane_fit = solve_three(normal, moments)
     row_coord = centred(row_pos * tile_len + jnp.arange(tile_len, dtype=jnp.int32), height)
     choose = warp_index[:, 0, 0, :]
+    ring_order = (
+        lax.broadcasted_iota(jnp.int32, (visit_count, visit_count), 0)
+        == (visit_pos - lax.broadcasted_iota(jnp.int32, (visit_count, visit_count), 1) - 1)
+        % visit_count
+    ).astype(jnp.float32)
+    picked_ring = jnp.dot(picked.astype(jnp.float32), ring_order, precision=lax.Precision.HIGHEST)
     partial_sum = warp_tiles(
-        choose, plane_fit, picked.astype(jnp.float32), xcoord.reshape(1, tile_len),
+        choose, plane_fit, picked_ring, xcoord.reshape(1, tile_len),
         row_coord.reshape(tile_len, 1), matched, resample_bank,
     )
-    numerator = ring_scatter(partial_sum, "visit", visit_count, visit_pos)[None]
+    numerator = ring_scatter(partial_sum, "visit", visit_count)[None]
     coadd_patch = numerator / denominator[:, None, None]
     return (coadd_patch, plane_fit)
 

time: 113 us -> 113 us (level)
    convert_element_type x1 -> x0, other arithmetic: 1.3 us -> none  [shards(): picked.astype(jnp.float32)]
  transfers between devices with their start and end apart: 12 -> 12, of which waited for: 5 -> 5; matrix products, arithmetic and copies ran while one was open for 8% -> 9% of each run, Pallas kernels for 13% -> 13%
where the time goes in v15:
time: 113 us; the launch traced here: 112 us
  waiting for transfers between devices  43.9 us (39%)
  Pallas kernels  24.3 us (22%)
  other arithmetic  17.3 us (15%)
  starting transfers between devices  16.8 us (15%)
  local copies, waits for them, and re-layouts  5.42 us (5%)
  matrix products  3.25 us (3%)
    ppermute x3, waiting for transfers between devices, ring_scatter(): lax.ppermute(outgoing.astype(jnp.bfloat16), axis, ring).astype(jnp.float32)  42.2 us
    pallas_call x2, Pallas kernels, band_tiles(): pl.pallas_call(functools.partial(band_body, first), grid=(count,), in_spe...  9.66 us
    pallas_call x1, Pallas kernels, warp_tiles(): pl.pallas_call(warp_body, grid_spec=grid_spec, out_shape=jax.ShapeDtypeSt...  9.21 us
    ppermute x3, starting transfers between devices, shards(): received.append(lax.ppermute(payload, 'visit', pairs))  7.86 us
    pallas_call x1, Pallas kernels, strip_tiles(): pl.pallas_call(strip_body, grid_spec=grid_spec, out_shape=jax.ShapeDtypeS...  5.44 us
    ppermute x1, starting transfers between devices, extended(): before = lax.ppermute(last, axis, up)  4.55 us
    concatenate x1, other arithmetic, extended(): value = jnp.concatenate([before, value, after], axis=dim)  2.9 us
    ppermute x3, starting transfers between devices, butterfly_sum(): values = jax.tree.map(lambda v: v + lax.ppermute(v, axis, pairs), values)  2.85 us
  transfers between devices with their start and end apart: 12, of which 5 were waited for; matrix products, arithmetic and copies ran while one was open for 9% of the time, Pallas kernels for 13%

profile of v15, /device:TPU:0, one launch (start us, length us, event | category | flops | bytes accessed | tf_op | source)
XLA Modules:
  0.0 112.0 jit_solution(12714958844884504782)
XLA Ops:
  0.7 0.9 iota_compare_fusion.3
  1.5 0.8 fusion.10
  3.1 0.8 slice_bitcast_fusion.6
  4.1 2.1 %convolution_convert_fusion = bf16[4,32,512]{2,1,0:T(8,128)(2,1)S(1)} fusion(bf16[4,512,512]{2,1,0:T(8,128)(2,1)} %param.11, s32[4]{0:T(128)S(1)} %get-tuple-element.35.off_ref), kind=kOutput, calls=%fused_computation.1 | convolution fusion | flops 67305472 | bytes 2228240 | tf_op jit(solution)/shard_map/esr,erl->esl/dot_general | solution.py:382
  6.9 4.0 %collective-permute-start.1 = (bf16[144,512]{1,0:T(8,128)(2,1)}, bf16[144,512]{1,0:T(8,128)(2,1)S(1)}, u32[]{:S(2)}, u32[]{:S(2)}) collective-permute-start(bf16[144,512]{1,0:T(8,128)(2,1)} %get-tuple-element.42), channel_id=1, source_target_pairs={{0,16},{8,24},{16,0},{24,8},{1,17},{9,25},{17,1},{25,9},{2,18},{10... | collective-permute-start | bytes 442376 | tf_op jit(solution)/shard_map/ppermute | solution.py:402
  11.0 1.6 %collective-permute-start = (bf16[144,512]{1,0:T(8,128)(2,1)}, bf16[144,512]{1,0:T(8,128)(2,1)}, u32[]{:S(2)}, u32[]{:S(2)}) collective-permute-start(bf16[144,512]{1,0:T(8,128)(2,1)} %get-tuple-element.42), channel_id=1, source_target_pairs={{0,8},{8,16},{16,24},{24,0},{1,9},{9,17},{17,25},{25,1},{2,10},{10... | collective-permute-start | bytes 442376 | tf_op jit(solution)/shard_map/ppermute | solution.py:402
  12.5 2.2 %collective-permute-start.2 = (bf16[144,512]{1,0:T(8,128)(2,1)}, bf16[144,512]{1,0:T(8,128)(2,1)}, u32[]{:S(2)}, u32[]{:S(2)}) collective-permute-start(bf16[144,512]{1,0:T(8,128)(2,1)} %get-tuple-element.42), channel_id=1, source_target_pairs={{0,24},{8,0},{16,8},{24,16},{1,25},{9,1},{17,9},{25,17},{2,26},{10... | collective-permute-start | bytes 442376 | tf_op jit(solution)/shard_map/ppermute | solution.py:402
  15.3 1.3 %collective-permute-start.4 = (bf16[4,8192]{1,0:T(4,128)(2,1)S(1)}, bf16[4,8192]{1,0:T(4,128)(2,1)S(1)}, u32[]{:S(2)}, u32[]{:S(2)}) collective-permute-start(bf16[4,8192]{1,0:T(4,128)(2,1)S(1)} %bitcast.102), channel_id=1, source_target_pairs={{1,0},{2,1},{3,2},{5,4},{6,5},{7,6},{9,8},{10,9},{11,10},{13,12},{... | collective-permute-start | bytes 196616 | tf_op jit(solution)/shard_map/ppermute | solution.py:42
  16.8 4.5 %collective-permute-start.3 = (bf16[4,8192]{1,0:T(4,128)(2,1)S(1)}, bf16[4,8192]{1,0:T(4,128)(2,1)S(1)}, u32[]{:S(2)}, u32[]{:S(2)}) collective-permute-start(bf16[4,8192]{1,0:T(4,128)(2,1)S(1)} %bitcast.104), channel_id=1, source_target_pairs={{0,1},{1,2},{2,3},{4,5},{5,6},{6,7},{8,9},{9,10},{10,11},{12,13},{... | collective-permute-start | bytes 196616 | tf_op jit(solution)/shard_map/ppermute | solution.py:41
  25.6 1.3 %collective-permute-done.5 = bf16[4,16,544]{2,1,0:T(8,128)(2,1)S(1)} collective-permute-done((bf16[4,16,544]{2,1,0:T(8,128)(2,1)S(1)}, bf16[4,16,544]{2,1,0:T(8,128)(2,1)S(1)}, u32[]{:S(2)}, u32[]{:S(2)}) %collective-permute-start.5) | collective-permute-done | bytes 69664 | tf_op jit(solution)/shard_map/ppermute | solution.py:34
  27.1 2.9 %pad_maximum_fusion.padded_ref = bf16[4,544,544]{2,1,0:T(8,128)(2,1)S(1)} fusion(bf16[4,16,544]{2,1,0:T(8,128)(2,1)S(1)} %get-tuple-element.44, bf16[4,512,16]{2,1,0:T(8,128)(2,1)} %bitcast.92, bf16[4,512,512]{2,1,0:T(8,128)(2,1)S(1)} %copy-done.3, bf16[4,512,16]{2,1,0:T(8,128)(2,1)} %bitcast.90, bf16[4,16,544]{2,1,0:T(8,128)(2,1)S(1)} %get-tuple-element.43), kind=kLoop, calls=%fused_computation | loop fusion | flops 11837440 | bytes 4734976 | tf_op jit(solution)/shard_map/concatenate | solution.py:46
  30.1 5.4 %shard_map.104 = f32[4,32,512]{2,1,0:T(8,128)S(1)} custom-call(s32[4]{0:T(128)S(1)} %get-tuple-element.35.off_ref, f32[4,3]{1,0:T(4,128)S(1)} %copy-done.1, bf16[3,256,256]{2,1,0:T(8,128)(2,1)S(1)} %copy-done, bf16[4,544,544]{2,1,0:T(8,128)(2,1)S(1)} %pad_maximum_fusion.padded_ref), custom_call_target="tpu_custom_call" | custom-call | flops 257949696 | bytes 2629632 | tf_op jit(solution)/shard_map/pallas_call | solution.py:207
  35.6 1.1 pad_maximum_fusion.1
  39.4 2.4 %collective-permute-start.7 = (f32[4,12]{1,0:T(4,128)S(1)}, f32[4,12]{1,0:T(4,128)S(1)}, u32[]{:S(2)}, u32[]{:S(2)}) collective-permute-start(f32[4,12]{1,0:T(4,128)S(1)} %fusion.26), channel_id=1, source_target_pairs={{0,1},{1,0},{2,3},{3,2},{4,5},{5,4},{6,7},{7,6},{8,9},{9,8},{10,11... | collective-permute-start | bytes 584 | tf_op jit(solution)/shard_map/ppermute | solution.py:96
  41.8 4.9 %shard_map.105.rest_0_ = f32[4,512,512]{2,1,0:T(8,128)} custom-call(f32[4,3]{1,0:T(4,128)S(1)} %copy-done.1, bf16[3,256,256]{2,1,0:T(8,128)(2,1)S(1)} %copy-done, bf16[4,544,544]{2,1,0:T(8,128)(2,1)S(1)} %pad_maximum_fusion.padded_ref), custom_call_target="tpu_custom_call" | custom-call | flops 1660944384 | bytes 3280896 | tf_op jit(solution)/shard_map/pallas_call | solution.py:264
  47.1 4.8 %shard_map.106.matched_ref = f32[4,512,512]{2,1,0:T(8,128)} custom-call(f32[4,3]{1,0:T(4,128)S(1)} %copy-done.1, bf16[3,256,256]{2,1,0:T(8,128)(2,1)S(1)} %copy-done, bf16[4,544,544]{2,1,0:T(8,128)(2,1)S(1)} %pad_maximum_fusion.padded_ref, f32[4,512,512]{2,1,0:T(8,128)} %shard_map.105.rest_0_), custom_call_target="tpu_custom_call", output_to_operand_aliasing={{}: (3, {})} | custom-call | flops 1660944384 | bytes 3280896 | tf_op jit(solution)/shard_map/pallas_call | solution.py:264
  52.2 1.1 %custom-call.4 = f32[4,3,3]{2,1,0:T(4,128)S(1)} custom-call(f32[4,3,3]{2,1,0:T(4,128)S(1)} %fusion.8), custom_call_target="Cholesky" | custom-call | tf_op jit(solution)/shard_map/jit(cholesky)/cholesky | solution.py:76
  54.4 9.2 %shard_map.107 = bf16[4,512,512]{2,1,0:T(8,128)(2,1)} custom-call(s32[4,2]{1,0:T(4,128)} %copy.119.idx_ref, f32[4,3]{1,0:T(4,128)} %pad_maximum_fusion.10.plane_ref, f32[4,4]{1,0:T(4,128)} %fusion.15.pick_ref, f32[1,512]{1,0:T(1,128)} %multiply_add_fusion.1.xrow_ref, f32[512,1]{1,0:T(8,128)} %multiply_add_fusion.ycol_ref, ...), custom_call_target="tpu_custom_call" | custom-call | flops 2147483648 | bytes 10485760 | tf_op jit(solution)/shard_map/pallas_call | solution.py:329
  63.6 1.2 %slice_bitcast_fusion.3 = bf16[512,512]{1,0:T(8,128)(2,1)S(1)} fusion(bf16[4,512,512]{2,1,0:T(8,128)(2,1)} %shard_map.107), kind=kLoop, calls=%fused_computation.13 | loop fusion | bytes 1048576 | tf_op jit(solution)/shard_map/squeeze | solution.py:344
  64.9 15.5 %collective-permute-done.9 = bf16[512,512]{1,0:T(8,128)(2,1)S(1)} collective-permute-done((bf16[512,512]{1,0:T(8,128)(2,1)S(1)}, bf16[512,512]{1,0:T(8,128)(2,1)S(1)}, u32[]{:S(2)}, u32[]{:S(2)}) %collective-permute-start.9) | collective-permute-done | bytes 524320 | tf_op jit(solution)/shard_map/ppermute | solution.py:346
  80.4 1.2 %fusion.3 = bf16[512,512]{1,0:T(8,128)(2,1)S(1)} fusion(bf16[512,512]{1,0:T(8,128)(2,1)S(1)} %collective-permute-done.9, bf16[4,512,512]{2,1,0:T(8,128)(2,1)} %shard_map.107), kind=kLoop, calls=%fused_computation.8 | loop fusion | flops 1048576 | bytes 1572864 | tf_op jit(solution)/shard_map/convert_element_type | solution.py:346
  81.6 14.6 %collective-permute-done.10 = bf16[512,512]{1,0:T(8,128)(2,1)S(1)} collective-permute-done((bf16[512,512]{1,0:T(8,128)(2,1)S(1)}, bf16[512,512]{1,0:T(8,128)(2,1)S(1)}, u32[]{:S(2)}, u32[]{:S(2)}) %collective-permute-start.10) | collective-permute-done | bytes 524320 | tf_op jit(solution)/shard_map/ppermute | solution.py:346
  98.1 12.0 %collective-permute-done.11 = bf16[512,512]{1,0:T(8,128)(2,1)S(1)} collective-permute-done((bf16[512,512]{1,0:T(8,128)(2,1)S(1)}, bf16[512,512]{1,0:T(8,128)(2,1)S(1)}, u32[]{:S(2)}, u32[]{:S(2)}) %collective-permute-start.11) | collective-permute-done | bytes 524320 | tf_op jit(solution)/shard_map/ppermute | solution.py:346
  110.2 1.8 %fusion.1 = f32[1,512,512]{2,1,0:T(8,128)} fusion(bf16[512,512]{1,0:T(8,128)(2,1)S(1)} %collective-permute-done.11, bf16[4,512,512]{2,1,0:T(8,128)(2,1)S(1)} %copy-done.4, f32[]{:T(128)} %convert_reduce_fusion), kind=kLoop, calls=%fused_computation.4 | loop fusion | flops 1048576 | bytes 2097156 | tf_op jit(solution)/shard_map/div | solution.py:474
  (98 shorter events, 13.3 us)
Async XLA Ops:
  0.6 14.2 %copy-start.2 = (bf16[4,512,512]{2,1,0:T(8,128)(2,1)S(1)}, bf16[4,512,512]{2,1,0:T(8,128)(2,1)}, u32[]{:S(2)}) copy-start(bf16[4,512,512]{2,1,0:T(8,128)(2,1)} %param.11) | copy-start | bytes 6291460
  4.1 19.3 %copy-start.10 = (bf16[4,1,1]{0,2,1:T(2,128)(2,1)S(1)}, bf16[4,1,1]{0,2,1:T(2,128)(2,1)}, u32[]{:S(2)}) copy-start(bf16[4,1,1]{0,2,1:T(2,128)(2,1)} %param.14) | copy-start | bytes 28
  6.9 28.6 %collective-permute-start.1 = (bf16[144,512]{1,0:T(8,128)(2,1)}, bf16[144,512]{1,0:T(8,128)(2,1)S(1)}, u32[]{:S(2)}, u32[]{:S(2)}) collective-permute-start(bf16[144,512]{1,0:T(8,128)(2,1)} %get-tuple-element.42), channel_id=1, source_target_pairs={{0,16},{8,24},{16,0},{24,8},{1,17},{9,25},{17,1},{25,9},{2,18},{10... | collective-permute-start | bytes 442376 | tf_op jit(solution)/shard_map/ppermute | solution.py:402
  11.0 24.6 %collective-permute-start = (bf16[144,512]{1,0:T(8,128)(2,1)}, bf16[144,512]{1,0:T(8,128)(2,1)}, u32[]{:S(2)}, u32[]{:S(2)}) collective-permute-start(bf16[144,512]{1,0:T(8,128)(2,1)} %get-tuple-element.42), channel_id=1, source_target_pairs={{0,8},{8,16},{16,24},{24,0},{1,9},{9,17},{17,25},{25,1},{2,10},{10... | collective-permute-start | bytes 442376 | tf_op jit(solution)/shard_map/ppermute | solution.py:402
  12.5 23.0 %collective-permute-start.2 = (bf16[144,512]{1,0:T(8,128)(2,1)}, bf16[144,512]{1,0:T(8,128)(2,1)}, u32[]{:S(2)}, u32[]{:S(2)}) collective-permute-start(bf16[144,512]{1,0:T(8,128)(2,1)} %get-tuple-element.42), channel_id=1, source_target_pairs={{0,24},{8,0},{16,8},{24,16},{1,25},{9,1},{17,9},{25,17},{2,26},{10... | collective-permute-start | bytes 442376 | tf_op jit(solution)/shard_map/ppermute | solution.py:402
  15.3 9.4 %collective-permute-start.4 = (bf16[4,8192]{1,0:T(4,128)(2,1)S(1)}, bf16[4,8192]{1,0:T(4,128)(2,1)S(1)}, u32[]{:S(2)}, u32[]{:S(2)}) collective-permute-start(bf16[4,8192]{1,0:T(4,128)(2,1)S(1)} %bitcast.102), channel_id=1, source_target_pairs={{1,0},{2,1},{3,2},{5,4},{6,5},{7,6},{9,8},{10,9},{11,10},{13,12},{... | collective-permute-start | bytes 196616 | tf_op jit(solution)/shard_map/ppermute | solution.py:42
  16.8 7.9 %collective-permute-start.3 = (bf16[4,8192]{1,0:T(4,128)(2,1)S(1)}, bf16[4,8192]{1,0:T(4,128)(2,1)S(1)}, u32[]{:S(2)}, u32[]{:S(2)}) collective-permute-start(bf16[4,8192]{1,0:T(4,128)(2,1)S(1)} %bitcast.104), channel_id=1, source_target_pairs={{0,1},{1,2},{2,3},{4,5},{5,6},{6,7},{8,9},{9,10},{10,11},{12,13},{... | collective-permute-start | bytes 196616 | tf_op jit(solution)/shard_map/ppermute | solution.py:41
  25.0 1.8 %copy-start.5 = (bf16[4,16,512]{1,2,0:T(8,128)(2,1)}, bf16[4,16,512]{1,2,0:T(8,128)(2,1)S(1)}, u32[]{:S(2)}) copy-start(bf16[4,16,512]{1,2,0:T(8,128)(2,1)S(1)} %copy.99) | copy-start | bytes 196612
  25.3 1.5 %copy-start.6 = (bf16[4,16,512]{1,2,0:T(8,128)(2,1)}, bf16[4,16,512]{1,2,0:T(8,128)(2,1)S(1)}, u32[]{:S(2)}) copy-start(bf16[4,16,512]{1,2,0:T(8,128)(2,1)S(1)} %copy.101) | copy-start | bytes 196612
  25.3 1.8 %copy-start.3 = (bf16[4,512,512]{2,1,0:T(8,128)(2,1)S(1)}, bf16[4,512,512]{2,1,0:T(8,128)(2,1)}, u32[]{:S(2)}) copy-start(bf16[4,512,512]{2,1,0:T(8,128)(2,1)} %param.11) | copy-start | bytes 6291460
  25.5 1.3 %collective-permute-start.5 = (bf16[4,16,544]{2,1,0:T(8,128)(2,1)S(1)}, bf16[4,16,544]{2,1,0:T(8,128)(2,1)S(1)}, u32[]{:S(2)}, u32[]{:S(2)}) collective-permute-start(bf16[4,16,544]{2,1,0:T(8,128)(2,1)S(1)} %fusion.7), channel_id=1, source_target_pairs={{0,4},{4,0},{1,5},{5,1},{2,6},{6,2},{3,7},{7,3},{8,12},{12,8},{9,1... | collective-permute-start | bytes 208904 | tf_op jit(solution)/shard_map/ppermute | solution.py:34
  27.1 2.9 %copy-start = (bf16[3,256,256]{2,1,0:T(8,128)(2,1)S(1)}, bf16[3,256,256]{2,1,0:T(8,128)(2,1)}, u32[]{:S(2)}) copy-start(bf16[3,256,256]{2,1,0:T(8,128)(2,1)} %constant.168.clone.tb_ref.blk_ref) | copy-start | bytes 1179652
  27.1 2.9 %copy-start.1 = (f32[4,3]{1,0:T(4,128)S(1)}, f32[4,3]{1,0:T(4,128)}, u32[]{:S(2)}) copy-start(f32[4,3]{1,0:T(4,128)} %coef_ref.5) | copy-start | bytes 148
  30.0 6.6 %copy-start.7 = (s32[4]{0:T(128)S(1)}, s32[4]{0:T(128)}, u32[]{:S(2)}) copy-start(s32[4]{0:T(128)} %get-tuple-element.58) | copy-start | bytes 52
  30.1 8.2 %copy-start.8 = (s32[4,1,1,2]{0,3,2,1:T(2,128)S(1)}, s32[4,1,1,2]{0,3,2,1:T(2,128)}, u32[]{:S(2)}) copy-start(s32[4,1,1,2]{0,3,2,1:T(2,128)} %param.16) | copy-start | bytes 100
  38.2 1.2 %collective-permute-start.6 = (f32[4,12]{1,0:T(4,128)S(1)}, f32[4,12]{1,0:T(4,128)S(1)}, u32[]{:S(2)}, u32[]{:S(2)}) collective-permute-start(f32[4,12]{1,0:T(4,128)S(1)} %pad_maximum_fusion.9), channel_id=1, source_target_pairs={{0,4},{4,0},{1,5},{5,1},{2,6},{6,2},{3,7},{7,3},{8,12},{12,8},{9,1... | collective-permute-start | bytes 584 | tf_op jit(solution)/shard_map/ppermute | solution.py:96
  39.4 7.2 %collective-permute-start.7 = (f32[4,12]{1,0:T(4,128)S(1)}, f32[4,12]{1,0:T(4,128)S(1)}, u32[]{:S(2)}, u32[]{:S(2)}) collective-permute-start(f32[4,12]{1,0:T(4,128)S(1)} %fusion.26), channel_id=1, source_target_pairs={{0,1},{1,0},{2,3},{3,2},{4,5},{5,4},{6,7},{7,6},{8,9},{9,8},{10,11... | collective-permute-start | bytes 584 | tf_op jit(solution)/shard_map/ppermute | solution.py:96
  46.7 6.8 %copy-start.9 = (pred[3,3]{1,0:T(4,128)(4,1)S(1)}, pred[3,3]{1,0:T(4,128)(4,1)}, u32[]{:S(2)}) copy-start(pred[3,3]{1,0:T(4,128)(4,1)} %iota_compare_fusion.2) | copy-start | bytes 31
  46.7 5.3 %collective-permute-start.8 = (f32[4,12]{1,0:T(4,128)S(1)}, f32[4,12]{1,0:T(4,128)S(1)}, u32[]{:S(2)}, u32[]{:S(2)}) collective-permute-start(f32[4,12]{1,0:T(4,128)S(1)} %add.241), channel_id=1, source_target_pairs={{0,2},{1,3},{2,0},{3,1},{4,6},{5,7},{6,4},{7,5},{8,10},{9,11},{10,... | collective-permute-start | bytes 584 | tf_op jit(solution)/shard_map/ppermute | solution.py:96
  63.6 32.7 %copy-start.4 = (bf16[4,512,512]{2,1,0:T(8,128)(2,1)S(1)}, bf16[4,512,512]{2,1,0:T(8,128)(2,1)}, u32[]{:S(2)}) copy-start(bf16[4,512,512]{2,1,0:T(8,128)(2,1)} %shard_map.107) | copy-start | bytes 6291460
  64.8 15.6 %collective-permute-start.9 = (bf16[512,512]{1,0:T(8,128)(2,1)S(1)}, bf16[512,512]{1,0:T(8,128)(2,1)S(1)}, u32[]{:S(2)}, u32[]{:S(2)}) collective-permute-start(bf16[512,512]{1,0:T(8,128)(2,1)S(1)} %slice_bitcast_fusion.3), channel_id=1, source_target_pairs={{0,8},{8,16},{16,24},{24,0},{1,9},{9,17},{17,25},{25,1},{2,10},{10... | collective-permute-start | bytes 1572872 | tf_op jit(solution)/shard_map/ppermute | solution.py:346
  81.5 14.7 %collective-permute-start.10 = (bf16[512,512]{1,0:T(8,128)(2,1)S(1)}, bf16[512,512]{1,0:T(8,128)(2,1)S(1)}, u32[]{:S(2)}, u32[]{:S(2)}) collective-permute-start(bf16[512,512]{1,0:T(8,128)(2,1)S(1)} %fusion.3), channel_id=1, source_target_pairs={{0,8},{8,16},{16,24},{24,0},{1,9},{9,17},{17,25},{25,1},{2,10},{10... | collective-permute-start | bytes 1572872 | tf_op jit(solution)/shard_map/ppermute | solution.py:346
  96.4 13.8 %collective-permute-start.11 = (bf16[512,512]{1,0:T(8,128)(2,1)S(1)}, bf16[512,512]{1,0:T(8,128)(2,1)S(1)}, u32[]{:S(2)}, u32[]{:S(2)}) collective-permute-start(bf16[512,512]{1,0:T(8,128)(2,1)S(1)} %fusion.2), channel_id=1, source_target_pairs={{0,8},{8,16},{16,24},{24,0},{1,9},{9,17},{17,25},{25,1},{2,10},{10... | collective-permute-start | bytes 1572872 | tf_op jit(solution)/shard_map/ppermute | solution.py:346

commit v16 on v15

--- a/solution.py
+++ b/solution.py
@@ -305,9 +305,10 @@
         out_ref[...] = acc_ref[...].astype(jnp.bfloat16)
 
 
-def warp_tiles(choose, plane, picked, xrow, ycol, matched, bank):
+def warp_tiles(choose, plane, picked, xrow, ycol, matched, bank, part, pieces):
     exp_dev, tile_len = matched.shape[0], matched.shape[1]
     patches = picked.shape[1]
+    rows = tile_len // pieces
     grid_spec = pltpu.PrefetchScalarGridSpec(
         num_scalar_prefetch=1,
         grid=(exp_dev,),
@@ -317,19 +318,20 @@
             pl.BlockSpec((1, tile_len), lambda e, idx: (0, 0)),
             pl.BlockSpec((tile_len, 1), lambda e, idx: (0, 0)),
             pl.BlockSpec((1, tile_len, tile_len), lambda e, idx: (e, 0, 0)),
-            pl.BlockSpec((1, tile_len, tile_len), lambda e, idx: (idx[e, 0], 0, 0)),
+            pl.BlockSpec((1, rows, tile_len), lambda e, idx: (idx[e, 0], part, 0)),
             pl.BlockSpec((1, tile_len, tile_len), lambda e, idx: (idx[e, 1], 0, 0)),
         ],
-        out_specs=pl.BlockSpec((patches, tile_len, tile_len), lambda e, idx: (0, 0, 0)),
-        scratch_shapes=[pltpu.VMEM((patches, tile_len, tile_len), jnp.float32)],
-    )
-    flops = exp_dev * 4 * tile_len ** 3
-    moved = exp_dev * tile_len * tile_len * (4 + 2 + 2) + patches * tile_len * tile_len * 2
+        out_specs=pl.BlockSpec((patches, rows, tile_len), lambda e, idx: (0, 0, 0)),
+        scratch_shapes=[pltpu.VMEM((patches, rows, tile_len), jnp.float32)],
+    )
+    flops = exp_dev * 4 * rows * tile_len * tile_len
+    moved = exp_dev * tile_len * tile_len * (4 + 2) + exp_dev * rows * tile_len * 2
+    moved = moved + patches * rows * tile_len * 2
     vmem = 60 * 1024 * 1024
     return pl.pallas_call(
         warp_body,
         grid_spec=grid_spec,
-        out_shape=jax.ShapeDtypeStruct((patches, tile_len, tile_len), jnp.bfloat16),
+        out_shape=jax.ShapeDtypeStruct((patches, rows, tile_len), jnp.bfloat16),
         compiler_params=pltpu.CompilerParams(
             dimension_semantics=("arbitrary",), vmem_limit_bytes=vmem
         ),
@@ -466,11 +468,12 @@
         % visit_count
     ).astype(jnp.float32)
     picked_ring = jnp.dot(picked.astype(jnp.float32), ring_order, precision=lax.Precision.HIGHEST)
-    partial_sum = warp_tiles(
+    halves = [warp_tiles(
         choose, plane_fit, picked_ring, xcoord.reshape(1, tile_len),
-        row_coord.reshape(tile_len, 1), matched, resample_bank,
-    )
-    numerator = ring_scatter(partial_sum, "visit", visit_count)[None]
+        row_coord.reshape(tile_len, 1), matched, resample_bank, part, 2) for part in range(2)]
+    numerator = jnp.concatenate(
+        [ring_scatter(piece, "visit", visit_count) for piece in halves], 0
+    )[None]
     coadd_patch = numerator / denominator[:, None, None]
     return (coadd_patch, plane_fit)
 

time: 113 us -> 106 us (0.938)
  waiting for transfers between devices: 43.9 us -> 30.1 us
  Pallas kernels: 24.3 us -> 29.8 us
    ppermute x3 -> x6, waiting for transfers between devices: 42.2 us -> 28.4 us  [ring_scatter(): lax.ppermute(outgoing.astype(jnp.bfloat16), axis, ring).astype(jnp.float32)]
    pallas_call x1 -> x2, Pallas kernels: 9.21 us -> 14.7 us  [warp_tiles(): pl.pallas_call(warp_body, grid_spec=grid_spec, out_shape=jax.ShapeDtypeSt...]
  transfers between devices with their start and end apart: 12 -> 15, of which waited for: 5 -> 8; matrix products, arithmetic and copies ran while one was open for 9% -> 13% of each run, Pallas kernels for 13% -> 21%
where the time goes in v16:
time: 106 us
  waiting for transfers between devices  30.1 us (28%)
  Pallas kernels  29.8 us (28%)
  other arithmetic  18.1 us (17%)
  starting transfers between devices  17 us (16%)
  local copies, waits for them, and re-layouts  6.23 us (6%)
  matrix products  3.27 us (3%)
  between operations  1.09 us (1%)
    ppermute x6, waiting for transfers between devices, ring_scatter(): lax.ppermute(outgoing.astype(jnp.bfloat16), axis, ring).astype(jnp.float32)  28.4 us
    pallas_call x2, Pallas kernels, warp_tiles(): pl.pallas_call(warp_body, grid_spec=grid_spec, out_shape=jax.ShapeDtypeSt...  14.7 us
    pallas_call x2, Pallas kernels, band_tiles(): pl.pallas_call(functools.partial(band_body, first), grid=(count,), in_spe...  9.67 us
    ppermute x3, starting transfers between devices, shards(): received.append(lax.ppermute(payload, 'visit', pairs))  7.86 us
    pallas_call x1, Pallas kernels, strip_tiles(): pl.pallas_call(strip_body, grid_spec=grid_spec, out_shape=jax.ShapeDtypeS...  5.43 us
    ppermute x1, starting transfers between devices, extended(): before = lax.ppermute(last, axis, up)  4.55 us
    concatenate x1, other arithmetic, extended(): value = jnp.concatenate([before, value, after], axis=dim)  2.9 us
    ppermute x3, starting transfers between devices, butterfly_sum(): values = jax.tree.map(lambda v: v + lax.ppermute(v, axis, pairs), values)  2.83 us
  transfers between devices with their start and end apart: 15, of which 8 were waited for; matrix products, arithmetic and copies ran while one was open for 13% of the time, Pallas kernels for 21%

profile of v16, /device:TPU:0, one launch (start us, length us, event | category | flops | bytes accessed | tf_op | source)
XLA Modules:
  0.0 105.7 jit_solution(12350387117395520560)
XLA Ops:
  4.1 2.1 %convolution_convert_fusion = bf16[4,32,512]{2,1,0:T(8,128)(2,1)S(1)} fusion(bf16[4,512,512]{2,1,0:T(8,128)(2,1)} %param.11, s32[4]{0:T(128)S(1)} %get-tuple-element.35.off_ref), kind=kOutput, calls=%fused_computation.1 | convolution fusion | flops 67305472 | bytes 2228240 | tf_op jit(solution)/shard_map/esr,erl->esl/dot_general | solution.py:384
  6.9 4.0 %collective-permute-start.1 = (bf16[144,512]{1,0:T(8,128)(2,1)}, bf16[144,512]{1,0:T(8,128)(2,1)S(1)}, u32[]{:S(2)}, u32[]{:S(2)}) collective-permute-start(bf16[144,512]{1,0:T(8,128)(2,1)} %get-tuple-element.42), channel_id=1, source_target_pairs={{0,16},{8,24},{16,0},{24,8},{1,17},{9,25},{17,1},{25,9},{2,18},{10... | collective-permute-start | bytes 442376 | tf_op jit(solution)/shard_map/ppermute | solution.py:404
  11.0 1.6 %collective-permute-start = (bf16[144,512]{1,0:T(8,128)(2,1)}, bf16[144,512]{1,0:T(8,128)(2,1)}, u32[]{:S(2)}, u32[]{:S(2)}) collective-permute-start(bf16[144,512]{1,0:T(8,128)(2,1)} %get-tuple-element.42), channel_id=1, source_target_pairs={{0,8},{8,16},{16,24},{24,0},{1,9},{9,17},{17,25},{25,1},{2,10},{10... | collective-permute-start | bytes 442376 | tf_op jit(solution)/shard_map/ppermute | solution.py:404
  12.5 2.2 %collective-permute-start.2 = (bf16[144,512]{1,0:T(8,128)(2,1)}, bf16[144,512]{1,0:T(8,128)(2,1)}, u32[]{:S(2)}, u32[]{:S(2)}) collective-permute-start(bf16[144,512]{1,0:T(8,128)(2,1)} %get-tuple-element.42), channel_id=1, source_target_pairs={{0,24},{8,0},{16,8},{24,16},{1,25},{9,1},{17,9},{25,17},{2,26},{10... | collective-permute-start | bytes 442376 | tf_op jit(solution)/shard_map/ppermute | solution.py:404
  15.3 1.3 %collective-permute-start.4 = (bf16[4,8192]{1,0:T(4,128)(2,1)S(1)}, bf16[4,8192]{1,0:T(4,128)(2,1)S(1)}, u32[]{:S(2)}, u32[]{:S(2)}) collective-permute-start(bf16[4,8192]{1,0:T(4,128)(2,1)S(1)} %bitcast.121), channel_id=1, source_target_pairs={{1,0},{2,1},{3,2},{5,4},{6,5},{7,6},{9,8},{10,9},{11,10},{13,12},{... | collective-permute-start | bytes 196616 | tf_op jit(solution)/shard_map/ppermute | solution.py:42
  16.8 4.5 %collective-permute-start.3 = (bf16[4,8192]{1,0:T(4,128)(2,1)S(1)}, bf16[4,8192]{1,0:T(4,128)(2,1)S(1)}, u32[]{:S(2)}, u32[]{:S(2)}) collective-permute-start(bf16[4,8192]{1,0:T(4,128)(2,1)S(1)} %bitcast.123), channel_id=1, source_target_pairs={{0,1},{1,2},{2,3},{4,5},{5,6},{6,7},{8,9},{9,10},{10,11},{12,13},{... | collective-permute-start | bytes 196616 | tf_op jit(solution)/shard_map/ppermute | solution.py:41
  25.6 1.3 %collective-permute-done.5 = bf16[4,16,544]{2,1,0:T(8,128)(2,1)S(1)} collective-permute-done((bf16[4,16,544]{2,1,0:T(8,128)(2,1)S(1)}, bf16[4,16,544]{2,1,0:T(8,128)(2,1)S(1)}, u32[]{:S(2)}, u32[]{:S(2)}) %collective-permute-start.5) | collective-permute-done | bytes 69664 | tf_op jit(solution)/shard_map/ppermute | solution.py:34
  27.1 2.9 %pad_maximum_fusion.padded_ref = bf16[4,544,544]{2,1,0:T(8,128)(2,1)S(1)} fusion(bf16[4,16,544]{2,1,0:T(8,128)(2,1)S(1)} %get-tuple-element.44, bf16[4,512,16]{2,1,0:T(8,128)(2,1)} %bitcast.111, bf16[4,512,512]{2,1,0:T(8,128)(2,1)S(1)} %copy-done.3, bf16[4,512,16]{2,1,0:T(8,128)(2,1)} %bitcast.109, bf16[4,16,544]{2,1,0:T(8,128)(2,1)S(1)} %get-tuple-element.43), kind=kLoop, calls=%fused_computation | loop fusion | flops 11837440 | bytes 4734976 | tf_op jit(solution)/shard_map/concatenate | solution.py:46
  30.1 5.4 %shard_map.104 = f32[4,32,512]{2,1,0:T(8,128)S(1)} custom-call(s32[4]{0:T(128)S(1)} %get-tuple-element.35.off_ref, f32[4,3]{1,0:T(4,128)S(1)} %copy-done.1, bf16[3,256,256]{2,1,0:T(8,128)(2,1)S(1)} %copy-done, bf16[4,544,544]{2,1,0:T(8,128)(2,1)S(1)} %pad_maximum_fusion.padded_ref), custom_call_target="tpu_custom_call" | custom-call | flops 257949696 | bytes 2629632 | tf_op jit(solution)/shard_map/pallas_call | solution.py:207
  35.6 1.1 %pad_maximum_fusion.1 = bf16[4,144,512]{2,1,0:T(8,128)(2,1)S(1)} fusion(bf16[1,144,512]{2,1,0:T(8,128)(2,1)} %bitcast.12, bf16[1,144,512]{2,1,0:T(8,128)(2,1)S(1)} %bitcast.113, bf16[1,144,512]{2,1,0:T(8,128)(2,1)} %bitcast.10, bf16[1,144,512]{2,1,0:T(8,128)(2,1)S(1)} %get-tuple-element.41), kind=kLoop, calls=%fused_computation.3 | loop fusion | flops 884736 | bytes 1179648 | tf_op jit(solution)/shard_map/stack | solution.py:405
  39.4 2.4 %collective-permute-start.7 = (f32[4,12]{1,0:T(4,128)S(1)}, f32[4,12]{1,0:T(4,128)S(1)}, u32[]{:S(2)}, u32[]{:S(2)}) collective-permute-start(f32[4,12]{1,0:T(4,128)S(1)} %fusion.28), channel_id=1, source_target_pairs={{0,1},{1,0},{2,3},{3,2},{4,5},{5,4},{6,7},{7,6},{8,9},{9,8},{10,11... | collective-permute-start | bytes 584 | tf_op jit(solution)/shard_map/ppermute | solution.py:96
  41.8 4.9 %shard_map.105.rest_0_ = f32[4,512,512]{2,1,0:T(8,128)} custom-call(f32[4,3]{1,0:T(4,128)S(1)} %copy-done.1, bf16[3,256,256]{2,1,0:T(8,128)(2,1)S(1)} %copy-done, bf16[4,544,544]{2,1,0:T(8,128)(2,1)S(1)} %pad_maximum_fusion.padded_ref), custom_call_target="tpu_custom_call" | custom-call | flops 1660944384 | bytes 3280896 | tf_op jit(solution)/shard_map/pallas_call | solution.py:264
  47.1 4.8 %shard_map.106.matched_ref = f32[4,512,512]{2,1,0:T(8,128)} custom-call(f32[4,3]{1,0:T(4,128)S(1)} %copy-done.1, bf16[3,256,256]{2,1,0:T(8,128)(2,1)S(1)} %copy-done, bf16[4,544,544]{2,1,0:T(8,128)(2,1)S(1)} %pad_maximum_fusion.padded_ref, f32[4,512,512]{2,1,0:T(8,128)} %shard_map.105.rest_0_), custom_call_target="tpu_custom_call", output_to_operand_aliasing={{}: (3, {})} | custom-call | flops 1660944384 | bytes 3280896 | tf_op jit(solution)/shard_map/pallas_call | solution.py:264
  52.2 1.1 %custom-call.4 = f32[4,3,3]{2,1,0:T(4,128)S(1)} custom-call(f32[4,3,3]{2,1,0:T(4,128)S(1)} %fusion.10), custom_call_target="Cholesky" | custom-call | tf_op jit(solution)/shard_map/jit(cholesky)/cholesky | solution.py:76
  54.4 7.3 %shard_map.108 = bf16[4,256,512]{2,1,0:T(8,128)(2,1)} custom-call(s32[4,2]{1,0:T(4,128)} %copy.122.idx_ref, f32[4,3]{1,0:T(4,128)} %pad_maximum_fusion.10.plane_ref, f32[4,4]{1,0:T(4,128)} %fusion.17.pick_ref, f32[1,512]{1,0:T(1,128)} %multiply_add_fusion.1.xrow_ref, f32[512,1]{1,0:T(8,128)} %multiply_add_fusion.ycol_ref, ...), custom_call_target="tpu_custom_call" | custom-call | flops 1073741824 | bytes 8388608 | tf_op jit(solution)/shard_map/pallas_call | solution.py:331
  62.7 7.4 %shard_map.107 = bf16[4,256,512]{2,1,0:T(8,128)(2,1)} custom-call(s32[4,2]{1,0:T(4,128)} %copy.122.idx_ref, f32[4,3]{1,0:T(4,128)} %pad_maximum_fusion.10.plane_ref, f32[4,4]{1,0:T(4,128)} %fusion.17.pick_ref, f32[1,512]{1,0:T(1,128)} %multiply_add_fusion.1.xrow_ref, f32[512,1]{1,0:T(8,128)} %multiply_add_fusion.ycol_ref, ...), custom_call_target="tpu_custom_call" | custom-call | flops 1073741824 | bytes 8388608 | tf_op jit(solution)/shard_map/pallas_call | solution.py:331
  70.1 1.1 slice_bitcast_fusion.9
  71.3 1.4 %collective-permute-done.12 = bf16[256,512]{1,0:T(8,128)(2,1)S(1)} collective-permute-done((bf16[256,512]{1,0:T(8,128)(2,1)S(1)}, bf16[256,512]{1,0:T(8,128)(2,1)S(1)}, u32[]{:S(2)}, u32[]{:S(2)}) %collective-permute-start.12) | collective-permute-done | bytes 262176 | tf_op jit(solution)/shard_map/ppermute | solution.py:348
  72.9 9.3 %collective-permute-done.9 = bf16[256,512]{1,0:T(8,128)(2,1)S(1)} collective-permute-done((bf16[256,512]{1,0:T(8,128)(2,1)S(1)}, bf16[256,512]{1,0:T(8,128)(2,1)S(1)}, u32[]{:S(2)}, u32[]{:S(2)}) %collective-permute-start.9) | collective-permute-done | bytes 262176 | tf_op jit(solution)/shard_map/ppermute | solution.py:348
  83.3 4.5 %collective-permute-done.13 = bf16[256,512]{1,0:T(8,128)(2,1)S(1)} collective-permute-done((bf16[256,512]{1,0:T(8,128)(2,1)S(1)}, bf16[256,512]{1,0:T(8,128)(2,1)S(1)}, u32[]{:S(2)}, u32[]{:S(2)}) %collective-permute-start.13) | collective-permute-done | bytes 262176 | tf_op jit(solution)/shard_map/ppermute | solution.py:348
  88.0 6.4 %collective-permute-done.10 = bf16[256,512]{1,0:T(8,128)(2,1)S(1)} collective-permute-done((bf16[256,512]{1,0:T(8,128)(2,1)S(1)}, bf16[256,512]{1,0:T(8,128)(2,1)S(1)}, u32[]{:S(2)}, u32[]{:S(2)}) %collective-permute-start.10) | collective-permute-done | bytes 262176 | tf_op jit(solution)/shard_map/ppermute | solution.py:348
  96.1 3.9 %collective-permute-done.14 = bf16[256,512]{1,0:T(8,128)(2,1)} collective-permute-done((bf16[256,512]{1,0:T(8,128)(2,1)S(1)}, bf16[256,512]{1,0:T(8,128)(2,1)}, u32[]{:S(2)}, u32[]{:S(2)}) %collective-permute-start.14) | collective-permute-done | bytes 262176 | tf_op jit(solution)/shard_map/ppermute | solution.py:348
  101.1 2.8 %collective-permute-done.11 = bf16[256,512]{1,0:T(8,128)(2,1)S(1)} collective-permute-done((bf16[256,512]{1,0:T(8,128)(2,1)S(1)}, bf16[256,512]{1,0:T(8,128)(2,1)S(1)}, u32[]{:S(2)}, u32[]{:S(2)}) %collective-permute-start.11) | collective-permute-done | bytes 262176 | tf_op jit(solution)/shard_map/ppermute | solution.py:348
  104.0 1.7 %maximum_divide_fusion = f32[1,512,512]{2,1,0:T(8,128)} fusion(f32[1,256,512]{2,1,0:T(8,128)S(1)} %fusion, f32[1,256,512]{2,1,0:T(8,128)S(1)} %fusion.3, f32[]{:T(128)} %convert_reduce_fusion), kind=kLoop, calls=%fused_computation.2 | loop fusion | flops 524288 | bytes 2097156 | tf_op jit(solution)/shard_map/div | solution.py:477
  (112 shorter events, 19.1 us)
Async XLA Ops:
  0.6 14.2 %copy-start.2 = (bf16[4,512,512]{2,1,0:T(8,128)(2,1)S(1)}, bf16[4,512,512]{2,1,0:T(8,128)(2,1)}, u32[]{:S(2)}) copy-start(bf16[4,512,512]{2,1,0:T(8,128)(2,1)} %param.11) | copy-start | bytes 6291460
  4.1 19.3 %copy-start.11 = (bf16[4,1,1]{0,2,1:T(2,128)(2,1)S(1)}, bf16[4,1,1]{0,2,1:T(2,128)(2,1)}, u32[]{:S(2)}) copy-start(bf16[4,1,1]{0,2,1:T(2,128)(2,1)} %param.14) | copy-start | bytes 28
  6.9 28.6 %collective-permute-start.1 = (bf16[144,512]{1,0:T(8,128)(2,1)}, bf16[144,512]{1,0:T(8,128)(2,1)S(1)}, u32[]{:S(2)}, u32[]{:S(2)}) collective-permute-start(bf16[144,512]{1,0:T(8,128)(2,1)} %get-tuple-element.42), channel_id=1, source_target_pairs={{0,16},{8,24},{16,0},{24,8},{1,17},{9,25},{17,1},{25,9},{2,18},{10... | collective-permute-start | bytes 442376 | tf_op jit(solution)/shard_map/ppermute | solution.py:404
  11.0 24.6 %collective-permute-start = (bf16[144,512]{1,0:T(8,128)(2,1)}, bf16[144,512]{1,0:T(8,128)(2,1)}, u32[]{:S(2)}, u32[]{:S(2)}) collective-permute-start(bf16[144,512]{1,0:T(8,128)(2,1)} %get-tuple-element.42), channel_id=1, source_target_pairs={{0,8},{8,16},{16,24},{24,0},{1,9},{9,17},{17,25},{25,1},{2,10},{10... | collective-permute-start | bytes 442376 | tf_op jit(solution)/shard_map/ppermute | solution.py:404
  12.5 23.0 %collective-permute-start.2 = (bf16[144,512]{1,0:T(8,128)(2,1)}, bf16[144,512]{1,0:T(8,128)(2,1)}, u32[]{:S(2)}, u32[]{:S(2)}) collective-permute-start(bf16[144,512]{1,0:T(8,128)(2,1)} %get-tuple-element.42), channel_id=1, source_target_pairs={{0,24},{8,0},{16,8},{24,16},{1,25},{9,1},{17,9},{25,17},{2,26},{10... | collective-permute-start | bytes 442376 | tf_op jit(solution)/shard_map/ppermute | solution.py:404
  15.3 9.4 %collective-permute-start.4 = (bf16[4,8192]{1,0:T(4,128)(2,1)S(1)}, bf16[4,8192]{1,0:T(4,128)(2,1)S(1)}, u32[]{:S(2)}, u32[]{:S(2)}) collective-permute-start(bf16[4,8192]{1,0:T(4,128)(2,1)S(1)} %bitcast.121), channel_id=1, source_target_pairs={{1,0},{2,1},{3,2},{5,4},{6,5},{7,6},{9,8},{10,9},{11,10},{13,12},{... | collective-permute-start | bytes 196616 | tf_op jit(solution)/shard_map/ppermute | solution.py:42
  16.8 7.9 %collective-permute-start.3 = (bf16[4,8192]{1,0:T(4,128)(2,1)S(1)}, bf16[4,8192]{1,0:T(4,128)(2,1)S(1)}, u32[]{:S(2)}, u32[]{:S(2)}) collective-permute-start(bf16[4,8192]{1,0:T(4,128)(2,1)S(1)} %bitcast.123), channel_id=1, source_target_pairs={{0,1},{1,2},{2,3},{4,5},{5,6},{6,7},{8,9},{9,10},{10,11},{12,13},{... | collective-permute-start | bytes 196616 | tf_op jit(solution)/shard_map/ppermute | solution.py:41
  25.5 1.3 %collective-permute-start.5 = (bf16[4,16,544]{2,1,0:T(8,128)(2,1)S(1)}, bf16[4,16,544]{2,1,0:T(8,128)(2,1)S(1)}, u32[]{:S(2)}, u32[]{:S(2)}) collective-permute-start(bf16[4,16,544]{2,1,0:T(8,128)(2,1)S(1)} %fusion.9), channel_id=1, source_target_pairs={{0,4},{4,0},{1,5},{5,1},{2,6},{6,2},{3,7},{7,3},{8,12},{12,8},{9,1... | collective-permute-start | bytes 208904 | tf_op jit(solution)/shard_map/ppermute | solution.py:34
  27.1 2.9 %copy-start = (bf16[3,256,256]{2,1,0:T(8,128)(2,1)S(1)}, bf16[3,256,256]{2,1,0:T(8,128)(2,1)}, u32[]{:S(2)}) copy-start(bf16[3,256,256]{2,1,0:T(8,128)(2,1)} %constant.168.clone.tb_ref.blk_ref) | copy-start | bytes 1179652
  27.1 2.9 %copy-start.1 = (f32[4,3]{1,0:T(4,128)S(1)}, f32[4,3]{1,0:T(4,128)}, u32[]{:S(2)}) copy-start(f32[4,3]{1,0:T(4,128)} %coef_ref.5) | copy-start | bytes 148
  30.1 6.6 %copy-start.8 = (s32[4]{0:T(128)S(1)}, s32[4]{0:T(128)}, u32[]{:S(2)}) copy-start(s32[4]{0:T(128)} %get-tuple-element.58) | copy-start | bytes 52
  30.1 8.1 %copy-start.9 = (s32[4,1,1,2]{0,3,2,1:T(2,128)S(1)}, s32[4,1,1,2]{0,3,2,1:T(2,128)}, u32[]{:S(2)}) copy-start(s32[4,1,1,2]{0,3,2,1:T(2,128)} %param.16) | copy-start | bytes 100
  38.2 1.2 %collective-permute-start.6 = (f32[4,12]{1,0:T(4,128)S(1)}, f32[4,12]{1,0:T(4,128)S(1)}, u32[]{:S(2)}, u32[]{:S(2)}) collective-permute-start(f32[4,12]{1,0:T(4,128)S(1)} %pad_maximum_fusion.9), channel_id=1, source_target_pairs={{0,4},{4,0},{1,5},{5,1},{2,6},{6,2},{3,7},{7,3},{8,12},{12,8},{9,1... | collective-permute-start | bytes 584 | tf_op jit(solution)/shard_map/ppermute | solution.py:96
  39.4 7.3 %collective-permute-start.7 = (f32[4,12]{1,0:T(4,128)S(1)}, f32[4,12]{1,0:T(4,128)S(1)}, u32[]{:S(2)}, u32[]{:S(2)}) collective-permute-start(f32[4,12]{1,0:T(4,128)S(1)} %fusion.28), channel_id=1, source_target_pairs={{0,1},{1,0},{2,3},{3,2},{4,5},{5,4},{6,7},{7,6},{8,9},{9,8},{10,11... | collective-permute-start | bytes 584 | tf_op jit(solution)/shard_map/ppermute | solution.py:96
  46.7 6.8 %copy-start.10 = (pred[3,3]{1,0:T(4,128)(4,1)S(1)}, pred[3,3]{1,0:T(4,128)(4,1)}, u32[]{:S(2)}) copy-start(pred[3,3]{1,0:T(4,128)(4,1)} %iota_compare_fusion.2) | copy-start | bytes 31
  46.7 5.2 %collective-permute-start.8 = (f32[4,12]{1,0:T(4,128)S(1)}, f32[4,12]{1,0:T(4,128)S(1)}, u32[]{:S(2)}, u32[]{:S(2)}) collective-permute-start(f32[4,12]{1,0:T(4,128)S(1)} %add.250), channel_id=1, source_target_pairs={{0,2},{1,3},{2,0},{3,1},{4,6},{5,7},{6,4},{7,5},{8,10},{9,11},{10,... | collective-permute-start | bytes 584 | tf_op jit(solution)/shard_map/ppermute | solution.py:96
  62.6 10.1 %copy-start.7 = (bf16[4,256,512]{2,1,0:T(8,128)(2,1)S(1)}, bf16[4,256,512]{2,1,0:T(8,128)(2,1)}, u32[]{:S(2)}) copy-start(bf16[4,256,512]{2,1,0:T(8,128)(2,1)} %shard_map.108) | copy-start | bytes 3145732
  62.6 10.1 %collective-permute-start.12 = (bf16[256,512]{1,0:T(8,128)(2,1)S(1)}, bf16[256,512]{1,0:T(8,128)(2,1)S(1)}, u32[]{:S(2)}, u32[]{:S(2)}) collective-permute-start(bf16[256,512]{1,0:T(8,128)(2,1)S(1)} %slice_bitcast_fusion.5), channel_id=1, source_target_pairs={{0,8},{8,16},{16,24},{24,0},{1,9},{9,17},{17,25},{25,1},{2,10},{10... | collective-permute-start | bytes 786440 | tf_op jit(solution)/shard_map/ppermute | solution.py:348
  70.1 24.2 %copy-start.6 = (bf16[4,256,512]{2,1,0:T(8,128)(2,1)S(1)}, bf16[4,256,512]{2,1,0:T(8,128)(2,1)}, u32[]{:S(2)}) copy-start(bf16[4,256,512]{2,1,0:T(8,128)(2,1)} %shard_map.107) | copy-start | bytes 3145732
  71.2 11.0 %collective-permute-start.9 = (bf16[256,512]{1,0:T(8,128)(2,1)S(1)}, bf16[256,512]{1,0:T(8,128)(2,1)S(1)}, u32[]{:S(2)}, u32[]{:S(2)}) collective-permute-start(bf16[256,512]{1,0:T(8,128)(2,1)S(1)} %slice_bitcast_fusion.9), channel_id=1, source_target_pairs={{0,8},{8,16},{16,24},{24,0},{1,9},{9,17},{17,25},{25,1},{2,10},{10... | collective-permute-start | bytes 786440 | tf_op jit(solution)/shard_map/ppermute | solution.py:348
  72.8 15.0 %collective-permute-start.13 = (bf16[256,512]{1,0:T(8,128)(2,1)S(1)}, bf16[256,512]{1,0:T(8,128)(2,1)S(1)}, u32[]{:S(2)}, u32[]{:S(2)}) collective-permute-start(bf16[256,512]{1,0:T(8,128)(2,1)S(1)} %fusion.2), channel_id=1, source_target_pairs={{0,8},{8,16},{16,24},{24,0},{1,9},{9,17},{17,25},{25,1},{2,10},{10... | collective-permute-start | bytes 786440 | tf_op jit(solution)/shard_map/ppermute | solution.py:348
  83.2 11.1 %collective-permute-start.10 = (bf16[256,512]{1,0:T(8,128)(2,1)S(1)}, bf16[256,512]{1,0:T(8,128)(2,1)S(1)}, u32[]{:S(2)}, u32[]{:S(2)}) collective-permute-start(bf16[256,512]{1,0:T(8,128)(2,1)S(1)} %fusion.5), channel_id=1, source_target_pairs={{0,8},{8,16},{16,24},{24,0},{1,9},{9,17},{17,25},{25,1},{2,10},{10... | collective-permute-start | bytes 786440 | tf_op jit(solution)/shard_map/ppermute | solution.py:348
  87.9 12.1 %collective-permute-start.14 = (bf16[256,512]{1,0:T(8,128)(2,1)S(1)}, bf16[256,512]{1,0:T(8,128)(2,1)}, u32[]{:S(2)}, u32[]{:S(2)}) collective-permute-start(bf16[256,512]{1,0:T(8,128)(2,1)S(1)} %fusion.1), channel_id=1, source_target_pairs={{0,8},{8,16},{16,24},{24,0},{1,9},{9,17},{17,25},{25,1},{2,10},{10... | collective-permute-start | bytes 786440 | tf_op jit(solution)/shard_map/ppermute | solution.py:348
  94.4 9.5 %collective-permute-start.11 = (bf16[256,512]{1,0:T(8,128)(2,1)S(1)}, bf16[256,512]{1,0:T(8,128)(2,1)S(1)}, u32[]{:S(2)}, u32[]{:S(2)}) collective-permute-start(bf16[256,512]{1,0:T(8,128)(2,1)S(1)} %fusion.4), channel_id=1, source_target_pairs={{0,8},{8,16},{16,24},{24,0},{1,9},{9,17},{17,25},{25,1},{2,10},{10... | collective-permute-start | bytes 786440 | tf_op jit(solution)/shard_map/ppermute | solution.py:348
  (3 other events, 5.1 us)

commit v17 on v16

--- a/solution.py
+++ b/solution.py
@@ -470,7 +470,7 @@
     picked_ring = jnp.dot(picked.astype(jnp.float32), ring_order, precision=lax.Precision.HIGHEST)
     halves = [warp_tiles(
         choose, plane_fit, picked_ring, xcoord.reshape(1, tile_len),
-        row_coord.reshape(tile_len, 1), matched, resample_bank, part, 2) for part in range(2)]
+        row_coord.reshape(tile_len, 1), matched, resample_bank, part, 4) for part in range(4)]
     numerator = jnp.concatenate(
         [ring_scatter(piece, "visit", visit_count) for piece in halves], 0
     )[None]

time: 106 us -> 123 us (1.16)
  Pallas kernels: 29.8 us -> 41.7 us
  starting transfers between devices: 17 us -> 24.6 us
  other arithmetic: 18.1 us -> 15.1 us
  waiting for transfers between devices: 30.1 us -> 32.1 us
  local copies, waits for them, and re-layouts: 6.23 us -> 4.93 us
    pallas_call x2 -> x4, Pallas kernels: 14.7 us -> 26.5 us  [warp_tiles(): pl.pallas_call(warp_body, grid_spec=grid_spec, out_shape=jax.ShapeDtypeSt...]
    ppermute x6 -> x12, starting transfers between devices: 0.44 us -> 5.59 us  [ring_scatter(): lax.ppermute(outgoing.astype(jnp.bfloat16), axis, ring).astype(jnp.float32)]
    ppermute x3, starting transfers between devices: 2.83 us -> 5.28 us  [butterfly_sum(): values = jax.tree.map(lambda v: v + lax.ppermute(v, axis, pairs), values)]
    ppermute x3, waiting for transfers between devices: 0.48 us -> 2.48 us  [butterfly_sum(): values = jax.tree.map(lambda v: v + lax.ppermute(v, axis, pairs), values)]
    ppermute x6 -> x12, waiting for transfers between devices: 28.4 us -> 28.3 us  [ring_scatter(): lax.ppermute(outgoing.astype(jnp.bfloat16), axis, ring).astype(jnp.float32)]
  transfers between devices with their start and end apart: 15 -> 21, of which waited for: 8 -> 16; matrix products, arithmetic and copies ran while one was open for 13% -> 8% of each run, Pallas kernels for 21% -> 12%
where the time goes in v17:
time: 123 us
  Pallas kernels  41.7 us (34%)
  waiting for transfers between devices  32.1 us (26%)
  starting transfers between devices  24.6 us (20%)
  other arithmetic  15.1 us (12%)
  local copies, waits for them, and re-layouts  4.93 us (4%)
  matrix products  3.26 us (3%)
    ppermute x12, waiting for transfers between devices, ring_scatter(): lax.ppermute(outgoing.astype(jnp.bfloat16), axis, ring).astype(jnp.float32)  28.3 us
    pallas_call x4, Pallas kernels, warp_tiles(): pl.pallas_call(warp_body, grid_spec=grid_spec, out_shape=jax.ShapeDtypeSt...  26.5 us
    pallas_call x2, Pallas kernels, band_tiles(): pl.pallas_call(functools.partial(band_body, first), grid=(count,), in_spe...  9.69 us
    ppermute x3, starting transfers between devices, shards(): received.append(lax.ppermute(payload, 'visit', pairs))  7.86 us
    ppermute x12, starting transfers between devices, ring_scatter(): lax.ppermute(outgoing.astype(jnp.bfloat16), axis, ring).astype(jnp.float32)  5.59 us
    pallas_call x1, Pallas kernels, strip_tiles(): pl.pallas_call(strip_body, grid_spec=grid_spec, out_shape=jax.ShapeDtypeS...  5.44 us
    ppermute x3, starting transfers between devices, butterfly_sum(): values = jax.tree.map(lambda v: v + lax.ppermute(v, axis, pairs), values)  5.28 us
    ppermute x1, starting transfers between devices, extended(): before = lax.ppermute(last, axis, up)  4.55 us
  transfers between devices with their start and end apart: 21, of which 16 were waited for; matrix products, arithmetic and copies ran while one was open for 8% of the time, Pallas kernels for 12%

profile of v17, /device:TPU:0, one launch (start us, length us, event | category | flops | bytes accessed | tf_op | source)
XLA Modules:
  0.0 122.8 jit_solution(8033093848199665655)
XLA Ops:
  4.2 2.1 %convolution_convert_fusion = bf16[4,32,512]{2,1,0:T(8,128)(2,1)S(1)} fusion(bf16[4,512,512]{2,1,0:T(8,128)(2,1)} %param.11, s32[4]{0:T(128)S(1)} %get-tuple-element.35.off_ref), kind=kOutput, calls=%fused_computation.1 | convolution fusion | flops 67305472 | bytes 2228240 | tf_op jit(solution)/shard_map/esr,erl->esl/dot_general | solution.py:384
  6.9 4.0 %collective-permute-start.1 = (bf16[144,512]{1,0:T(8,128)(2,1)}, bf16[144,512]{1,0:T(8,128)(2,1)S(1)}, u32[]{:S(2)}, u32[]{:S(2)}) collective-permute-start(bf16[144,512]{1,0:T(8,128)(2,1)} %get-tuple-element.42), channel_id=1, source_target_pairs={{0,16},{8,24},{16,0},{24,8},{1,17},{9,25},{17,1},{25,9},{2,18},{10... | collective-permute-start | bytes 442376 | tf_op jit(solution)/shard_map/ppermute | solution.py:404
  12.6 2.2 %collective-permute-start.2 = (bf16[144,512]{1,0:T(8,128)(2,1)}, bf16[144,512]{1,0:T(8,128)(2,1)}, u32[]{:S(2)}, u32[]{:S(2)}) collective-permute-start(bf16[144,512]{1,0:T(8,128)(2,1)} %get-tuple-element.42), channel_id=1, source_target_pairs={{0,24},{8,0},{16,8},{24,16},{1,25},{9,1},{17,9},{25,17},{2,26},{10... | collective-permute-start | bytes 442376 | tf_op jit(solution)/shard_map/ppermute | solution.py:404
  16.9 4.5 %collective-permute-start.3 = (bf16[4,8192]{1,0:T(4,128)(2,1)S(1)}, bf16[4,8192]{1,0:T(4,128)(2,1)S(1)}, u32[]{:S(2)}, u32[]{:S(2)}) collective-permute-start(bf16[4,8192]{1,0:T(4,128)(2,1)S(1)} %bitcast.161), channel_id=1, source_target_pairs={{0,1},{1,2},{2,3},{4,5},{5,6},{6,7},{8,9},{9,10},{10,11},{12,13},{... | collective-permute-start | bytes 196616 | tf_op jit(solution)/shard_map/ppermute | solution.py:41
  28.4 5.4 %shard_map.104 = f32[4,32,512]{2,1,0:T(8,128)S(1)} custom-call(s32[4]{0:T(128)S(1)} %get-tuple-element.35.off_ref, f32[4,3]{1,0:T(4,128)S(1)} %copy-done.1, bf16[3,256,256]{2,1,0:T(8,128)(2,1)S(1)} %copy-done, bf16[4,544,544]{2,1,0:T(8,128)(2,1)S(1)} %pad_maximum_fusion.padded_ref), custom_call_target="tpu_custom_call" | custom-call | flops 257949696 | bytes 2629632 | tf_op jit(solution)/shard_map/pallas_call | solution.py:207
  33.8 4.9 %shard_map.105.rest_0_ = f32[4,512,512]{2,1,0:T(8,128)} custom-call(f32[4,3]{1,0:T(4,128)S(1)} %copy-done.1, bf16[3,256,256]{2,1,0:T(8,128)(2,1)S(1)} %copy-done, bf16[4,544,544]{2,1,0:T(8,128)(2,1)S(1)} %pad_maximum_fusion.padded_ref), custom_call_target="tpu_custom_call" | custom-call | flops 1660944384 | bytes 3280896 | tf_op jit(solution)/shard_map/pallas_call | solution.py:264
  38.7 4.8 %shard_map.106.matched_ref = f32[4,512,512]{2,1,0:T(8,128)} custom-call(f32[4,3]{1,0:T(4,128)S(1)} %copy-done.1, bf16[3,256,256]{2,1,0:T(8,128)(2,1)S(1)} %copy-done, bf16[4,544,544]{2,1,0:T(8,128)(2,1)S(1)} %pad_maximum_fusion.padded_ref, f32[4,512,512]{2,1,0:T(8,128)} %shard_map.105.rest_0_), custom_call_target="tpu_custom_call", output_to_operand_aliasing={{}: (3, {})} | custom-call | flops 1660944384 | bytes 3280896 | tf_op jit(solution)/shard_map/pallas_call | solution.py:264
  47.4 2.4 %collective-permute-start.7 = (f32[4,12]{1,0:T(4,128)S(1)}, f32[4,12]{1,0:T(4,128)S(1)}, u32[]{:S(2)}, u32[]{:S(2)}) collective-permute-start(f32[4,12]{1,0:T(4,128)S(1)} %fusion.34), channel_id=1, source_target_pairs={{0,1},{1,0},{2,3},{3,2},{4,5},{5,4},{6,7},{7,6},{8,9},{9,8},{10,11... | collective-permute-start | bytes 584 | tf_op jit(solution)/shard_map/ppermute | solution.py:96
  51.4 2.7 %collective-permute-start.8 = (f32[4,12]{1,0:T(4,128)S(1)}, f32[4,12]{1,0:T(4,128)S(1)}, u32[]{:S(2)}, u32[]{:S(2)}) collective-permute-start(f32[4,12]{1,0:T(4,128)S(1)} %add.268), channel_id=1, source_target_pairs={{0,2},{1,3},{2,0},{3,1},{4,6},{5,7},{6,4},{7,5},{8,10},{9,11},{10,... | collective-permute-start | bytes 584 | tf_op jit(solution)/shard_map/ppermute | solution.py:96
  58.1 6.6 %shard_map.110 = bf16[4,128,512]{2,1,0:T(8,128)(2,1)} custom-call(s32[4,2]{1,0:T(4,128)} %copy.96.idx_ref, f32[4,3]{1,0:T(4,128)} %pad_maximum_fusion.10.plane_ref, f32[4,4]{1,0:T(4,128)} %fusion.23.pick_ref, f32[1,512]{1,0:T(1,128)} %multiply_add_fusion.1.xrow_ref, f32[512,1]{1,0:T(8,128)} %multiply_add_fusion.ycol_ref, ...), custom_call_target="tpu_custom_call" | custom-call | flops 536870912 | bytes 7340032 | tf_op jit(solution)/shard_map/pallas_call | solution.py:331
  64.7 6.6 %shard_map.109 = bf16[4,128,512]{2,1,0:T(8,128)(2,1)} custom-call(s32[4,2]{1,0:T(4,128)} %copy.96.idx_ref, f32[4,3]{1,0:T(4,128)} %pad_maximum_fusion.10.plane_ref, f32[4,4]{1,0:T(4,128)} %fusion.23.pick_ref, f32[1,512]{1,0:T(1,128)} %multiply_add_fusion.1.xrow_ref, f32[512,1]{1,0:T(8,128)} %multiply_add_fusion.ycol_ref, ...), custom_call_target="tpu_custom_call" | custom-call | flops 536870912 | bytes 7340032 | tf_op jit(solution)/shard_map/pallas_call | solution.py:331
  71.2 6.6 %shard_map.108 = bf16[4,128,512]{2,1,0:T(8,128)(2,1)} custom-call(s32[4,2]{1,0:T(4,128)} %copy.96.idx_ref, f32[4,3]{1,0:T(4,128)} %pad_maximum_fusion.10.plane_ref, f32[4,4]{1,0:T(4,128)} %fusion.23.pick_ref, f32[1,512]{1,0:T(1,128)} %multiply_add_fusion.1.xrow_ref, f32[512,1]{1,0:T(8,128)} %multiply_add_fusion.ycol_ref, ...), custom_call_target="tpu_custom_call" | custom-call | flops 536870912 | bytes 7340032 | tf_op jit(solution)/shard_map/pallas_call | solution.py:331
  77.9 6.8 %shard_map.107 = bf16[4,128,512]{2,1,0:T(8,128)(2,1)} custom-call(s32[4,2]{1,0:T(4,128)} %copy.96.idx_ref, f32[4,3]{1,0:T(4,128)} %pad_maximum_fusion.10.plane_ref, f32[4,4]{1,0:T(4,128)} %fusion.23.pick_ref, f32[1,512]{1,0:T(1,128)} %multiply_add_fusion.1.xrow_ref, f32[512,1]{1,0:T(8,128)} %multiply_add_fusion.ycol_ref, ...), custom_call_target="tpu_custom_call" | custom-call | flops 536870912 | bytes 7340032 | tf_op jit(solution)/shard_map/pallas_call | solution.py:331
  86.9 3.9 %collective-permute-start.9 = (bf16[128,512]{1,0:T(8,128)(2,1)S(1)}, bf16[128,512]{1,0:T(8,128)(2,1)S(1)}, u32[]{:S(2)}, u32[]{:S(2)}) collective-permute-start(bf16[128,512]{1,0:T(8,128)(2,1)S(1)} %slice_bitcast_fusion.17), channel_id=1, source_target_pairs={{0,8},{8,16},{16,24},{24,0},{1,9},{9,17},{17,25},{25,1},{2,10},{10... | collective-permute-start | bytes 393224 | tf_op jit(solution)/shard_map/ppermute | solution.py:348
  90.8 2.2 %collective-permute-done.18 = bf16[128,512]{1,0:T(8,128)(2,1)S(1)} collective-permute-done((bf16[128,512]{1,0:T(8,128)(2,1)S(1)}, bf16[128,512]{1,0:T(8,128)(2,1)S(1)}, u32[]{:S(2)}, u32[]{:S(2)}) %collective-permute-start.18) | collective-permute-done | bytes 131104 | tf_op jit(solution)/shard_map/ppermute | solution.py:348
  93.0 2.7 %collective-permute-done.15 = bf16[128,512]{1,0:T(8,128)(2,1)S(1)} collective-permute-done((bf16[128,512]{1,0:T(8,128)(2,1)S(1)}, bf16[128,512]{1,0:T(8,128)(2,1)S(1)}, u32[]{:S(2)}, u32[]{:S(2)}) %collective-permute-start.15) | collective-permute-done | bytes 131104 | tf_op jit(solution)/shard_map/ppermute | solution.py:348
  95.9 2.7 %collective-permute-done.12 = bf16[128,512]{1,0:T(8,128)(2,1)S(1)} collective-permute-done((bf16[128,512]{1,0:T(8,128)(2,1)S(1)}, bf16[128,512]{1,0:T(8,128)(2,1)S(1)}, u32[]{:S(2)}, u32[]{:S(2)}) %collective-permute-start.12) | collective-permute-done | bytes 131104 | tf_op jit(solution)/shard_map/ppermute | solution.py:348
  98.7 2.7 %collective-permute-done.9 = bf16[128,512]{1,0:T(8,128)(2,1)S(1)} collective-permute-done((bf16[128,512]{1,0:T(8,128)(2,1)S(1)}, bf16[128,512]{1,0:T(8,128)(2,1)S(1)}, u32[]{:S(2)}, u32[]{:S(2)}) %collective-permute-start.9) | collective-permute-done | bytes 131104 | tf_op jit(solution)/shard_map/ppermute | solution.py:348
  102.4 1.8 %collective-permute-done.19 = bf16[128,512]{1,0:T(8,128)(2,1)S(1)} collective-permute-done((bf16[128,512]{1,0:T(8,128)(2,1)S(1)}, bf16[128,512]{1,0:T(8,128)(2,1)S(1)}, u32[]{:S(2)}, u32[]{:S(2)}) %collective-permute-start.19) | collective-permute-done | bytes 131104 | tf_op jit(solution)/shard_map/ppermute | solution.py:348
  104.3 2.7 %collective-permute-done.16 = bf16[128,512]{1,0:T(8,128)(2,1)S(1)} collective-permute-done((bf16[128,512]{1,0:T(8,128)(2,1)S(1)}, bf16[128,512]{1,0:T(8,128)(2,1)S(1)}, u32[]{:S(2)}, u32[]{:S(2)}) %collective-permute-start.16) | collective-permute-done | bytes 131104 | tf_op jit(solution)/shard_map/ppermute | solution.py:348
  107.1 2.7 %collective-permute-done.13 = bf16[128,512]{1,0:T(8,128)(2,1)S(1)} collective-permute-done((bf16[128,512]{1,0:T(8,128)(2,1)S(1)}, bf16[128,512]{1,0:T(8,128)(2,1)S(1)}, u32[]{:S(2)}, u32[]{:S(2)}) %collective-permute-start.13) | collective-permute-done | bytes 131104 | tf_op jit(solution)/shard_map/ppermute | solution.py:348
  109.9 2.7 %collective-permute-done.10 = bf16[128,512]{1,0:T(8,128)(2,1)S(1)} collective-permute-done((bf16[128,512]{1,0:T(8,128)(2,1)S(1)}, bf16[128,512]{1,0:T(8,128)(2,1)S(1)}, u32[]{:S(2)}, u32[]{:S(2)}) %collective-permute-start.10) | collective-permute-done | bytes 131104 | tf_op jit(solution)/shard_map/ppermute | solution.py:348
  112.7 2.7 %collective-permute-done.20 = bf16[128,512]{1,0:T(8,128)(2,1)S(1)} collective-permute-done((bf16[128,512]{1,0:T(8,128)(2,1)S(1)}, bf16[128,512]{1,0:T(8,128)(2,1)S(1)}, u32[]{:S(2)}, u32[]{:S(2)}) %collective-permute-start.20) | collective-permute-done | bytes 131104 | tf_op jit(solution)/shard_map/ppermute | solution.py:348
  115.4 2.7 %collective-permute-done.17 = bf16[128,512]{1,0:T(8,128)(2,1)S(1)} collective-permute-done((bf16[128,512]{1,0:T(8,128)(2,1)S(1)}, bf16[128,512]{1,0:T(8,128)(2,1)S(1)}, u32[]{:S(2)}, u32[]{:S(2)}) %collective-permute-start.17) | collective-permute-done | bytes 131104 | tf_op jit(solution)/shard_map/ppermute | solution.py:348
  (128 shorter events, 32.5 us)
Async XLA Ops:
  4.1 18.8 %copy-start.7 = (s32[4,1,1,2]{0,3,2,1:T(2,128)S(1)}, s32[4,1,1,2]{0,3,2,1:T(2,128)}, u32[]{:S(2)}) copy-start(s32[4,1,1,2]{0,3,2,1:T(2,128)} %param.16) | copy-start | bytes 100
  4.1 19.4 %copy-start.8 = (bf16[4,1,1]{0,2,1:T(2,128)(2,1)S(1)}, bf16[4,1,1]{0,2,1:T(2,128)(2,1)}, u32[]{:S(2)}) copy-start(bf16[4,1,1]{0,2,1:T(2,128)(2,1)} %param.14) | copy-start | bytes 28
  6.9 36.6 %collective-permute-start.1 = (bf16[144,512]{1,0:T(8,128)(2,1)}, bf16[144,512]{1,0:T(8,128)(2,1)S(1)}, u32[]{:S(2)}, u32[]{:S(2)}) collective-permute-start(bf16[144,512]{1,0:T(8,128)(2,1)} %get-tuple-element.42), channel_id=1, source_target_pairs={{0,16},{8,24},{16,0},{24,8},{1,17},{9,25},{17,1},{25,9},{2,18},{10... | collective-permute-start | bytes 442376 | tf_op jit(solution)/shard_map/ppermute | solution.py:404
  11.0 32.5 %collective-permute-start = (bf16[144,512]{1,0:T(8,128)(2,1)}, bf16[144,512]{1,0:T(8,128)(2,1)}, u32[]{:S(2)}, u32[]{:S(2)}) collective-permute-start(bf16[144,512]{1,0:T(8,128)(2,1)} %get-tuple-element.42), channel_id=1, source_target_pairs={{0,8},{8,16},{16,24},{24,0},{1,9},{9,17},{17,25},{25,1},{2,10},{10... | collective-permute-start | bytes 442376 | tf_op jit(solution)/shard_map/ppermute | solution.py:404
  12.6 31.0 %collective-permute-start.2 = (bf16[144,512]{1,0:T(8,128)(2,1)}, bf16[144,512]{1,0:T(8,128)(2,1)}, u32[]{:S(2)}, u32[]{:S(2)}) collective-permute-start(bf16[144,512]{1,0:T(8,128)(2,1)} %get-tuple-element.42), channel_id=1, source_target_pairs={{0,24},{8,0},{16,8},{24,16},{1,25},{9,1},{17,9},{25,17},{2,26},{10... | collective-permute-start | bytes 442376 | tf_op jit(solution)/shard_map/ppermute | solution.py:404
  15.3 9.1 %collective-permute-start.4 = (bf16[4,8192]{1,0:T(4,128)(2,1)S(1)}, bf16[4,8192]{1,0:T(4,128)(2,1)S(1)}, u32[]{:S(2)}, u32[]{:S(2)}) collective-permute-start(bf16[4,8192]{1,0:T(4,128)(2,1)S(1)} %bitcast.159), channel_id=1, source_target_pairs={{1,0},{2,1},{3,2},{5,4},{6,5},{7,6},{9,8},{10,9},{11,10},{13,12},{... | collective-permute-start | bytes 196616 | tf_op jit(solution)/shard_map/ppermute | solution.py:42
  16.9 7.5 %collective-permute-start.3 = (bf16[4,8192]{1,0:T(4,128)(2,1)S(1)}, bf16[4,8192]{1,0:T(4,128)(2,1)S(1)}, u32[]{:S(2)}, u32[]{:S(2)}) collective-permute-start(bf16[4,8192]{1,0:T(4,128)(2,1)S(1)} %bitcast.161), channel_id=1, source_target_pairs={{0,1},{1,2},{2,3},{4,5},{5,6},{6,7},{8,9},{9,10},{10,11},{12,13},{... | collective-permute-start | bytes 196616 | tf_op jit(solution)/shard_map/ppermute | solution.py:41
  25.2 1.3 %collective-permute-start.5 = (bf16[4,16,544]{2,1,0:T(8,128)(2,1)S(1)}, bf16[4,16,544]{2,1,0:T(8,128)(2,1)S(1)}, u32[]{:S(2)}, u32[]{:S(2)}) collective-permute-start(bf16[4,16,544]{2,1,0:T(8,128)(2,1)S(1)} %fusion.15), channel_id=1, source_target_pairs={{0,4},{4,0},{1,5},{5,1},{2,6},{6,2},{3,7},{7,3},{8,12},{12,8},{9,1... | collective-permute-start | bytes 208904 | tf_op jit(solution)/shard_map/ppermute | solution.py:34
  46.2 1.2 collective-permute-start.6
  47.4 4.0 %collective-permute-start.7 = (f32[4,12]{1,0:T(4,128)S(1)}, f32[4,12]{1,0:T(4,128)S(1)}, u32[]{:S(2)}, u32[]{:S(2)}) collective-permute-start(f32[4,12]{1,0:T(4,128)S(1)} %fusion.34), channel_id=1, source_target_pairs={{0,1},{1,0},{2,3},{3,2},{4,5},{5,4},{6,7},{7,6},{8,9},{9,8},{10,11... | collective-permute-start | bytes 584 | tf_op jit(solution)/shard_map/ppermute | solution.py:96
  51.4 4.3 %collective-permute-start.8 = (f32[4,12]{1,0:T(4,128)S(1)}, f32[4,12]{1,0:T(4,128)S(1)}, u32[]{:S(2)}, u32[]{:S(2)}) collective-permute-start(f32[4,12]{1,0:T(4,128)S(1)} %add.268), channel_id=1, source_target_pairs={{0,2},{1,3},{2,0},{3,1},{4,6},{5,7},{6,4},{7,5},{8,10},{9,11},{10,... | collective-permute-start | bytes 584 | tf_op jit(solution)/shard_map/ppermute | solution.py:96
  84.6 28.0 %copy-start.3 = (bf16[4,128,512]{2,1,0:T(8,128)(2,1)S(1)}, bf16[4,128,512]{2,1,0:T(8,128)(2,1)}, u32[]{:S(2)}) copy-start(bf16[4,128,512]{2,1,0:T(8,128)(2,1)} %shard_map.107) | copy-start | bytes 1572868
  84.7 8.3 %collective-permute-start.18 = (bf16[128,512]{1,0:T(8,128)(2,1)S(1)}, bf16[128,512]{1,0:T(8,128)(2,1)S(1)}, u32[]{:S(2)}, u32[]{:S(2)}) collective-permute-start(bf16[128,512]{1,0:T(8,128)(2,1)S(1)} %slice_bitcast_fusion.5), channel_id=1, source_target_pairs={{0,8},{8,16},{16,24},{24,0},{1,9},{9,17},{17,25},{25,1},{2,10},{10... | collective-permute-start | bytes 393224 | tf_op jit(solution)/shard_map/ppermute | solution.py:348
  84.8 11.0 %collective-permute-start.15 = (bf16[128,512]{1,0:T(8,128)(2,1)S(1)}, bf16[128,512]{1,0:T(8,128)(2,1)S(1)}, u32[]{:S(2)}, u32[]{:S(2)}) collective-permute-start(bf16[128,512]{1,0:T(8,128)(2,1)S(1)} %slice_bitcast_fusion.9), channel_id=1, source_target_pairs={{0,8},{8,16},{16,24},{24,0},{1,9},{9,17},{17,25},{25,1},{2,10},{10... | collective-permute-start | bytes 393224 | tf_op jit(solution)/shard_map/ppermute | solution.py:348
  84.8 13.7 %collective-permute-start.12 = (bf16[128,512]{1,0:T(8,128)(2,1)S(1)}, bf16[128,512]{1,0:T(8,128)(2,1)S(1)}, u32[]{:S(2)}, u32[]{:S(2)}) collective-permute-start(bf16[128,512]{1,0:T(8,128)(2,1)S(1)} %slice_bitcast_fusion.13), channel_id=1, source_target_pairs={{0,8},{8,16},{16,24},{24,0},{1,9},{9,17},{17,25},{25,1},{2,10},{10... | collective-permute-start | bytes 393224 | tf_op jit(solution)/shard_map/ppermute | solution.py:348
  86.9 14.5 %collective-permute-start.9 = (bf16[128,512]{1,0:T(8,128)(2,1)S(1)}, bf16[128,512]{1,0:T(8,128)(2,1)S(1)}, u32[]{:S(2)}, u32[]{:S(2)}) collective-permute-start(bf16[128,512]{1,0:T(8,128)(2,1)S(1)} %slice_bitcast_fusion.17), channel_id=1, source_target_pairs={{0,8},{8,16},{16,24},{24,0},{1,9},{9,17},{17,25},{25,1},{2,10},{10... | collective-permute-start | bytes 393224 | tf_op jit(solution)/shard_map/ppermute | solution.py:348
  93.0 11.2 %collective-permute-start.19 = (bf16[128,512]{1,0:T(8,128)(2,1)S(1)}, bf16[128,512]{1,0:T(8,128)(2,1)S(1)}, u32[]{:S(2)}, u32[]{:S(2)}) collective-permute-start(bf16[128,512]{1,0:T(8,128)(2,1)S(1)} %fusion.4), channel_id=1, source_target_pairs={{0,8},{8,16},{16,24},{24,0},{1,9},{9,17},{17,25},{25,1},{2,10},{10... | collective-permute-start | bytes 393224 | tf_op jit(solution)/shard_map/ppermute | solution.py:348
  95.8 11.2 %collective-permute-start.16 = (bf16[128,512]{1,0:T(8,128)(2,1)S(1)}, bf16[128,512]{1,0:T(8,128)(2,1)S(1)}, u32[]{:S(2)}, u32[]{:S(2)}) collective-permute-start(bf16[128,512]{1,0:T(8,128)(2,1)S(1)} %fusion.7), channel_id=1, source_target_pairs={{0,8},{8,16},{16,24},{24,0},{1,9},{9,17},{17,25},{25,1},{2,10},{10... | collective-permute-start | bytes 393224 | tf_op jit(solution)/shard_map/ppermute | solution.py:348
  98.6 11.2 %collective-permute-start.13 = (bf16[128,512]{1,0:T(8,128)(2,1)S(1)}, bf16[128,512]{1,0:T(8,128)(2,1)S(1)}, u32[]{:S(2)}, u32[]{:S(2)}) collective-permute-start(bf16[128,512]{1,0:T(8,128)(2,1)S(1)} %fusion.10), channel_id=1, source_target_pairs={{0,8},{8,16},{16,24},{24,0},{1,9},{9,17},{17,25},{25,1},{2,10},{10... | collective-permute-start | bytes 393224 | tf_op jit(solution)/shard_map/ppermute | solution.py:348
  102.3 10.3 %collective-permute-start.10 = (bf16[128,512]{1,0:T(8,128)(2,1)S(1)}, bf16[128,512]{1,0:T(8,128)(2,1)S(1)}, u32[]{:S(2)}, u32[]{:S(2)}) collective-permute-start(bf16[128,512]{1,0:T(8,128)(2,1)S(1)} %fusion.13), channel_id=1, source_target_pairs={{0,8},{8,16},{16,24},{24,0},{1,9},{9,17},{17,25},{25,1},{2,10},{10... | collective-permute-start | bytes 393224 | tf_op jit(solution)/shard_map/ppermute | solution.py:348
  104.2 11.2 %collective-permute-start.20 = (bf16[128,512]{1,0:T(8,128)(2,1)S(1)}, bf16[128,512]{1,0:T(8,128)(2,1)S(1)}, u32[]{:S(2)}, u32[]{:S(2)}) collective-permute-start(bf16[128,512]{1,0:T(8,128)(2,1)S(1)} %fusion.3), channel_id=1, source_target_pairs={{0,8},{8,16},{16,24},{24,0},{1,9},{9,17},{17,25},{25,1},{2,10},{10... | collective-permute-start | bytes 393224 | tf_op jit(solution)/shard_map/ppermute | solution.py:348
  107.0 11.1 %collective-permute-start.17 = (bf16[128,512]{1,0:T(8,128)(2,1)S(1)}, bf16[128,512]{1,0:T(8,128)(2,1)S(1)}, u32[]{:S(2)}, u32[]{:S(2)}) collective-permute-start(bf16[128,512]{1,0:T(8,128)(2,1)S(1)} %fusion.6), channel_id=1, source_target_pairs={{0,8},{8,16},{16,24},{24,0},{1,9},{9,17},{17,25},{25,1},{2,10},{10... | collective-permute-start | bytes 393224 | tf_op jit(solution)/shard_map/ppermute | solution.py:348
  109.8 9.7 %collective-permute-start.14 = (bf16[128,512]{1,0:T(8,128)(2,1)S(1)}, bf16[128,512]{1,0:T(8,128)(2,1)S(1)}, u32[]{:S(2)}, u32[]{:S(2)}) collective-permute-start(bf16[128,512]{1,0:T(8,128)(2,1)S(1)} %fusion.9), channel_id=1, source_target_pairs={{0,8},{8,16},{16,24},{24,0},{1,9},{9,17},{17,25},{25,1},{2,10},{10... | collective-permute-start | bytes 393224 | tf_op jit(solution)/shard_map/ppermute | solution.py:348
  112.6 8.3 %collective-permute-start.11 = (bf16[128,512]{1,0:T(8,128)(2,1)S(1)}, bf16[128,512]{1,0:T(8,128)(2,1)S(1)}, u32[]{:S(2)}, u32[]{:S(2)}) collective-permute-start(bf16[128,512]{1,0:T(8,128)(2,1)S(1)} %fusion.12), channel_id=1, source_target_pairs={{0,8},{8,16},{16,24},{24,0},{1,9},{9,17},{17,25},{25,1},{2,10},{10... | collective-permute-start | bytes 393224 | tf_op jit(solution)/shard_map/ppermute | solution.py:348
  (6 other events, 38.4 us)

commit v18 on v16

--- a/solution.py
+++ b/solution.py
@@ -73,7 +73,17 @@
 
 
 def solve_three(normal, moments):
-    lower = jnp.linalg.cholesky(normal)
+    l00 = jnp.sqrt(normal[..., 0, 0])
+    l10 = normal[..., 1, 0] / l00
+    l20 = normal[..., 2, 0] / l00
+    l11 = jnp.sqrt(normal[..., 1, 1] - l10 * l10)
+    l21 = (normal[..., 2, 1] - l20 * l10) / l11
+    l22 = jnp.sqrt(normal[..., 2, 2] - l20 * l20 - l21 * l21)
+    zero = jnp.zeros_like(l00)
+    lower = jnp.stack(
+        [jnp.stack([l00, zero, zero], -1), jnp.stack([l10, l11, zero], -1),
+         jnp.stack([l20, l21, l22], -1)], -2,
+    )
     first = moments[..., 0] / lower[..., 0, 0]
     second = (moments[..., 1] - lower[..., 1, 0] * first) / lower[..., 1, 1]
     third = (moments[..., 2] - lower[..., 2, 0] * first - lower[..., 2, 1] * second) / lower[

time: 106 us -> 105 us (level)
  other arithmetic: 18.1 us -> 15.7 us
    another operation x5 -> x2, other arithmetic: 1.37 us -> 0.08 us  [the longest x1 0.07 us: solve_three(): jnp.stack([l10, l11, zero], -1)]
  transfers between devices with their start and end apart: 15 -> 15, of which waited for: 8 -> 8; matrix products, arithmetic and copies ran while one was open for 13% -> 12% of each run, Pallas kernels for 21% -> 22%
where the time goes in v18:
time: 105 us
  waiting for transfers between devices  30.7 us (29%)
  Pallas kernels  29.9 us (28%)
  starting transfers between devices  17.3 us (16%)
  other arithmetic  15.7 us (15%)
  local copies, waits for them, and re-layouts  6.67 us (6%)
  matrix products  3.27 us (3%)
  between operations  1.08 us (1%)
    ppermute x6, waiting for transfers between devices, ring_scatter(): lax.ppermute(outgoing.astype(jnp.bfloat16), axis, ring).astype(jnp.float32)  28.4 us
    pallas_call x2, Pallas kernels, warp_tiles(): pl.pallas_call(warp_body, grid_spec=grid_spec, out_shape=jax.ShapeDtypeSt...  14.8 us
    pallas_call x2, Pallas kernels, band_tiles(): pl.pallas_call(functools.partial(band_body, first), grid=(count,), in_spe...  9.67 us
    ppermute x3, starting transfers between devices, shards(): received.append(lax.ppermute(payload, 'visit', pairs))  7.86 us
    pallas_call x1, Pallas kernels, strip_tiles(): pl.pallas_call(strip_body, grid_spec=grid_spec, out_shape=jax.ShapeDtypeS...  5.44 us
    ppermute x1, starting transfers between devices, extended(): before = lax.ppermute(last, axis, up)  4.55 us
    ppermute x3, starting transfers between devices, butterfly_sum(): values = jax.tree.map(lambda v: v + lax.ppermute(v, axis, pairs), values)  3.14 us
    concatenate x1, other arithmetic, extended(): value = jnp.concatenate([before, value, after], axis=dim)  2.9 us
  transfers between devices with their start and end apart: 15, of which 8 were waited for; matrix products, arithmetic and copies ran while one was open for 12% of the time, Pallas kernels for 22%

profile of v18, /device:TPU:0, one launch (start us, length us, event | category | flops | bytes accessed | tf_op | source)
XLA Modules:
  0.0 104.6 jit_solution(11163744191650618375)
XLA Ops:
  4.2 2.1 %convolution_convert_fusion = bf16[4,32,512]{2,1,0:T(8,128)(2,1)S(1)} fusion(bf16[4,512,512]{2,1,0:T(8,128)(2,1)} %param.11, s32[4]{0:T(128)S(1)} %get-tuple-element.42.off_ref), kind=kOutput, calls=%fused_computation.1 | convolution fusion | flops 67305472 | bytes 2228240 | tf_op jit(solution)/shard_map/esr,erl->esl/dot_general | solution.py:394
  7.0 4.0 %collective-permute-start.1 = (bf16[144,512]{1,0:T(8,128)(2,1)}, bf16[144,512]{1,0:T(8,128)(2,1)S(1)}, u32[]{:S(2)}, u32[]{:S(2)}) collective-permute-start(bf16[144,512]{1,0:T(8,128)(2,1)} %get-tuple-element.53), channel_id=1, source_target_pairs={{0,16},{8,24},{16,0},{24,8},{1,17},{9,25},{17,1},{25,9},{2,18},{10... | collective-permute-start | bytes 442376 | tf_op jit(solution)/shard_map/ppermute | solution.py:414
  11.0 1.6 %collective-permute-start = (bf16[144,512]{1,0:T(8,128)(2,1)}, bf16[144,512]{1,0:T(8,128)(2,1)}, u32[]{:S(2)}, u32[]{:S(2)}) collective-permute-start(bf16[144,512]{1,0:T(8,128)(2,1)} %get-tuple-element.53), channel_id=1, source_target_pairs={{0,8},{8,16},{16,24},{24,0},{1,9},{9,17},{17,25},{25,1},{2,10},{10... | collective-permute-start | bytes 442376 | tf_op jit(solution)/shard_map/ppermute | solution.py:414
  12.6 2.2 %collective-permute-start.2 = (bf16[144,512]{1,0:T(8,128)(2,1)}, bf16[144,512]{1,0:T(8,128)(2,1)}, u32[]{:S(2)}, u32[]{:S(2)}) collective-permute-start(bf16[144,512]{1,0:T(8,128)(2,1)} %get-tuple-element.53), channel_id=1, source_target_pairs={{0,24},{8,0},{16,8},{24,16},{1,25},{9,1},{17,9},{25,17},{2,26},{10... | collective-permute-start | bytes 442376 | tf_op jit(solution)/shard_map/ppermute | solution.py:414
  15.3 1.3 %collective-permute-start.4 = (bf16[4,8192]{1,0:T(4,128)(2,1)S(1)}, bf16[4,8192]{1,0:T(4,128)(2,1)S(1)}, u32[]{:S(2)}, u32[]{:S(2)}) collective-permute-start(bf16[4,8192]{1,0:T(4,128)(2,1)S(1)} %bitcast.229), channel_id=1, source_target_pairs={{1,0},{2,1},{3,2},{5,4},{6,5},{7,6},{9,8},{10,9},{11,10},{13,12},{... | collective-permute-start | bytes 196616 | tf_op jit(solution)/shard_map/ppermute | solution.py:42
  16.9 4.5 %collective-permute-start.3 = (bf16[4,8192]{1,0:T(4,128)(2,1)S(1)}, bf16[4,8192]{1,0:T(4,128)(2,1)S(1)}, u32[]{:S(2)}, u32[]{:S(2)}) collective-permute-start(bf16[4,8192]{1,0:T(4,128)(2,1)S(1)} %bitcast.231), channel_id=1, source_target_pairs={{0,1},{1,2},{2,3},{4,5},{5,6},{6,7},{8,9},{9,10},{10,11},{12,13},{... | collective-permute-start | bytes 196616 | tf_op jit(solution)/shard_map/ppermute | solution.py:41
  25.2 1.3 %collective-permute-done.5 = bf16[4,16,544]{2,1,0:T(8,128)(2,1)S(1)} collective-permute-done((bf16[4,16,544]{2,1,0:T(8,128)(2,1)S(1)}, bf16[4,16,544]{2,1,0:T(8,128)(2,1)S(1)}, u32[]{:S(2)}, u32[]{:S(2)}) %collective-permute-start.5) | collective-permute-done | bytes 69664 | tf_op jit(solution)/shard_map/ppermute | solution.py:34
  26.8 2.9 %pad_maximum_fusion.padded_ref = bf16[4,544,544]{2,1,0:T(8,128)(2,1)S(1)} fusion(bf16[4,16,544]{2,1,0:T(8,128)(2,1)S(1)} %get-tuple-element.55, bf16[4,512,16]{2,1,0:T(8,128)(2,1)} %bitcast.219, bf16[4,512,512]{2,1,0:T(8,128)(2,1)S(1)} %copy-done.3, bf16[4,512,16]{2,1,0:T(8,128)(2,1)} %bitcast.217, bf16[4,16,544]{2,1,0:T(8,128)(2,1)S(1)} %get-tuple-element.54), kind=kLoop, calls=%fused_computation | loop fusion | flops 11837440 | bytes 4734976 | tf_op jit(solution)/shard_map/concatenate | solution.py:46
  29.7 5.4 %shard_map.104 = f32[4,32,512]{2,1,0:T(8,128)S(1)} custom-call(s32[4]{0:T(128)S(1)} %get-tuple-element.42.off_ref, f32[4,3]{1,0:T(4,128)S(1)} %copy-done.1, bf16[3,256,256]{2,1,0:T(8,128)(2,1)S(1)} %copy-done, bf16[4,544,544]{2,1,0:T(8,128)(2,1)S(1)} %pad_maximum_fusion.padded_ref), custom_call_target="tpu_custom_call" | custom-call | flops 257949696 | bytes 2629632 | tf_op jit(solution)/shard_map/pallas_call | solution.py:217
  35.2 1.1 %pad_maximum_fusion.1 = bf16[4,144,512]{2,1,0:T(8,128)(2,1)S(1)} fusion(bf16[1,144,512]{2,1,0:T(8,128)(2,1)} %bitcast.12, bf16[1,144,512]{2,1,0:T(8,128)(2,1)S(1)} %bitcast.221, bf16[1,144,512]{2,1,0:T(8,128)(2,1)} %bitcast.10, bf16[1,144,512]{2,1,0:T(8,128)(2,1)S(1)} %get-tuple-element.52), kind=kLoop, calls=%fused_computation.3 | loop fusion | flops 884736 | bytes 1179648 | tf_op jit(solution)/shard_map/stack | solution.py:415
  37.9 1.1 %collective-permute-done.6 = f32[4,12]{1,0:T(4,128)S(1)} collective-permute-done((f32[4,12]{1,0:T(4,128)S(1)}, f32[4,12]{1,0:T(4,128)S(1)}, u32[]{:S(2)}, u32[]{:S(2)}) %collective-permute-start.6) | collective-permute-done | bytes 224 | tf_op jit(solution)/shard_map/ppermute | solution.py:106
  39.1 2.4 %collective-permute-start.7 = (f32[4,12]{1,0:T(4,128)S(1)}, f32[4,12]{1,0:T(4,128)S(1)}, u32[]{:S(2)}, u32[]{:S(2)}) collective-permute-start(f32[4,12]{1,0:T(4,128)S(1)} %fusion.42), channel_id=1, source_target_pairs={{0,1},{1,0},{2,3},{3,2},{4,5},{5,4},{6,7},{7,6},{8,9},{9,8},{10,11... | collective-permute-start | bytes 584 | tf_op jit(solution)/shard_map/ppermute | solution.py:106
  41.5 4.9 %shard_map.105.rest_0_ = f32[4,512,512]{2,1,0:T(8,128)} custom-call(f32[4,3]{1,0:T(4,128)S(1)} %copy-done.1, bf16[3,256,256]{2,1,0:T(8,128)(2,1)S(1)} %copy-done, bf16[4,544,544]{2,1,0:T(8,128)(2,1)S(1)} %pad_maximum_fusion.padded_ref), custom_call_target="tpu_custom_call" | custom-call | flops 1660944384 | bytes 3280896 | tf_op jit(solution)/shard_map/pallas_call | solution.py:274
  47.1 4.8 %shard_map.106.matched_ref = f32[4,512,512]{2,1,0:T(8,128)} custom-call(f32[4,3]{1,0:T(4,128)S(1)} %copy-done.1, bf16[3,256,256]{2,1,0:T(8,128)(2,1)S(1)} %copy-done, bf16[4,544,544]{2,1,0:T(8,128)(2,1)S(1)} %pad_maximum_fusion.padded_ref, f32[4,512,512]{2,1,0:T(8,128)} %shard_map.105.rest_0_), custom_call_target="tpu_custom_call", output_to_operand_aliasing={{}: (3, {})} | custom-call | flops 1660944384 | bytes 3280896 | tf_op jit(solution)/shard_map/pallas_call | solution.py:274
  53.3 7.3 %shard_map.108 = bf16[4,256,512]{2,1,0:T(8,128)(2,1)} custom-call(s32[4,2]{1,0:T(4,128)} %copy.130.idx_ref, f32[4,3]{1,0:T(4,128)} %pad_maximum_fusion.11.plane_ref, f32[4,4]{1,0:T(4,128)} %fusion.24.pick_ref, f32[1,512]{1,0:T(1,128)} %multiply_add_fusion.1.xrow_ref, f32[512,1]{1,0:T(8,128)} %multiply_add_fusion.ycol_ref, ...), custom_call_target="tpu_custom_call" | custom-call | flops 1073741824 | bytes 8388608 | tf_op jit(solution)/shard_map/pallas_call | solution.py:341
  61.7 7.5 %shard_map.107 = bf16[4,256,512]{2,1,0:T(8,128)(2,1)} custom-call(s32[4,2]{1,0:T(4,128)} %copy.130.idx_ref, f32[4,3]{1,0:T(4,128)} %pad_maximum_fusion.11.plane_ref, f32[4,4]{1,0:T(4,128)} %fusion.24.pick_ref, f32[1,512]{1,0:T(1,128)} %multiply_add_fusion.1.xrow_ref, f32[512,1]{1,0:T(8,128)} %multiply_add_fusion.ycol_ref, ...), custom_call_target="tpu_custom_call" | custom-call | flops 1073741824 | bytes 8388608 | tf_op jit(solution)/shard_map/pallas_call | solution.py:341
  69.1 1.1 %slice_bitcast_fusion.9 = bf16[256,512]{1,0:T(8,128)(2,1)S(1)} fusion(bf16[4,256,512]{2,1,0:T(8,128)(2,1)} %shard_map.107), kind=kLoop, calls=%fused_computation.27 | loop fusion | bytes 524288 | tf_op jit(solution)/shard_map/squeeze | solution.py:356
  70.3 1.4 %collective-permute-done.12 = bf16[256,512]{1,0:T(8,128)(2,1)S(1)} collective-permute-done((bf16[256,512]{1,0:T(8,128)(2,1)S(1)}, bf16[256,512]{1,0:T(8,128)(2,1)S(1)}, u32[]{:S(2)}, u32[]{:S(2)}) %collective-permute-start.12) | collective-permute-done | bytes 262176 | tf_op jit(solution)/shard_map/ppermute | solution.py:358
  71.8 9.4 %collective-permute-done.9 = bf16[256,512]{1,0:T(8,128)(2,1)S(1)} collective-permute-done((bf16[256,512]{1,0:T(8,128)(2,1)S(1)}, bf16[256,512]{1,0:T(8,128)(2,1)S(1)}, u32[]{:S(2)}, u32[]{:S(2)}) %collective-permute-start.9) | collective-permute-done | bytes 262176 | tf_op jit(solution)/shard_map/ppermute | solution.py:358
  82.3 4.5 %collective-permute-done.13 = bf16[256,512]{1,0:T(8,128)(2,1)S(1)} collective-permute-done((bf16[256,512]{1,0:T(8,128)(2,1)S(1)}, bf16[256,512]{1,0:T(8,128)(2,1)S(1)}, u32[]{:S(2)}, u32[]{:S(2)}) %collective-permute-start.13) | collective-permute-done | bytes 262176 | tf_op jit(solution)/shard_map/ppermute | solution.py:358
  87.0 6.4 %collective-permute-done.10 = bf16[256,512]{1,0:T(8,128)(2,1)S(1)} collective-permute-done((bf16[256,512]{1,0:T(8,128)(2,1)S(1)}, bf16[256,512]{1,0:T(8,128)(2,1)S(1)}, u32[]{:S(2)}, u32[]{:S(2)}) %collective-permute-start.10) | collective-permute-done | bytes 262176 | tf_op jit(solution)/shard_map/ppermute | solution.py:358
  95.1 3.9 %collective-permute-done.14 = bf16[256,512]{1,0:T(8,128)(2,1)} collective-permute-done((bf16[256,512]{1,0:T(8,128)(2,1)S(1)}, bf16[256,512]{1,0:T(8,128)(2,1)}, u32[]{:S(2)}, u32[]{:S(2)}) %collective-permute-start.14) | collective-permute-done | bytes 262176 | tf_op jit(solution)/shard_map/ppermute | solution.py:358
  100.1 2.8 %collective-permute-done.11 = bf16[256,512]{1,0:T(8,128)(2,1)S(1)} collective-permute-done((bf16[256,512]{1,0:T(8,128)(2,1)S(1)}, bf16[256,512]{1,0:T(8,128)(2,1)S(1)}, u32[]{:S(2)}, u32[]{:S(2)}) %collective-permute-start.11) | collective-permute-done | bytes 262176 | tf_op jit(solution)/shard_map/ppermute | solution.py:358
  102.9 1.7 %maximum_divide_fusion = f32[1,512,512]{2,1,0:T(8,128)} fusion(f32[1,256,512]{2,1,0:T(8,128)S(1)} %fusion, f32[1,256,512]{2,1,0:T(8,128)S(1)} %fusion.3, f32[]{:T(128)} %convert_reduce_fusion), kind=kLoop, calls=%fused_computation.2 | loop fusion | flops 524288 | bytes 2097156 | tf_op jit(solution)/shard_map/div | solution.py:487
  (108 shorter events, 18.0 us)
Async XLA Ops:
  0.6 14.2 %copy-start.2 = (bf16[4,512,512]{2,1,0:T(8,128)(2,1)S(1)}, bf16[4,512,512]{2,1,0:T(8,128)(2,1)}, u32[]{:S(2)}) copy-start(bf16[4,512,512]{2,1,0:T(8,128)(2,1)} %param.11) | copy-start | bytes 6291460
  4.1 18.2 %copy-start.8 = (s32[4,1,1,2]{0,3,2,1:T(2,128)S(1)}, s32[4,1,1,2]{0,3,2,1:T(2,128)}, u32[]{:S(2)}) copy-start(s32[4,1,1,2]{0,3,2,1:T(2,128)} %param.16) | copy-start | bytes 100
  4.1 18.9 %copy-start.9 = (bf16[4,1,1]{0,2,1:T(2,128)(2,1)S(1)}, bf16[4,1,1]{0,2,1:T(2,128)(2,1)}, u32[]{:S(2)}) copy-start(bf16[4,1,1]{0,2,1:T(2,128)(2,1)} %param.14) | copy-start | bytes 28
  7.0 28.2 %collective-permute-start.1 = (bf16[144,512]{1,0:T(8,128)(2,1)}, bf16[144,512]{1,0:T(8,128)(2,1)S(1)}, u32[]{:S(2)}, u32[]{:S(2)}) collective-permute-start(bf16[144,512]{1,0:T(8,128)(2,1)} %get-tuple-element.53), channel_id=1, source_target_pairs={{0,16},{8,24},{16,0},{24,8},{1,17},{9,25},{17,1},{25,9},{2,18},{10... | collective-permute-start | bytes 442376 | tf_op jit(solution)/shard_map/ppermute | solution.py:414
  11.0 24.2 %collective-permute-start = (bf16[144,512]{1,0:T(8,128)(2,1)}, bf16[144,512]{1,0:T(8,128)(2,1)}, u32[]{:S(2)}, u32[]{:S(2)}) collective-permute-start(bf16[144,512]{1,0:T(8,128)(2,1)} %get-tuple-element.53), channel_id=1, source_target_pairs={{0,8},{8,16},{16,24},{24,0},{1,9},{9,17},{17,25},{25,1},{2,10},{10... | collective-permute-start | bytes 442376 | tf_op jit(solution)/shard_map/ppermute | solution.py:414
  12.6 22.6 %collective-permute-start.2 = (bf16[144,512]{1,0:T(8,128)(2,1)}, bf16[144,512]{1,0:T(8,128)(2,1)}, u32[]{:S(2)}, u32[]{:S(2)}) collective-permute-start(bf16[144,512]{1,0:T(8,128)(2,1)} %get-tuple-element.53), channel_id=1, source_target_pairs={{0,24},{8,0},{16,8},{24,16},{1,25},{9,1},{17,9},{25,17},{2,26},{10... | collective-permute-start | bytes 442376 | tf_op jit(solution)/shard_map/ppermute | solution.py:414
  15.3 9.1 %collective-permute-start.4 = (bf16[4,8192]{1,0:T(4,128)(2,1)S(1)}, bf16[4,8192]{1,0:T(4,128)(2,1)S(1)}, u32[]{:S(2)}, u32[]{:S(2)}) collective-permute-start(bf16[4,8192]{1,0:T(4,128)(2,1)S(1)} %bitcast.229), channel_id=1, source_target_pairs={{1,0},{2,1},{3,2},{5,4},{6,5},{7,6},{9,8},{10,9},{11,10},{13,12},{... | collective-permute-start | bytes 196616 | tf_op jit(solution)/shard_map/ppermute | solution.py:42
  16.9 7.5 %collective-permute-start.3 = (bf16[4,8192]{1,0:T(4,128)(2,1)S(1)}, bf16[4,8192]{1,0:T(4,128)(2,1)S(1)}, u32[]{:S(2)}, u32[]{:S(2)}) collective-permute-start(bf16[4,8192]{1,0:T(4,128)(2,1)S(1)} %bitcast.231), channel_id=1, source_target_pairs={{0,1},{1,2},{2,3},{4,5},{5,6},{6,7},{8,9},{9,10},{10,11},{12,13},{... | collective-permute-start | bytes 196616 | tf_op jit(solution)/shard_map/ppermute | solution.py:41
  24.7 1.8 %copy-start.4 = (bf16[4,16,512]{1,2,0:T(8,128)(2,1)}, bf16[4,16,512]{1,2,0:T(8,128)(2,1)S(1)}, u32[]{:S(2)}) copy-start(bf16[4,16,512]{1,2,0:T(8,128)(2,1)S(1)} %copy.108) | copy-start | bytes 196612
  25.0 1.8 %copy-start.3 = (bf16[4,512,512]{2,1,0:T(8,128)(2,1)S(1)}, bf16[4,512,512]{2,1,0:T(8,128)(2,1)}, u32[]{:S(2)}) copy-start(bf16[4,512,512]{2,1,0:T(8,128)(2,1)} %param.11) | copy-start | bytes 6291460
  25.1 1.3 %collective-permute-start.5 = (bf16[4,16,544]{2,1,0:T(8,128)(2,1)S(1)}, bf16[4,16,544]{2,1,0:T(8,128)(2,1)S(1)}, u32[]{:S(2)}, u32[]{:S(2)}) collective-permute-start(bf16[4,16,544]{2,1,0:T(8,128)(2,1)S(1)} %fusion.9), channel_id=1, source_target_pairs={{0,4},{4,0},{1,5},{5,1},{2,6},{6,2},{3,7},{7,3},{8,12},{12,8},{9,1... | collective-permute-start | bytes 208904 | tf_op jit(solution)/shard_map/ppermute | solution.py:34
  26.8 2.9 %copy-start = (bf16[3,256,256]{2,1,0:T(8,128)(2,1)S(1)}, bf16[3,256,256]{2,1,0:T(8,128)(2,1)}, u32[]{:S(2)}) copy-start(bf16[3,256,256]{2,1,0:T(8,128)(2,1)} %constant.134.clone.tb_ref.blk_ref) | copy-start | bytes 1179652
  26.8 2.9 %copy-start.1 = (f32[4,3]{1,0:T(4,128)S(1)}, f32[4,3]{1,0:T(4,128)}, u32[]{:S(2)}) copy-start(f32[4,3]{1,0:T(4,128)} %coef_ref.5) | copy-start | bytes 148
  37.8 1.2 %collective-permute-start.6 = (f32[4,12]{1,0:T(4,128)S(1)}, f32[4,12]{1,0:T(4,128)S(1)}, u32[]{:S(2)}, u32[]{:S(2)}) collective-permute-start(f32[4,12]{1,0:T(4,128)S(1)} %pad_maximum_fusion.9), channel_id=1, source_target_pairs={{0,4},{4,0},{1,5},{5,1},{2,6},{6,2},{3,7},{7,3},{8,12},{12,8},{9,1... | collective-permute-start | bytes 584 | tf_op jit(solution)/shard_map/ppermute | solution.py:106
  39.1 7.2 %collective-permute-start.7 = (f32[4,12]{1,0:T(4,128)S(1)}, f32[4,12]{1,0:T(4,128)S(1)}, u32[]{:S(2)}, u32[]{:S(2)}) collective-permute-start(f32[4,12]{1,0:T(4,128)S(1)} %fusion.42), channel_id=1, source_target_pairs={{0,1},{1,0},{2,3},{3,2},{4,5},{5,4},{6,7},{7,6},{8,9},{9,8},{10,11... | collective-permute-start | bytes 584 | tf_op jit(solution)/shard_map/ppermute | solution.py:106
  46.3 5.6 %collective-permute-start.8 = (f32[4,12]{1,0:T(4,128)S(1)}, f32[4,12]{1,0:T(4,128)S(1)}, u32[]{:S(2)}, u32[]{:S(2)}) collective-permute-start(f32[4,12]{1,0:T(4,128)S(1)} %add.243), channel_id=1, source_target_pairs={{0,2},{1,3},{2,0},{3,1},{4,6},{5,7},{6,4},{7,5},{8,10},{9,11},{10,... | collective-permute-start | bytes 584 | tf_op jit(solution)/shard_map/ppermute | solution.py:106
  61.6 10.1 %copy-start.7 = (bf16[4,256,512]{2,1,0:T(8,128)(2,1)S(1)}, bf16[4,256,512]{2,1,0:T(8,128)(2,1)}, u32[]{:S(2)}) copy-start(bf16[4,256,512]{2,1,0:T(8,128)(2,1)} %shard_map.108) | copy-start | bytes 3145732
  61.6 10.0 %collective-permute-start.12 = (bf16[256,512]{1,0:T(8,128)(2,1)S(1)}, bf16[256,512]{1,0:T(8,128)(2,1)S(1)}, u32[]{:S(2)}, u32[]{:S(2)}) collective-permute-start(bf16[256,512]{1,0:T(8,128)(2,1)S(1)} %slice_bitcast_fusion.5), channel_id=1, source_target_pairs={{0,8},{8,16},{16,24},{24,0},{1,9},{9,17},{17,25},{25,1},{2,10},{10... | collective-permute-start | bytes 786440 | tf_op jit(solution)/shard_map/ppermute | solution.py:358
  69.1 24.2 %copy-start.6 = (bf16[4,256,512]{2,1,0:T(8,128)(2,1)S(1)}, bf16[4,256,512]{2,1,0:T(8,128)(2,1)}, u32[]{:S(2)}) copy-start(bf16[4,256,512]{2,1,0:T(8,128)(2,1)} %shard_map.107) | copy-start | bytes 3145732
  70.2 11.0 %collective-permute-start.9 = (bf16[256,512]{1,0:T(8,128)(2,1)S(1)}, bf16[256,512]{1,0:T(8,128)(2,1)S(1)}, u32[]{:S(2)}, u32[]{:S(2)}) collective-permute-start(bf16[256,512]{1,0:T(8,128)(2,1)S(1)} %slice_bitcast_fusion.9), channel_id=1, source_target_pairs={{0,8},{8,16},{16,24},{24,0},{1,9},{9,17},{17,25},{25,1},{2,10},{10... | collective-permute-start | bytes 786440 | tf_op jit(solution)/shard_map/ppermute | solution.py:358
  71.7 15.1 %collective-permute-start.13 = (bf16[256,512]{1,0:T(8,128)(2,1)S(1)}, bf16[256,512]{1,0:T(8,128)(2,1)S(1)}, u32[]{:S(2)}, u32[]{:S(2)}) collective-permute-start(bf16[256,512]{1,0:T(8,128)(2,1)S(1)} %fusion.2), channel_id=1, source_target_pairs={{0,8},{8,16},{16,24},{24,0},{1,9},{9,17},{17,25},{25,1},{2,10},{10... | collective-permute-start | bytes 786440 | tf_op jit(solution)/shard_map/ppermute | solution.py:358
  82.2 11.1 %collective-permute-start.10 = (bf16[256,512]{1,0:T(8,128)(2,1)S(1)}, bf16[256,512]{1,0:T(8,128)(2,1)S(1)}, u32[]{:S(2)}, u32[]{:S(2)}) collective-permute-start(bf16[256,512]{1,0:T(8,128)(2,1)S(1)} %fusion.5), channel_id=1, source_target_pairs={{0,8},{8,16},{16,24},{24,0},{1,9},{9,17},{17,25},{25,1},{2,10},{10... | collective-permute-start | bytes 786440 | tf_op jit(solution)/shard_map/ppermute | solution.py:358
  86.9 12.1 %collective-permute-start.14 = (bf16[256,512]{1,0:T(8,128)(2,1)S(1)}, bf16[256,512]{1,0:T(8,128)(2,1)}, u32[]{:S(2)}, u32[]{:S(2)}) collective-permute-start(bf16[256,512]{1,0:T(8,128)(2,1)S(1)} %fusion.1), channel_id=1, source_target_pairs={{0,8},{8,16},{16,24},{24,0},{1,9},{9,17},{17,25},{25,1},{2,10},{10... | collective-permute-start | bytes 786440 | tf_op jit(solution)/shard_map/ppermute | solution.py:358
  93.4 9.4 %collective-permute-start.11 = (bf16[256,512]{1,0:T(8,128)(2,1)S(1)}, bf16[256,512]{1,0:T(8,128)(2,1)S(1)}, u32[]{:S(2)}, u32[]{:S(2)}) collective-permute-start(bf16[256,512]{1,0:T(8,128)(2,1)S(1)} %fusion.4), channel_id=1, source_target_pairs={{0,8},{8,16},{16,24},{24,0},{1,9},{9,17},{17,25},{25,1},{2,10},{10... | collective-permute-start | bytes 786440 | tf_op jit(solution)/shard_map/ppermute | solution.py:358
  (1 other events, 1.5 us)

commit v19 on v18

--- a/solution.py
+++ b/solution.py
@@ -286,7 +286,8 @@
 
 
 def warp_body(idx_ref, plane_ref, pick_ref, xrow_ref, ycol_ref, matched_ref, rmap_ref, cmap_ref,
-              out_ref, acc_ref):
+              *rest):
+    out_refs, acc_ref = rest[:-1], rest[-1]
     e = pl.program_id(0)
     background = (
         plane_ref[e, 0] + plane_ref[e, 1] * xrow_ref[...]
@@ -312,7 +313,8 @@
 
     @pl.when(e == pl.num_programs(0) - 1)
     def _():
-        out_ref[...] = acc_ref[...].astype(jnp.bfloat16)
+        for v in range(patches):
+            out_refs[v][...] = acc_ref[v].astype(jnp.bfloat16)
 
 
 def warp_tiles(choose, plane, picked, xrow, ycol, matched, bank, part, pieces):
@@ -331,7 +333,7 @@
             pl.BlockSpec((1, rows, tile_len), lambda e, idx: (idx[e, 0], part, 0)),
             pl.BlockSpec((1, tile_len, tile_len), lambda e, idx: (idx[e, 1], 0, 0)),
         ],
-        out_specs=pl.BlockSpec((patches, rows, tile_len), lambda e, idx: (0, 0, 0)),
+        out_specs=[pl.BlockSpec((rows, tile_len), lambda e, idx: (0, 0)) for _ in range(patches)],
         scratch_shapes=[pltpu.VMEM((patches, rows, tile_len), jnp.float32)],
     )
     flops = exp_dev * 4 * rows * tile_len * tile_len
@@ -341,7 +343,7 @@
     return pl.pallas_call(
         warp_body,
         grid_spec=grid_spec,
-        out_shape=jax.ShapeDtypeStruct((patches, rows, tile_len), jnp.bfloat16),
+        out_shape=[jax.ShapeDtypeStruct((rows, tile_len), jnp.bfloat16) for _ in range(patches)],
         compiler_params=pltpu.CompilerParams(
             dimension_semantics=("arbitrary",), vmem_limit_bytes=vmem
         ),

time: 105 us -> 104 us (level)
  local copies, waits for them, and re-layouts: 6.67 us -> 4.64 us
    squeeze x2 -> x0, local copies, waits for them, and re-layouts: 2.02 us -> none  [ring_scatter(): own = parts[step].astype(jnp.float32)]
  transfers between devices with their start and end apart: 15 -> 15, of which waited for: 8 -> 8; matrix products, arithmetic and copies ran while one was open for 12% -> 11% of each run, Pallas kernels for 22% -> 22%
where the time goes in v19:
time: 104 us; the launch traced here: 103 us
  waiting for transfers between devices  30.8 us (30%)
  Pallas kernels  30.2 us (29%)
  starting transfers between devices  17.3 us (17%)
  other arithmetic  15.6 us (15%)
  local copies, waits for them, and re-layouts  4.64 us (4%)
  matrix products  3.22 us (3%)
  between operations  1.08 us (1%)
    ppermute x6, waiting for transfers between devices, ring_scatter(): lax.ppermute(outgoing.astype(jnp.bfloat16), axis, ring).astype(jnp.float32)  28.5 us
    pallas_call x2, Pallas kernels, warp_tiles(): pl.pallas_call(warp_body, grid_spec=grid_spec, out_shape=[jax.ShapeDtypeS...  15.1 us
    pallas_call x2, Pallas kernels, band_tiles(): pl.pallas_call(functools.partial(band_body, first), grid=(count,), in_spe...  9.67 us
    ppermute x3, starting transfers between devices, shards(): received.append(lax.ppermute(payload, 'visit', pairs))  7.86 us
    pallas_call x1, Pallas kernels, strip_tiles(): pl.pallas_call(strip_body, grid_spec=grid_spec, out_shape=jax.ShapeDtypeS...  5.44 us
    ppermute x1, starting transfers between devices, extended(): before = lax.ppermute(last, axis, up)  4.55 us
    ppermute x3, starting transfers between devices, butterfly_sum(): values = jax.tree.map(lambda v: v + lax.ppermute(v, axis, pairs), values)  3.22 us
    concatenate x1, other arithmetic, extended(): value = jnp.concatenate([before, value, after], axis=dim)  2.9 us
  transfers between devices with their start and end apart: 15, of which 8 were waited for; matrix products, arithmetic and copies ran while one was open for 11% of the time, Pallas kernels for 22%

profile of v19, /device:TPU:0, one launch (start us, length us, event | category | flops | bytes accessed | tf_op | source)
XLA Modules:
  0.0 102.8 jit_solution(8594645160124692609)
XLA Ops:
  4.2 2.1 %convolution_convert_fusion = bf16[4,32,512]{2,1,0:T(8,128)(2,1)S(1)} fusion(bf16[4,512,512]{2,1,0:T(8,128)(2,1)} %param.11, s32[4]{0:T(128)S(1)} %get-tuple-element.58.off_ref), kind=kOutput, calls=%fused_computation.1 | convolution fusion | flops 67305472 | bytes 2228240 | tf_op jit(solution)/shard_map/esr,erl->esl/dot_general | solution.py:396
  7.0 4.0 %collective-permute-start.1 = (bf16[144,512]{1,0:T(8,128)(2,1)}, bf16[144,512]{1,0:T(8,128)(2,1)S(1)}, u32[]{:S(2)}, u32[]{:S(2)}) collective-permute-start(bf16[144,512]{1,0:T(8,128)(2,1)} %get-tuple-element.69), channel_id=1, source_target_pairs={{0,16},{8,24},{16,0},{24,8},{1,17},{9,25},{17,1},{25,9},{2,18},{10... | collective-permute-start | bytes 442376 | tf_op jit(solution)/shard_map/ppermute | solution.py:416
  11.0 1.6 %collective-permute-start = (bf16[144,512]{1,0:T(8,128)(2,1)}, bf16[144,512]{1,0:T(8,128)(2,1)}, u32[]{:S(2)}, u32[]{:S(2)}) collective-permute-start(bf16[144,512]{1,0:T(8,128)(2,1)} %get-tuple-element.69), channel_id=1, source_target_pairs={{0,8},{8,16},{16,24},{24,0},{1,9},{9,17},{17,25},{25,1},{2,10},{10... | collective-permute-start | bytes 442376 | tf_op jit(solution)/shard_map/ppermute | solution.py:416
  12.6 2.2 %collective-permute-start.2 = (bf16[144,512]{1,0:T(8,128)(2,1)}, bf16[144,512]{1,0:T(8,128)(2,1)}, u32[]{:S(2)}, u32[]{:S(2)}) collective-permute-start(bf16[144,512]{1,0:T(8,128)(2,1)} %get-tuple-element.69), channel_id=1, source_target_pairs={{0,24},{8,0},{16,8},{24,16},{1,25},{9,1},{17,9},{25,17},{2,26},{10... | collective-permute-start | bytes 442376 | tf_op jit(solution)/shard_map/ppermute | solution.py:416
  15.3 1.3 %collective-permute-start.4 = (bf16[4,8192]{1,0:T(4,128)(2,1)S(1)}, bf16[4,8192]{1,0:T(4,128)(2,1)S(1)}, u32[]{:S(2)}, u32[]{:S(2)}) collective-permute-start(bf16[4,8192]{1,0:T(4,128)(2,1)S(1)} %bitcast.195), channel_id=1, source_target_pairs={{1,0},{2,1},{3,2},{5,4},{6,5},{7,6},{9,8},{10,9},{11,10},{13,12},{... | collective-permute-start | bytes 196616 | tf_op jit(solution)/shard_map/ppermute | solution.py:42
  16.9 4.5 %collective-permute-start.3 = (bf16[4,8192]{1,0:T(4,128)(2,1)S(1)}, bf16[4,8192]{1,0:T(4,128)(2,1)S(1)}, u32[]{:S(2)}, u32[]{:S(2)}) collective-permute-start(bf16[4,8192]{1,0:T(4,128)(2,1)S(1)} %bitcast.197), channel_id=1, source_target_pairs={{0,1},{1,2},{2,3},{4,5},{5,6},{6,7},{8,9},{9,10},{10,11},{12,13},{... | collective-permute-start | bytes 196616 | tf_op jit(solution)/shard_map/ppermute | solution.py:41
  25.2 1.3 %collective-permute-done.5 = bf16[4,16,544]{2,1,0:T(8,128)(2,1)S(1)} collective-permute-done((bf16[4,16,544]{2,1,0:T(8,128)(2,1)S(1)}, bf16[4,16,544]{2,1,0:T(8,128)(2,1)S(1)}, u32[]{:S(2)}, u32[]{:S(2)}) %collective-permute-start.5) | collective-permute-done | bytes 69664 | tf_op jit(solution)/shard_map/ppermute | solution.py:34
  26.7 2.9 %pad_maximum_fusion.padded_ref = bf16[4,544,544]{2,1,0:T(8,128)(2,1)S(1)} fusion(bf16[4,16,544]{2,1,0:T(8,128)(2,1)S(1)} %get-tuple-element.71, bf16[4,512,16]{2,1,0:T(8,128)(2,1)} %bitcast.185, bf16[4,512,512]{2,1,0:T(8,128)(2,1)S(1)} %copy-done.3, bf16[4,512,16]{2,1,0:T(8,128)(2,1)} %bitcast.183, bf16[4,16,544]{2,1,0:T(8,128)(2,1)S(1)} %get-tuple-element.70), kind=kLoop, calls=%fused_computation | loop fusion | flops 11837440 | bytes 4734976 | tf_op jit(solution)/shard_map/concatenate | solution.py:46
  29.6 5.4 %shard_map.104 = f32[4,32,512]{2,1,0:T(8,128)S(1)} custom-call(s32[4]{0:T(128)S(1)} %get-tuple-element.58.off_ref, f32[4,3]{1,0:T(4,128)S(1)} %copy-done.1, bf16[3,256,256]{2,1,0:T(8,128)(2,1)S(1)} %copy-done, bf16[4,544,544]{2,1,0:T(8,128)(2,1)S(1)} %pad_maximum_fusion.padded_ref), custom_call_target="tpu_custom_call" | custom-call | flops 257949696 | bytes 2629632 | tf_op jit(solution)/shard_map/pallas_call | solution.py:217
  35.1 1.1 %pad_maximum_fusion.1 = bf16[4,144,512]{2,1,0:T(8,128)(2,1)S(1)} fusion(bf16[1,144,512]{2,1,0:T(8,128)(2,1)} %bitcast.12, bf16[1,144,512]{2,1,0:T(8,128)(2,1)S(1)} %bitcast.187, bf16[1,144,512]{2,1,0:T(8,128)(2,1)} %bitcast.10, bf16[1,144,512]{2,1,0:T(8,128)(2,1)S(1)} %get-tuple-element.68), kind=kLoop, calls=%fused_computation.3 | loop fusion | flops 884736 | bytes 1179648 | tf_op jit(solution)/shard_map/stack | solution.py:417
  37.8 1.1 %collective-permute-done.6 = f32[4,12]{1,0:T(4,128)S(1)} collective-permute-done((f32[4,12]{1,0:T(4,128)S(1)}, f32[4,12]{1,0:T(4,128)S(1)}, u32[]{:S(2)}, u32[]{:S(2)}) %collective-permute-start.6) | collective-permute-done | bytes 224 | tf_op jit(solution)/shard_map/ppermute | solution.py:106
  39.0 2.4 %collective-permute-start.7 = (f32[4,12]{1,0:T(4,128)S(1)}, f32[4,12]{1,0:T(4,128)S(1)}, u32[]{:S(2)}, u32[]{:S(2)}) collective-permute-start(f32[4,12]{1,0:T(4,128)S(1)} %fusion.36), channel_id=1, source_target_pairs={{0,1},{1,0},{2,3},{3,2},{4,5},{5,4},{6,7},{7,6},{8,9},{9,8},{10,11... | collective-permute-start | bytes 584 | tf_op jit(solution)/shard_map/ppermute | solution.py:106
  41.4 4.9 %shard_map.105.rest_0_ = f32[4,512,512]{2,1,0:T(8,128)} custom-call(f32[4,3]{1,0:T(4,128)S(1)} %copy-done.1, bf16[3,256,256]{2,1,0:T(8,128)(2,1)S(1)} %copy-done, bf16[4,544,544]{2,1,0:T(8,128)(2,1)S(1)} %pad_maximum_fusion.padded_ref), custom_call_target="tpu_custom_call" | custom-call | flops 1660944384 | bytes 3280896 | tf_op jit(solution)/shard_map/pallas_call | solution.py:274
  47.1 4.8 %shard_map.106.matched_ref = f32[4,512,512]{2,1,0:T(8,128)} custom-call(f32[4,3]{1,0:T(4,128)S(1)} %copy-done.1, bf16[3,256,256]{2,1,0:T(8,128)(2,1)S(1)} %copy-done, bf16[4,544,544]{2,1,0:T(8,128)(2,1)S(1)} %pad_maximum_fusion.padded_ref, f32[4,512,512]{2,1,0:T(8,128)} %shard_map.105.rest_0_), custom_call_target="tpu_custom_call", output_to_operand_aliasing={{}: (3, {})} | custom-call | flops 1660944384 | bytes 3280896 | tf_op jit(solution)/shard_map/pallas_call | solution.py:274
  53.3 7.4 %shard_map.108 = (bf16[256,512]{1,0:T(8,128)(2,1)}, bf16[256,512]{1,0:T(8,128)(2,1)}, bf16[256,512]{1,0:T(8,128)(2,1)}, bf16[256,512]{1,0:T(8,128)(2,1)}) custom-call(s32[4,2]{1,0:T(4,128)} %copy.130.idx_ref, f32[4,3]{1,0:T(4,128)} %pad_maximum_fusion.11.plane_ref, f32[4,4]{1,0:T(4,128)} %fusion.18.pick_ref, f32[1,512]{1,0:T(1,128)} %multiply_add_fusion.1.xrow_ref, ...), custom_call_target="tpu_custom_call" | custom-call | flops 1073741824 | bytes 8388608 | tf_op jit(solution)/shard_map/pallas_call | solution.py:343
  60.8 7.7 %shard_map.107 = (bf16[256,512]{1,0:T(8,128)(2,1)}, bf16[256,512]{1,0:T(8,128)(2,1)}, bf16[256,512]{1,0:T(8,128)(2,1)}, bf16[256,512]{1,0:T(8,128)(2,1)}) custom-call(s32[4,2]{1,0:T(4,128)} %copy.130.idx_ref, f32[4,3]{1,0:T(4,128)} %pad_maximum_fusion.11.plane_ref, f32[4,4]{1,0:T(4,128)} %fusion.18.pick_ref, f32[1,512]{1,0:T(1,128)} %multiply_add_fusion.1.xrow_ref, ...), custom_call_target="tpu_custom_call" | custom-call | flops 1073741824 | bytes 8388608 | tf_op jit(solution)/shard_map/pallas_call | solution.py:343
  68.5 2.3 %collective-permute-done.12 = bf16[256,512]{1,0:T(8,128)(2,1)S(1)} collective-permute-done((bf16[256,512]{1,0:T(8,128)(2,1)}, bf16[256,512]{1,0:T(8,128)(2,1)S(1)}, u32[]{:S(2)}, u32[]{:S(2)}) %collective-permute-start.12) | collective-permute-done | bytes 262176 | tf_op jit(solution)/shard_map/ppermute | solution.py:360
  70.9 8.8 %collective-permute-done.9 = bf16[256,512]{1,0:T(8,128)(2,1)S(1)} collective-permute-done((bf16[256,512]{1,0:T(8,128)(2,1)}, bf16[256,512]{1,0:T(8,128)(2,1)S(1)}, u32[]{:S(2)}, u32[]{:S(2)}) %collective-permute-start.9) | collective-permute-done | bytes 262176 | tf_op jit(solution)/shard_map/ppermute | solution.py:360
  79.8 1.0 add_convert_fusion.3
  80.8 4.5 %collective-permute-done.13 = bf16[256,512]{1,0:T(8,128)(2,1)S(1)} collective-permute-done((bf16[256,512]{1,0:T(8,128)(2,1)S(1)}, bf16[256,512]{1,0:T(8,128)(2,1)S(1)}, u32[]{:S(2)}, u32[]{:S(2)}) %collective-permute-start.13) | collective-permute-done | bytes 262176 | tf_op jit(solution)/shard_map/ppermute | solution.py:360
  85.5 6.4 %collective-permute-done.10 = bf16[256,512]{1,0:T(8,128)(2,1)S(1)} collective-permute-done((bf16[256,512]{1,0:T(8,128)(2,1)S(1)}, bf16[256,512]{1,0:T(8,128)(2,1)S(1)}, u32[]{:S(2)}, u32[]{:S(2)}) %collective-permute-start.10) | collective-permute-done | bytes 262176 | tf_op jit(solution)/shard_map/ppermute | solution.py:360
  94.5 3.0 %collective-permute-done.14 = bf16[256,512]{1,0:T(8,128)(2,1)S(1)} collective-permute-done((bf16[256,512]{1,0:T(8,128)(2,1)S(1)}, bf16[256,512]{1,0:T(8,128)(2,1)S(1)}, u32[]{:S(2)}, u32[]{:S(2)}) %collective-permute-start.14) | collective-permute-done | bytes 262176 | tf_op jit(solution)/shard_map/ppermute | solution.py:360
  97.6 3.5 %collective-permute-done.11 = bf16[256,512]{1,0:T(8,128)(2,1)S(1)} collective-permute-done((bf16[256,512]{1,0:T(8,128)(2,1)S(1)}, bf16[256,512]{1,0:T(8,128)(2,1)S(1)}, u32[]{:S(2)}, u32[]{:S(2)}) %collective-permute-start.11) | collective-permute-done | bytes 262176 | tf_op jit(solution)/shard_map/ppermute | solution.py:360
  101.2 1.7 %maximum_divide_fusion = f32[1,512,512]{2,1,0:T(8,128)} fusion(f32[1,256,512]{2,1,0:T(8,128)S(1)} %add_bitcast_fusion, f32[1,256,512]{2,1,0:T(8,128)S(1)} %add_bitcast_fusion.1, f32[]{:T(128)} %convert_reduce_fusion), kind=kLoop, calls=%fused_computation.2 | loop fusion | flops 524288 | bytes 2097156 | tf_op jit(solution)/shard_map/div | solution.py:489
  (110 shorter events, 16.0 us)
Async XLA Ops:
  0.6 14.2 %copy-start.2 = (bf16[4,512,512]{2,1,0:T(8,128)(2,1)S(1)}, bf16[4,512,512]{2,1,0:T(8,128)(2,1)}, u32[]{:S(2)}) copy-start(bf16[4,512,512]{2,1,0:T(8,128)(2,1)} %param.11) | copy-start | bytes 6291460
  4.1 18.2 %copy-start.10 = (s32[4,1,1,2]{0,3,2,1:T(2,128)S(1)}, s32[4,1,1,2]{0,3,2,1:T(2,128)}, u32[]{:S(2)}) copy-start(s32[4,1,1,2]{0,3,2,1:T(2,128)} %param.16) | copy-start | bytes 100
  4.1 18.8 %copy-start.11 = (bf16[4,1,1]{0,2,1:T(2,128)(2,1)S(1)}, bf16[4,1,1]{0,2,1:T(2,128)(2,1)}, u32[]{:S(2)}) copy-start(bf16[4,1,1]{0,2,1:T(2,128)(2,1)} %param.14) | copy-start | bytes 28
  7.0 28.1 %collective-permute-start.1 = (bf16[144,512]{1,0:T(8,128)(2,1)}, bf16[144,512]{1,0:T(8,128)(2,1)S(1)}, u32[]{:S(2)}, u32[]{:S(2)}) collective-permute-start(bf16[144,512]{1,0:T(8,128)(2,1)} %get-tuple-element.69), channel_id=1, source_target_pairs={{0,16},{8,24},{16,0},{24,8},{1,17},{9,25},{17,1},{25,9},{2,18},{10... | collective-permute-start | bytes 442376 | tf_op jit(solution)/shard_map/ppermute | solution.py:416
  11.0 24.1 %collective-permute-start = (bf16[144,512]{1,0:T(8,128)(2,1)}, bf16[144,512]{1,0:T(8,128)(2,1)}, u32[]{:S(2)}, u32[]{:S(2)}) collective-permute-start(bf16[144,512]{1,0:T(8,128)(2,1)} %get-tuple-element.69), channel_id=1, source_target_pairs={{0,8},{8,16},{16,24},{24,0},{1,9},{9,17},{17,25},{25,1},{2,10},{10... | collective-permute-start | bytes 442376 | tf_op jit(solution)/shard_map/ppermute | solution.py:416
  12.6 22.5 %collective-permute-start.2 = (bf16[144,512]{1,0:T(8,128)(2,1)}, bf16[144,512]{1,0:T(8,128)(2,1)}, u32[]{:S(2)}, u32[]{:S(2)}) collective-permute-start(bf16[144,512]{1,0:T(8,128)(2,1)} %get-tuple-element.69), channel_id=1, source_target_pairs={{0,24},{8,0},{16,8},{24,16},{1,25},{9,1},{17,9},{25,17},{2,26},{10... | collective-permute-start | bytes 442376 | tf_op jit(solution)/shard_map/ppermute | solution.py:416
  15.3 9.0 %collective-permute-start.4 = (bf16[4,8192]{1,0:T(4,128)(2,1)S(1)}, bf16[4,8192]{1,0:T(4,128)(2,1)S(1)}, u32[]{:S(2)}, u32[]{:S(2)}) collective-permute-start(bf16[4,8192]{1,0:T(4,128)(2,1)S(1)} %bitcast.195), channel_id=1, source_target_pairs={{1,0},{2,1},{3,2},{5,4},{6,5},{7,6},{9,8},{10,9},{11,10},{13,12},{... | collective-permute-start | bytes 196616 | tf_op jit(solution)/shard_map/ppermute | solution.py:42
  16.9 7.5 %collective-permute-start.3 = (bf16[4,8192]{1,0:T(4,128)(2,1)S(1)}, bf16[4,8192]{1,0:T(4,128)(2,1)S(1)}, u32[]{:S(2)}, u32[]{:S(2)}) collective-permute-start(bf16[4,8192]{1,0:T(4,128)(2,1)S(1)} %bitcast.197), channel_id=1, source_target_pairs={{0,1},{1,2},{2,3},{4,5},{5,6},{6,7},{8,9},{9,10},{10,11},{12,13},{... | collective-permute-start | bytes 196616 | tf_op jit(solution)/shard_map/ppermute | solution.py:41
  25.1 1.3 %collective-permute-start.5 = (bf16[4,16,544]{2,1,0:T(8,128)(2,1)S(1)}, bf16[4,16,544]{2,1,0:T(8,128)(2,1)S(1)}, u32[]{:S(2)}, u32[]{:S(2)}) collective-permute-start(bf16[4,16,544]{2,1,0:T(8,128)(2,1)S(1)} %fusion.3), channel_id=1, source_target_pairs={{0,4},{4,0},{1,5},{5,1},{2,6},{6,2},{3,7},{7,3},{8,12},{12,8},{9,1... | collective-permute-start | bytes 208904 | tf_op jit(solution)/shard_map/ppermute | solution.py:34
  26.7 2.9 %copy-start = (bf16[3,256,256]{2,1,0:T(8,128)(2,1)S(1)}, bf16[3,256,256]{2,1,0:T(8,128)(2,1)}, u32[]{:S(2)}) copy-start(bf16[3,256,256]{2,1,0:T(8,128)(2,1)} %constant.134.clone.tb_ref.blk_ref) | copy-start | bytes 1179652
  26.7 2.9 %copy-start.1 = (f32[4,3]{1,0:T(4,128)S(1)}, f32[4,3]{1,0:T(4,128)}, u32[]{:S(2)}) copy-start(f32[4,3]{1,0:T(4,128)} %coef_ref.5) | copy-start | bytes 148
  37.7 1.2 %collective-permute-start.6 = (f32[4,12]{1,0:T(4,128)S(1)}, f32[4,12]{1,0:T(4,128)S(1)}, u32[]{:S(2)}, u32[]{:S(2)}) collective-permute-start(f32[4,12]{1,0:T(4,128)S(1)} %pad_maximum_fusion.9), channel_id=1, source_target_pairs={{0,4},{4,0},{1,5},{5,1},{2,6},{6,2},{3,7},{7,3},{8,12},{12,8},{9,1... | collective-permute-start | bytes 584 | tf_op jit(solution)/shard_map/ppermute | solution.py:106
  39.0 7.2 %collective-permute-start.7 = (f32[4,12]{1,0:T(4,128)S(1)}, f32[4,12]{1,0:T(4,128)S(1)}, u32[]{:S(2)}, u32[]{:S(2)}) collective-permute-start(f32[4,12]{1,0:T(4,128)S(1)} %fusion.36), channel_id=1, source_target_pairs={{0,1},{1,0},{2,3},{3,2},{4,5},{5,4},{6,7},{7,6},{8,9},{9,8},{10,11... | collective-permute-start | bytes 584 | tf_op jit(solution)/shard_map/ppermute | solution.py:106
  46.2 5.6 %collective-permute-start.8 = (f32[4,12]{1,0:T(4,128)S(1)}, f32[4,12]{1,0:T(4,128)S(1)}, u32[]{:S(2)}, u32[]{:S(2)}) collective-permute-start(f32[4,12]{1,0:T(4,128)S(1)} %add.243), channel_id=1, source_target_pairs={{0,2},{1,3},{2,0},{3,1},{4,6},{5,7},{6,4},{7,5},{8,10},{9,11},{10,... | collective-permute-start | bytes 584 | tf_op jit(solution)/shard_map/ppermute | solution.py:106
  60.7 10.1 %copy-start.7 = (bf16[256,512]{1,0:T(8,128)(2,1)S(1)}, bf16[256,512]{1,0:T(8,128)(2,1)}, u32[]{:S(2)}) copy-start(bf16[256,512]{1,0:T(8,128)(2,1)} %get-tuple-element.27) | copy-start | bytes 786436
  60.7 24.7 %copy-start.6 = (bf16[256,512]{1,0:T(8,128)(2,1)S(1)}, bf16[256,512]{1,0:T(8,128)(2,1)}, u32[]{:S(2)}) copy-start(bf16[256,512]{1,0:T(8,128)(2,1)} %get-tuple-element.28) | copy-start | bytes 786436
  60.7 10.1 %collective-permute-start.12 = (bf16[256,512]{1,0:T(8,128)(2,1)}, bf16[256,512]{1,0:T(8,128)(2,1)S(1)}, u32[]{:S(2)}, u32[]{:S(2)}) collective-permute-start(bf16[256,512]{1,0:T(8,128)(2,1)} %get-tuple-element.26), channel_id=1, source_target_pairs={{0,8},{8,16},{16,24},{24,0},{1,9},{9,17},{17,25},{25,1},{2,10},{10... | collective-permute-start | bytes 786440 | tf_op jit(solution)/shard_map/ppermute | solution.py:360
  68.5 29.0 %copy-start.8 = (bf16[256,512]{1,0:T(8,128)(2,1)S(1)}, bf16[256,512]{1,0:T(8,128)(2,1)}, u32[]{:S(2)}) copy-start(bf16[256,512]{1,0:T(8,128)(2,1)} %get-tuple-element.29) | copy-start | bytes 786436
  68.5 32.6 %copy-start.9 = (bf16[256,512]{1,0:T(8,128)(2,1)S(1)}, bf16[256,512]{1,0:T(8,128)(2,1)}, u32[]{:S(2)}) copy-start(bf16[256,512]{1,0:T(8,128)(2,1)} %get-tuple-element.25) | copy-start | bytes 786436
  68.5 11.3 %collective-permute-start.9 = (bf16[256,512]{1,0:T(8,128)(2,1)}, bf16[256,512]{1,0:T(8,128)(2,1)S(1)}, u32[]{:S(2)}, u32[]{:S(2)}) collective-permute-start(bf16[256,512]{1,0:T(8,128)(2,1)} %get-tuple-element.22), channel_id=1, source_target_pairs={{0,8},{8,16},{16,24},{24,0},{1,9},{9,17},{17,25},{25,1},{2,10},{10... | collective-permute-start | bytes 786440 | tf_op jit(solution)/shard_map/ppermute | solution.py:360
  70.9 14.5 %collective-permute-start.13 = (bf16[256,512]{1,0:T(8,128)(2,1)S(1)}, bf16[256,512]{1,0:T(8,128)(2,1)S(1)}, u32[]{:S(2)}, u32[]{:S(2)}) collective-permute-start(bf16[256,512]{1,0:T(8,128)(2,1)S(1)} %add_convert_fusion.1), channel_id=1, source_target_pairs={{0,8},{8,16},{16,24},{24,0},{1,9},{9,17},{17,25},{25,1},{2,10},{10... | collective-permute-start | bytes 786440 | tf_op jit(solution)/shard_map/ppermute | solution.py:360
  80.8 11.1 %collective-permute-start.10 = (bf16[256,512]{1,0:T(8,128)(2,1)S(1)}, bf16[256,512]{1,0:T(8,128)(2,1)S(1)}, u32[]{:S(2)}, u32[]{:S(2)}) collective-permute-start(bf16[256,512]{1,0:T(8,128)(2,1)S(1)} %add_convert_fusion.3), channel_id=1, source_target_pairs={{0,8},{8,16},{16,24},{24,0},{1,9},{9,17},{17,25},{25,1},{2,10},{10... | collective-permute-start | bytes 786440 | tf_op jit(solution)/shard_map/ppermute | solution.py:360
  85.4 12.0 %collective-permute-start.14 = (bf16[256,512]{1,0:T(8,128)(2,1)S(1)}, bf16[256,512]{1,0:T(8,128)(2,1)S(1)}, u32[]{:S(2)}, u32[]{:S(2)}) collective-permute-start(bf16[256,512]{1,0:T(8,128)(2,1)S(1)} %add_convert_fusion), channel_id=1, source_target_pairs={{0,8},{8,16},{16,24},{24,0},{1,9},{9,17},{17,25},{25,1},{2,10},{10... | collective-permute-start | bytes 786440 | tf_op jit(solution)/shard_map/ppermute | solution.py:360
  92.9 8.2 %collective-permute-start.11 = (bf16[256,512]{1,0:T(8,128)(2,1)S(1)}, bf16[256,512]{1,0:T(8,128)(2,1)S(1)}, u32[]{:S(2)}, u32[]{:S(2)}) collective-permute-start(bf16[256,512]{1,0:T(8,128)(2,1)S(1)} %add_convert_fusion.2), channel_id=1, source_target_pairs={{0,8},{8,16},{16,24},{24,0},{1,9},{9,17},{17,25},{25,1},{2,10},{10... | collective-permute-start | bytes 786440 | tf_op jit(solution)/shard_map/ppermute | solution.py:360
  (3 other events, 5.1 us)

commit v20 on v19

--- a/solution.py
+++ b/solution.py
@@ -285,13 +285,18 @@
     )(*operands)
 
 
-def warp_body(idx_ref, plane_ref, pick_ref, xrow_ref, ycol_ref, matched_ref, rmap_ref, cmap_ref,
+def warp_body(extent, idx_ref, plane_ref, pick_ref, origin_ref, matched_ref, rmap_ref, cmap_ref,
               *rest):
     out_refs, acc_ref = rest[:-1], rest[-1]
     e = pl.program_id(0)
+    side = matched_ref.shape[1]
+    across_index = lax.broadcasted_iota(jnp.int32, (side, side), 1) + origin_ref[0]
+    down_index = lax.broadcasted_iota(jnp.int32, (side, side), 0) + origin_ref[1]
+    xrow = (across_index.astype(jnp.float32) + 0.5) / extent[0] * 2.0 - 1.0
+    ycol = (down_index.astype(jnp.float32) + 0.5) / extent[1] * 2.0 - 1.0
     background = (
-        plane_ref[e, 0] + plane_ref[e, 1] * xrow_ref[...]
-    ) + plane_ref[e, 2] * ycol_ref[...]
+        plane_ref[e, 0] + plane_ref[e, 1] * xrow
+    ) + plane_ref[e, 2] * ycol
     corrected = (matched_ref[0] - background).astype(jnp.bfloat16)
     halfway = jnp.dot(rmap_ref[0], corrected, preferred_element_type=jnp.float32)
     warped = lax.dot_general(
@@ -317,7 +322,7 @@
             out_refs[v][...] = acc_ref[v].astype(jnp.bfloat16)
 
 
-def warp_tiles(choose, plane, picked, xrow, ycol, matched, bank, part, pieces):
+def warp_tiles(choose, plane, picked, origin, extent, matched, bank, part, pieces):
     exp_dev, tile_len = matched.shape[0], matched.shape[1]
     patches = picked.shape[1]
     rows = tile_len // pieces
@@ -327,8 +332,7 @@
         in_specs=[
             pl.BlockSpec(memory_space=pltpu.SMEM),
             pl.BlockSpec(memory_space=pltpu.SMEM),
-            pl.BlockSpec((1, tile_len), lambda e, idx: (0, 0)),
-            pl.BlockSpec((tile_len, 1), lambda e, idx: (0, 0)),
+            pl.BlockSpec(memory_space=pltpu.SMEM),
             pl.BlockSpec((1, tile_len, tile_len), lambda e, idx: (e, 0, 0)),
             pl.BlockSpec((1, rows, tile_len), lambda e, idx: (idx[e, 0], part, 0)),
             pl.BlockSpec((1, tile_len, tile_len), lambda e, idx: (idx[e, 1], 0, 0)),
@@ -341,14 +345,14 @@
     moved = moved + patches * rows * tile_len * 2
     vmem = 60 * 1024 * 1024
     return pl.pallas_call(
-        warp_body,
+        functools.partial(warp_body, extent),
         grid_spec=grid_spec,
         out_shape=[jax.ShapeDtypeStruct((rows, tile_len), jnp.bfloat16) for _ in range(patches)],
         compiler_params=pltpu.CompilerParams(
             dimension_semantics=("arbitrary",), vmem_limit_bytes=vmem
         ),
         cost_estimate=pl.CostEstimate(flops=flops, bytes_accessed=moved, transcendentals=0),
-    )(choose, plane, picked, xrow, ycol, matched, bank, bank)
+    )(choose, plane, picked, origin, matched, bank, bank)
 
 
 def ring_scatter(parts, axis, size):
@@ -481,8 +485,9 @@
     ).astype(jnp.float32)
     picked_ring = jnp.dot(picked.astype(jnp.float32), ring_order, precision=lax.Precision.HIGHEST)
     halves = [warp_tiles(
-        choose, plane_fit, picked_ring, xcoord.reshape(1, tile_len),
-        row_coord.reshape(tile_len, 1), matched, resample_bank, part, 2) for part in range(2)]
+        choose, plane_fit, picked_ring,
+        jnp.stack([col_pos * tile_len, row_pos * tile_len]).astype(jnp.int32),
+        (float(breadth), float(height)), matched, resample_bank, part, 2) for part in range(2)]
     numerator = jnp.concatenate(
         [ring_scatter(piece, "visit", visit_count) for piece in halves], 0
     )[None]

time: 104 us -> 103 us (level)
    sub x4 -> x2, other arithmetic: 1.41 us -> 0.08 us  [centred(): return (index.astype(jnp.float32) + 0.5) / length * 2.0 - 1.0]
where the time goes in v20:
time: 103 us; the launch traced here: 102 us
  waiting for transfers between devices  30.2 us (29%)
  Pallas kernels  29.6 us (29%)
  starting transfers between devices  18.1 us (18%)
  other arithmetic  15.5 us (15%)
  local copies, waits for them, and re-layouts  4.65 us (5%)
  matrix products  3.25 us (3%)
  between operations  1.09 us (1%)
    ppermute x6, waiting for transfers between devices, ring_scatter(): lax.ppermute(outgoing.astype(jnp.bfloat16), axis, ring).astype(jnp.float32)  28.4 us
    pallas_call x2, Pallas kernels, warp_tiles(): pl.pallas_call(functools.partial(warp_body, extent), grid_spec=grid_spec,...  14.5 us
    pallas_call x2, Pallas kernels, band_tiles(): pl.pallas_call(functools.partial(band_body, first), grid=(count,), in_spe...  9.66 us
    ppermute x3, starting transfers between devices, shards(): received.append(lax.ppermute(payload, 'visit', pairs))  7.86 us
    pallas_call x1, Pallas kernels, strip_tiles(): pl.pallas_call(strip_body, grid_spec=grid_spec, out_shape=jax.ShapeDtypeS...  5.43 us
    ppermute x1, starting transfers between devices, extended(): before = lax.ppermute(last, axis, up)  4.55 us
    ppermute x3, starting transfers between devices, butterfly_sum(): values = jax.tree.map(lambda v: v + lax.ppermute(v, axis, pairs), values)  4 us
    concatenate x1, other arithmetic, extended(): value = jnp.concatenate([before, value, after], axis=dim)  2.9 us
  transfers between devices with their start and end apart: 15, of which 8 were waited for; matrix products, arithmetic and copies ran while one was open for 11% of the time, Pallas kernels for 22%

profile of v20, /device:TPU:0, one launch (start us, length us, event | category | flops | bytes accessed | tf_op | source)
XLA Modules:
  0.0 102.4 jit_solution(970615442333954013)
XLA Ops:
  4.2 2.1 %convolution_convert_fusion = bf16[4,32,512]{2,1,0:T(8,128)(2,1)S(1)} fusion(bf16[4,512,512]{2,1,0:T(8,128)(2,1)} %param.11, s32[4]{0:T(128)S(1)} %get-tuple-element.58.off_ref), kind=kOutput, calls=%fused_computation.1 | convolution fusion | flops 67305472 | bytes 2228240 | tf_op jit(solution)/shard_map/esr,erl->esl/dot_general | solution.py:400
  7.0 4.0 %collective-permute-start.1 = (bf16[144,512]{1,0:T(8,128)(2,1)}, bf16[144,512]{1,0:T(8,128)(2,1)S(1)}, u32[]{:S(2)}, u32[]{:S(2)}) collective-permute-start(bf16[144,512]{1,0:T(8,128)(2,1)} %get-tuple-element.69), channel_id=1, source_target_pairs={{0,16},{8,24},{16,0},{24,8},{1,17},{9,25},{17,1},{25,9},{2,18},{10... | collective-permute-start | bytes 442376 | tf_op jit(solution)/shard_map/ppermute | solution.py:420
  11.0 1.6 %collective-permute-start = (bf16[144,512]{1,0:T(8,128)(2,1)}, bf16[144,512]{1,0:T(8,128)(2,1)}, u32[]{:S(2)}, u32[]{:S(2)}) collective-permute-start(bf16[144,512]{1,0:T(8,128)(2,1)} %get-tuple-element.69), channel_id=1, source_target_pairs={{0,8},{8,16},{16,24},{24,0},{1,9},{9,17},{17,25},{25,1},{2,10},{10... | collective-permute-start | bytes 442376 | tf_op jit(solution)/shard_map/ppermute | solution.py:420
  12.6 2.2 %collective-permute-start.2 = (bf16[144,512]{1,0:T(8,128)(2,1)}, bf16[144,512]{1,0:T(8,128)(2,1)}, u32[]{:S(2)}, u32[]{:S(2)}) collective-permute-start(bf16[144,512]{1,0:T(8,128)(2,1)} %get-tuple-element.69), channel_id=1, source_target_pairs={{0,24},{8,0},{16,8},{24,16},{1,25},{9,1},{17,9},{25,17},{2,26},{10... | collective-permute-start | bytes 442376 | tf_op jit(solution)/shard_map/ppermute | solution.py:420
  15.3 1.3 %collective-permute-start.4 = (bf16[4,8192]{1,0:T(4,128)(2,1)S(1)}, bf16[4,8192]{1,0:T(4,128)(2,1)S(1)}, u32[]{:S(2)}, u32[]{:S(2)}) collective-permute-start(bf16[4,8192]{1,0:T(4,128)(2,1)S(1)} %bitcast.197), channel_id=1, source_target_pairs={{1,0},{2,1},{3,2},{5,4},{6,5},{7,6},{9,8},{10,9},{11,10},{13,12},{... | collective-permute-start | bytes 196616 | tf_op jit(solution)/shard_map/ppermute | solution.py:42
  16.9 4.5 %collective-permute-start.3 = (bf16[4,8192]{1,0:T(4,128)(2,1)S(1)}, bf16[4,8192]{1,0:T(4,128)(2,1)S(1)}, u32[]{:S(2)}, u32[]{:S(2)}) collective-permute-start(bf16[4,8192]{1,0:T(4,128)(2,1)S(1)} %bitcast.199), channel_id=1, source_target_pairs={{0,1},{1,2},{2,3},{4,5},{5,6},{6,7},{8,9},{9,10},{10,11},{12,13},{... | collective-permute-start | bytes 196616 | tf_op jit(solution)/shard_map/ppermute | solution.py:41
  25.9 2.9 %pad_maximum_fusion.padded_ref = bf16[4,544,544]{2,1,0:T(8,128)(2,1)S(1)} fusion(bf16[4,16,544]{2,1,0:T(8,128)(2,1)S(1)} %get-tuple-element.71, bf16[4,512,16]{2,1,0:T(8,128)(2,1)} %bitcast.187, bf16[4,512,512]{2,1,0:T(8,128)(2,1)S(1)} %copy-done.3, bf16[4,512,16]{2,1,0:T(8,128)(2,1)} %bitcast.185, bf16[4,16,544]{2,1,0:T(8,128)(2,1)S(1)} %get-tuple-element.70), kind=kLoop, calls=%fused_computation | loop fusion | flops 11837440 | bytes 4734976 | tf_op jit(solution)/shard_map/concatenate | solution.py:46
  28.9 5.4 %shard_map.104 = f32[4,32,512]{2,1,0:T(8,128)S(1)} custom-call(s32[4]{0:T(128)S(1)} %get-tuple-element.58.off_ref, f32[4,3]{1,0:T(4,128)S(1)} %copy-done.1, bf16[3,256,256]{2,1,0:T(8,128)(2,1)S(1)} %copy-done, bf16[4,544,544]{2,1,0:T(8,128)(2,1)S(1)} %pad_maximum_fusion.padded_ref), custom_call_target="tpu_custom_call" | custom-call | flops 257949696 | bytes 2629632 | tf_op jit(solution)/shard_map/pallas_call | solution.py:217
  34.3 1.1 %pad_maximum_fusion.1 = bf16[4,144,512]{2,1,0:T(8,128)(2,1)S(1)} fusion(bf16[1,144,512]{2,1,0:T(8,128)(2,1)} %bitcast.12, bf16[1,144,512]{2,1,0:T(8,128)(2,1)S(1)} %bitcast.189, bf16[1,144,512]{2,1,0:T(8,128)(2,1)} %bitcast.10, bf16[1,144,512]{2,1,0:T(8,128)(2,1)S(1)} %get-tuple-element.68), kind=kLoop, calls=%fused_computation.3 | loop fusion | flops 884736 | bytes 1179648 | tf_op jit(solution)/shard_map/stack | solution.py:421
  37.1 1.1 %collective-permute-done.6 = f32[4,12]{1,0:T(4,128)S(1)} collective-permute-done((f32[4,12]{1,0:T(4,128)S(1)}, f32[4,12]{1,0:T(4,128)S(1)}, u32[]{:S(2)}, u32[]{:S(2)}) %collective-permute-start.6) | collective-permute-done | bytes 224 | tf_op jit(solution)/shard_map/ppermute | solution.py:106
  38.2 2.4 %collective-permute-start.7 = (f32[4,12]{1,0:T(4,128)S(1)}, f32[4,12]{1,0:T(4,128)S(1)}, u32[]{:S(2)}, u32[]{:S(2)}) collective-permute-start(f32[4,12]{1,0:T(4,128)S(1)} %fusion.36), channel_id=1, source_target_pairs={{0,1},{1,0},{2,3},{3,2},{4,5},{5,4},{6,7},{7,6},{8,9},{9,8},{10,11... | collective-permute-start | bytes 584 | tf_op jit(solution)/shard_map/ppermute | solution.py:106
  40.6 4.9 %shard_map.105.rest_0_ = f32[4,512,512]{2,1,0:T(8,128)} custom-call(f32[4,3]{1,0:T(4,128)S(1)} %copy-done.1, bf16[3,256,256]{2,1,0:T(8,128)(2,1)S(1)} %copy-done, bf16[4,544,544]{2,1,0:T(8,128)(2,1)S(1)} %pad_maximum_fusion.padded_ref), custom_call_target="tpu_custom_call" | custom-call | flops 1660944384 | bytes 3280896 | tf_op jit(solution)/shard_map/pallas_call | solution.py:274
  45.5 1.6 %collective-permute-start.8 = (f32[4,12]{1,0:T(4,128)S(1)}, f32[4,12]{1,0:T(4,128)S(1)}, u32[]{:S(2)}, u32[]{:S(2)}) collective-permute-start(f32[4,12]{1,0:T(4,128)S(1)} %add.189), channel_id=1, source_target_pairs={{0,2},{1,3},{2,0},{3,1},{4,6},{5,7},{6,4},{7,5},{8,10},{9,11},{10,... | collective-permute-start | bytes 584 | tf_op jit(solution)/shard_map/ppermute | solution.py:106
  47.1 4.8 %shard_map.106.matched_ref = f32[4,512,512]{2,1,0:T(8,128)} custom-call(f32[4,3]{1,0:T(4,128)S(1)} %copy-done.1, bf16[3,256,256]{2,1,0:T(8,128)(2,1)S(1)} %copy-done, bf16[4,544,544]{2,1,0:T(8,128)(2,1)S(1)} %pad_maximum_fusion.padded_ref, f32[4,512,512]{2,1,0:T(8,128)} %shard_map.105.rest_0_), custom_call_target="tpu_custom_call", output_to_operand_aliasing={{}: (3, {})} | custom-call | flops 1660944384 | bytes 3280896 | tf_op jit(solution)/shard_map/pallas_call | solution.py:274
  53.3 7.2 %shard_map.108 = (bf16[256,512]{1,0:T(8,128)(2,1)}, bf16[256,512]{1,0:T(8,128)(2,1)}, bf16[256,512]{1,0:T(8,128)(2,1)}, bf16[256,512]{1,0:T(8,128)(2,1)}) custom-call(s32[4,2]{1,0:T(4,128)} %copy.98.idx_ref, f32[4,3]{1,0:T(4,128)} %pad_maximum_fusion.11.plane_ref, f32[4,4]{1,0:T(4,128)} %fusion.18.pick_ref, s32[2]{0:T(128)} %pad_add_fusion.origin_ref, ...), custom_call_target="tpu_custom_call" | custom-call | flops 1073741824 | bytes 8388608 | tf_op jit(solution)/shard_map/pallas_call | solution.py:347
  60.6 7.3 %shard_map.107 = (bf16[256,512]{1,0:T(8,128)(2,1)}, bf16[256,512]{1,0:T(8,128)(2,1)}, bf16[256,512]{1,0:T(8,128)(2,1)}, bf16[256,512]{1,0:T(8,128)(2,1)}) custom-call(s32[4,2]{1,0:T(4,128)} %copy.98.idx_ref, f32[4,3]{1,0:T(4,128)} %pad_maximum_fusion.11.plane_ref, f32[4,4]{1,0:T(4,128)} %fusion.18.pick_ref, s32[2]{0:T(128)} %pad_add_fusion.origin_ref, ...), custom_call_target="tpu_custom_call" | custom-call | flops 1073741824 | bytes 8388608 | tf_op jit(solution)/shard_map/pallas_call | solution.py:347
  68.0 2.7 %collective-permute-done.12 = bf16[256,512]{1,0:T(8,128)(2,1)S(1)} collective-permute-done((bf16[256,512]{1,0:T(8,128)(2,1)}, bf16[256,512]{1,0:T(8,128)(2,1)S(1)}, u32[]{:S(2)}, u32[]{:S(2)}) %collective-permute-start.12) | collective-permute-done | bytes 262176 | tf_op jit(solution)/shard_map/ppermute | solution.py:364
  70.8 8.3 %collective-permute-done.9 = bf16[256,512]{1,0:T(8,128)(2,1)S(1)} collective-permute-done((bf16[256,512]{1,0:T(8,128)(2,1)}, bf16[256,512]{1,0:T(8,128)(2,1)S(1)}, u32[]{:S(2)}, u32[]{:S(2)}) %collective-permute-start.9) | collective-permute-done | bytes 262176 | tf_op jit(solution)/shard_map/ppermute | solution.py:364
  80.2 4.5 %collective-permute-done.13 = bf16[256,512]{1,0:T(8,128)(2,1)S(1)} collective-permute-done((bf16[256,512]{1,0:T(8,128)(2,1)S(1)}, bf16[256,512]{1,0:T(8,128)(2,1)S(1)}, u32[]{:S(2)}, u32[]{:S(2)}) %collective-permute-start.13) | collective-permute-done | bytes 262176 | tf_op jit(solution)/shard_map/ppermute | solution.py:364
  84.9 6.4 %collective-permute-done.10 = bf16[256,512]{1,0:T(8,128)(2,1)S(1)} collective-permute-done((bf16[256,512]{1,0:T(8,128)(2,1)S(1)}, bf16[256,512]{1,0:T(8,128)(2,1)S(1)}, u32[]{:S(2)}, u32[]{:S(2)}) %collective-permute-start.10) | collective-permute-done | bytes 262176 | tf_op jit(solution)/shard_map/ppermute | solution.py:364
  91.3 1.0 add_convert_fusion.2
  94.0 2.9 %collective-permute-done.14 = bf16[256,512]{1,0:T(8,128)(2,1)S(1)} collective-permute-done((bf16[256,512]{1,0:T(8,128)(2,1)S(1)}, bf16[256,512]{1,0:T(8,128)(2,1)S(1)}, u32[]{:S(2)}, u32[]{:S(2)}) %collective-permute-start.14) | collective-permute-done | bytes 262176 | tf_op jit(solution)/shard_map/ppermute | solution.py:364
  97.0 3.6 %collective-permute-done.11 = bf16[256,512]{1,0:T(8,128)(2,1)S(1)} collective-permute-done((bf16[256,512]{1,0:T(8,128)(2,1)S(1)}, bf16[256,512]{1,0:T(8,128)(2,1)S(1)}, u32[]{:S(2)}, u32[]{:S(2)}) %collective-permute-start.11) | collective-permute-done | bytes 262176 | tf_op jit(solution)/shard_map/ppermute | solution.py:364
  100.6 1.8 %maximum_divide_fusion = f32[1,512,512]{2,1,0:T(8,128)} fusion(f32[1,256,512]{2,1,0:T(8,128)S(1)} %add_bitcast_fusion, f32[1,256,512]{2,1,0:T(8,128)S(1)} %add_bitcast_fusion.1, f32[]{:T(128)} %convert_reduce_fusion), kind=kLoop, calls=%fused_computation.2 | loop fusion | flops 524288 | bytes 2097156 | tf_op jit(solution)/shard_map/div | solution.py:494
  (111 shorter events, 15.7 us)
Async XLA Ops:
  0.6 14.2 %copy-start.2 = (bf16[4,512,512]{2,1,0:T(8,128)(2,1)S(1)}, bf16[4,512,512]{2,1,0:T(8,128)(2,1)}, u32[]{:S(2)}) copy-start(bf16[4,512,512]{2,1,0:T(8,128)(2,1)} %param.11) | copy-start | bytes 6291460
  4.1 17.9 %copy-start.11 = (s32[4,1,1,2]{0,3,2,1:T(2,128)S(1)}, s32[4,1,1,2]{0,3,2,1:T(2,128)}, u32[]{:S(2)}) copy-start(s32[4,1,1,2]{0,3,2,1:T(2,128)} %param.16) | copy-start | bytes 100
  4.1 18.6 %copy-start.12 = (bf16[4,1,1]{0,2,1:T(2,128)(2,1)S(1)}, bf16[4,1,1]{0,2,1:T(2,128)(2,1)}, u32[]{:S(2)}) copy-start(bf16[4,1,1]{0,2,1:T(2,128)(2,1)} %param.14) | copy-start | bytes 28
  7.0 27.4 %collective-permute-start.1 = (bf16[144,512]{1,0:T(8,128)(2,1)}, bf16[144,512]{1,0:T(8,128)(2,1)S(1)}, u32[]{:S(2)}, u32[]{:S(2)}) collective-permute-start(bf16[144,512]{1,0:T(8,128)(2,1)} %get-tuple-element.69), channel_id=1, source_target_pairs={{0,16},{8,24},{16,0},{24,8},{1,17},{9,25},{17,1},{25,9},{2,18},{10... | collective-permute-start | bytes 442376 | tf_op jit(solution)/shard_map/ppermute | solution.py:420
  11.0 23.3 %collective-permute-start = (bf16[144,512]{1,0:T(8,128)(2,1)}, bf16[144,512]{1,0:T(8,128)(2,1)}, u32[]{:S(2)}, u32[]{:S(2)}) collective-permute-start(bf16[144,512]{1,0:T(8,128)(2,1)} %get-tuple-element.69), channel_id=1, source_target_pairs={{0,8},{8,16},{16,24},{24,0},{1,9},{9,17},{17,25},{25,1},{2,10},{10... | collective-permute-start | bytes 442376 | tf_op jit(solution)/shard_map/ppermute | solution.py:420
  12.6 21.8 %collective-permute-start.2 = (bf16[144,512]{1,0:T(8,128)(2,1)}, bf16[144,512]{1,0:T(8,128)(2,1)}, u32[]{:S(2)}, u32[]{:S(2)}) collective-permute-start(bf16[144,512]{1,0:T(8,128)(2,1)} %get-tuple-element.69), channel_id=1, source_target_pairs={{0,24},{8,0},{16,8},{24,16},{1,25},{9,1},{17,9},{25,17},{2,26},{10... | collective-permute-start | bytes 442376 | tf_op jit(solution)/shard_map/ppermute | solution.py:420
  15.3 8.2 %collective-permute-start.4 = (bf16[4,8192]{1,0:T(4,128)(2,1)S(1)}, bf16[4,8192]{1,0:T(4,128)(2,1)S(1)}, u32[]{:S(2)}, u32[]{:S(2)}) collective-permute-start(bf16[4,8192]{1,0:T(4,128)(2,1)S(1)} %bitcast.197), channel_id=1, source_target_pairs={{1,0},{2,1},{3,2},{5,4},{6,5},{7,6},{9,8},{10,9},{11,10},{13,12},{... | collective-permute-start | bytes 196616 | tf_op jit(solution)/shard_map/ppermute | solution.py:42
  16.9 6.7 %collective-permute-start.3 = (bf16[4,8192]{1,0:T(4,128)(2,1)S(1)}, bf16[4,8192]{1,0:T(4,128)(2,1)S(1)}, u32[]{:S(2)}, u32[]{:S(2)}) collective-permute-start(bf16[4,8192]{1,0:T(4,128)(2,1)S(1)} %bitcast.199), channel_id=1, source_target_pairs={{0,1},{1,2},{2,3},{4,5},{5,6},{6,7},{8,9},{9,10},{10,11},{12,13},{... | collective-permute-start | bytes 196616 | tf_op jit(solution)/shard_map/ppermute | solution.py:41
  24.3 1.3 %collective-permute-start.5 = (bf16[4,16,544]{2,1,0:T(8,128)(2,1)S(1)}, bf16[4,16,544]{2,1,0:T(8,128)(2,1)S(1)}, u32[]{:S(2)}, u32[]{:S(2)}) collective-permute-start(bf16[4,16,544]{2,1,0:T(8,128)(2,1)S(1)} %fusion.3), channel_id=1, source_target_pairs={{0,4},{4,0},{1,5},{5,1},{2,6},{6,2},{3,7},{7,3},{8,12},{12,8},{9,1... | collective-permute-start | bytes 208904 | tf_op jit(solution)/shard_map/ppermute | solution.py:34
  25.9 2.9 %copy-start.1 = (f32[4,3]{1,0:T(4,128)S(1)}, f32[4,3]{1,0:T(4,128)}, u32[]{:S(2)}) copy-start(f32[4,3]{1,0:T(4,128)} %coef_ref.5) | copy-start | bytes 148
  28.9 6.6 %copy-start.10 = (s32[4]{0:T(128)S(1)}, s32[4]{0:T(128)}, u32[]{:S(2)}) copy-start(s32[4]{0:T(128)} %get-tuple-element.82) | copy-start | bytes 52
  37.0 1.2 %collective-permute-start.6 = (f32[4,12]{1,0:T(4,128)S(1)}, f32[4,12]{1,0:T(4,128)S(1)}, u32[]{:S(2)}, u32[]{:S(2)}) collective-permute-start(f32[4,12]{1,0:T(4,128)S(1)} %pad_maximum_fusion.9), channel_id=1, source_target_pairs={{0,4},{4,0},{1,5},{5,1},{2,6},{6,2},{3,7},{7,3},{8,12},{12,8},{9,1... | collective-permute-start | bytes 584 | tf_op jit(solution)/shard_map/ppermute | solution.py:106
  38.2 7.3 %collective-permute-start.7 = (f32[4,12]{1,0:T(4,128)S(1)}, f32[4,12]{1,0:T(4,128)S(1)}, u32[]{:S(2)}, u32[]{:S(2)}) collective-permute-start(f32[4,12]{1,0:T(4,128)S(1)} %fusion.36), channel_id=1, source_target_pairs={{0,1},{1,0},{2,3},{3,2},{4,5},{5,4},{6,7},{7,6},{8,9},{9,8},{10,11... | collective-permute-start | bytes 584 | tf_op jit(solution)/shard_map/ppermute | solution.py:106
  45.5 6.4 %collective-permute-start.8 = (f32[4,12]{1,0:T(4,128)S(1)}, f32[4,12]{1,0:T(4,128)S(1)}, u32[]{:S(2)}, u32[]{:S(2)}) collective-permute-start(f32[4,12]{1,0:T(4,128)S(1)} %add.189), channel_id=1, source_target_pairs={{0,2},{1,3},{2,0},{3,1},{4,6},{5,7},{6,4},{7,5},{8,10},{9,11},{10,... | collective-permute-start | bytes 584 | tf_op jit(solution)/shard_map/ppermute | solution.py:106
  60.5 10.2 %copy-start.7 = (bf16[256,512]{1,0:T(8,128)(2,1)S(1)}, bf16[256,512]{1,0:T(8,128)(2,1)}, u32[]{:S(2)}) copy-start(bf16[256,512]{1,0:T(8,128)(2,1)} %get-tuple-element.27) | copy-start | bytes 786436
  60.5 24.3 %copy-start.6 = (bf16[256,512]{1,0:T(8,128)(2,1)S(1)}, bf16[256,512]{1,0:T(8,128)(2,1)}, u32[]{:S(2)}) copy-start(bf16[256,512]{1,0:T(8,128)(2,1)} %get-tuple-element.28) | copy-start | bytes 786436
  60.5 10.2 %collective-permute-start.12 = (bf16[256,512]{1,0:T(8,128)(2,1)}, bf16[256,512]{1,0:T(8,128)(2,1)S(1)}, u32[]{:S(2)}, u32[]{:S(2)}) collective-permute-start(bf16[256,512]{1,0:T(8,128)(2,1)} %get-tuple-element.26), channel_id=1, source_target_pairs={{0,8},{8,16},{16,24},{24,0},{1,9},{9,17},{17,25},{25,1},{2,10},{10... | collective-permute-start | bytes 786440 | tf_op jit(solution)/shard_map/ppermute | solution.py:364
  67.9 29.0 %copy-start.8 = (bf16[256,512]{1,0:T(8,128)(2,1)S(1)}, bf16[256,512]{1,0:T(8,128)(2,1)}, u32[]{:S(2)}) copy-start(bf16[256,512]{1,0:T(8,128)(2,1)} %get-tuple-element.29) | copy-start | bytes 786436
  67.9 32.6 %copy-start.9 = (bf16[256,512]{1,0:T(8,128)(2,1)S(1)}, bf16[256,512]{1,0:T(8,128)(2,1)}, u32[]{:S(2)}) copy-start(bf16[256,512]{1,0:T(8,128)(2,1)} %get-tuple-element.25) | copy-start | bytes 786436
  67.9 11.2 %collective-permute-start.9 = (bf16[256,512]{1,0:T(8,128)(2,1)}, bf16[256,512]{1,0:T(8,128)(2,1)S(1)}, u32[]{:S(2)}, u32[]{:S(2)}) collective-permute-start(bf16[256,512]{1,0:T(8,128)(2,1)} %get-tuple-element.22), channel_id=1, source_target_pairs={{0,8},{8,16},{16,24},{24,0},{1,9},{9,17},{17,25},{25,1},{2,10},{10... | collective-permute-start | bytes 786440 | tf_op jit(solution)/shard_map/ppermute | solution.py:364
  70.7 14.0 %collective-permute-start.13 = (bf16[256,512]{1,0:T(8,128)(2,1)S(1)}, bf16[256,512]{1,0:T(8,128)(2,1)S(1)}, u32[]{:S(2)}, u32[]{:S(2)}) collective-permute-start(bf16[256,512]{1,0:T(8,128)(2,1)S(1)} %add_convert_fusion.1), channel_id=1, source_target_pairs={{0,8},{8,16},{16,24},{24,0},{1,9},{9,17},{17,25},{25,1},{2,10},{10... | collective-permute-start | bytes 786440 | tf_op jit(solution)/shard_map/ppermute | solution.py:364
  80.2 11.1 %collective-permute-start.10 = (bf16[256,512]{1,0:T(8,128)(2,1)S(1)}, bf16[256,512]{1,0:T(8,128)(2,1)S(1)}, u32[]{:S(2)}, u32[]{:S(2)}) collective-permute-start(bf16[256,512]{1,0:T(8,128)(2,1)S(1)} %add_convert_fusion.3), channel_id=1, source_target_pairs={{0,8},{8,16},{16,24},{24,0},{1,9},{9,17},{17,25},{25,1},{2,10},{10... | collective-permute-start | bytes 786440 | tf_op jit(solution)/shard_map/ppermute | solution.py:364
  84.8 12.0 %collective-permute-start.14 = (bf16[256,512]{1,0:T(8,128)(2,1)S(1)}, bf16[256,512]{1,0:T(8,128)(2,1)S(1)}, u32[]{:S(2)}, u32[]{:S(2)}) collective-permute-start(bf16[256,512]{1,0:T(8,128)(2,1)S(1)} %add_convert_fusion), channel_id=1, source_target_pairs={{0,8},{8,16},{16,24},{24,0},{1,9},{9,17},{17,25},{25,1},{2,10},{10... | collective-permute-start | bytes 786440 | tf_op jit(solution)/shard_map/ppermute | solution.py:364
  92.3 8.3 %collective-permute-start.11 = (bf16[256,512]{1,0:T(8,128)(2,1)S(1)}, bf16[256,512]{1,0:T(8,128)(2,1)S(1)}, u32[]{:S(2)}, u32[]{:S(2)}) collective-permute-start(bf16[256,512]{1,0:T(8,128)(2,1)S(1)} %add_convert_fusion.2), channel_id=1, source_target_pairs={{0,8},{8,16},{16,24},{24,0},{1,9},{9,17},{17,25},{25,1},{2,10},{10... | collective-permute-start | bytes 786440 | tf_op jit(solution)/shard_map/ppermute | solution.py:364
  (4 other events, 8.0 us)
